TPU v7x, 32 devices: a whole 2x2x4 slice. The times are simulated.
32 devices in a mesh: bucket: 4 (over y, x), group: 8 (over z, core).
Axes of the slice: x: 2, y: 2, z: 4, core: 2. Of those that a mesh axis runs over, the one named last changes fastest.
Arguments:
- embeddings: bfloat16 [4, 8, 4, 128, 768], P('bucket', 'group'), may hold values from -6 to 6
- counts: int32 [4, 8, 4, 1], P('bucket', 'group'), may hold values from 42 to 128, as said below
Outputs:
- neighbour_sums: bfloat16 [4, 8, 512, 768], P('bucket', 'group')
Inputs may be any that keep to these rules, and one draw needn't show every extreme that they name: `counts`: each count is a live prefix of its 128 slots; in every draw some slot range is full.
All inputs are finite; a program needn't handle non-finite values.
Results may differ from a plain program's by a relative error of at most 0.0052.
Values may be sent and summed in bfloat16 or wider, within the bound.
No kernel may reach another device: no remote copies, remote signals or barrier semaphores. Data moves between devices by JAX's collectives and lax.ppermute only.
A program may use at most 128 MiB of HBM per device.

v0:
```python
import jax
import jax.numpy as jnp
from jax import lax
from jax.sharding import PartitionSpec as P

ROUNDS = 4


EPS = 1e-06
TEMP = 12.0


def normalize(block):
    values = block.astype(jnp.float32)
    return (values * lax.rsqrt(jnp.sum(values * values, axis=-1, keepdims=True) + EPS)).astype(
        jnp.bfloat16
    )


def weigh(unit_a, unit_b, live_b, extra):
    scores = jnp.dot(unit_a, unit_b.T, preferred_element_type=jnp.float32)
    return jnp.exp(TEMP * scores) * live_b[None, :] * extra


def per_device(embeddings, counts):
    slabs, slab_counts = (
        lax.all_to_all(embeddings, "bucket", split_axis=2, concat_axis=0, tiled=True),
        lax.all_to_all(counts, "bucket", split_axis=2, concat_axis=0, tiled=True),
    )
    sources = slabs.shape[0]
    slot_rows = slabs.shape[3]
    width = slabs.shape[4]
    rows = sources * slot_rows
    data = slabs.reshape(rows, width)
    slot_index = lax.broadcasted_iota(jnp.int32, (sources, slot_rows), 1)
    live = (slot_index < slab_counts.reshape(sources, 1)).astype(jnp.float32).reshape(rows)
    marks = live.astype(jnp.bfloat16)
    unit = normalize(data)
    not_self = 1.0 - jnp.eye(rows, dtype=jnp.float32)
    own = weigh(unit, unit, live, not_self)
    summed = jnp.dot(own.astype(jnp.bfloat16), data, preferred_element_type=jnp.float32)
    squares = jnp.sum(own * own, axis=1)
    all_data, all_marks = (
        lax.all_gather(data, "group", axis=0, tiled=True),
        lax.all_gather(marks, "group", axis=0, tiled=True),
    )
    blocks = lax.axis_size("group")
    position = lax.axis_index("group")
    for dist in range(1, ROUNDS + 1):
        for sign in (1, -1):
            other = (position + sign * dist) % blocks
            start = other * rows
            got_data = lax.dynamic_slice_in_dim(all_data, start, rows, 0)
            got_live = lax.dynamic_slice_in_dim(all_marks, start, rows, 0).astype(jnp.float32)
            weights = weigh(unit, normalize(got_data), got_live, 1.0)
            summed = summed + jnp.dot(
                weights.astype(jnp.bfloat16), got_data, preferred_element_type=jnp.float32
            )
            squares = squares + jnp.sum(weights * weights, axis=1)
    result = summed * lax.rsqrt(squares)[:, None] * live[:, None]
    return result.astype(jnp.bfloat16).reshape(1, 1, rows, width)


def solution(mesh):
    in_specs = (P("bucket", "group", None, None, None), P("bucket", "group", None, None))
    out_specs = P("bucket", "group", None, None)
    return jax.shard_map(
        per_device, mesh=mesh, in_specs=in_specs, out_specs=out_specs, check_vma=False
    )
```

profile of v0, /device:TPU:0, one launch (start us, length us, event | category | flops | bytes accessed | tf_op | source)
XLA Modules:
  0.0 112.1 jit_solution(2783596257850077988)
XLA Ops:
  6.5 0.0 copy-start.2
  6.5 0.0 all-gather.3.cloned.1.call-start
  6.5 17.3 %all_to_all.8 = bf16[1,1,4,128,768]{4,3,1,0,2:T(8,128)(2,1)} all-to-all(bf16[1,1,4,128,768]{4,3,1,0,2:T(8,128)(2,1)} %bitcast.36), channel_id=1, replica_groups=mesh['bucket'=4,'group'=8] {'bucket'}, dimensions={2} | all-to-all | bytes 1572864 | tf_op jit(solution)/shard_map/all_to_all | solution.py:27
  23.8 0.0 copy-start
  23.8 0.0 all-gather.3.cloned.1.call-update
  23.9 0.0 copy-done.2
  23.9 0.7 copy.6
  24.5 3.2 %all-to-all-start.1 = ((s32[1,1,4,1]{3,1,0,2:T(1,128)}), s32[1,1,4,1]{3,1,0,2:T(1,128)S(1)}, u32[]{:S(2)}, u32[]{:S(2)}) async-start(s32[1,1,4,1]{3,1,0,2:T(1,128)} %copy.6), calls=%async_computation.1 | async-start | bytes 4096 | tf_op jit(solution)/shard_map/all_to_all | solution.py:28
  27.9 4.4 %all-to-all-done.1 = s32[1,1,4,1]{3,1,0,2:T(1,128)S(1)} async-done(((s32[1,1,4,1]{3,1,0,2:T(1,128)}), s32[1,1,4,1]{3,1,0,2:T(1,128)S(1)}, u32[]{:S(2)}, u32[]{:S(2)}) %all-to-all-start.1) | async-done | bytes 48 | tf_op jit(solution)/shard_map/all_to_all | solution.py:28
  32.3 0.2 reduce.1
  32.5 0.1 convert_bitcast_fusion
  32.6 13.6 %all-gather = bf16[8,1,512]{2,1,0:T(2,128)(2,1)S(1)} all-gather(bf16[1,1,512]{2,1,0:T(2,128)(2,1)S(1)} %reshape.165), channel_id=1, replica_groups=mesh['bucket'=4,'group'=8] {'group'}, dimensions={0}, use_global_device_ids=true | all-gather | bytes 9216 | tf_op jit(solution)/shard_map/all_gather | solution.py:45
  46.3 0.1 dynamic-slice_convert_fusion
  46.4 0.0 copy-done
  46.4 0.2 fusion
  46.6 0.2 multiply_convert_fusion.1
  46.8 0.2 fusion.1
  47.0 0.7 multiply_reduce_fusion.8
  47.8 0.6 fusion.85
  48.4 40.3 %all-gather.3.cloned.1.call-done = bf16[4096,768]{1,0:T(8,128)(2,1)} async-done(((bf16[512,768]{1,0:T(8,128)(2,1)}), bf16[4096,768]{1,0:T(8,128)(2,1)}) %all-gather.3.cloned.1.call-update) | async-done | bytes 6291472 | tf_op jit(solution)/shard_map/all_gather | solution.py:44
  88.6 0.0 copy-start.1
  88.6 4.2 %fusion.16 = (f32[512]{0:T(512)S(1)}, f32[512]{0:T(512)S(1)}, f32[512]{0:T(512)S(1)}, f32[512]{0:T(512)S(1)}, f32[512]{0:T(512)S(1)}, /*index=5*/f32[512]{0:T(512)S(1)}, f32[512]{0:T(512)S(1)}, f32[512]{0:T(512)S(1)}) fusion(bf16[4096,768]{1,0:T(8,128)(2,1)} %all-gather.3.cloned.1.call-done, s32[]{:T(128)S(6)} %select_n.82, s32[]{:T(128)S(6)} %select_n.80, ...), kind=kLoop, calls=%fused_computation.34 | loop fusion | flops 9433088 | bytes 6307872 | tf_op jit(solution)/shard_map/reduce_sum | solution.py:15
  93.0 0.4 copy-done.1
  93.3 0.7 multiply_reduce_fusion.1
  94.0 0.7 multiply_reduce_fusion.2
  94.8 0.7 multiply_reduce_fusion.3
  95.5 0.7 multiply_reduce_fusion.4
  96.2 0.7 multiply_reduce_fusion.5
  97.0 0.7 multiply_reduce_fusion.6
  97.7 0.7 multiply_reduce_fusion.7
  98.4 0.7 multiply_reduce_fusion
  99.2 0.6 fusion.57
  99.8 0.6 fusion.60
  100.4 0.6 fusion.63
  101.0 0.6 fusion.66
  101.6 0.6 fusion.69
  102.2 0.6 fusion.72
  102.8 0.6 fusion.75
  103.4 1.8 %fusion.37 = bf16[1,1,512,768]{3,2,1,0:T(8,128)(2,1)} fusion(f32[512,768]{1,0:T(8,128)S(1)} %fusion.57, f32[512,768]{1,0:T(8,128)S(1)} %fusion.60, f32[512,768]{1,0:T(8,128)S(1)} %fusion.63, f32[512,768]{1,0:T(8,128)S(1)} %fusion.66, f32[512,768]{1,0:T(8,128)S(1)} %fusion.69, f32[512,768]{1,0:T(8,128)S(1)} %fusion.72, f32[512,768]{1,0:T(8,128)S(1)} %fusion.85, ...), kind=kOutput, calls=%fused_computation.66 | convolution fusion | flops 406978560 | bytes 14684164 | tf_op jit(solution)/shard_map/dot_general | solution.py:56
  (9 shorter events, 0.1 us)
Async XLA Ops:
  6.5 17.3 %copy-start.2 = (s32[1,1,4,1]{2,3,1,0:T(1,128)S(1)}, s32[1,1,4,1]{2,3,1,0:T(1,128)}, u32[]{:S(2)}) copy-start(s32[1,1,4,1]{2,3,1,0:T(1,128)} %param.3) | copy-start | bytes 52
  6.5 82.1 %all-gather.3.cloned.1.call-start = ((), (), s32[]{:S(2)}) async-start(), calls=%async_computation.2 | async-start | bytes 7077888 | tf_op jit(solution)/shard_map/all_gather | solution.py:44
  23.8 22.5 %copy-start = (bf16[1,1,4,128,768]{4,3,1,0,2:T(8,128)(2,1)S(1)}, bf16[1,1,4,128,768]{4,3,1,0,2:T(8,128)(2,1)}, u32[]{:S(2)}) copy-start(bf16[1,1,4,128,768]{4,3,1,0,2:T(8,128)(2,1)} %all_to_all.8) | copy-start | bytes 2359300
  24.5 7.8 %all-to-all-start.1 = ((s32[1,1,4,1]{3,1,0,2:T(1,128)}), s32[1,1,4,1]{3,1,0,2:T(1,128)S(1)}, u32[]{:S(2)}, u32[]{:S(2)}) async-start(s32[1,1,4,1]{3,1,0,2:T(1,128)} %copy.6), calls=%async_computation.1 | async-start | bytes 4096 | tf_op jit(solution)/shard_map/all_to_all | solution.py:28
  88.6 4.7 %copy-start.1 = (bf16[4096,768]{1,0:T(8,128)(2,1)S(1)}, bf16[4096,768]{1,0:T(8,128)(2,1)}, u32[]{:S(2)}) copy-start(bf16[4096,768]{1,0:T(8,128)(2,1)} %all-gather.3.cloned.1.call-done) | copy-start | bytes 18874372
Sparse Core Ops, SparseCore 0:
  24.0 64.6 all-gather.2
where the time goes:
time: 112 us
  waiting for transfers between devices  44.7 us (40%)
  blocking collectives  30.9 us (28%)
  between operations  13.7 us (12%)
  matrix products  13.2 us (12%)
  other arithmetic  5.33 us (5%)
  starting transfers between devices  3.22 us (3%)
    all_gather x1, waiting for transfers between devices, per_device(): lax.all_gather(data, 'group', axis=0, tiled=True)  40.3 us
    all_to_all x1, blocking collectives, per_device(): lax.all_to_all(embeddings, 'bucket', split_axis=2, concat_axis=0, tiled=T...  17.3 us
    all_gather x1, blocking collectives, per_device(): lax.all_gather(marks, 'group', axis=0, tiled=True)  13.6 us
    dot_general x9, matrix products, weigh(): scores = jnp.dot(unit_a, unit_b.T, preferred_element_type=jnp.float32)  6.57 us
    dot_general x8, matrix products, per_device(): jnp.dot(weights.astype(jnp.bfloat16), got_data, preferred_element_type=jn...  6.04 us
    reduce_sum x2, other arithmetic, normalize(): jnp.sum(values * values, axis=-1, keepdims=True) + EPS  4.47 us
    all_to_all x1, waiting for transfers between devices, per_device(): lax.all_to_all(counts, 'bucket', split_axis=2, concat_axis=0, tiled=True)  4.43 us
    all_to_all x1, starting transfers between devices, per_device(): lax.all_to_all(counts, 'bucket', split_axis=2, concat_axis=0, tiled=True)  3.22 us
  transfers between devices with their start and end apart: 2, of which 2 were waited for; matrix products, arithmetic and copies ran while one was open for 3% of the time, Pallas kernels for 0%

commit v1 on v0

v1 whole, which is shorter than its diff:
```python
import jax
import jax.numpy as jnp
from jax import lax
from jax.sharding import Mesh, PartitionSpec as P

ROUNDS = 4


EPS = 1e-06
TEMP = 12.0
CORES = 2


def normalize(block):
    values = block.astype(jnp.float32)
    return (values * lax.rsqrt(jnp.sum(values * values, axis=-1, keepdims=True) + EPS)).astype(
        jnp.bfloat16
    )


def weigh(unit_a, unit_b, live_b, extra):
    scores = jnp.dot(unit_a, unit_b.T, preferred_element_type=jnp.float32)
    return jnp.exp(TEMP * scores) * live_b[None, :] * extra


def per_device(embeddings, counts):
    all_counts = lax.all_gather(counts, ("bucket", "chip", "core"), axis=0, tiled=True)
    slabs = lax.all_to_all(embeddings, "bucket", split_axis=2, concat_axis=0, tiled=True)
    sources = slabs.shape[0]
    slot_rows = slabs.shape[3]
    width = slabs.shape[4]
    rows = sources * slot_rows
    data = slabs.reshape(rows, width)
    bucket = lax.axis_index("bucket")
    chips = lax.axis_size("chip")
    cores = lax.axis_size("core")
    blocks = chips * cores
    position = lax.axis_index("chip") * cores + lax.axis_index("core")
    all_counts = all_counts.reshape(sources, blocks, counts.shape[2])
    mine = lax.dynamic_index_in_dim(all_counts, bucket, axis=2, keepdims=False)
    block_counts = mine.T
    slot_index = lax.broadcasted_iota(jnp.int32, (blocks, sources, slot_rows), 2)
    all_live = (slot_index < block_counts[:, :, None]).astype(jnp.float32).reshape(blocks, rows)
    live = lax.dynamic_index_in_dim(all_live, position, axis=0, keepdims=False)
    unit = normalize(data)
    not_self = 1.0 - jnp.eye(rows, dtype=jnp.float32)
    own = weigh(unit, unit, live, not_self)
    summed = jnp.dot(own.astype(jnp.bfloat16), data, preferred_element_type=jnp.float32)
    squares = jnp.sum(own * own, axis=1)
    along = lax.all_gather(data, "chip", axis=0, tiled=False)
    both = lax.all_gather(along, "core", axis=1, tiled=False)
    all_data = both.reshape(blocks * rows, width)
    for dist in range(1, ROUNDS + 1):
        for sign in (1, -1):
            other = (position + sign * dist) % blocks
            start = other * rows
            got_data = lax.dynamic_slice_in_dim(all_data, start, rows, 0)
            got_live = lax.dynamic_index_in_dim(all_live, other, axis=0, keepdims=False)
            weights = weigh(unit, normalize(got_data), got_live, 1.0)
            summed = summed + jnp.dot(
                weights.astype(jnp.bfloat16), got_data, preferred_element_type=jnp.float32
            )
            squares = squares + jnp.sum(weights * weights, axis=1)
    result = summed * lax.rsqrt(squares)[:, None] * live[:, None]
    return result.astype(jnp.bfloat16).reshape(1, 1, rows, width)


def solution(mesh):
    devices = mesh.devices
    split = Mesh(
        devices.reshape(devices.shape[0], devices.shape[1] // CORES, CORES),
        ("bucket", "chip", "core"),
    )
    group = ("chip", "core")
    in_specs = (P("bucket", group, None, None, None), P("bucket", group, None, None))
    out_specs = P("bucket", group, None, None)
    return jax.shard_map(
        per_device, mesh=split, in_specs=in_specs, out_specs=out_specs, check_vma=False
    )
```

time: 112 us -> 153 us (1.37)
  blocking collectives: 30.9 us -> 56.2 us
  waiting for transfers between devices: 44.7 us -> 63.5 us
  starting transfers between devices: 3.22 us -> 0.04 us
    all_gather x1, blocking collectives: 13.6 us -> 39.1 us  [per_device(): lax.all_gather(counts, ('bucket', 'chip', 'core'), axis=0, tiled=True)]
    all_gather x1 -> x2, waiting for transfers between devices: 40.3 us -> 63.5 us  [the longest x1 63.5 us: per_device(): along = lax.all_gather(data, 'chip', axis=0, tiled=False)]
    all_to_all x1 -> x0, waiting for transfers between devices: 4.43 us -> none  [per_device(): lax.all_to_all(counts, 'bucket', split_axis=2, concat_axis=0, tiled=True)]
    all_to_all x1 -> x0, starting transfers between devices: 3.22 us -> none  [per_device(): lax.all_to_all(counts, 'bucket', split_axis=2, concat_axis=0, tiled=True)]
  transfers between devices with their start and end apart: 2 -> 2, of which waited for: 2 -> 1; matrix products, arithmetic and copies ran while one was open for 3% -> 1% of each run, Pallas kernels for 0% -> 0%
where the time goes in v1:
time: 153 us
  waiting for transfers between devices  63.5 us (42%)
  blocking collectives  56.2 us (37%)
  between operations  13.7 us (9%)
  matrix products  13.2 us (9%)
  other arithmetic  5.02 us (3%)
    all_gather x1, waiting for transfers between devices, per_device(): along = lax.all_gather(data, 'chip', axis=0, tiled=False)  63.5 us
    all_gather x1, blocking collectives, per_device(): lax.all_gather(counts, ('bucket', 'chip', 'core'), axis=0, tiled=True)  39.1 us
    all_to_all x1, blocking collectives, per_device(): lax.all_to_all(embeddings, 'bucket', split_axis=2, concat_axis=0, tiled=T...  17.2 us
    dot_general x9, matrix products, weigh(): scores = jnp.dot(unit_a, unit_b.T, preferred_element_type=jnp.float32)  6.58 us
    dot_general x8, matrix products, per_device(): jnp.dot(weights.astype(jnp.bfloat16), got_data, preferred_element_type=jn...  6.04 us
    reduce_sum x2, other arithmetic, normalize(): jnp.sum(values * values, axis=-1, keepdims=True) + EPS  4.49 us
  transfers between devices with their start and end apart: 2, of which 1 were waited for; matrix products, arithmetic and copies ran while one was open for 1% of the time, Pallas kernels for 0%

profile of v1, /device:TPU:0, one launch (start us, length us, event | category | flops | bytes accessed | tf_op | source)
XLA Modules:
  0.0 152.8 jit_solution(10136074342992450509)
XLA Ops:
  6.5 0.0 all-gather.4.cloned.1.call-start
  6.5 17.2 %all_to_all.4 = bf16[1,1,4,128,768]{4,3,1,0,2:T(8,128)(2,1)} all-to-all(bf16[1,1,4,128,768]{4,3,1,0,2:T(8,128)(2,1)} %bitcast.68), channel_id=1, replica_groups=mesh['bucket'=4,'chip'=4,'core'=2] {'bucket'}, dimensions={2} | all-to-all | bytes 1572864 | tf_op jit(solution)/shard_map/all_to_all | solution.py:28
  23.7 0.0 all-gather.4.cloned.1.call-update
  23.7 0.0 all-gather.6.cloned.1.call-start
  23.8 63.5 %all-gather.4.cloned.1.call-done = bf16[4,512,768]{2,1,0:T(8,128)(2,1)} async-done(((bf16[1,512,768]{2,1,0:T(8,128)(2,1)}), bf16[4,512,768]{2,1,0:T(8,128)(2,1)}) %all-gather.4.cloned.1.call-update) | async-done | bytes 3145744 | tf_op jit(solution)/shard_map/all_gather | solution.py:50
  87.2 0.0 copy-start.2
  87.2 0.0 copy-start
  87.2 0.0 all-gather.6.cloned.1.call-update
  87.5 0.4 copy-done.2
  87.9 39.1 %all_gather.12 = s32[32,1,4,1]{2,3,1,0:T(1,128)S(1)} all-gather(s32[1,1,4,1]{2,3,1,0:T(1,128)S(1)} %copy-done.2), channel_id=1, replica_groups=mesh['bucket'=4,'chip'=4,'core'=2] {'bucket','chip','core'}, dimensions={0}, use_global_device_ids=true | all-gather | bytes 528 | tf_op jit(solution)/shard_map/all_gather | solution.py:27
  127.0 0.1 constant_dynamic-slice_fusion.9
  127.0 0.1 copy.7
  127.2 0.1 fusion.87
  127.3 0.0 copy-done
  127.3 0.2 fusion
  127.5 0.2 multiply_convert_fusion.1
  127.7 0.2 fusion.1
  127.9 0.7 multiply_reduce_fusion.8
  128.7 0.6 fusion.85
  129.3 0.0 all-gather.6.cloned.1.call-done
  129.3 0.0 copy-start.1
  129.3 4.3 %fusion.16 = (f32[512]{0:T(512)S(1)}, f32[512]{0:T(512)S(1)}, f32[512]{0:T(512)S(1)}, f32[512]{0:T(512)S(1)}, f32[512]{0:T(512)S(1)}, /*index=5*/f32[512]{0:T(512)S(1)}, f32[512]{0:T(512)S(1)}, f32[512]{0:T(512)S(1)}) fusion(bf16[4096,768]{1,0:T(8,128)(2,1)} %bitcast.51, s32[]{:T(128)S(6)} %select_n.115, s32[]{:T(128)S(6)} %select_n.112, s32[]{:T(128)S(6)} %select_n.109, ...), kind=kLoop, calls=%fused_computation.34 | loop fusion | flops 9433088 | bytes 6307872 | tf_op jit(solution)/shard_map/reduce_sum | solution.py:16
  133.6 0.4 copy-done.1
  134.0 0.7 multiply_reduce_fusion.1
  134.7 0.6 fusion.57
  135.3 0.7 multiply_reduce_fusion.2
  136.1 0.6 fusion.60
  136.7 0.7 multiply_reduce_fusion.3
  137.4 0.6 fusion.63
  138.0 0.7 multiply_reduce_fusion.4
  138.8 0.6 fusion.66
  139.4 0.7 multiply_reduce_fusion.5
  140.1 0.6 fusion.69
  140.7 0.7 multiply_reduce_fusion.6
  141.5 0.6 fusion.72
  142.1 0.7 multiply_reduce_fusion.7
  142.8 0.6 fusion.75
  143.4 0.7 multiply_reduce_fusion
  144.1 1.8 %fusion.37 = bf16[1,1,512,768]{3,2,1,0:T(8,128)(2,1)} fusion(f32[512,768]{1,0:T(8,128)S(1)} %fusion.57, f32[512,768]{1,0:T(8,128)S(1)} %fusion.60, f32[512,768]{1,0:T(8,128)S(1)} %fusion.63, f32[512,768]{1,0:T(8,128)S(1)} %fusion.66, f32[512,768]{1,0:T(8,128)S(1)} %fusion.69, f32[512,768]{1,0:T(8,128)S(1)} %fusion.72, f32[512,768]{1,0:T(8,128)S(1)} %fusion.85, ...), kind=kOutput, calls=%fused_computation.66 | convolution fusion | flops 406978560 | bytes 14684164 | tf_op jit(solution)/shard_map/dot_general | solution.py:60
  (8 shorter events, 0.1 us)
Async XLA Ops:
  6.5 80.7 %all-gather.4.cloned.1.call-start = ((), (), s32[]{:S(2)}) async-start(), calls=%async_computation.1 | async-start | bytes 3932160 | tf_op jit(solution)/shard_map/all_gather | solution.py:50
  23.7 105.6 %all-gather.6.cloned.1.call-start = ((), (), s32[]{:S(2)}) async-start(), calls=%async_computation.2 | async-start | bytes 9437184 | tf_op jit(solution)/shard_map/all_gather | solution.py:51
  87.2 0.7 copy-start.2
  87.2 40.0 %copy-start = (bf16[1,1,4,128,768]{4,3,1,0,2:T(8,128)(2,1)S(1)}, bf16[1,1,4,128,768]{4,3,1,0,2:T(8,128)(2,1)}, u32[]{:S(2)}) copy-start(bf16[1,1,4,128,768]{4,3,1,0,2:T(8,128)(2,1)} %all_to_all.4) | copy-start | bytes 2359300
  129.3 4.7 %copy-start.1 = (bf16[4,1024,768]{2,1,0:T(8,128)(2,1)S(1)}, bf16[4,1024,768]{2,1,0:T(8,128)(2,1)}, u32[]{:S(2)}) copy-start(bf16[4,1024,768]{2,1,0:T(8,128)(2,1)} %all-gather.6.cloned.1.call-done) | copy-start | bytes 18874372
Sparse Core Ops, SparseCore 0:
  23.8 63.3 all-gather.3
  88.8 15.3 all-gather.5

commit v2 on v1

v2 whole, which is shorter than its diff:
```python
import jax
import jax.numpy as jnp
from jax import lax
from jax.sharding import Mesh, PartitionSpec as P

ROUNDS = 4


EPS = 1e-06
TEMP = 12.0
CORES = 2


def normalize(block):
    values = block.astype(jnp.float32)
    return (values * lax.rsqrt(jnp.sum(values * values, axis=-1, keepdims=True) + EPS)).astype(
        jnp.bfloat16
    )


def weigh(unit_a, unit_b, live_b, extra):
    scores = jnp.dot(unit_a, unit_b.T, preferred_element_type=jnp.float32)
    return jnp.exp(TEMP * scores) * live_b[None, :] * extra


def live_of(block_counts, slot_rows):
    sources = block_counts.shape[0]
    slot_index = lax.broadcasted_iota(jnp.int32, (sources, slot_rows), 1)
    return (slot_index < block_counts.reshape(sources, 1)).astype(jnp.float32).reshape(-1)


def per_device(embeddings, counts):
    slabs, slab_counts = (
        lax.all_to_all(embeddings, "bucket", split_axis=2, concat_axis=0, tiled=True),
        lax.all_to_all(counts, "bucket", split_axis=2, concat_axis=0, tiled=True),
    )
    sources = slabs.shape[0]
    slot_rows = slabs.shape[3]
    width = slabs.shape[4]
    rows = sources * slot_rows
    data = slabs.reshape(rows, width)
    own_counts = slab_counts.reshape(sources)
    live = live_of(own_counts, slot_rows)
    chips = lax.axis_size("chip")
    cores = lax.axis_size("core")
    blocks = chips * cores
    chip = lax.axis_index("chip")
    core = lax.axis_index("core")
    position = chip * cores + core

    unit = normalize(data)
    not_self = 1.0 - jnp.eye(rows, dtype=jnp.float32)
    own = weigh(unit, unit, live, not_self)
    summed = jnp.dot(own.astype(jnp.bfloat16), data, preferred_element_type=jnp.float32)
    squares = jnp.sum(own * own, axis=1)

    def times_listed(other_chip, other_core):
        block = other_chip * cores + other_core
        listed = jnp.int32(0)
        for dist in range(1, ROUNDS + 1):
            for sign in (1, -1):
                listed = listed + (((position + sign * dist) % blocks) == block).astype(jnp.int32)
        exists = (other_chip >= 0) & (other_chip < chips)
        return jnp.where(exists, listed, 0).astype(jnp.float32)

    def add_pair(acc, got, weight):
        summed, squares = acc
        got_data = got[:rows]
        got_counts = got[rows, :sources].astype(jnp.int32)
        weights = weigh(unit, normalize(got_data), live_of(got_counts, slot_rows), 1.0)
        part = jnp.dot(weights.astype(jnp.bfloat16), got_data, preferred_element_type=jnp.float32)
        return (summed + weight * part, squares + weight * jnp.sum(weights * weights, axis=1))

    swap = [(c, (c + 1) % cores) for c in range(cores)]
    up = [(c, c + 1) for c in range(chips - 1)]
    down = [(c + 1, c) for c in range(chips - 1)]
    acc = (summed, squares)
    tail = jnp.zeros((16, width), jnp.bfloat16).at[0, :sources].set(own_counts.astype(jnp.bfloat16))
    mine = jnp.concatenate([data, tail], axis=0)
    other_core = (core + 1) % cores
    swapped = lax.ppermute(mine, "core", swap)
    acc = add_pair(acc, swapped, times_listed(chip, other_core))
    from_below, from_above = mine, mine
    for step in range(1, chips):
        from_below = lax.ppermute(from_below, "chip", up)
        from_above = lax.ppermute(from_above, "chip", down)
        below_swapped = lax.ppermute(from_below, "core", swap)
        above_swapped = lax.ppermute(from_above, "core", swap)
        acc = add_pair(acc, from_below, times_listed(chip - step, core))
        acc = add_pair(acc, from_above, times_listed(chip + step, core))
        acc = add_pair(acc, below_swapped, times_listed(chip - step, other_core))
        acc = add_pair(acc, above_swapped, times_listed(chip + step, other_core))
    summed, squares = acc
    result = summed * lax.rsqrt(squares)[:, None] * live[:, None]
    return result.astype(jnp.bfloat16).reshape(1, 1, rows, width)


def solution(mesh):
    devices = mesh.devices
    split = Mesh(
        devices.reshape(devices.shape[0], devices.shape[1] // CORES, CORES),
        ("bucket", "chip", "core"),
    )
    group = ("chip", "core")
    in_specs = (P("bucket", group, None, None, None), P("bucket", group, None, None))
    out_specs = P("bucket", group, None, None)
    return jax.shard_map(
        per_device, mesh=split, in_specs=in_specs, out_specs=out_specs, check_vma=False
    )
```

time: 153 us -> 103 us (0.67)
  blocking collectives: 56.2 us -> 9.66 us
  starting transfers between devices: 0.04 us -> 24 us
  waiting for transfers between devices: 63.5 us -> 41 us
  between operations: 13.7 us -> 1.12 us
  matrix products: 13.2 us -> 21.1 us
    all_gather x2 -> x0, waiting for transfers between devices: 63.5 us -> none  [the longest x1 63.5 us: per_device(): along = lax.all_gather(data, 'chip', axis=0, tiled=False)]
    all_gather x1 -> x0, blocking collectives: 39.1 us -> none  [per_device(): lax.all_gather(counts, ('bucket', 'chip', 'core'), axis=0, tiled=True)]
    ppermute x0 -> x13, waiting for transfers between devices: none -> 32.5 us  [the longest x3 22.3 us: per_device(): from_above = lax.ppermute(from_above, 'chip', down)]
    ppermute x0 -> x13, starting transfers between devices: none -> 20.5 us  [the longest x3 14.9 us: per_device(): from_below = lax.ppermute(from_below, 'chip', up)]
    all_to_all x0 -> x1, waiting for transfers between devices: none -> 8.53 us  [per_device(): lax.all_to_all(embeddings, 'bucket', split_axis=2, concat_axis=0, tiled=T...]
    all_to_all x1, blocking collectives: 17.2 us -> 9.66 us  [per_device(): lax.all_to_all(counts, 'bucket', split_axis=2, concat_axis=0, tiled=True)]
    dot_general x8 -> x13, matrix products: 6.04 us -> 10.4 us  [add_pair(): jnp.dot(weights.astype(jnp.bfloat16), got_data, preferred_element_type=jn...]
    dot_general x9 -> x14, matrix products: 6.58 us -> 10.1 us  [weigh(): scores = jnp.dot(unit_a, unit_b.T, preferred_element_type=jnp.float32)]
  transfers between devices with their start and end apart: 2 -> 14, of which waited for: 1 -> 6; matrix products, arithmetic and copies ran while one was open for 1% -> 20% of each run, Pallas kernels for 0% -> 0%
where the time goes in v2:
time: 103 us
  waiting for transfers between devices  41 us (40%)
  starting transfers between devices  24 us (23%)
  matrix products  21.1 us (20%)
  blocking collectives  9.66 us (9%)
  other arithmetic  5.13 us (5%)
  between operations  1.12 us (1%)
    ppermute x3, waiting for transfers between devices, per_device(): from_above = lax.ppermute(from_above, 'chip', down)  22.3 us
    ppermute x3, starting transfers between devices, per_device(): from_below = lax.ppermute(from_below, 'chip', up)  14.9 us
    dot_general x13, matrix products, add_pair(): jnp.dot(weights.astype(jnp.bfloat16), got_data, preferred_element_type=jn...  10.4 us
    ppermute x3, waiting for transfers between devices, per_device(): from_below = lax.ppermute(from_below, 'chip', up)  10.2 us
    dot_general x14, matrix products, weigh(): scores = jnp.dot(unit_a, unit_b.T, preferred_element_type=jnp.float32)  10.1 us
    all_to_all x1, blocking collectives, per_device(): lax.all_to_all(counts, 'bucket', split_axis=2, concat_axis=0, tiled=True)  9.66 us
    all_to_all x1, waiting for transfers between devices, per_device(): lax.all_to_all(embeddings, 'bucket', split_axis=2, concat_axis=0, tiled=T...  8.53 us
    ppermute x3, starting transfers between devices, per_device(): from_above = lax.ppermute(from_above, 'chip', down)  3.86 us
  transfers between devices with their start and end apart: 14, of which 6 were waited for; matrix products, arithmetic and copies ran while one was open for 20% of the time, Pallas kernels for 0%

profile of v2, /device:TPU:0, one launch (start us, length us, event | category | flops | bytes accessed | tf_op | source)
XLA Modules:
  0.0 102.8 jit_solution(6747199507715599504)
XLA Ops:
  0.0 0.7 copy.6
  0.7 9.7 %all_to_all.8 = s32[1,1,4,1]{3,1,0,2:T(1,128)S(1)} all-to-all(s32[1,1,4,1]{3,1,0,2:T(1,128)S(1)} %copy.6), channel_id=1, replica_groups=mesh['bucket'=4,'chip'=4,'core'=2] {'bucket'}, dimensions={2} | all-to-all | bytes 32 | tf_op jit(solution)/shard_map/all_to_all | solution.py:35
  10.4 3.5 %all-to-all-start = ((bf16[1,1,4,128,768]{4,3,1,0,2:T(8,128)(2,1)}), bf16[1,1,4,128,768]{4,3,1,0,2:T(8,128)(2,1)S(1)}, u32[]{:S(2)}, u32[]{:S(2)}) async-start(bf16[1,1,4,128,768]{4,3,1,0,2:T(8,128)(2,1)} %bitcast.134), calls=%async_computation | async-start | bytes 1572864 | tf_op jit(solution)/shard_map/all_to_all | solution.py:34
  15.0 8.5 %all-to-all-done = bf16[1,1,4,128,768]{4,3,1,0,2:T(8,128)(2,1)S(1)} async-done(((bf16[1,1,4,128,768]{4,3,1,0,2:T(8,128)(2,1)}), bf16[1,1,4,128,768]{4,3,1,0,2:T(8,128)(2,1)S(1)}, u32[]{:S(2)}, u32[]{:S(2)}) %all-to-all-start) | async-done | bytes 786464 | tf_op jit(solution)/shard_map/all_to_all | solution.py:34
  23.6 1.3 %collective-permute-start.2 = (bf16[528,768]{1,0:T(8,128)(2,1)S(1)}, bf16[528,768]{1,0:T(8,128)(2,1)S(1)}, u32[]{:S(2)}, u32[]{:S(2)}) collective-permute-start(bf16[528,768]{1,0:T(8,128)(2,1)S(1)} %fusion.59), channel_id=1, source_target_pairs={{2,0},{4,2},{6,4},{3,1},{5,3},{7,5},{10,8},{12,10},{14,12},{11,9},... | collective-permute-start | bytes 2433032 | tf_op jit(solution)/shard_map/ppermute | solution.py:86
  24.9 4.6 %collective-permute-start.1 = (bf16[528,768]{1,0:T(8,128)(2,1)S(1)}, bf16[528,768]{1,0:T(8,128)(2,1)S(1)}, u32[]{:S(2)}, u32[]{:S(2)}) collective-permute-start(bf16[528,768]{1,0:T(8,128)(2,1)S(1)} %fusion.59), channel_id=1, source_target_pairs={{0,2},{2,4},{4,6},{1,3},{3,5},{5,7},{8,10},{10,12},{12,14},{9,11},... | collective-permute-start | bytes 2433032 | tf_op jit(solution)/shard_map/ppermute | solution.py:85
  29.6 0.2 fusion.1
  30.0 0.7 multiply_reduce_fusion.13
  30.8 0.6 fusion.137
  31.6 12.9 %collective-permute-done.2 = bf16[528,768]{1,0:T(8,128)(2,1)S(1)} collective-permute-done((bf16[528,768]{1,0:T(8,128)(2,1)S(1)}, bf16[528,768]{1,0:T(8,128)(2,1)S(1)}, u32[]{:S(2)}, u32[]{:S(2)}) %collective-permute-start.2) | collective-permute-done | bytes 811040 | tf_op jit(solution)/shard_map/ppermute | solution.py:86
  44.8 0.9 collective-permute-done.1
  46.1 1.3 %collective-permute-start.6 = (bf16[528,768]{1,0:T(8,128)(2,1)S(1)}, bf16[528,768]{1,0:T(8,128)(2,1)S(1)}, u32[]{:S(2)}, u32[]{:S(2)}) collective-permute-start(bf16[528,768]{1,0:T(8,128)(2,1)S(1)} %collective-permute-done.2), channel_id=1, source_target_pairs={{2,0},{4,2},{6,4},{3,1},{5,3},{7,5},{10,8},{12,10},{14,12},{11,9},... | collective-permute-start | bytes 2433032 | tf_op jit(solution)/shard_map/ppermute | solution.py:86
  47.4 5.1 %collective-permute-start.5 = (bf16[528,768]{1,0:T(8,128)(2,1)S(1)}, bf16[528,768]{1,0:T(8,128)(2,1)S(1)}, u32[]{:S(2)}, u32[]{:S(2)}) collective-permute-start(bf16[528,768]{1,0:T(8,128)(2,1)S(1)} %collective-permute-done.1), channel_id=1, source_target_pairs={{0,2},{2,4},{4,6},{1,3},{3,5},{5,7},{8,10},{10,12},{12,14},{9,11},... | collective-permute-start | bytes 2433032 | tf_op jit(solution)/shard_map/ppermute | solution.py:85
  52.6 0.5 collective-permute-start.3
  53.1 0.7 multiply_reduce_fusion.10
  53.8 0.6 fusion.116
  54.4 0.7 multiply_reduce_fusion.11
  55.1 0.6 fusion.119
  55.9 0.7 multiply_reduce_fusion.12
  56.7 0.6 fusion.122
  57.3 9.4 %collective-permute-done.6 = bf16[528,768]{1,0:T(8,128)(2,1)S(1)} collective-permute-done((bf16[528,768]{1,0:T(8,128)(2,1)S(1)}, bf16[528,768]{1,0:T(8,128)(2,1)S(1)}, u32[]{:S(2)}, u32[]{:S(2)}) %collective-permute-start.6) | collective-permute-done | bytes 811040 | tf_op jit(solution)/shard_map/ppermute | solution.py:86
  66.7 1.1 %collective-permute-done.5 = bf16[528,768]{1,0:T(8,128)(2,1)S(1)} collective-permute-done((bf16[528,768]{1,0:T(8,128)(2,1)S(1)}, bf16[528,768]{1,0:T(8,128)(2,1)S(1)}, u32[]{:S(2)}, u32[]{:S(2)}) %collective-permute-start.5) | collective-permute-done | bytes 811040 | tf_op jit(solution)/shard_map/ppermute | solution.py:85
  68.8 1.3 %collective-permute-start.10 = (bf16[528,768]{1,0:T(8,128)(2,1)S(1)}, bf16[528,768]{1,0:T(8,128)(2,1)S(1)}, u32[]{:S(2)}, u32[]{:S(2)}) collective-permute-start(bf16[528,768]{1,0:T(8,128)(2,1)S(1)} %collective-permute-done.6), channel_id=1, source_target_pairs={{2,0},{4,2},{6,4},{3,1},{5,3},{7,5},{10,8},{12,10},{14,12},{11,9},... | collective-permute-start | bytes 2433032 | tf_op jit(solution)/shard_map/ppermute | solution.py:86
  70.1 5.2 %collective-permute-start.9 = (bf16[528,768]{1,0:T(8,128)(2,1)S(1)}, bf16[528,768]{1,0:T(8,128)(2,1)S(1)}, u32[]{:S(2)}, u32[]{:S(2)}) collective-permute-start(bf16[528,768]{1,0:T(8,128)(2,1)S(1)} %collective-permute-done.5), channel_id=1, source_target_pairs={{0,2},{2,4},{4,6},{1,3},{3,5},{5,7},{8,10},{10,12},{12,14},{9,11},... | collective-permute-start | bytes 2433032 | tf_op jit(solution)/shard_map/ppermute | solution.py:85
  75.4 0.5 collective-permute-start.7
  75.9 0.7 multiply_reduce_fusion.6
  76.7 0.6 fusion.104
  77.3 0.7 multiply_reduce_fusion.7
  78.0 0.6 fusion.107
  78.6 0.7 multiply_reduce_fusion.8
  79.3 0.6 fusion.110
  80.2 0.7 multiply_reduce_fusion.9
  80.9 0.6 fusion.113
  81.5 8.2 %collective-permute-done.9 = bf16[528,768]{1,0:T(8,128)(2,1)S(1)} collective-permute-done((bf16[528,768]{1,0:T(8,128)(2,1)S(1)}, bf16[528,768]{1,0:T(8,128)(2,1)S(1)}, u32[]{:S(2)}, u32[]{:S(2)}) %collective-permute-start.9) | collective-permute-done | bytes 811040 | tf_op jit(solution)/shard_map/ppermute | solution.py:85
  91.0 0.5 collective-permute-start.11
  91.5 0.7 multiply_reduce_fusion.3
  92.2 0.6 fusion.95
  92.8 0.7 multiply_reduce_fusion.2
  93.6 0.6 fusion.92
  94.2 0.7 multiply_reduce_fusion.4
  94.9 0.7 multiply_reduce_fusion.5
  95.6 0.6 fusion.101
  96.2 0.6 fusion.98
  97.1 0.2 fusion.25
  97.5 0.7 multiply_reduce_fusion
  98.2 0.7 multiply_reduce_fusion.1
  98.9 0.6 fusion.89
  99.5 3.2 %fusion.58 = bf16[1,1,512,768]{3,2,1,0:T(8,128)(2,1)} fusion(f32[512,768]{1,0:T(8,128)S(1)} %fusion.89, f32[512,768]{1,0:T(8,128)S(1)} %fusion.92, f32[512,768]{1,0:T(8,128)S(1)} %fusion.95, f32[512,768]{1,0:T(8,128)S(1)} %fusion.98, f32[512,768]{1,0:T(8,128)S(1)} %fusion.101, f32[512,768]{1,0:T(8,128)S(1)} %fusion.104, f32[512,768]{1,0:T(8,128)S(1)} %fusion.107, ...), kind=kOutput, calls=%fused_computation.103 | convolution fusion | flops 414056448 | bytes 22548532 | tf_op jit(solution)/shard_map/dot_general | solution.py:71
  (71 shorter events, 4.9 us)
Async XLA Ops:
  10.4 13.1 %all-to-all-start = ((bf16[1,1,4,128,768]{4,3,1,0,2:T(8,128)(2,1)}), bf16[1,1,4,128,768]{4,3,1,0,2:T(8,128)(2,1)S(1)}, u32[]{:S(2)}, u32[]{:S(2)}) async-start(bf16[1,1,4,128,768]{4,3,1,0,2:T(8,128)(2,1)} %bitcast.134), calls=%async_computation | async-start | bytes 1572864 | tf_op jit(solution)/shard_map/all_to_all | solution.py:34
  23.6 20.9 %collective-permute-start.2 = (bf16[528,768]{1,0:T(8,128)(2,1)S(1)}, bf16[528,768]{1,0:T(8,128)(2,1)S(1)}, u32[]{:S(2)}, u32[]{:S(2)}) collective-permute-start(bf16[528,768]{1,0:T(8,128)(2,1)S(1)} %fusion.59), channel_id=1, source_target_pairs={{2,0},{4,2},{6,4},{3,1},{5,3},{7,5},{10,8},{12,10},{14,12},{11,9},... | collective-permute-start | bytes 2433032 | tf_op jit(solution)/shard_map/ppermute | solution.py:86
  24.9 20.8 %collective-permute-start.1 = (bf16[528,768]{1,0:T(8,128)(2,1)S(1)}, bf16[528,768]{1,0:T(8,128)(2,1)S(1)}, u32[]{:S(2)}, u32[]{:S(2)}) collective-permute-start(bf16[528,768]{1,0:T(8,128)(2,1)S(1)} %fusion.59), channel_id=1, source_target_pairs={{0,2},{2,4},{4,6},{1,3},{3,5},{5,7},{8,10},{10,12},{12,14},{9,11},... | collective-permute-start | bytes 2433032 | tf_op jit(solution)/shard_map/ppermute | solution.py:85
  29.5 16.5 %collective-permute-start = (bf16[528,768]{1,0:T(8,128)(2,1)S(1)}, bf16[528,768]{1,0:T(8,128)(2,1)S(1)}, u32[]{:S(2)}, u32[]{:S(2)}) collective-permute-start(bf16[528,768]{1,0:T(8,128)(2,1)S(1)} %fusion.59), channel_id=1, source_target_pairs={{0,1},{1,0},{2,3},{3,2},{4,5},{5,4},{6,7},{7,6},{8,9},{9,8},{10,11... | collective-permute-start | bytes 2433032 | tf_op jit(solution)/shard_map/ppermute | solution.py:81
  46.1 20.5 %collective-permute-start.6 = (bf16[528,768]{1,0:T(8,128)(2,1)S(1)}, bf16[528,768]{1,0:T(8,128)(2,1)S(1)}, u32[]{:S(2)}, u32[]{:S(2)}) collective-permute-start(bf16[528,768]{1,0:T(8,128)(2,1)S(1)} %collective-permute-done.2), channel_id=1, source_target_pairs={{2,0},{4,2},{6,4},{3,1},{5,3},{7,5},{10,8},{12,10},{14,12},{11,9},... | collective-permute-start | bytes 2433032 | tf_op jit(solution)/shard_map/ppermute | solution.py:86
  47.4 20.4 %collective-permute-start.5 = (bf16[528,768]{1,0:T(8,128)(2,1)S(1)}, bf16[528,768]{1,0:T(8,128)(2,1)S(1)}, u32[]{:S(2)}, u32[]{:S(2)}) collective-permute-start(bf16[528,768]{1,0:T(8,128)(2,1)S(1)} %collective-permute-done.1), channel_id=1, source_target_pairs={{0,2},{2,4},{4,6},{1,3},{3,5},{5,7},{8,10},{10,12},{12,14},{9,11},... | collective-permute-start | bytes 2433032 | tf_op jit(solution)/shard_map/ppermute | solution.py:85
  52.5 15.4 %collective-permute-start.4 = (bf16[528,768]{1,0:T(8,128)(2,1)S(1)}, bf16[528,768]{1,0:T(8,128)(2,1)S(1)}, u32[]{:S(2)}, u32[]{:S(2)}) collective-permute-start(bf16[528,768]{1,0:T(8,128)(2,1)S(1)} %collective-permute-done.2), channel_id=1, source_target_pairs={{0,1},{1,0},{2,3},{3,2},{4,5},{5,4},{6,7},{7,6},{8,9},{9,8},{10,11... | collective-permute-start | bytes 2433032 | tf_op jit(solution)/shard_map/ppermute | solution.py:88
  52.6 16.2 %collective-permute-start.3 = (bf16[528,768]{1,0:T(8,128)(2,1)S(1)}, bf16[528,768]{1,0:T(8,128)(2,1)S(1)}, u32[]{:S(2)}, u32[]{:S(2)}) collective-permute-start(bf16[528,768]{1,0:T(8,128)(2,1)S(1)} %collective-permute-done.1), channel_id=1, source_target_pairs={{0,1},{1,0},{2,3},{3,2},{4,5},{5,4},{6,7},{7,6},{8,9},{9,8},{10,11... | collective-permute-start | bytes 2433032 | tf_op jit(solution)/shard_map/ppermute | solution.py:87
  68.8 20.9 %collective-permute-start.10 = (bf16[528,768]{1,0:T(8,128)(2,1)S(1)}, bf16[528,768]{1,0:T(8,128)(2,1)S(1)}, u32[]{:S(2)}, u32[]{:S(2)}) collective-permute-start(bf16[528,768]{1,0:T(8,128)(2,1)S(1)} %collective-permute-done.6), channel_id=1, source_target_pairs={{2,0},{4,2},{6,4},{3,1},{5,3},{7,5},{10,8},{12,10},{14,12},{11,9},... | collective-permute-start | bytes 2433032 | tf_op jit(solution)/shard_map/ppermute | solution.py:86
  70.1 19.6 %collective-permute-start.9 = (bf16[528,768]{1,0:T(8,128)(2,1)S(1)}, bf16[528,768]{1,0:T(8,128)(2,1)S(1)}, u32[]{:S(2)}, u32[]{:S(2)}) collective-permute-start(bf16[528,768]{1,0:T(8,128)(2,1)S(1)} %collective-permute-done.5), channel_id=1, source_target_pairs={{0,2},{2,4},{4,6},{1,3},{3,5},{5,7},{8,10},{10,12},{12,14},{9,11},... | collective-permute-start | bytes 2433032 | tf_op jit(solution)/shard_map/ppermute | solution.py:85
  75.4 14.5 %collective-permute-start.8 = (bf16[528,768]{1,0:T(8,128)(2,1)S(1)}, bf16[528,768]{1,0:T(8,128)(2,1)S(1)}, u32[]{:S(2)}, u32[]{:S(2)}) collective-permute-start(bf16[528,768]{1,0:T(8,128)(2,1)S(1)} %collective-permute-done.6), channel_id=1, source_target_pairs={{0,1},{1,0},{2,3},{3,2},{4,5},{5,4},{6,7},{7,6},{8,9},{9,8},{10,11... | collective-permute-start | bytes 2433032 | tf_op jit(solution)/shard_map/ppermute | solution.py:88
  75.4 15.2 %collective-permute-start.7 = (bf16[528,768]{1,0:T(8,128)(2,1)S(1)}, bf16[528,768]{1,0:T(8,128)(2,1)S(1)}, u32[]{:S(2)}, u32[]{:S(2)}) collective-permute-start(bf16[528,768]{1,0:T(8,128)(2,1)S(1)} %collective-permute-done.5), channel_id=1, source_target_pairs={{0,1},{1,0},{2,3},{3,2},{4,5},{5,4},{6,7},{7,6},{8,9},{9,8},{10,11... | collective-permute-start | bytes 2433032 | tf_op jit(solution)/shard_map/ppermute | solution.py:87
  91.0 5.8 %collective-permute-start.12 = (bf16[528,768]{1,0:T(8,128)(2,1)S(1)}, bf16[528,768]{1,0:T(8,128)(2,1)S(1)}, u32[]{:S(2)}, u32[]{:S(2)}) collective-permute-start(bf16[528,768]{1,0:T(8,128)(2,1)S(1)} %collective-permute-done.10), channel_id=1, source_target_pairs={{0,1},{1,0},{2,3},{3,2},{4,5},{5,4},{6,7},{7,6},{8,9},{9,8},{10,11... | collective-permute-start | bytes 2433032 | tf_op jit(solution)/shard_map/ppermute | solution.py:88
  91.0 6.1 %collective-permute-start.11 = (bf16[528,768]{1,0:T(8,128)(2,1)S(1)}, bf16[528,768]{1,0:T(8,128)(2,1)S(1)}, u32[]{:S(2)}, u32[]{:S(2)}) collective-permute-start(bf16[528,768]{1,0:T(8,128)(2,1)S(1)} %collective-permute-done.9), channel_id=1, source_target_pairs={{0,1},{1,0},{2,3},{3,2},{4,5},{5,4},{6,7},{7,6},{8,9},{9,8},{10,11... | collective-permute-start | bytes 2433032 | tf_op jit(solution)/shard_map/ppermute | solution.py:87

commit v3 on v2

--- a/solution.py
+++ b/solution.py
@@ -30,16 +30,16 @@
 
 
 def per_device(embeddings, counts):
-    slabs, slab_counts = (
-        lax.all_to_all(embeddings, "bucket", split_axis=2, concat_axis=0, tiled=True),
-        lax.all_to_all(counts, "bucket", split_axis=2, concat_axis=0, tiled=True),
-    )
+    slot_rows = embeddings.shape[3]
+    width = embeddings.shape[4]
+    count_rows = jnp.zeros(embeddings.shape[:3] + (16, width), jnp.bfloat16)
+    count_rows = count_rows.at[:, :, :, 0, 0].set(counts[..., 0].astype(jnp.bfloat16))
+    packed = jnp.concatenate([embeddings, count_rows], axis=3)
+    slabs = lax.all_to_all(packed, "bucket", split_axis=2, concat_axis=0, tiled=True)
     sources = slabs.shape[0]
-    slot_rows = slabs.shape[3]
-    width = slabs.shape[4]
     rows = sources * slot_rows
-    data = slabs.reshape(rows, width)
-    own_counts = slab_counts.reshape(sources)
+    data = slabs[:, :, :, :slot_rows].reshape(rows, width)
+    own_counts = slabs[:, 0, 0, slot_rows, 0].astype(jnp.int32)
     live = live_of(own_counts, slot_rows)
     chips = lax.axis_size("chip")
     cores = lax.axis_size("core")

time: 103 us -> 99.7 us (0.968)
  blocking collectives: 9.66 us -> 0 us
  waiting for transfers between devices: 41 us -> 44.4 us
  other arithmetic: 5.13 us -> 7.91 us
  starting transfers between devices: 24 us -> 25.7 us
    all_to_all x1 -> x0, blocking collectives: 9.66 us -> none  [per_device(): lax.all_to_all(counts, 'bucket', split_axis=2, concat_axis=0, tiled=True)]
    all_to_all x1, waiting for transfers between devices: 8.53 us -> 11.9 us  [per_device(): lax.all_to_all(packed, 'bucket', split_axis=2, concat_axis=0, tiled=True)]
    concatenate x0 -> x1, other arithmetic: none -> 2.12 us  [per_device(): packed = jnp.concatenate([embeddings, count_rows], axis=3)]
    all_to_all x1, starting transfers between devices: 3.5 us -> 5.19 us  [per_device(): lax.all_to_all(packed, 'bucket', split_axis=2, concat_axis=0, tiled=True)]
where the time goes in v3:
time: 99.7 us; the launch traced here: 99.3 us
  waiting for transfers between devices  44.4 us (45%)
  starting transfers between devices  25.7 us (26%)
  matrix products  20.9 us (21%)
  other arithmetic  7.91 us (8%)
    ppermute x3, waiting for transfers between devices, per_device(): from_above = lax.ppermute(from_above, 'chip', down)  22.3 us
    ppermute x3, starting transfers between devices, per_device(): from_below = lax.ppermute(from_below, 'chip', up)  14.9 us
    all_to_all x1, waiting for transfers between devices, per_device(): lax.all_to_all(packed, 'bucket', split_axis=2, concat_axis=0, tiled=True)  11.9 us
    ppermute x3, waiting for transfers between devices, per_device(): from_below = lax.ppermute(from_below, 'chip', up)  10.2 us
    dot_general x13, matrix products, add_pair(): jnp.dot(weights.astype(jnp.bfloat16), got_data, preferred_element_type=jn...  10.1 us
    dot_general x14, matrix products, weigh(): scores = jnp.dot(unit_a, unit_b.T, preferred_element_type=jnp.float32)  10.1 us
    all_to_all x1, starting transfers between devices, per_device(): lax.all_to_all(packed, 'bucket', split_axis=2, concat_axis=0, tiled=True)  5.19 us
    ppermute x3, starting transfers between devices, per_device(): from_above = lax.ppermute(from_above, 'chip', down)  3.86 us
  transfers between devices with their start and end apart: 14, of which 6 were waited for; matrix products, arithmetic and copies ran while one was open for 20% of the time, Pallas kernels for 0%

profile of v3, /device:TPU:0, one launch (start us, length us, event | category | flops | bytes accessed | tf_op | source)
XLA Modules:
  0.0 99.3 jit_solution(15712495758249944824)
XLA Ops:
  0.0 0.7 convert_bitcast_fusion.14
  0.8 2.1 %fusion.60 = bf16[1,1,4,144,768]{4,3,1,0,2:T(8,128)(2,1)} fusion(bf16[1,1,4,1,1]{4,3,1,0,2:T(2,128)(2,1)S(1)} %copy.7, bf16[1,1,4,128,768]{4,3,1,0,2:T(8,128)(2,1)} %bitcast.142), kind=kLoop, calls=%fused_computation.121 | loop fusion | flops 2654208 | bytes 1671176 | tf_op jit(solution)/shard_map/concatenate | solution.py:37
  2.9 5.2 %all-to-all-start = ((bf16[1,1,4,144,768]{4,3,1,0,2:T(8,128)(2,1)}), bf16[1,1,4,144,768]{4,3,1,0,2:T(8,128)(2,1)S(1)}, u32[]{:S(2)}, u32[]{:S(2)}) async-start(bf16[1,1,4,144,768]{4,3,1,0,2:T(8,128)(2,1)} %fusion.60), calls=%async_computation | async-start | bytes 1769472 | tf_op jit(solution)/shard_map/all_to_all | solution.py:38
  8.1 11.9 %all-to-all-done = bf16[1,1,4,144,768]{4,3,1,0,2:T(8,128)(2,1)S(1)} async-done(((bf16[1,1,4,144,768]{4,3,1,0,2:T(8,128)(2,1)}), bf16[1,1,4,144,768]{4,3,1,0,2:T(8,128)(2,1)S(1)}, u32[]{:S(2)}, u32[]{:S(2)}) %all-to-all-start) | async-done | bytes 884768 | tf_op jit(solution)/shard_map/all_to_all | solution.py:38
  20.4 1.3 %collective-permute-start.2 = (bf16[528,768]{1,0:T(8,128)(2,1)S(1)}, bf16[528,768]{1,0:T(8,128)(2,1)S(1)}, u32[]{:S(2)}, u32[]{:S(2)}) collective-permute-start(bf16[528,768]{1,0:T(8,128)(2,1)S(1)} %fusion.61), channel_id=1, source_target_pairs={{2,0},{4,2},{6,4},{3,1},{5,3},{7,5},{10,8},{12,10},{14,12},{11,9},... | collective-permute-start | bytes 2433032 | tf_op jit(solution)/shard_map/ppermute | solution.py:86
  21.7 4.6 %collective-permute-start.1 = (bf16[528,768]{1,0:T(8,128)(2,1)S(1)}, bf16[528,768]{1,0:T(8,128)(2,1)S(1)}, u32[]{:S(2)}, u32[]{:S(2)}) collective-permute-start(bf16[528,768]{1,0:T(8,128)(2,1)S(1)} %fusion.61), channel_id=1, source_target_pairs={{0,2},{2,4},{4,6},{1,3},{3,5},{5,7},{8,10},{10,12},{12,14},{9,11},... | collective-permute-start | bytes 2433032 | tf_op jit(solution)/shard_map/ppermute | solution.py:85
  26.9 0.8 multiply_reduce_fusion.13
  27.6 0.6 fusion.139
  28.4 12.9 %collective-permute-done.2 = bf16[528,768]{1,0:T(8,128)(2,1)S(1)} collective-permute-done((bf16[528,768]{1,0:T(8,128)(2,1)S(1)}, bf16[528,768]{1,0:T(8,128)(2,1)S(1)}, u32[]{:S(2)}, u32[]{:S(2)}) %collective-permute-start.2) | collective-permute-done | bytes 811040 | tf_op jit(solution)/shard_map/ppermute | solution.py:86
  41.7 0.9 collective-permute-done.1
  43.0 1.3 %collective-permute-start.6 = (bf16[528,768]{1,0:T(8,128)(2,1)S(1)}, bf16[528,768]{1,0:T(8,128)(2,1)S(1)}, u32[]{:S(2)}, u32[]{:S(2)}) collective-permute-start(bf16[528,768]{1,0:T(8,128)(2,1)S(1)} %collective-permute-done.2), channel_id=1, source_target_pairs={{2,0},{4,2},{6,4},{3,1},{5,3},{7,5},{10,8},{12,10},{14,12},{11,9},... | collective-permute-start | bytes 2433032 | tf_op jit(solution)/shard_map/ppermute | solution.py:86
  44.2 5.1 %collective-permute-start.5 = (bf16[528,768]{1,0:T(8,128)(2,1)S(1)}, bf16[528,768]{1,0:T(8,128)(2,1)S(1)}, u32[]{:S(2)}, u32[]{:S(2)}) collective-permute-start(bf16[528,768]{1,0:T(8,128)(2,1)S(1)} %collective-permute-done.1), channel_id=1, source_target_pairs={{0,2},{2,4},{4,6},{1,3},{3,5},{5,7},{8,10},{10,12},{12,14},{9,11},... | collective-permute-start | bytes 2433032 | tf_op jit(solution)/shard_map/ppermute | solution.py:85
  49.4 0.5 collective-permute-start.3
  49.9 0.7 multiply_reduce_fusion.10
  50.6 0.6 fusion.118
  51.2 0.7 multiply_reduce_fusion.11
  51.9 0.6 fusion.121
  52.5 0.2 fusion.4
  52.8 0.7 multiply_reduce_fusion.12
  53.5 0.6 fusion.124
  54.1 9.4 %collective-permute-done.6 = bf16[528,768]{1,0:T(8,128)(2,1)S(1)} collective-permute-done((bf16[528,768]{1,0:T(8,128)(2,1)S(1)}, bf16[528,768]{1,0:T(8,128)(2,1)S(1)}, u32[]{:S(2)}, u32[]{:S(2)}) %collective-permute-start.6) | collective-permute-done | bytes 811040 | tf_op jit(solution)/shard_map/ppermute | solution.py:86
  63.6 1.1 %collective-permute-done.5 = bf16[528,768]{1,0:T(8,128)(2,1)S(1)} collective-permute-done((bf16[528,768]{1,0:T(8,128)(2,1)S(1)}, bf16[528,768]{1,0:T(8,128)(2,1)S(1)}, u32[]{:S(2)}, u32[]{:S(2)}) %collective-permute-start.5) | collective-permute-done | bytes 811040 | tf_op jit(solution)/shard_map/ppermute | solution.py:85
  65.7 1.3 %collective-permute-start.10 = (bf16[528,768]{1,0:T(8,128)(2,1)S(1)}, bf16[528,768]{1,0:T(8,128)(2,1)S(1)}, u32[]{:S(2)}, u32[]{:S(2)}) collective-permute-start(bf16[528,768]{1,0:T(8,128)(2,1)S(1)} %collective-permute-done.6), channel_id=1, source_target_pairs={{2,0},{4,2},{6,4},{3,1},{5,3},{7,5},{10,8},{12,10},{14,12},{11,9},... | collective-permute-start | bytes 2433032 | tf_op jit(solution)/shard_map/ppermute | solution.py:86
  66.9 5.2 %collective-permute-start.9 = (bf16[528,768]{1,0:T(8,128)(2,1)S(1)}, bf16[528,768]{1,0:T(8,128)(2,1)S(1)}, u32[]{:S(2)}, u32[]{:S(2)}) collective-permute-start(bf16[528,768]{1,0:T(8,128)(2,1)S(1)} %collective-permute-done.5), channel_id=1, source_target_pairs={{0,2},{2,4},{4,6},{1,3},{3,5},{5,7},{8,10},{10,12},{12,14},{9,11},... | collective-permute-start | bytes 2433032 | tf_op jit(solution)/shard_map/ppermute | solution.py:85
  72.3 0.5 collective-permute-start.8
  72.8 0.7 multiply_reduce_fusion.6
  73.5 0.6 fusion.106
  74.1 0.7 multiply_reduce_fusion.7
  74.8 0.6 fusion.109
  75.4 0.7 multiply_reduce_fusion.8
  76.2 0.6 fusion.112
  77.0 0.7 multiply_reduce_fusion.9
  77.7 0.6 fusion.115
  78.3 8.2 %collective-permute-done.9 = bf16[528,768]{1,0:T(8,128)(2,1)S(1)} collective-permute-done((bf16[528,768]{1,0:T(8,128)(2,1)S(1)}, bf16[528,768]{1,0:T(8,128)(2,1)S(1)}, u32[]{:S(2)}, u32[]{:S(2)}) %collective-permute-start.9) | collective-permute-done | bytes 811040 | tf_op jit(solution)/shard_map/ppermute | solution.py:85
  87.8 0.5 collective-permute-start.11
  88.3 0.7 multiply_reduce_fusion.3
  89.1 0.6 fusion.97
  89.7 0.7 multiply_reduce_fusion.2
  90.4 0.6 fusion.94
  91.0 0.7 multiply_reduce_fusion.5
  91.7 0.7 multiply_reduce_fusion.4
  92.4 0.6 fusion.103
  93.0 0.6 fusion.100
  94.0 0.2 fusion.26
  94.3 0.7 multiply_reduce_fusion
  95.0 0.7 multiply_reduce_fusion.1
  95.8 0.6 fusion.91
  96.4 3.0 %fusion.59 = bf16[1,1,512,768]{3,2,1,0:T(8,128)(2,1)} fusion(f32[512,768]{1,0:T(8,128)S(1)} %fusion.91, f32[512,768]{1,0:T(8,128)S(1)} %fusion.94, f32[512,768]{1,0:T(8,128)S(1)} %fusion.97, f32[512,768]{1,0:T(8,128)S(1)} %fusion.100, f32[512,768]{1,0:T(8,128)S(1)} %fusion.103, f32[512,768]{1,0:T(8,128)S(1)} %fusion.106, f32[512,768]{1,0:T(8,128)S(1)} %fusion.109, ...), kind=kOutput, calls=%fused_computation.105 | convolution fusion | flops 414056448 | bytes 22548532 | tf_op jit(solution)/shard_map/dot_general | solution.py:71
  (73 shorter events, 5.1 us)
Async XLA Ops:
  2.9 17.1 %all-to-all-start = ((bf16[1,1,4,144,768]{4,3,1,0,2:T(8,128)(2,1)}), bf16[1,1,4,144,768]{4,3,1,0,2:T(8,128)(2,1)S(1)}, u32[]{:S(2)}, u32[]{:S(2)}) async-start(bf16[1,1,4,144,768]{4,3,1,0,2:T(8,128)(2,1)} %fusion.60), calls=%async_computation | async-start | bytes 1769472 | tf_op jit(solution)/shard_map/all_to_all | solution.py:38
  20.4 20.9 %collective-permute-start.2 = (bf16[528,768]{1,0:T(8,128)(2,1)S(1)}, bf16[528,768]{1,0:T(8,128)(2,1)S(1)}, u32[]{:S(2)}, u32[]{:S(2)}) collective-permute-start(bf16[528,768]{1,0:T(8,128)(2,1)S(1)} %fusion.61), channel_id=1, source_target_pairs={{2,0},{4,2},{6,4},{3,1},{5,3},{7,5},{10,8},{12,10},{14,12},{11,9},... | collective-permute-start | bytes 2433032 | tf_op jit(solution)/shard_map/ppermute | solution.py:86
  21.7 20.8 %collective-permute-start.1 = (bf16[528,768]{1,0:T(8,128)(2,1)S(1)}, bf16[528,768]{1,0:T(8,128)(2,1)S(1)}, u32[]{:S(2)}, u32[]{:S(2)}) collective-permute-start(bf16[528,768]{1,0:T(8,128)(2,1)S(1)} %fusion.61), channel_id=1, source_target_pairs={{0,2},{2,4},{4,6},{1,3},{3,5},{5,7},{8,10},{10,12},{12,14},{9,11},... | collective-permute-start | bytes 2433032 | tf_op jit(solution)/shard_map/ppermute | solution.py:85
  26.3 16.5 %collective-permute-start = (bf16[528,768]{1,0:T(8,128)(2,1)S(1)}, bf16[528,768]{1,0:T(8,128)(2,1)S(1)}, u32[]{:S(2)}, u32[]{:S(2)}) collective-permute-start(bf16[528,768]{1,0:T(8,128)(2,1)S(1)} %fusion.61), channel_id=1, source_target_pairs={{0,1},{1,0},{2,3},{3,2},{4,5},{5,4},{6,7},{7,6},{8,9},{9,8},{10,11... | collective-permute-start | bytes 2433032 | tf_op jit(solution)/shard_map/ppermute | solution.py:81
  43.0 20.5 %collective-permute-start.6 = (bf16[528,768]{1,0:T(8,128)(2,1)S(1)}, bf16[528,768]{1,0:T(8,128)(2,1)S(1)}, u32[]{:S(2)}, u32[]{:S(2)}) collective-permute-start(bf16[528,768]{1,0:T(8,128)(2,1)S(1)} %collective-permute-done.2), channel_id=1, source_target_pairs={{2,0},{4,2},{6,4},{3,1},{5,3},{7,5},{10,8},{12,10},{14,12},{11,9},... | collective-permute-start | bytes 2433032 | tf_op jit(solution)/shard_map/ppermute | solution.py:86
  44.2 20.4 %collective-permute-start.5 = (bf16[528,768]{1,0:T(8,128)(2,1)S(1)}, bf16[528,768]{1,0:T(8,128)(2,1)S(1)}, u32[]{:S(2)}, u32[]{:S(2)}) collective-permute-start(bf16[528,768]{1,0:T(8,128)(2,1)S(1)} %collective-permute-done.1), channel_id=1, source_target_pairs={{0,2},{2,4},{4,6},{1,3},{3,5},{5,7},{8,10},{10,12},{12,14},{9,11},... | collective-permute-start | bytes 2433032 | tf_op jit(solution)/shard_map/ppermute | solution.py:85
  49.3 15.4 %collective-permute-start.4 = (bf16[528,768]{1,0:T(8,128)(2,1)S(1)}, bf16[528,768]{1,0:T(8,128)(2,1)S(1)}, u32[]{:S(2)}, u32[]{:S(2)}) collective-permute-start(bf16[528,768]{1,0:T(8,128)(2,1)S(1)} %collective-permute-done.2), channel_id=1, source_target_pairs={{0,1},{1,0},{2,3},{3,2},{4,5},{5,4},{6,7},{7,6},{8,9},{9,8},{10,11... | collective-permute-start | bytes 2433032 | tf_op jit(solution)/shard_map/ppermute | solution.py:88
  49.4 16.2 %collective-permute-start.3 = (bf16[528,768]{1,0:T(8,128)(2,1)S(1)}, bf16[528,768]{1,0:T(8,128)(2,1)S(1)}, u32[]{:S(2)}, u32[]{:S(2)}) collective-permute-start(bf16[528,768]{1,0:T(8,128)(2,1)S(1)} %collective-permute-done.1), channel_id=1, source_target_pairs={{0,1},{1,0},{2,3},{3,2},{4,5},{5,4},{6,7},{7,6},{8,9},{9,8},{10,11... | collective-permute-start | bytes 2433032 | tf_op jit(solution)/shard_map/ppermute | solution.py:87
  65.7 20.9 %collective-permute-start.10 = (bf16[528,768]{1,0:T(8,128)(2,1)S(1)}, bf16[528,768]{1,0:T(8,128)(2,1)S(1)}, u32[]{:S(2)}, u32[]{:S(2)}) collective-permute-start(bf16[528,768]{1,0:T(8,128)(2,1)S(1)} %collective-permute-done.6), channel_id=1, source_target_pairs={{2,0},{4,2},{6,4},{3,1},{5,3},{7,5},{10,8},{12,10},{14,12},{11,9},... | collective-permute-start | bytes 2433032 | tf_op jit(solution)/shard_map/ppermute | solution.py:86
  66.9 19.6 %collective-permute-start.9 = (bf16[528,768]{1,0:T(8,128)(2,1)S(1)}, bf16[528,768]{1,0:T(8,128)(2,1)S(1)}, u32[]{:S(2)}, u32[]{:S(2)}) collective-permute-start(bf16[528,768]{1,0:T(8,128)(2,1)S(1)} %collective-permute-done.5), channel_id=1, source_target_pairs={{0,2},{2,4},{4,6},{1,3},{3,5},{5,7},{8,10},{10,12},{12,14},{9,11},... | collective-permute-start | bytes 2433032 | tf_op jit(solution)/shard_map/ppermute | solution.py:85
  72.2 14.5 %collective-permute-start.7 = (bf16[528,768]{1,0:T(8,128)(2,1)S(1)}, bf16[528,768]{1,0:T(8,128)(2,1)S(1)}, u32[]{:S(2)}, u32[]{:S(2)}) collective-permute-start(bf16[528,768]{1,0:T(8,128)(2,1)S(1)} %collective-permute-done.5), channel_id=1, source_target_pairs={{0,1},{1,0},{2,3},{3,2},{4,5},{5,4},{6,7},{7,6},{8,9},{9,8},{10,11... | collective-permute-start | bytes 2433032 | tf_op jit(solution)/shard_map/ppermute | solution.py:87
  72.3 15.2 %collective-permute-start.8 = (bf16[528,768]{1,0:T(8,128)(2,1)S(1)}, bf16[528,768]{1,0:T(8,128)(2,1)S(1)}, u32[]{:S(2)}, u32[]{:S(2)}) collective-permute-start(bf16[528,768]{1,0:T(8,128)(2,1)S(1)} %collective-permute-done.6), channel_id=1, source_target_pairs={{0,1},{1,0},{2,3},{3,2},{4,5},{5,4},{6,7},{7,6},{8,9},{9,8},{10,11... | collective-permute-start | bytes 2433032 | tf_op jit(solution)/shard_map/ppermute | solution.py:88
  87.8 5.8 %collective-permute-start.12 = (bf16[528,768]{1,0:T(8,128)(2,1)S(1)}, bf16[528,768]{1,0:T(8,128)(2,1)S(1)}, u32[]{:S(2)}, u32[]{:S(2)}) collective-permute-start(bf16[528,768]{1,0:T(8,128)(2,1)S(1)} %collective-permute-done.10), channel_id=1, source_target_pairs={{0,1},{1,0},{2,3},{3,2},{4,5},{5,4},{6,7},{7,6},{8,9},{9,8},{10,11... | collective-permute-start | bytes 2433032 | tf_op jit(solution)/shard_map/ppermute | solution.py:88
  87.8 6.1 %collective-permute-start.11 = (bf16[528,768]{1,0:T(8,128)(2,1)S(1)}, bf16[528,768]{1,0:T(8,128)(2,1)S(1)}, u32[]{:S(2)}, u32[]{:S(2)}) collective-permute-start(bf16[528,768]{1,0:T(8,128)(2,1)S(1)} %collective-permute-done.9), channel_id=1, source_target_pairs={{0,1},{1,0},{2,3},{3,2},{4,5},{5,4},{6,7},{7,6},{8,9},{9,8},{10,11... | collective-permute-start | bytes 2433032 | tf_op jit(solution)/shard_map/ppermute | solution.py:87

commit v4 on v3

--- a/solution.py
+++ b/solution.py
@@ -63,13 +63,16 @@
         exists = (other_chip >= 0) & (other_chip < chips)
         return jnp.where(exists, listed, 0).astype(jnp.float32)
 
-    def add_pair(acc, got, weight):
+    def pair_terms(acc, got, weight):
         summed, squares = acc
         got_data = got[:rows]
         got_counts = got[rows, :sources].astype(jnp.int32)
         weights = weigh(unit, normalize(got_data), live_of(got_counts, slot_rows), 1.0)
         part = jnp.dot(weights.astype(jnp.bfloat16), got_data, preferred_element_type=jnp.float32)
         return (summed + weight * part, squares + weight * jnp.sum(weights * weights, axis=1))
+
+    def add_pair(acc, got, weight):
+        return lax.cond(weight > 0, pair_terms, lambda acc, got, weight: acc, acc, got, weight)
 
     swap = [(c, (c + 1) % cores) for c in range(cores)]
     up = [(c, c + 1) for c in range(chips - 1)]
@@ -78,12 +81,14 @@
     tail = jnp.zeros((16, width), jnp.bfloat16).at[0, :sources].set(own_counts.astype(jnp.bfloat16))
     mine = jnp.concatenate([data, tail], axis=0)
     other_core = (core + 1) % cores
+    received = (lax.ppermute(mine, "chip", up), lax.ppermute(mine, "chip", down))
     swapped = lax.ppermute(mine, "core", swap)
     acc = add_pair(acc, swapped, times_listed(chip, other_core))
-    from_below, from_above = mine, mine
     for step in range(1, chips):
-        from_below = lax.ppermute(from_below, "chip", up)
-        from_above = lax.ppermute(from_above, "chip", down)
+        acc, received = lax.optimization_barrier((acc, received))
+        from_below, from_above = received
+        if step + 1 < chips:
+            received = (lax.ppermute(from_below, "chip", up), lax.ppermute(from_above, "chip", down))
         below_swapped = lax.ppermute(from_below, "core", swap)
         above_swapped = lax.ppermute(from_above, "core", swap)
         acc = add_pair(acc, from_below, times_listed(chip - step, core))

time: 99.7 us -> 109 us (1.093)
  other arithmetic: 7.91 us -> 13.5 us
  matrix products: 20.9 us -> 23 us
  waiting for transfers between devices: 44.4 us -> 46.3 us
  starting transfers between devices: 25.7 us -> 24 us
    dot_general x14 -> x8, matrix products: 10.1 us -> 14.5 us  [weigh(): scores = jnp.dot(unit_a, unit_b.T, preferred_element_type=jnp.float32)]
    dot_general x13 -> x7, matrix products: 10.1 us -> 7.92 us  [pair_terms(): jnp.dot(weights.astype(jnp.bfloat16), got_data, preferred_element_type=jn...]
    reduce_sum x14 -> x8, other arithmetic: 3.19 us -> 5.22 us  [normalize(): jnp.sum(values * values, axis=-1, keepdims=True) + EPS]
    convert_element_type x13 -> x7, other arithmetic: 0.07 us -> 2.05 us  [pair_terms(): got_counts = got[rows, :sources].astype(jnp.int32)]
    ppermute x6, waiting for transfers between devices: 32.5 us -> 34.4 us  [the longest x2 11.5 us: per_device(): lax.ppermute(from_above, 'chip', down)]
    ppermute x6, starting transfers between devices: 18.8 us -> 17.2 us  [the longest x2 8.93 us: per_device(): lax.ppermute(from_below, 'chip', up)]
    reshape x0 -> x1, other arithmetic: none -> 1.09 us  [per_device(): return result.astype(jnp.bfloat16).reshape(1, 1, rows, width)]
  transfers between devices with their start and end apart: 14 -> 14, of which waited for: 6 -> 7; matrix products, arithmetic and copies ran while one was open for 20% -> 27% of each run, Pallas kernels for 0% -> 0%
where the time goes in v4:
time: 109 us; the launch traced here: 108 us
  waiting for transfers between devices  46.3 us (42%)
  starting transfers between devices  24 us (22%)
  matrix products  23 us (21%)
  other arithmetic  13.5 us (12%)
    dot_general x8, matrix products, weigh(): scores = jnp.dot(unit_a, unit_b.T, preferred_element_type=jnp.float32)  14.5 us
    all_to_all x1, waiting for transfers between devices, per_device(): lax.all_to_all(packed, 'bucket', split_axis=2, concat_axis=0, tiled=True)  11.9 us
    ppermute x2, waiting for transfers between devices, per_device(): lax.ppermute(from_above, 'chip', down)  11.5 us
    ppermute x1, waiting for transfers between devices, per_device(): lax.ppermute(mine, 'chip', up)  10.2 us
    ppermute x2, starting transfers between devices, per_device(): lax.ppermute(from_below, 'chip', up)  8.93 us
    dot_general x7, matrix products, pair_terms(): jnp.dot(weights.astype(jnp.bfloat16), got_data, preferred_element_type=jn...  7.92 us
    ppermute x2, waiting for transfers between devices, per_device(): lax.ppermute(from_below, 'chip', up)  7.64 us
    reduce_sum x8, other arithmetic, normalize(): jnp.sum(values * values, axis=-1, keepdims=True) + EPS  5.22 us
  transfers between devices with their start and end apart: 14, of which 7 were waited for; matrix products, arithmetic and copies ran while one was open for 27% of the time, Pallas kernels for 0%

profile of v4, /device:TPU:0, one launch (start us, length us, event | category | flops | bytes accessed | tf_op | source)
XLA Modules:
  0.0 107.6 jit_solution(3141960131857637713)
XLA Ops:
  0.0 0.7 convert_bitcast_fusion.14
  0.8 2.1 %fusion.124 = bf16[1,1,4,144,768]{4,3,1,0,2:T(8,128)(2,1)} fusion(bf16[1,1,4,1,1]{4,3,1,0,2:T(2,128)(2,1)S(1)} %copy.7, bf16[1,1,4,128,768]{4,3,1,0,2:T(8,128)(2,1)} %bitcast.116), kind=kLoop, calls=%fused_computation.250 | loop fusion | flops 2654208 | bytes 1671176 | tf_op jit(solution)/shard_map/concatenate | solution.py:37
  2.9 5.2 %all-to-all-start = ((bf16[1,1,4,144,768]{4,3,1,0,2:T(8,128)(2,1)}), bf16[1,1,4,144,768]{4,3,1,0,2:T(8,128)(2,1)S(1)}, u32[]{:S(2)}, u32[]{:S(2)}) async-start(bf16[1,1,4,144,768]{4,3,1,0,2:T(8,128)(2,1)} %fusion.124), calls=%async_computation | async-start | bytes 1769472 | tf_op jit(solution)/shard_map/all_to_all | solution.py:38
  8.1 11.9 %all-to-all-done = bf16[1,1,4,144,768]{4,3,1,0,2:T(8,128)(2,1)S(1)} async-done(((bf16[1,1,4,144,768]{4,3,1,0,2:T(8,128)(2,1)}), bf16[1,1,4,144,768]{4,3,1,0,2:T(8,128)(2,1)S(1)}, u32[]{:S(2)}, u32[]{:S(2)}) %all-to-all-start) | async-done | bytes 884768 | tf_op jit(solution)/shard_map/all_to_all | solution.py:38
  20.7 4.4 %collective-permute-start.1 = (bf16[528,768]{1,0:T(8,128)(2,1)S(1)}, bf16[528,768]{1,0:T(8,128)(2,1)}, u32[]{:S(2)}, u32[]{:S(2)}) collective-permute-start(bf16[528,768]{1,0:T(8,128)(2,1)S(1)} %fusion.125), channel_id=1, source_target_pairs={{0,2},{2,4},{4,6},{1,3},{3,5},{5,7},{8,10},{10,12},{12,14},{9,11},... | collective-permute-start | bytes 2433032 | tf_op jit(solution)/shard_map/ppermute | solution.py:84
  25.1 1.3 %collective-permute-start.2 = (bf16[528,768]{1,0:T(8,128)(2,1)S(1)}, bf16[528,768]{1,0:T(8,128)(2,1)}, u32[]{:S(2)}, u32[]{:S(2)}) collective-permute-start(bf16[528,768]{1,0:T(8,128)(2,1)S(1)} %fusion.125), channel_id=1, source_target_pairs={{2,0},{4,2},{6,4},{3,1},{5,3},{7,5},{10,8},{12,10},{14,12},{11,9},... | collective-permute-start | bytes 2433032 | tf_op jit(solution)/shard_map/ppermute | solution.py:84
  26.7 0.7 multiply_reduce_fusion.13
  27.4 0.6 fusion.127
  28.0 1.1 %multiply_convert_fusion.1 = bf16[512,768]{1,0:T(8,128)(2,1)} fusion(f32[512]{0:T(512)S(1)} %get-tuple-element.378, bf16[4,1,1,128,768]{4,3,0,2,1:T(8,128)(2,1)S(1)} %slice.133), kind=kLoop, calls=%fused_computation.243 | loop fusion | flops 1179648 | bytes 1574912 | tf_op jit(solution)/shard_map/convert_element_type | solution.py:16
  29.1 2.9 %conditional.13 = ((f32[512,768]{1,0:T(8,128)S(1)}, f32[512]{0:T(512)S(1)})) conditional(s32[]{:T(128)} %convert_element_type.993, (f32[512,768]{1,0:T(8,128)S(1)}, f32[512]{0:T(512)S(1)}) %tuple.98, (f32[]{:T(128)}, bf16[528,768]{1,0:T(8,128)(2,1)S(1)}, bf16[512,768]{1,0:T(8,128)(2,1)}, f32[512,768]{1,0:T(8,128)S(1)}, f32[512]{0:T(512)S(1)}) %tuple.99), branch_computations={%region_2.0_spmd, %region_3.6_spmd} | conditional | flops 809764352 | bytes 7360584 | solution.py:75
  29.5 1.9 %multiply_reduce_fusion = (f32[512]{0:T(512)S(1)}, bf16[512,512]{1,0:T(8,128)(2,1)S(1)}) fusion(f32[512]{0:T(512)S(1)} %convert_bitcast_fusion, bf16[512,768]{1,0:T(8,128)(2,1)} %get-tuple-element.214, f32[512]{0:T(512)S(1)} %add_rsqrt_fusion, bf16[528,768]{1,0:T(8,128)(2,1)S(1)} %get-tuple-element.213), kind=kOutput, calls=%fused_computation.8 | convolution fusion | flops 405143040 | bytes 2103296 | tf_op jit(solution)/shard_map/cond/branch_1_fun/dot_general | solution.py:22
  31.3 0.6 multiply_add_fusion
  32.0 10.2 %collective-permute-done.1 = bf16[528,768]{1,0:T(8,128)(2,1)} collective-permute-done((bf16[528,768]{1,0:T(8,128)(2,1)S(1)}, bf16[528,768]{1,0:T(8,128)(2,1)}, u32[]{:S(2)}, u32[]{:S(2)}) %collective-permute-start.1) | collective-permute-done | bytes 811040 | tf_op jit(solution)/shard_map/ppermute | solution.py:84
  42.2 5.1 %collective-permute-done.2 = bf16[528,768]{1,0:T(8,128)(2,1)} collective-permute-done((bf16[528,768]{1,0:T(8,128)(2,1)S(1)}, bf16[528,768]{1,0:T(8,128)(2,1)}, u32[]{:S(2)}, u32[]{:S(2)}) %collective-permute-start.2) | collective-permute-done | bytes 811040 | tf_op jit(solution)/shard_map/ppermute | solution.py:84
  47.3 0.5 collective-permute-start.4
  47.8 3.5 %collective-permute-start.5 = (bf16[528,768]{1,0:T(8,128)(2,1)}, bf16[528,768]{1,0:T(8,128)(2,1)}, u32[]{:S(2)}, u32[]{:S(2)}) collective-permute-start(bf16[528,768]{1,0:T(8,128)(2,1)} %collective-permute-done.1), channel_id=1, source_target_pairs={{0,2},{2,4},{4,6},{1,3},{3,5},{5,7},{8,10},{10,12},{12,14},{9,11},... | collective-permute-start | bytes 2433032 | tf_op jit(solution)/shard_map/ppermute | solution.py:91
  51.3 1.3 %collective-permute-start.6 = (bf16[528,768]{1,0:T(8,128)(2,1)}, bf16[528,768]{1,0:T(8,128)(2,1)}, u32[]{:S(2)}, u32[]{:S(2)}) collective-permute-start(bf16[528,768]{1,0:T(8,128)(2,1)} %collective-permute-done.2), channel_id=1, source_target_pairs={{2,0},{4,2},{6,4},{3,1},{5,3},{7,5},{10,8},{12,10},{14,12},{11,9},... | collective-permute-start | bytes 2433032 | tf_op jit(solution)/shard_map/ppermute | solution.py:91
  52.8 6.0 %conditional.15 = ((f32[512,768]{1,0:T(8,128)S(1)}, f32[512]{0:T(512)S(1)})) conditional(s32[]{:T(128)} %convert_element_type.973, (f32[512,768]{1,0:T(8,128)S(1)}, f32[512]{0:T(512)S(1)}) %get-tuple-element.463, (f32[]{:T(128)}, bf16[528,768]{1,0:T(8,128)(2,1)}, bf16[512,768]{1,0:T(8,128)(2,1)}, f32[512,768]{1,0:T(8,128)S(1)}, ...), branch_computations={%region_10.11_spmd, %region_11.0_spmd} | conditional | flops 809764352 | bytes 7361092 | solution.py:75
  52.8 1.4 %fusion.18 = f32[512]{0:T(512)S(1)} fusion(bf16[528,768]{1,0:T(8,128)(2,1)} %get-tuple-element.223), kind=kLoop, calls=%fused_computation.38 | loop fusion | flops 1179136 | bytes 788480 | tf_op jit(solution)/shard_map/cond/branch_1_fun/reduce_sum | solution.py:16
  54.1 0.7 bitcast_convert_fusion.2
  54.9 2.1 %multiply_reduce_fusion.2 = (f32[512]{0:T(512)S(1)}, bf16[512,512]{1,0:T(8,128)(2,1)S(1)}) fusion(f32[512]{0:T(512)S(1)} %convert_bitcast_fusion.2, bf16[512,768]{1,0:T(8,128)(2,1)} %get-tuple-element.224, f32[512]{0:T(512)S(1)} %add_rsqrt_fusion.2, bf16[528,768]{1,0:T(8,128)(2,1)} %get-tuple-element.223), kind=kOutput, calls=%fused_computation.44 | convolution fusion | flops 405143040 | bytes 2103296 | tf_op jit(solution)/shard_map/cond/branch_1_fun/dot_general | solution.py:22
  57.0 1.8 %multiply_add_fusion.4 = f32[512,768]{1,0:T(8,128)S(1)} fusion(f32[512,768]{1,0:T(8,128)S(1)} %get-tuple-element.221, f32[]{:T(128)} %get-tuple-element.222, bf16[528,768]{1,0:T(8,128)(2,1)} %get-tuple-element.223, bf16[512,512]{1,0:T(8,128)(2,1)S(1)} %get-tuple-element.357), kind=kOutput, calls=%fused_computation.40 | convolution fusion | flops 403439616 | bytes 4456960 | tf_op jit(solution)/shard_map/cond/branch_1_fun/dot_general | solution.py:71
  58.8 2.9 %conditional.17 = ((f32[512,768]{1,0:T(8,128)S(1)}, f32[512]{0:T(512)S(1)})) conditional(s32[]{:T(128)} %convert_element_type.953, (f32[512,768]{1,0:T(8,128)S(1)}, f32[512]{0:T(512)S(1)}) %get-tuple-element.465, (f32[]{:T(128)}, bf16[528,768]{1,0:T(8,128)(2,1)S(1)}, bf16[512,768]{1,0:T(8,128)(2,1)}, f32[512,768]{1,0:T(8,128)S(1)}, ...), branch_computations={%region_18.19_spmd, %region_19.0_spmd} | conditional | flops 809764352 | bytes 7360584 | solution.py:75
  59.2 1.9 %multiply_reduce_fusion.4 = (f32[512]{0:T(512)S(1)}, bf16[512,512]{1,0:T(8,128)(2,1)S(1)}) fusion(f32[512]{0:T(512)S(1)} %convert_bitcast_fusion.4, bf16[512,768]{1,0:T(8,128)(2,1)} %get-tuple-element.234, f32[512]{0:T(512)S(1)} %add_rsqrt_fusion.4, bf16[528,768]{1,0:T(8,128)(2,1)S(1)} %get-tuple-element.233), kind=kOutput, calls=%fused_computation.80 | convolution fusion | flops 405143040 | bytes 2103296 | tf_op jit(solution)/shard_map/cond/branch_1_fun/dot_general | solution.py:22
  61.0 0.6 multiply_add_fusion.8
  61.7 6.5 %collective-permute-done.5 = bf16[528,768]{1,0:T(8,128)(2,1)} collective-permute-done((bf16[528,768]{1,0:T(8,128)(2,1)}, bf16[528,768]{1,0:T(8,128)(2,1)}, u32[]{:S(2)}, u32[]{:S(2)}) %collective-permute-start.5) | collective-permute-done | bytes 811040 | tf_op jit(solution)/shard_map/ppermute | solution.py:91
  68.2 5.0 %collective-permute-done.6 = bf16[528,768]{1,0:T(8,128)(2,1)} collective-permute-done((bf16[528,768]{1,0:T(8,128)(2,1)}, bf16[528,768]{1,0:T(8,128)(2,1)}, u32[]{:S(2)}, u32[]{:S(2)}) %collective-permute-start.6) | collective-permute-done | bytes 811040 | tf_op jit(solution)/shard_map/ppermute | solution.py:91
  73.7 1.3 %collective-permute-start.10 = (bf16[528,768]{1,0:T(8,128)(2,1)}, bf16[528,768]{1,0:T(8,128)(2,1)}, u32[]{:S(2)}, u32[]{:S(2)}) collective-permute-start(bf16[528,768]{1,0:T(8,128)(2,1)} %collective-permute-done.6), channel_id=1, source_target_pairs={{2,0},{4,2},{6,4},{3,1},{5,3},{7,5},{10,8},{12,10},{14,12},{11,9},... | collective-permute-start | bytes 2433032 | tf_op jit(solution)/shard_map/ppermute | solution.py:91
  75.0 5.5 %collective-permute-start.9 = (bf16[528,768]{1,0:T(8,128)(2,1)}, bf16[528,768]{1,0:T(8,128)(2,1)}, u32[]{:S(2)}, u32[]{:S(2)}) collective-permute-start(bf16[528,768]{1,0:T(8,128)(2,1)} %collective-permute-done.5), channel_id=1, source_target_pairs={{0,2},{2,4},{4,6},{1,3},{3,5},{5,7},{8,10},{10,12},{12,14},{9,11},... | collective-permute-start | bytes 2433032 | tf_op jit(solution)/shard_map/ppermute | solution.py:91
  80.4 6.0 %conditional.19 = ((f32[512,768]{1,0:T(8,128)S(1)}, f32[512]{0:T(512)S(1)})) conditional(s32[]{:T(128)} %convert_element_type.933, (f32[512,768]{1,0:T(8,128)S(1)}, f32[512]{0:T(512)S(1)}) %get-tuple-element.467, (f32[]{:T(128)}, bf16[528,768]{1,0:T(8,128)(2,1)}, bf16[512,768]{1,0:T(8,128)(2,1)}, f32[512,768]{1,0:T(8,128)S(1)}, ...), branch_computations={%region_26.27_spmd, %region_27.0_spmd} | conditional | flops 809764352 | bytes 7361092 | solution.py:75
  80.4 1.4 %fusion.54 = f32[512]{0:T(512)S(1)} fusion(bf16[528,768]{1,0:T(8,128)(2,1)} %get-tuple-element.243), kind=kLoop, calls=%fused_computation.110 | loop fusion | flops 1179136 | bytes 788480 | tf_op jit(solution)/shard_map/cond/branch_1_fun/reduce_sum | solution.py:16
  81.8 0.7 bitcast_convert_fusion.6
  82.5 2.1 %multiply_reduce_fusion.6 = (f32[512]{0:T(512)S(1)}, bf16[512,512]{1,0:T(8,128)(2,1)S(1)}) fusion(f32[512]{0:T(512)S(1)} %convert_bitcast_fusion.6, bf16[512,768]{1,0:T(8,128)(2,1)} %get-tuple-element.244, f32[512]{0:T(512)S(1)} %add_rsqrt_fusion.6, bf16[528,768]{1,0:T(8,128)(2,1)} %get-tuple-element.243), kind=kOutput, calls=%fused_computation.116 | convolution fusion | flops 405143040 | bytes 2103296 | tf_op jit(solution)/shard_map/cond/branch_1_fun/dot_general | solution.py:22
  84.6 1.8 %multiply_add_fusion.12 = f32[512,768]{1,0:T(8,128)S(1)} fusion(f32[512,768]{1,0:T(8,128)S(1)} %get-tuple-element.241, f32[]{:T(128)} %get-tuple-element.242, bf16[528,768]{1,0:T(8,128)(2,1)} %get-tuple-element.243, bf16[512,512]{1,0:T(8,128)(2,1)S(1)} %get-tuple-element.365), kind=kOutput, calls=%fused_computation.112 | convolution fusion | flops 403439616 | bytes 4456960 | tf_op jit(solution)/shard_map/cond/branch_1_fun/dot_general | solution.py:71
  86.5 2.9 %conditional.21 = ((f32[512,768]{1,0:T(8,128)S(1)}, f32[512]{0:T(512)S(1)})) conditional(s32[]{:T(128)} %convert_element_type.913, (f32[512,768]{1,0:T(8,128)S(1)}, f32[512]{0:T(512)S(1)}) %get-tuple-element.469, (f32[]{:T(128)}, bf16[528,768]{1,0:T(8,128)(2,1)S(1)}, bf16[512,768]{1,0:T(8,128)(2,1)}, f32[512,768]{1,0:T(8,128)S(1)}, ...), branch_computations={%region_34.35_spmd, %region_35.0_spmd} | conditional | flops 809764352 | bytes 7360584 | solution.py:75
  86.8 1.9 %multiply_reduce_fusion.8 = (f32[512]{0:T(512)S(1)}, bf16[512,512]{1,0:T(8,128)(2,1)S(1)}) fusion(f32[512]{0:T(512)S(1)} %convert_bitcast_fusion.8, bf16[512,768]{1,0:T(8,128)(2,1)} %get-tuple-element.254, f32[512]{0:T(512)S(1)} %add_rsqrt_fusion.8, bf16[528,768]{1,0:T(8,128)(2,1)S(1)} %get-tuple-element.253), kind=kOutput, calls=%fused_computation.152 | convolution fusion | flops 405143040 | bytes 2103296 | tf_op jit(solution)/shard_map/cond/branch_1_fun/dot_general | solution.py:22
  88.7 0.6 multiply_add_fusion.16
  89.3 6.5 %collective-permute-done.10 = bf16[528,768]{1,0:T(8,128)(2,1)} collective-permute-done((bf16[528,768]{1,0:T(8,128)(2,1)}, bf16[528,768]{1,0:T(8,128)(2,1)}, u32[]{:S(2)}, u32[]{:S(2)}) %collective-permute-start.10) | collective-permute-done | bytes 811040 | tf_op jit(solution)/shard_map/ppermute | solution.py:91
  95.8 1.2 %collective-permute-done.9 = bf16[528,768]{1,0:T(8,128)(2,1)} collective-permute-done((bf16[528,768]{1,0:T(8,128)(2,1)}, bf16[528,768]{1,0:T(8,128)(2,1)}, u32[]{:S(2)}, u32[]{:S(2)}) %collective-permute-start.9) | collective-permute-done | bytes 811040 | tf_op jit(solution)/shard_map/ppermute | solution.py:91
  97.5 6.0 %conditional.23 = ((f32[512,768]{1,0:T(8,128)S(1)}, f32[512]{0:T(512)S(1)})) conditional(s32[]{:T(128)} %convert_element_type.893, (f32[512,768]{1,0:T(8,128)S(1)}, f32[512]{0:T(512)S(1)}) %get-tuple-element.471, (f32[]{:T(128)}, bf16[528,768]{1,0:T(8,128)(2,1)}, bf16[512,768]{1,0:T(8,128)(2,1)}, f32[512,768]{1,0:T(8,128)S(1)}, ...), branch_computations={%region_42.43_spmd, %region_43.0_spmd} | conditional | flops 809764352 | bytes 7361092 | solution.py:75
  97.5 1.4 %fusion.90 = f32[512]{0:T(512)S(1)} fusion(bf16[528,768]{1,0:T(8,128)(2,1)} %get-tuple-element.263), kind=kLoop, calls=%fused_computation.182 | loop fusion | flops 1179136 | bytes 788480 | tf_op jit(solution)/shard_map/cond/branch_1_fun/reduce_sum | solution.py:16
  98.9 0.7 bitcast_convert_fusion.10
  99.7 2.1 %multiply_reduce_fusion.10 = (f32[512]{0:T(512)S(1)}, bf16[512,512]{1,0:T(8,128)(2,1)S(1)}) fusion(f32[512]{0:T(512)S(1)} %convert_bitcast_fusion.10, bf16[512,768]{1,0:T(8,128)(2,1)} %get-tuple-element.264, f32[512]{0:T(512)S(1)} %add_rsqrt_fusion.10, bf16[528,768]{1,0:T(8,128)(2,1)} %get-tuple-element.263), kind=kOutput, calls=%fused_computation.188 | convolution fusion | flops 405143040 | bytes 2103296 | tf_op jit(solution)/shard_map/cond/branch_1_fun/dot_general | solution.py:22
  101.8 1.8 %multiply_add_fusion.20 = f32[512,768]{1,0:T(8,128)S(1)} fusion(f32[512,768]{1,0:T(8,128)S(1)} %get-tuple-element.261, f32[]{:T(128)} %get-tuple-element.262, bf16[528,768]{1,0:T(8,128)(2,1)} %get-tuple-element.263, bf16[512,512]{1,0:T(8,128)(2,1)S(1)} %get-tuple-element.373), kind=kOutput, calls=%fused_computation.184 | convolution fusion | flops 403439616 | bytes 4456960 | tf_op jit(solution)/shard_map/cond/branch_1_fun/dot_general | solution.py:71
  103.6 2.9 %conditional.25 = ((f32[512,768]{1,0:T(8,128)S(1)}, f32[512]{0:T(512)S(1)})) conditional(s32[]{:T(128)} %convert_element_type.873, (f32[512,768]{1,0:T(8,128)S(1)}, f32[512]{0:T(512)S(1)}) %get-tuple-element.473, (f32[]{:T(128)}, bf16[528,768]{1,0:T(8,128)(2,1)S(1)}, bf16[512,768]{1,0:T(8,128)(2,1)}, f32[512,768]{1,0:T(8,128)S(1)}, ...), branch_computations={%region_50.51_spmd, %region_51.0_spmd} | conditional | flops 809764352 | bytes 7360584 | solution.py:75
  103.9 1.9 %multiply_reduce_fusion.12 = (f32[512]{0:T(512)S(1)}, bf16[512,512]{1,0:T(8,128)(2,1)S(1)}) fusion(f32[512]{0:T(512)S(1)} %convert_bitcast_fusion.12, bf16[512,768]{1,0:T(8,128)(2,1)} %get-tuple-element.274, f32[512]{0:T(512)S(1)} %add_rsqrt_fusion.12, bf16[528,768]{1,0:T(8,128)(2,1)S(1)} %get-tuple-element.273), kind=kOutput, calls=%fused_computation.224 | convolution fusion | flops 405143040 | bytes 2103296 | tf_op jit(solution)/shard_map/cond/branch_1_fun/dot_general | solution.py:22
  105.8 0.6 multiply_add_fusion.24
  106.5 1.1 %fusion.126 = bf16[1,1,512,768]{3,2,1,0:T(8,128)(2,1)} fusion(f32[512,768]{1,0:T(8,128)S(1)} %get-tuple-element.350, f32[512]{0:T(512)S(1)} %convert_bitcast_fusion.13, f32[512]{0:T(512)S(1)} %rsqrt.121), kind=kLoop, calls=%fused_computation.252 | loop fusion | flops 1179648 | bytes 2363392 | tf_op jit(solution)/shard_map/reshape | solution.py:100
  (58 shorter events, 3.7 us)
Async XLA Ops:
  2.9 17.1 %all-to-all-start = ((bf16[1,1,4,144,768]{4,3,1,0,2:T(8,128)(2,1)}), bf16[1,1,4,144,768]{4,3,1,0,2:T(8,128)(2,1)S(1)}, u32[]{:S(2)}, u32[]{:S(2)}) async-start(bf16[1,1,4,144,768]{4,3,1,0,2:T(8,128)(2,1)} %fusion.124), calls=%async_computation | async-start | bytes 1769472 | tf_op jit(solution)/shard_map/all_to_all | solution.py:38
  20.6 8.5 %collective-permute-start = (bf16[528,768]{1,0:T(8,128)(2,1)S(1)}, bf16[528,768]{1,0:T(8,128)(2,1)S(1)}, u32[]{:S(2)}, u32[]{:S(2)}) collective-permute-start(bf16[528,768]{1,0:T(8,128)(2,1)S(1)} %fusion.125), channel_id=1, source_target_pairs={{0,1},{1,0},{2,3},{3,2},{4,5},{5,4},{6,7},{7,6},{8,9},{9,8},{10,11... | collective-permute-start | bytes 2433032 | tf_op jit(solution)/shard_map/ppermute | solution.py:85
  20.7 21.5 %collective-permute-start.1 = (bf16[528,768]{1,0:T(8,128)(2,1)S(1)}, bf16[528,768]{1,0:T(8,128)(2,1)}, u32[]{:S(2)}, u32[]{:S(2)}) collective-permute-start(bf16[528,768]{1,0:T(8,128)(2,1)S(1)} %fusion.125), channel_id=1, source_target_pairs={{0,2},{2,4},{4,6},{1,3},{3,5},{5,7},{8,10},{10,12},{12,14},{9,11},... | collective-permute-start | bytes 2433032 | tf_op jit(solution)/shard_map/ppermute | solution.py:84
  25.1 22.2 %collective-permute-start.2 = (bf16[528,768]{1,0:T(8,128)(2,1)S(1)}, bf16[528,768]{1,0:T(8,128)(2,1)}, u32[]{:S(2)}, u32[]{:S(2)}) collective-permute-start(bf16[528,768]{1,0:T(8,128)(2,1)S(1)} %fusion.125), channel_id=1, source_target_pairs={{2,0},{4,2},{6,4},{3,1},{5,3},{7,5},{10,8},{12,10},{14,12},{11,9},... | collective-permute-start | bytes 2433032 | tf_op jit(solution)/shard_map/ppermute | solution.py:84
  47.3 11.5 %collective-permute-start.3 = (bf16[528,768]{1,0:T(8,128)(2,1)}, bf16[528,768]{1,0:T(8,128)(2,1)S(1)}, u32[]{:S(2)}, u32[]{:S(2)}) collective-permute-start(bf16[528,768]{1,0:T(8,128)(2,1)} %collective-permute-done.1), channel_id=1, source_target_pairs={{0,1},{1,0},{2,3},{3,2},{4,5},{5,4},{6,7},{7,6},{8,9},{9,8},{10,11... | collective-permute-start | bytes 2433032 | tf_op jit(solution)/shard_map/ppermute | solution.py:92
  47.3 11.6 %collective-permute-start.4 = (bf16[528,768]{1,0:T(8,128)(2,1)}, bf16[528,768]{1,0:T(8,128)(2,1)S(1)}, u32[]{:S(2)}, u32[]{:S(2)}) collective-permute-start(bf16[528,768]{1,0:T(8,128)(2,1)} %collective-permute-done.2), channel_id=1, source_target_pairs={{0,1},{1,0},{2,3},{3,2},{4,5},{5,4},{6,7},{7,6},{8,9},{9,8},{10,11... | collective-permute-start | bytes 2433032 | tf_op jit(solution)/shard_map/ppermute | solution.py:93
  47.8 20.4 %collective-permute-start.5 = (bf16[528,768]{1,0:T(8,128)(2,1)}, bf16[528,768]{1,0:T(8,128)(2,1)}, u32[]{:S(2)}, u32[]{:S(2)}) collective-permute-start(bf16[528,768]{1,0:T(8,128)(2,1)} %collective-permute-done.1), channel_id=1, source_target_pairs={{0,2},{2,4},{4,6},{1,3},{3,5},{5,7},{8,10},{10,12},{12,14},{9,11},... | collective-permute-start | bytes 2433032 | tf_op jit(solution)/shard_map/ppermute | solution.py:91
  51.3 21.9 %collective-permute-start.6 = (bf16[528,768]{1,0:T(8,128)(2,1)}, bf16[528,768]{1,0:T(8,128)(2,1)}, u32[]{:S(2)}, u32[]{:S(2)}) collective-permute-start(bf16[528,768]{1,0:T(8,128)(2,1)} %collective-permute-done.2), channel_id=1, source_target_pairs={{2,0},{4,2},{6,4},{3,1},{5,3},{7,5},{10,8},{12,10},{14,12},{11,9},... | collective-permute-start | bytes 2433032 | tf_op jit(solution)/shard_map/ppermute | solution.py:91
  73.2 13.3 %collective-permute-start.7 = (bf16[528,768]{1,0:T(8,128)(2,1)}, bf16[528,768]{1,0:T(8,128)(2,1)S(1)}, u32[]{:S(2)}, u32[]{:S(2)}) collective-permute-start(bf16[528,768]{1,0:T(8,128)(2,1)} %collective-permute-done.5), channel_id=1, source_target_pairs={{0,1},{1,0},{2,3},{3,2},{4,5},{5,4},{6,7},{7,6},{8,9},{9,8},{10,11... | collective-permute-start | bytes 2433032 | tf_op jit(solution)/shard_map/ppermute | solution.py:92
  73.2 13.3 %collective-permute-start.8 = (bf16[528,768]{1,0:T(8,128)(2,1)}, bf16[528,768]{1,0:T(8,128)(2,1)S(1)}, u32[]{:S(2)}, u32[]{:S(2)}) collective-permute-start(bf16[528,768]{1,0:T(8,128)(2,1)} %collective-permute-done.6), channel_id=1, source_target_pairs={{0,1},{1,0},{2,3},{3,2},{4,5},{5,4},{6,7},{7,6},{8,9},{9,8},{10,11... | collective-permute-start | bytes 2433032 | tf_op jit(solution)/shard_map/ppermute | solution.py:93
  73.7 22.2 %collective-permute-start.10 = (bf16[528,768]{1,0:T(8,128)(2,1)}, bf16[528,768]{1,0:T(8,128)(2,1)}, u32[]{:S(2)}, u32[]{:S(2)}) collective-permute-start(bf16[528,768]{1,0:T(8,128)(2,1)} %collective-permute-done.6), channel_id=1, source_target_pairs={{2,0},{4,2},{6,4},{3,1},{5,3},{7,5},{10,8},{12,10},{14,12},{11,9},... | collective-permute-start | bytes 2433032 | tf_op jit(solution)/shard_map/ppermute | solution.py:91
  75.0 22.1 %collective-permute-start.9 = (bf16[528,768]{1,0:T(8,128)(2,1)}, bf16[528,768]{1,0:T(8,128)(2,1)}, u32[]{:S(2)}, u32[]{:S(2)}) collective-permute-start(bf16[528,768]{1,0:T(8,128)(2,1)} %collective-permute-done.5), channel_id=1, source_target_pairs={{0,2},{2,4},{4,6},{1,3},{3,5},{5,7},{8,10},{10,12},{12,14},{9,11},... | collective-permute-start | bytes 2433032 | tf_op jit(solution)/shard_map/ppermute | solution.py:91
  97.0 6.5 %collective-permute-start.11 = (bf16[528,768]{1,0:T(8,128)(2,1)}, bf16[528,768]{1,0:T(8,128)(2,1)S(1)}, u32[]{:S(2)}, u32[]{:S(2)}) collective-permute-start(bf16[528,768]{1,0:T(8,128)(2,1)} %collective-permute-done.9), channel_id=1, source_target_pairs={{0,1},{1,0},{2,3},{3,2},{4,5},{5,4},{6,7},{7,6},{8,9},{9,8},{10,11... | collective-permute-start | bytes 2433032 | tf_op jit(solution)/shard_map/ppermute | solution.py:92
  97.0 6.6 %collective-permute-start.12 = (bf16[528,768]{1,0:T(8,128)(2,1)}, bf16[528,768]{1,0:T(8,128)(2,1)S(1)}, u32[]{:S(2)}, u32[]{:S(2)}) collective-permute-start(bf16[528,768]{1,0:T(8,128)(2,1)} %collective-permute-done.10), channel_id=1, source_target_pairs={{0,1},{1,0},{2,3},{3,2},{4,5},{5,4},{6,7},{7,6},{8,9},{9,8},{10,11... | collective-permute-start | bytes 2433032 | tf_op jit(solution)/shard_map/ppermute | solution.py:93

commit v5 on v4

--- a/solution.py
+++ b/solution.py
@@ -72,7 +72,7 @@
         return (summed + weight * part, squares + weight * jnp.sum(weights * weights, axis=1))
 
     def add_pair(acc, got, weight):
-        return lax.cond(weight > 0, pair_terms, lambda acc, got, weight: acc, acc, got, weight)
+        return pair_terms(acc, got, weight)
 
     swap = [(c, (c + 1) % cores) for c in range(cores)]
     up = [(c, c + 1) for c in range(chips - 1)]
@@ -87,8 +87,21 @@
     for step in range(1, chips):
         acc, received = lax.optimization_barrier((acc, received))
         from_below, from_above = received
-        if step + 1 < chips:
+        if step + 2 < chips:
             received = (lax.ppermute(from_below, "chip", up), lax.ppermute(from_above, "chip", down))
+        elif step + 2 == chips and chips >= 4:
+            ends = [(chips - 2, chips - 1), (1, 0)]
+            outgoing = jnp.where(chip == chips - 2, from_below, from_above)
+            last = lax.ppermute(outgoing, "chip", ends)
+            received = (last, last)
+        elif step + 2 == chips:
+            received = (lax.ppermute(from_below, "chip", up), lax.ppermute(from_above, "chip", down))
+        if step + 1 == chips and chips >= 4:
+            far_chip = jnp.where(chip == 0, chips - 1, jnp.where(chip == chips - 1, 0, -1))
+            far_swapped = lax.ppermute(from_below, "core", swap)
+            acc = add_pair(acc, from_below, times_listed(far_chip, core))
+            acc = add_pair(acc, far_swapped, times_listed(far_chip, other_core))
+            continue
         below_swapped = lax.ppermute(from_below, "core", swap)
         above_swapped = lax.ppermute(from_above, "core", swap)
         acc = add_pair(acc, from_below, times_listed(chip - step, core))

time: 109 us -> 101 us (0.927)
  waiting for transfers between devices: 46.3 us -> 57.8 us
  starting transfers between devices: 24 us -> 17.6 us
  other arithmetic: 13.5 us -> 7.31 us
  matrix products: 23 us -> 17.4 us
    ppermute x0 -> x2, waiting for transfers between devices: none -> 14.9 us  [the longest x1 14.2 us: per_device(): last = lax.ppermute(outgoing, 'chip', ends)]
    ppermute x2 -> x1, waiting for transfers between devices: 11.5 us -> 4.16 us  [per_device(): lax.ppermute(from_above, 'chip', down)]
    dot_general x8 -> x12, matrix products: 14.5 us -> 8.75 us  [weigh(): scores = jnp.dot(unit_a, unit_b.T, preferred_element_type=jnp.float32)]
    ppermute x2 -> x1, starting transfers between devices: 8.93 us -> 3.47 us  [per_device(): lax.ppermute(from_below, 'chip', up)]
    ppermute x1, waiting for transfers between devices: 10.2 us -> 12.9 us  [per_device(): lax.ppermute(mine, 'chip', up)]
    reduce_sum x8 -> x11, other arithmetic: 5.22 us -> 2.66 us  [normalize(): jnp.sum(values * values, axis=-1, keepdims=True) + EPS]
    ppermute x2 -> x1, waiting for transfers between devices: 7.64 us -> 9.81 us  [per_device(): lax.ppermute(from_below, 'chip', up)]
    convert_element_type x7 -> x10, other arithmetic: 2.05 us -> 0.05 us  [pair_terms(): got_counts = got[rows, :sources].astype(jnp.int32)]
  transfers between devices with their start and end apart: 14 -> 12, of which waited for: 7 -> 7; matrix products, arithmetic and copies ran while one was open for 27% -> 18% of each run, Pallas kernels for 0% -> 0%
where the time goes in v5:
time: 101 us
  waiting for transfers between devices  57.8 us (57%)
  starting transfers between devices  17.6 us (17%)
  matrix products  17.4 us (17%)
  other arithmetic  7.31 us (7%)
    ppermute x1, waiting for transfers between devices, per_device(): last = lax.ppermute(outgoing, 'chip', ends)  14.2 us
    ppermute x1, waiting for transfers between devices, per_device(): lax.ppermute(mine, 'chip', up)  12.9 us
    all_to_all x1, waiting for transfers between devices, per_device(): lax.all_to_all(packed, 'bucket', split_axis=2, concat_axis=0, tiled=True)  11.9 us
    ppermute x1, waiting for transfers between devices, per_device(): lax.ppermute(from_below, 'chip', up)  9.81 us
    dot_general x12, matrix products, weigh(): scores = jnp.dot(unit_a, unit_b.T, preferred_element_type=jnp.float32)  8.75 us
    dot_general x11, matrix products, pair_terms(): jnp.dot(weights.astype(jnp.bfloat16), got_data, preferred_element_type=jn...  8.01 us
    all_to_all x1, starting transfers between devices, per_device(): lax.all_to_all(packed, 'bucket', split_axis=2, concat_axis=0, tiled=True)  5.19 us
    ppermute x1, waiting for transfers between devices, per_device(): lax.ppermute(mine, 'chip', down)  4.16 us
  transfers between devices with their start and end apart: 12, of which 7 were waited for; matrix products, arithmetic and copies ran while one was open for 18% of the time, Pallas kernels for 0%

profile of v5, /device:TPU:0, one launch (start us, length us, event | category | flops | bytes accessed | tf_op | source)
XLA Modules:
  0.0 100.5 jit_solution(3550951425272764160)
XLA Ops:
  0.0 0.7 convert_bitcast_fusion.12
  0.8 2.1 %fusion.52 = bf16[1,1,4,144,768]{4,3,1,0,2:T(8,128)(2,1)} fusion(bf16[1,1,4,1,1]{4,3,1,0,2:T(2,128)(2,1)S(1)} %copy.7, bf16[1,1,4,128,768]{4,3,1,0,2:T(8,128)(2,1)} %bitcast.114), kind=kLoop, calls=%fused_computation.108 | loop fusion | flops 2654208 | bytes 1671176 | tf_op jit(solution)/shard_map/concatenate | solution.py:37
  2.9 5.2 %all-to-all-start = ((bf16[1,1,4,144,768]{4,3,1,0,2:T(8,128)(2,1)}), bf16[1,1,4,144,768]{4,3,1,0,2:T(8,128)(2,1)S(1)}, u32[]{:S(2)}, u32[]{:S(2)}) async-start(bf16[1,1,4,144,768]{4,3,1,0,2:T(8,128)(2,1)} %fusion.52), calls=%async_computation | async-start | bytes 1769472 | tf_op jit(solution)/shard_map/all_to_all | solution.py:38
  8.1 11.9 %all-to-all-done = bf16[1,1,4,144,768]{4,3,1,0,2:T(8,128)(2,1)S(1)} async-done(((bf16[1,1,4,144,768]{4,3,1,0,2:T(8,128)(2,1)}), bf16[1,1,4,144,768]{4,3,1,0,2:T(8,128)(2,1)S(1)}, u32[]{:S(2)}, u32[]{:S(2)}) %all-to-all-start) | async-done | bytes 884768 | tf_op jit(solution)/shard_map/all_to_all | solution.py:38
  20.0 0.2 fusion.2
  20.5 3.6 %collective-permute-start.1 = (bf16[528,768]{1,0:T(8,128)(2,1)S(1)}, bf16[528,768]{1,0:T(8,128)(2,1)S(1)}, u32[]{:S(2)}, u32[]{:S(2)}) collective-permute-start(bf16[528,768]{1,0:T(8,128)(2,1)S(1)} %fusion.53), channel_id=1, source_target_pairs={{0,2},{2,4},{4,6},{1,3},{3,5},{5,7},{8,10},{10,12},{12,14},{9,11},... | collective-permute-start | bytes 2433032 | tf_op jit(solution)/shard_map/ppermute | solution.py:84
  24.1 1.3 %collective-permute-start.2 = (bf16[528,768]{1,0:T(8,128)(2,1)S(1)}, bf16[528,768]{1,0:T(8,128)(2,1)S(1)}, u32[]{:S(2)}, u32[]{:S(2)}) collective-permute-start(bf16[528,768]{1,0:T(8,128)(2,1)S(1)} %fusion.53), channel_id=1, source_target_pairs={{2,0},{4,2},{6,4},{3,1},{5,3},{7,5},{10,8},{12,10},{14,12},{11,9},... | collective-permute-start | bytes 2433032 | tf_op jit(solution)/shard_map/ppermute | solution.py:84
  26.1 0.7 multiply_reduce_fusion.11
  26.8 0.6 fusion.116
  27.7 0.7 multiply_reduce_fusion.10
  28.5 0.6 multiply_add_fusion.2
  29.1 12.9 %collective-permute-done.1 = bf16[528,768]{1,0:T(8,128)(2,1)S(1)} collective-permute-done((bf16[528,768]{1,0:T(8,128)(2,1)S(1)}, bf16[528,768]{1,0:T(8,128)(2,1)S(1)}, u32[]{:S(2)}, u32[]{:S(2)}) %collective-permute-start.1) | collective-permute-done | bytes 811040 | tf_op jit(solution)/shard_map/ppermute | solution.py:84
  42.0 4.2 %collective-permute-done.2 = bf16[528,768]{1,0:T(8,128)(2,1)S(1)} collective-permute-done((bf16[528,768]{1,0:T(8,128)(2,1)S(1)}, bf16[528,768]{1,0:T(8,128)(2,1)S(1)}, u32[]{:S(2)}, u32[]{:S(2)}) %collective-permute-start.2) | collective-permute-done | bytes 811040 | tf_op jit(solution)/shard_map/ppermute | solution.py:84
  46.2 0.4 fusion.6
  46.6 0.6 collective-permute-start.4
  47.1 3.5 %collective-permute-start.5 = (bf16[528,768]{1,0:T(8,128)(2,1)S(1)}, bf16[528,768]{1,0:T(8,128)(2,1)S(1)}, u32[]{:S(2)}, u32[]{:S(2)}) collective-permute-start(bf16[528,768]{1,0:T(8,128)(2,1)S(1)} %collective-permute-done.1), channel_id=1, source_target_pairs={{0,2},{2,4},{4,6},{1,3},{3,5},{5,7},{8,10},{10,12},{12,14},{9,11},... | collective-permute-start | bytes 2433032 | tf_op jit(solution)/shard_map/ppermute | solution.py:91
  50.6 1.3 %collective-permute-start.6 = (bf16[528,768]{1,0:T(8,128)(2,1)S(1)}, bf16[528,768]{1,0:T(8,128)(2,1)S(1)}, u32[]{:S(2)}, u32[]{:S(2)}) collective-permute-start(bf16[528,768]{1,0:T(8,128)(2,1)S(1)} %collective-permute-done.2), channel_id=1, source_target_pairs={{2,0},{4,2},{6,4},{3,1},{5,3},{7,5},{10,8},{12,10},{14,12},{11,9},... | collective-permute-start | bytes 2433032 | tf_op jit(solution)/shard_map/ppermute | solution.py:91
  52.1 0.7 multiply_reduce_fusion.8
  52.8 0.7 multiply_reduce_fusion.9
  53.5 0.6 fusion.100
  54.1 0.6 fusion.103
  54.7 0.2 fusion.10
  55.1 0.2 fusion.12
  55.4 0.7 multiply_reduce_fusion.7
  56.1 0.7 multiply_reduce_fusion.6
  56.8 0.6 fusion.86
  57.4 0.8 multiply_add_fusion.1
  58.2 9.8 %collective-permute-done.5 = bf16[528,768]{1,0:T(8,128)(2,1)S(1)} collective-permute-done((bf16[528,768]{1,0:T(8,128)(2,1)S(1)}, bf16[528,768]{1,0:T(8,128)(2,1)S(1)}, u32[]{:S(2)}, u32[]{:S(2)}) %collective-permute-start.5) | collective-permute-done | bytes 811040 | tf_op jit(solution)/shard_map/ppermute | solution.py:91
  68.0 4.2 %collective-permute-done.6 = bf16[528,768]{1,0:T(8,128)(2,1)S(1)} collective-permute-done((bf16[528,768]{1,0:T(8,128)(2,1)S(1)}, bf16[528,768]{1,0:T(8,128)(2,1)S(1)}, u32[]{:S(2)}, u32[]{:S(2)}) %collective-permute-start.6) | collective-permute-done | bytes 811040 | tf_op jit(solution)/shard_map/ppermute | solution.py:91
  72.5 0.2 fusion.14
  72.8 0.6 collective-permute-start.8
  73.6 1.5 %collective-permute-start.9 = (bf16[528,768]{1,0:T(8,128)(2,1)S(1)}, bf16[528,768]{1,0:T(8,128)(2,1)S(1)}, u32[]{:S(2)}, u32[]{:S(2)}) collective-permute-start(bf16[528,768]{1,0:T(8,128)(2,1)S(1)} %broadcast_select_fusion), channel_id=1, source_target_pairs={{4,6},{2,0},{5,7},{3,1},{12,14},{10,8},{13,15},{11,9},{20,22},{18,... | collective-permute-start | bytes 2433032 | tf_op jit(solution)/shard_map/ppermute | solution.py:95
  75.1 0.7 multiply_reduce_fusion.4
  75.8 0.7 multiply_reduce_fusion.5
  76.5 0.6 fusion.94
  77.1 0.6 fusion.97
  77.7 0.2 fusion.18
  78.1 0.2 fusion.20
  78.4 0.7 multiply_reduce_fusion.3
  79.1 0.7 multiply_reduce_fusion.2
  79.9 0.6 fusion.81
  80.5 0.8 multiply_add_fusion
  81.2 14.2 %collective-permute-done.9 = bf16[528,768]{1,0:T(8,128)(2,1)S(1)} collective-permute-done((bf16[528,768]{1,0:T(8,128)(2,1)S(1)}, bf16[528,768]{1,0:T(8,128)(2,1)S(1)}, u32[]{:S(2)}, u32[]{:S(2)}) %collective-permute-start.9) | collective-permute-done | bytes 811040 | tf_op jit(solution)/shard_map/ppermute | solution.py:95
  95.8 0.7 multiply_reduce_fusion.1
  96.5 0.6 fusion.91
  97.1 0.7 collective-permute-done.10
  98.1 0.7 multiply_reduce_fusion
  98.9 1.7 %fusion.51 = bf16[1,1,512,768]{3,2,1,0:T(8,128)(2,1)} fusion(f32[512,768]{1,0:T(8,128)S(1)} %multiply_add_fusion, f32[512,768]{1,0:T(8,128)S(1)} %fusion.91, f32[512]{0:T(512)S(1)} %convert_bitcast_fusion.11, f32[512]{0:T(512)S(1)} %add_rsqrt_fusion, f32[]{:T(128)S(6)} %convert_element_type.884, f32[]{:T(128)S(6)} %convert_element_type.868, ...), kind=kOutput, calls=%fused_computation.94 | convolution fusion | flops 405405696 | bytes 5246984 | tf_op jit(solution)/shard_map/dot_general | solution.py:71
  (59 shorter events, 3.1 us)
Async XLA Ops:
  2.9 17.1 %all-to-all-start = ((bf16[1,1,4,144,768]{4,3,1,0,2:T(8,128)(2,1)}), bf16[1,1,4,144,768]{4,3,1,0,2:T(8,128)(2,1)S(1)}, u32[]{:S(2)}, u32[]{:S(2)}) async-start(bf16[1,1,4,144,768]{4,3,1,0,2:T(8,128)(2,1)} %fusion.52), calls=%async_computation | async-start | bytes 1769472 | tf_op jit(solution)/shard_map/all_to_all | solution.py:38
  20.4 7.0 %collective-permute-start = (bf16[528,768]{1,0:T(8,128)(2,1)S(1)}, bf16[528,768]{1,0:T(8,128)(2,1)S(1)}, u32[]{:S(2)}, u32[]{:S(2)}) collective-permute-start(bf16[528,768]{1,0:T(8,128)(2,1)S(1)} %fusion.53), channel_id=1, source_target_pairs={{0,1},{1,0},{2,3},{3,2},{4,5},{5,4},{6,7},{7,6},{8,9},{9,8},{10,11... | collective-permute-start | bytes 2433032 | tf_op jit(solution)/shard_map/ppermute | solution.py:85
  20.5 21.5 %collective-permute-start.1 = (bf16[528,768]{1,0:T(8,128)(2,1)S(1)}, bf16[528,768]{1,0:T(8,128)(2,1)S(1)}, u32[]{:S(2)}, u32[]{:S(2)}) collective-permute-start(bf16[528,768]{1,0:T(8,128)(2,1)S(1)} %fusion.53), channel_id=1, source_target_pairs={{0,2},{2,4},{4,6},{1,3},{3,5},{5,7},{8,10},{10,12},{12,14},{9,11},... | collective-permute-start | bytes 2433032 | tf_op jit(solution)/shard_map/ppermute | solution.py:84
  24.1 22.1 %collective-permute-start.2 = (bf16[528,768]{1,0:T(8,128)(2,1)S(1)}, bf16[528,768]{1,0:T(8,128)(2,1)S(1)}, u32[]{:S(2)}, u32[]{:S(2)}) collective-permute-start(bf16[528,768]{1,0:T(8,128)(2,1)S(1)} %fusion.53), channel_id=1, source_target_pairs={{2,0},{4,2},{6,4},{3,1},{5,3},{7,5},{10,8},{12,10},{14,12},{11,9},... | collective-permute-start | bytes 2433032 | tf_op jit(solution)/shard_map/ppermute | solution.py:84
  46.2 8.6 %collective-permute-start.3 = (bf16[528,768]{1,0:T(8,128)(2,1)S(1)}, bf16[528,768]{1,0:T(8,128)(2,1)S(1)}, u32[]{:S(2)}, u32[]{:S(2)}) collective-permute-start(bf16[528,768]{1,0:T(8,128)(2,1)S(1)} %collective-permute-done.1), channel_id=1, source_target_pairs={{0,1},{1,0},{2,3},{3,2},{4,5},{5,4},{6,7},{7,6},{8,9},{9,8},{10,11... | collective-permute-start | bytes 2433032 | tf_op jit(solution)/shard_map/ppermute | solution.py:105
  46.6 8.5 %collective-permute-start.4 = (bf16[528,768]{1,0:T(8,128)(2,1)S(1)}, bf16[528,768]{1,0:T(8,128)(2,1)S(1)}, u32[]{:S(2)}, u32[]{:S(2)}) collective-permute-start(bf16[528,768]{1,0:T(8,128)(2,1)S(1)} %collective-permute-done.2), channel_id=1, source_target_pairs={{0,1},{1,0},{2,3},{3,2},{4,5},{5,4},{6,7},{7,6},{8,9},{9,8},{10,11... | collective-permute-start | bytes 2433032 | tf_op jit(solution)/shard_map/ppermute | solution.py:106
  47.1 20.9 %collective-permute-start.5 = (bf16[528,768]{1,0:T(8,128)(2,1)S(1)}, bf16[528,768]{1,0:T(8,128)(2,1)S(1)}, u32[]{:S(2)}, u32[]{:S(2)}) collective-permute-start(bf16[528,768]{1,0:T(8,128)(2,1)S(1)} %collective-permute-done.1), channel_id=1, source_target_pairs={{0,2},{2,4},{4,6},{1,3},{3,5},{5,7},{8,10},{10,12},{12,14},{9,11},... | collective-permute-start | bytes 2433032 | tf_op jit(solution)/shard_map/ppermute | solution.py:91
  50.6 21.6 %collective-permute-start.6 = (bf16[528,768]{1,0:T(8,128)(2,1)S(1)}, bf16[528,768]{1,0:T(8,128)(2,1)S(1)}, u32[]{:S(2)}, u32[]{:S(2)}) collective-permute-start(bf16[528,768]{1,0:T(8,128)(2,1)S(1)} %collective-permute-done.2), channel_id=1, source_target_pairs={{2,0},{4,2},{6,4},{3,1},{5,3},{7,5},{10,8},{12,10},{14,12},{11,9},... | collective-permute-start | bytes 2433032 | tf_op jit(solution)/shard_map/ppermute | solution.py:91
  72.4 5.3 %collective-permute-start.7 = (bf16[528,768]{1,0:T(8,128)(2,1)S(1)}, bf16[528,768]{1,0:T(8,128)(2,1)S(1)}, u32[]{:S(2)}, u32[]{:S(2)}) collective-permute-start(bf16[528,768]{1,0:T(8,128)(2,1)S(1)} %collective-permute-done.5), channel_id=1, source_target_pairs={{0,1},{1,0},{2,3},{3,2},{4,5},{5,4},{6,7},{7,6},{8,9},{9,8},{10,11... | collective-permute-start | bytes 2433032 | tf_op jit(solution)/shard_map/ppermute | solution.py:105
  72.8 5.3 %collective-permute-start.8 = (bf16[528,768]{1,0:T(8,128)(2,1)S(1)}, bf16[528,768]{1,0:T(8,128)(2,1)S(1)}, u32[]{:S(2)}, u32[]{:S(2)}) collective-permute-start(bf16[528,768]{1,0:T(8,128)(2,1)S(1)} %collective-permute-done.6), channel_id=1, source_target_pairs={{0,1},{1,0},{2,3},{3,2},{4,5},{5,4},{6,7},{7,6},{8,9},{9,8},{10,11... | collective-permute-start | bytes 2433032 | tf_op jit(solution)/shard_map/ppermute | solution.py:106
  73.6 21.9 %collective-permute-start.9 = (bf16[528,768]{1,0:T(8,128)(2,1)S(1)}, bf16[528,768]{1,0:T(8,128)(2,1)S(1)}, u32[]{:S(2)}, u32[]{:S(2)}) collective-permute-start(bf16[528,768]{1,0:T(8,128)(2,1)S(1)} %broadcast_select_fusion), channel_id=1, source_target_pairs={{4,6},{2,0},{5,7},{3,1},{12,14},{10,8},{13,15},{11,9},{20,22},{18,... | collective-permute-start | bytes 2433032 | tf_op jit(solution)/shard_map/ppermute | solution.py:95
  95.5 2.3 %collective-permute-start.10 = (bf16[528,768]{1,0:T(8,128)(2,1)S(1)}, bf16[528,768]{1,0:T(8,128)(2,1)S(1)}, u32[]{:S(2)}, u32[]{:S(2)}) collective-permute-start(bf16[528,768]{1,0:T(8,128)(2,1)S(1)} %collective-permute-done.9), channel_id=1, source_target_pairs={{0,1},{1,0},{2,3},{3,2},{4,5},{5,4},{6,7},{7,6},{8,9},{9,8},{10,11... | collective-permute-start | bytes 2433032 | tf_op jit(solution)/shard_map/ppermute | solution.py:101

commit v6 on v3

v6 whole, which is shorter than its diff:
```python
import jax
import jax.numpy as jnp
from jax import lax
from jax.sharding import Mesh, PartitionSpec as P

ROUNDS = 4


EPS = 1e-06
TEMP = 12.0
CORES = 2
COUNT_ROWS = 16


def normalize(block):
    values = block.astype(jnp.float32)
    return (values * lax.rsqrt(jnp.sum(values * values, axis=-1, keepdims=True) + EPS)).astype(
        jnp.bfloat16
    )


def weigh(unit_a, unit_b, live_b, extra):
    scores = jnp.dot(unit_a, unit_b.T, preferred_element_type=jnp.float32)
    return jnp.exp(TEMP * scores) * live_b[None, :] * extra


def split_pieces(pieces, slot_rows):
    n, _, width = pieces.shape
    data = pieces[:, :slot_rows].reshape(n * slot_rows, width)
    piece_counts = pieces[:, slot_rows, 0].astype(jnp.int32)
    slot_index = lax.broadcasted_iota(jnp.int32, (n, slot_rows), 1)
    live = (slot_index < piece_counts[:, None]).astype(jnp.float32).reshape(-1)
    return data, live


def per_device(embeddings, counts):
    buckets = lax.axis_size("bucket")
    bucket = lax.axis_index("bucket")
    slot_rows = embeddings.shape[3]
    width = embeddings.shape[4]
    count_rows = jnp.zeros(embeddings.shape[2:3] + (COUNT_ROWS, width), jnp.bfloat16)
    count_rows = count_rows.at[:, 0, 0].set(counts[0, 0, :, 0].astype(jnp.bfloat16))
    packed = jnp.concatenate([embeddings[0, 0], count_rows], axis=1)

    arrived = [lax.dynamic_index_in_dim(packed, bucket, axis=0, keepdims=False)]
    for m in range(1, buckets):
        outgoing = lax.dynamic_index_in_dim(packed, bucket ^ m, axis=0, keepdims=False)
        arrived.append(lax.ppermute(outgoing, "bucket", [(i, i ^ m) for i in range(buckets)]))
    half = buckets // 2
    halves = [jnp.stack(arrived[:half]), jnp.stack(arrived[half:])]

    own_data, live = split_pieces(jnp.stack(arrived), slot_rows)
    rows = own_data.shape[0]
    chips = lax.axis_size("chip")
    cores = lax.axis_size("core")
    blocks = chips * cores
    chip = lax.axis_index("chip")
    core = lax.axis_index("core")
    position = chip * cores + core
    other_core = (core + 1) % cores

    unit = normalize(own_data)
    not_self = 1.0 - jnp.eye(rows, dtype=jnp.float32)
    own = weigh(unit, unit, live, not_self)
    summed = jnp.dot(own.astype(jnp.bfloat16), own_data, preferred_element_type=jnp.float32)
    squares = jnp.sum(own * own, axis=1)
    acc = (summed, squares)

    def times_listed(other_chip, other_core):
        block = other_chip * cores + other_core
        listed = jnp.int32(0)
        for dist in range(1, ROUNDS + 1):
            for sign in (1, -1):
                listed = listed + (((position + sign * dist) % blocks) == block).astype(jnp.int32)
        exists = (other_chip >= 0) & (other_chip < chips)
        return jnp.where(exists, listed, 0).astype(jnp.float32)

    def add_pair(acc, got, weight):
        summed, squares = acc
        got_data, got_live = split_pieces(got, slot_rows)
        weights = weigh(unit, normalize(got_data), got_live, 1.0)
        part = jnp.dot(weights.astype(jnp.bfloat16), got_data, preferred_element_type=jnp.float32)
        return (summed + weight * part, squares + weight * jnp.sum(weights * weights, axis=1))

    swap = [(c, (c + 1) % cores) for c in range(cores)]
    up = [(c, c + 1) for c in range(chips - 1)]
    down = [(c + 1, c) for c in range(chips - 1)]
    ends = chips >= 4

    def relay(piece):
        yield lax.ppermute(piece, "core", swap), times_listed(chip, other_core)
        from_below, from_above = piece, piece
        for step in range(1, chips):
            if ends and step + 1 == chips:
                outgoing = jnp.where(chip == chips - 2, from_below, from_above)
                far = lax.ppermute(outgoing, "chip", [(chips - 2, chips - 1), (1, 0)])
                far_chip = jnp.where(chip == 0, chips - 1, jnp.where(chip == chips - 1, 0, -1))
                yield far, times_listed(far_chip, core)
                yield lax.ppermute(far, "core", swap), times_listed(far_chip, other_core)
                return
            from_below = lax.ppermute(from_below, "chip", up)
            from_above = lax.ppermute(from_above, "chip", down)
            yield from_below, times_listed(chip - step, core)
            yield from_above, times_listed(chip + step, core)
            yield lax.ppermute(from_below, "core", swap), times_listed(chip - step, other_core)
            yield lax.ppermute(from_above, "core", swap), times_listed(chip + step, other_core)

    first, second = relay(halves[0]), relay(halves[1])
    for a, b in zip(first, second):
        acc = add_pair(acc, *a)
        acc = add_pair(acc, *b)
        acc = lax.optimization_barrier(acc)
    summed, squares = acc
    result = summed * lax.rsqrt(squares)[:, None] * live[:, None]
    result = result.astype(jnp.bfloat16).reshape(buckets, slot_rows, width)
    order = jnp.arange(buckets, dtype=jnp.int32) ^ bucket
    result = jnp.take(result, order, axis=0)
    return result.reshape(1, 1, rows, width)


def solution(mesh):
    devices = mesh.devices
    split = Mesh(
        devices.reshape(devices.shape[0], devices.shape[1] // CORES, CORES),
        ("bucket", "chip", "core"),
    )
    group = ("chip", "core")
    in_specs = (P("bucket", group, None, None, None), P("bucket", group, None, None))
    out_specs = P("bucket", group, None, None)
    return jax.shard_map(
        per_device, mesh=split, in_specs=in_specs, out_specs=out_specs, check_vma=False
    )
```

time: 99.7 us -> 117 us (1.17)
  other arithmetic: 7.91 us -> 15.1 us
  waiting for transfers between devices: 44.4 us -> 48.6 us
  starting transfers between devices: 25.7 us -> 28.4 us
  local copies, waits for them, and re-layouts: 0.16 us -> 1.85 us
  between operations: 0.36 us -> 1.57 us
    ppermute x13 -> x25, waiting for transfers between devices: 32.5 us -> 48.6 us  [the longest x4 15.8 us: relay(): from_below = lax.ppermute(from_below, 'chip', up)]
    all_to_all x1 -> x0, waiting for transfers between devices: 11.9 us -> none  [per_device(): lax.all_to_all(packed, 'bucket', split_axis=2, concat_axis=0, tiled=True)]
    ppermute x13 -> x25, starting transfers between devices: 20.5 us -> 28.4 us  [the longest x4 12.7 us: relay(): from_below = lax.ppermute(from_below, 'chip', up)]
    all_to_all x1 -> x0, starting transfers between devices: 5.19 us -> none  [per_device(): lax.all_to_all(packed, 'bucket', split_axis=2, concat_axis=0, tiled=True)]
    convert_element_type x30 -> x48, other arithmetic: 2.02 us -> 5.35 us  [the longest x23 2.83 us: split_pieces(): piece_counts = pieces[:, slot_rows, 0].astype(jnp.int32)]
    convert_element_type x2 -> x23, other arithmetic: 0.43 us -> 3.12 us  [normalize(): (values * lax.rsqrt(jnp.sum(values * values, axis=-1, keepdims=True) + EP...]
    dot_general x13 -> x22, matrix products: 10.1 us -> 9.12 us  [add_pair(): jnp.dot(weights.astype(jnp.bfloat16), got_data, preferred_element_type=jn...]
    dot_general x14 -> x23, matrix products: 10.1 us -> 10.9 us  [weigh(): scores = jnp.dot(unit_a, unit_b.T, preferred_element_type=jnp.float32)]
  transfers between devices with their start and end apart: 14 -> 25, of which waited for: 6 -> 12; matrix products, arithmetic and copies ran while one was open for 20% -> 20% of each run, Pallas kernels for 0% -> 0%
where the time goes in v6:
time: 117 us; the launch traced here: 116 us
  waiting for transfers between devices  48.6 us (42%)
  starting transfers between devices  28.4 us (24%)
  matrix products  20.6 us (18%)
  other arithmetic  15.1 us (13%)
  local copies, waits for them, and re-layouts  1.85 us (2%)
  between operations  1.57 us (1%)
    ppermute x4, waiting for transfers between devices, relay(): from_below = lax.ppermute(from_below, 'chip', up)  15.8 us
    ppermute x2, waiting for transfers between devices, relay(): far = lax.ppermute(outgoing, 'chip', [(chips - 2, chips - 1), (1, 0)])  13.5 us
    ppermute x4, starting transfers between devices, relay(): from_below = lax.ppermute(from_below, 'chip', up)  12.7 us
    dot_general x23, matrix products, weigh(): scores = jnp.dot(unit_a, unit_b.T, preferred_element_type=jnp.float32)  10.9 us
    ppermute x3, waiting for transfers between devices, per_device(): lax.ppermute(outgoing, 'bucket', [(i, i ^ m) for i in range(buckets)])  9.29 us
    dot_general x22, matrix products, add_pair(): jnp.dot(weights.astype(jnp.bfloat16), got_data, preferred_element_type=jn...  9.12 us
    ppermute x4, waiting for transfers between devices, relay(): from_above = lax.ppermute(from_above, 'chip', down)  8.38 us
    ppermute x4, starting transfers between devices, relay(): from_above = lax.ppermute(from_above, 'chip', down)  5.35 us
  transfers between devices with their start and end apart: 25, of which 12 were waited for; matrix products, arithmetic and copies ran while one was open for 20% of the time, Pallas kernels for 0%

profile of v6, /device:TPU:0, one launch (start us, length us, event | category | flops | bytes accessed | tf_op | source)
XLA Modules:
  0.0 116.2 jit_solution(834416788404397060)
XLA Ops:
  0.0 0.7 convert_bitcast_fusion.1
  0.8 1.2 %fusion.50 = bf16[4,144,768]{2,1,0:T(8,128)(2,1)S(1)} fusion(bf16[4,1,1]{2,1,0:T(2,128)(2,1)S(1)} %copy.5, bf16[4,128,768]{2,1,0:T(8,128)(2,1)} %bitcast.236), kind=kLoop, calls=%fused_computation.135 | loop fusion | flops 2654208 | bytes 1671176 | tf_op jit(solution)/shard_map/concatenate | solution.py:43
  2.1 4.0 %collective-permute-start.2 = (bf16[144,768]{1,0:T(8,128)(2,1)S(1)}, bf16[144,768]{1,0:T(8,128)(2,1)S(1)}, u32[]{:S(2)}, u32[]{:S(2)}) collective-permute-start(bf16[144,768]{1,0:T(8,128)(2,1)S(1)} %get-tuple-element.62), channel_id=1, source_target_pairs={{0,24},{8,16},{16,8},{24,0},{1,25},{9,17},{17,9},{25,1},{2,26},{10... | collective-permute-start | bytes 663560 | tf_op jit(solution)/shard_map/ppermute | solution.py:48
  6.0 0.5 collective-permute-start.1
  7.2 5.2 %collective-permute-done.2 = bf16[144,768]{1,0:T(8,128)(2,1)S(1)} collective-permute-done((bf16[144,768]{1,0:T(8,128)(2,1)S(1)}, bf16[144,768]{1,0:T(8,128)(2,1)S(1)}, u32[]{:S(2)}, u32[]{:S(2)}) %collective-permute-start.2) | collective-permute-done | bytes 221216 | tf_op jit(solution)/shard_map/ppermute | solution.py:48
  12.4 3.8 %collective-permute-done.1 = bf16[144,768]{1,0:T(8,128)(2,1)S(1)} collective-permute-done((bf16[144,768]{1,0:T(8,128)(2,1)S(1)}, bf16[144,768]{1,0:T(8,128)(2,1)S(1)}, u32[]{:S(2)}, u32[]{:S(2)}) %collective-permute-start.1) | collective-permute-done | bytes 221216 | tf_op jit(solution)/shard_map/ppermute | solution.py:48
  17.2 3.5 %collective-permute-start.5 = (bf16[2,144,768]{2,1,0:T(8,128)(2,1)S(1)}, bf16[2,144,768]{2,1,0:T(8,128)(2,1)S(1)}, u32[]{:S(2)}, u32[]{:S(2)}) collective-permute-start(bf16[2,144,768]{2,1,0:T(8,128)(2,1)S(1)} %pad_maximum_fusion.1), channel_id=1, source_target_pairs={{0,2},{2,4},{4,6},{1,3},{3,5},{5,7},{8,10},{10,12},{12,14},{9,11},... | collective-permute-start | bytes 1327112 | tf_op jit(solution)/shard_map/ppermute | solution.py:101
  21.0 3.5 %collective-permute-start.6 = (bf16[2,144,768]{2,1,0:T(8,128)(2,1)S(1)}, bf16[2,144,768]{2,1,0:T(8,128)(2,1)S(1)}, u32[]{:S(2)}, u32[]{:S(2)}) collective-permute-start(bf16[2,144,768]{2,1,0:T(8,128)(2,1)S(1)} %pad_maximum_fusion.2), channel_id=1, source_target_pairs={{0,2},{2,4},{4,6},{1,3},{3,5},{5,7},{8,10},{10,12},{12,14},{9,11},... | collective-permute-start | bytes 1327112 | tf_op jit(solution)/shard_map/ppermute | solution.py:101
  24.5 1.3 %collective-permute-start.7 = (bf16[2,144,768]{2,1,0:T(8,128)(2,1)S(1)}, bf16[2,144,768]{2,1,0:T(8,128)(2,1)S(1)}, u32[]{:S(2)}, u32[]{:S(2)}) collective-permute-start(bf16[2,144,768]{2,1,0:T(8,128)(2,1)S(1)} %pad_maximum_fusion.1), channel_id=1, source_target_pairs={{2,0},{4,2},{6,4},{3,1},{5,3},{7,5},{10,8},{12,10},{14,12},{11,9},... | collective-permute-start | bytes 1327112 | tf_op jit(solution)/shard_map/ppermute | solution.py:102
  26.1 0.7 multiply_reduce_fusion
  27.2 0.6 fusion.95
  27.8 1.3 %collective-permute-start.8 = (bf16[2,144,768]{2,1,0:T(8,128)(2,1)S(1)}, bf16[2,144,768]{2,1,0:T(8,128)(2,1)S(1)}, u32[]{:S(2)}, u32[]{:S(2)}) collective-permute-start(bf16[2,144,768]{2,1,0:T(8,128)(2,1)S(1)} %pad_maximum_fusion.2), channel_id=1, source_target_pairs={{2,0},{4,2},{6,4},{3,1},{5,3},{7,5},{10,8},{12,10},{14,12},{11,9},... | collective-permute-start | bytes 1327112 | tf_op jit(solution)/shard_map/ppermute | solution.py:102
  31.1 0.5 multiply_reduce_fusion.21
  32.4 7.9 %collective-permute-done.6 = bf16[2,144,768]{2,1,0:T(8,128)(2,1)S(1)} collective-permute-done((bf16[2,144,768]{2,1,0:T(8,128)(2,1)S(1)}, bf16[2,144,768]{2,1,0:T(8,128)(2,1)S(1)}, u32[]{:S(2)}, u32[]{:S(2)}) %collective-permute-start.6) | collective-permute-done | bytes 442400 | tf_op jit(solution)/shard_map/ppermute | solution.py:101
  40.8 0.5 multiply_reduce_fusion.20
  43.1 4.8 %collective-permute-done.8 = bf16[2,144,768]{2,1,0:T(8,128)(2,1)S(1)} collective-permute-done((bf16[2,144,768]{2,1,0:T(8,128)(2,1)S(1)}, bf16[2,144,768]{2,1,0:T(8,128)(2,1)S(1)}, u32[]{:S(2)}, u32[]{:S(2)}) %collective-permute-start.8) | collective-permute-done | bytes 442400 | tf_op jit(solution)/shard_map/ppermute | solution.py:102
  49.5 0.5 multiply_reduce_fusion.17
  50.6 0.5 collective-permute-start.10
  51.6 3.5 %collective-permute-start.13 = (bf16[2,144,768]{2,1,0:T(8,128)(2,1)S(1)}, bf16[2,144,768]{2,1,0:T(8,128)(2,1)S(1)}, u32[]{:S(2)}, u32[]{:S(2)}) collective-permute-start(bf16[2,144,768]{2,1,0:T(8,128)(2,1)S(1)} %collective-permute-done.5), channel_id=1, source_target_pairs={{0,2},{2,4},{4,6},{1,3},{3,5},{5,7},{8,10},{10,12},{12,14},{9,11},... | collective-permute-start | bytes 1327112 | tf_op jit(solution)/shard_map/ppermute | solution.py:101
  55.1 2.2 %collective-permute-start.14 = (bf16[2,144,768]{2,1,0:T(8,128)(2,1)S(1)}, bf16[2,144,768]{2,1,0:T(8,128)(2,1)S(1)}, u32[]{:S(2)}, u32[]{:S(2)}) collective-permute-start(bf16[2,144,768]{2,1,0:T(8,128)(2,1)S(1)} %collective-permute-done.6), channel_id=1, source_target_pairs={{0,2},{2,4},{4,6},{1,3},{3,5},{5,7},{8,10},{10,12},{12,14},{9,11},... | collective-permute-start | bytes 1327112 | tf_op jit(solution)/shard_map/ppermute | solution.py:101
  57.7 1.3 %collective-permute-start.15 = (bf16[2,144,768]{2,1,0:T(8,128)(2,1)S(1)}, bf16[2,144,768]{2,1,0:T(8,128)(2,1)S(1)}, u32[]{:S(2)}, u32[]{:S(2)}) collective-permute-start(bf16[2,144,768]{2,1,0:T(8,128)(2,1)S(1)} %collective-permute-done.7), channel_id=1, source_target_pairs={{2,0},{4,2},{6,4},{3,1},{5,3},{7,5},{10,8},{12,10},{14,12},{11,9},... | collective-permute-start | bytes 1327112 | tf_op jit(solution)/shard_map/ppermute | solution.py:102
  59.5 0.5 multiply_reduce_fusion.16
  60.5 0.5 multiply_reduce_fusion.15
  61.5 1.5 %collective-permute-start.16 = (bf16[2,144,768]{2,1,0:T(8,128)(2,1)S(1)}, bf16[2,144,768]{2,1,0:T(8,128)(2,1)S(1)}, u32[]{:S(2)}, u32[]{:S(2)}) collective-permute-start(bf16[2,144,768]{2,1,0:T(8,128)(2,1)S(1)} %collective-permute-done.8), channel_id=1, source_target_pairs={{2,0},{4,2},{6,4},{3,1},{5,3},{7,5},{10,8},{12,10},{14,12},{11,9},... | collective-permute-start | bytes 1327112 | tf_op jit(solution)/shard_map/ppermute | solution.py:102
  64.9 0.5 multiply_reduce_fusion.13
  66.3 7.9 %collective-permute-done.14 = bf16[2,144,768]{2,1,0:T(8,128)(2,1)S(1)} collective-permute-done((bf16[2,144,768]{2,1,0:T(8,128)(2,1)S(1)}, bf16[2,144,768]{2,1,0:T(8,128)(2,1)S(1)}, u32[]{:S(2)}, u32[]{:S(2)}) %collective-permute-start.14) | collective-permute-done | bytes 442400 | tf_op jit(solution)/shard_map/ppermute | solution.py:101
  74.7 0.5 multiply_reduce_fusion.12
  75.8 0.5 multiply_reduce_fusion.11
  77.1 3.6 %collective-permute-done.16 = bf16[2,144,768]{2,1,0:T(8,128)(2,1)S(1)} collective-permute-done((bf16[2,144,768]{2,1,0:T(8,128)(2,1)S(1)}, bf16[2,144,768]{2,1,0:T(8,128)(2,1)S(1)}, u32[]{:S(2)}, u32[]{:S(2)}) %collective-permute-start.16) | collective-permute-done | bytes 442400 | tf_op jit(solution)/shard_map/ppermute | solution.py:102
  81.2 0.5 multiply_reduce_fusion.10
  82.2 0.5 multiply_reduce_fusion.9
  83.3 1.3 %collective-permute-start.21 = (bf16[2,144,768]{2,1,0:T(8,128)(2,1)S(1)}, bf16[2,144,768]{2,1,0:T(8,128)(2,1)S(1)}, u32[]{:S(2)}, u32[]{:S(2)}) collective-permute-start(bf16[2,144,768]{2,1,0:T(8,128)(2,1)S(1)} %broadcast_select_fusion.2), channel_id=1, source_target_pairs={{4,6},{2,0},{5,7},{3,1},{12,14},{10,8},{13,15},{11,9},{20,22},{18,... | collective-permute-start | bytes 1327112 | tf_op jit(solution)/shard_map/ppermute | solution.py:96
  84.6 1.3 %collective-permute-start.22 = (bf16[2,144,768]{2,1,0:T(8,128)(2,1)S(1)}, bf16[2,144,768]{2,1,0:T(8,128)(2,1)S(1)}, u32[]{:S(2)}, u32[]{:S(2)}) collective-permute-start(bf16[2,144,768]{2,1,0:T(8,128)(2,1)S(1)} %broadcast_select_fusion.1), channel_id=1, source_target_pairs={{4,6},{2,0},{5,7},{3,1},{12,14},{10,8},{13,15},{11,9},{20,22},{18,... | collective-permute-start | bytes 1327112 | tf_op jit(solution)/shard_map/ppermute | solution.py:96
  85.9 0.6 collective-permute-start.18
  87.4 0.5 collective-permute-done.18
  88.4 0.5 multiply_reduce_fusion.8
  89.5 0.5 multiply_reduce_fusion.7
  92.4 0.5 multiply_reduce_fusion.5
  93.3 4.9 %collective-permute-done.21 = bf16[2,144,768]{2,1,0:T(8,128)(2,1)S(1)} collective-permute-done((bf16[2,144,768]{2,1,0:T(8,128)(2,1)S(1)}, bf16[2,144,768]{2,1,0:T(8,128)(2,1)S(1)}, u32[]{:S(2)}, u32[]{:S(2)}) %collective-permute-start.21) | collective-permute-done | bytes 442400 | tf_op jit(solution)/shard_map/ppermute | solution.py:96
  98.6 8.6 %collective-permute-done.22 = bf16[2,144,768]{2,1,0:T(8,128)(2,1)S(1)} collective-permute-done((bf16[2,144,768]{2,1,0:T(8,128)(2,1)S(1)}, bf16[2,144,768]{2,1,0:T(8,128)(2,1)S(1)}, u32[]{:S(2)}, u32[]{:S(2)}) %collective-permute-start.22) | collective-permute-done | bytes 442400 | tf_op jit(solution)/shard_map/ppermute | solution.py:96
  107.7 0.5 multiply_reduce_fusion.4
  108.8 0.5 multiply_reduce_fusion.3
  109.8 0.5 collective-permute-start.24
  110.4 0.8 collective-permute-done.23
  112.3 0.5 multiply_reduce_fusion.2
  113.4 0.5 multiply_reduce_fusion.1
  114.6 0.6 gather_fusion
  115.2 1.0 broadcast_select_fusion
  (217 shorter events, 27.2 us)
Async XLA Ops:
  2.1 10.3 %collective-permute-start.2 = (bf16[144,768]{1,0:T(8,128)(2,1)S(1)}, bf16[144,768]{1,0:T(8,128)(2,1)S(1)}, u32[]{:S(2)}, u32[]{:S(2)}) collective-permute-start(bf16[144,768]{1,0:T(8,128)(2,1)S(1)} %get-tuple-element.62), channel_id=1, source_target_pairs={{0,24},{8,16},{16,8},{24,0},{1,25},{9,17},{17,9},{25,1},{2,26},{10... | collective-permute-start | bytes 663560 | tf_op jit(solution)/shard_map/ppermute | solution.py:48
  6.0 10.2 %collective-permute-start.1 = (bf16[144,768]{1,0:T(8,128)(2,1)S(1)}, bf16[144,768]{1,0:T(8,128)(2,1)S(1)}, u32[]{:S(2)}, u32[]{:S(2)}) collective-permute-start(bf16[144,768]{1,0:T(8,128)(2,1)S(1)} %get-tuple-element.63), channel_id=1, source_target_pairs={{0,16},{8,24},{16,0},{24,8},{1,17},{9,25},{17,1},{25,9},{2,18},{10... | collective-permute-start | bytes 663560 | tf_op jit(solution)/shard_map/ppermute | solution.py:48
  6.6 10.0 %collective-permute-start = (bf16[144,768]{1,0:T(8,128)(2,1)S(1)}, bf16[144,768]{1,0:T(8,128)(2,1)S(1)}, u32[]{:S(2)}, u32[]{:S(2)}) collective-permute-start(bf16[144,768]{1,0:T(8,128)(2,1)S(1)} %get-tuple-element.64), channel_id=1, source_target_pairs={{0,8},{8,0},{16,24},{24,16},{1,9},{9,1},{17,25},{25,17},{2,10},{10... | collective-permute-start | bytes 663560 | tf_op jit(solution)/shard_map/ppermute | solution.py:48
  16.6 9.2 %copy-start = (bf16[4,144,768]{2,1,0:T(8,128)(2,1)}, bf16[4,144,768]{2,1,0:T(8,128)(2,1)S(1)}, u32[]{:S(2)}) copy-start(bf16[4,144,768]{2,1,0:T(8,128)(2,1)S(1)} %pad_maximum_fusion) | copy-start | bytes 2654212
  17.1 10.7 %collective-permute-start.3 = (bf16[2,144,768]{2,1,0:T(8,128)(2,1)S(1)}, bf16[2,144,768]{2,1,0:T(8,128)(2,1)S(1)}, u32[]{:S(2)}, u32[]{:S(2)}) collective-permute-start(bf16[2,144,768]{2,1,0:T(8,128)(2,1)S(1)} %pad_maximum_fusion.1), channel_id=1, source_target_pairs={{0,1},{1,0},{2,3},{3,2},{4,5},{5,4},{6,7},{7,6},{8,9},{9,8},{10,11... | collective-permute-start | bytes 1327112 | tf_op jit(solution)/shard_map/ppermute | solution.py:91
  17.2 14.8 %collective-permute-start.5 = (bf16[2,144,768]{2,1,0:T(8,128)(2,1)S(1)}, bf16[2,144,768]{2,1,0:T(8,128)(2,1)S(1)}, u32[]{:S(2)}, u32[]{:S(2)}) collective-permute-start(bf16[2,144,768]{2,1,0:T(8,128)(2,1)S(1)} %pad_maximum_fusion.1), channel_id=1, source_target_pairs={{0,2},{2,4},{4,6},{1,3},{3,5},{5,7},{8,10},{10,12},{12,14},{9,11},... | collective-permute-start | bytes 1327112 | tf_op jit(solution)/shard_map/ppermute | solution.py:101
  20.7 8.7 %collective-permute-start.4 = (bf16[2,144,768]{2,1,0:T(8,128)(2,1)S(1)}, bf16[2,144,768]{2,1,0:T(8,128)(2,1)S(1)}, u32[]{:S(2)}, u32[]{:S(2)}) collective-permute-start(bf16[2,144,768]{2,1,0:T(8,128)(2,1)S(1)} %pad_maximum_fusion.2), channel_id=1, source_target_pairs={{0,1},{1,0},{2,3},{3,2},{4,5},{5,4},{6,7},{7,6},{8,9},{9,8},{10,11... | collective-permute-start | bytes 1327112 | tf_op jit(solution)/shard_map/ppermute | solution.py:91
  21.0 19.2 %collective-permute-start.6 = (bf16[2,144,768]{2,1,0:T(8,128)(2,1)S(1)}, bf16[2,144,768]{2,1,0:T(8,128)(2,1)S(1)}, u32[]{:S(2)}, u32[]{:S(2)}) collective-permute-start(bf16[2,144,768]{2,1,0:T(8,128)(2,1)S(1)} %pad_maximum_fusion.2), channel_id=1, source_target_pairs={{0,2},{2,4},{4,6},{1,3},{3,5},{5,7},{8,10},{10,12},{12,14},{9,11},... | collective-permute-start | bytes 1327112 | tf_op jit(solution)/shard_map/ppermute | solution.py:101
  24.5 18.3 %collective-permute-start.7 = (bf16[2,144,768]{2,1,0:T(8,128)(2,1)S(1)}, bf16[2,144,768]{2,1,0:T(8,128)(2,1)S(1)}, u32[]{:S(2)}, u32[]{:S(2)}) collective-permute-start(bf16[2,144,768]{2,1,0:T(8,128)(2,1)S(1)} %pad_maximum_fusion.1), channel_id=1, source_target_pairs={{2,0},{4,2},{6,4},{3,1},{5,3},{7,5},{10,8},{12,10},{14,12},{11,9},... | collective-permute-start | bytes 1327112 | tf_op jit(solution)/shard_map/ppermute | solution.py:102
  26.1 1.1 slice-start
  27.8 20.1 %collective-permute-start.8 = (bf16[2,144,768]{2,1,0:T(8,128)(2,1)S(1)}, bf16[2,144,768]{2,1,0:T(8,128)(2,1)S(1)}, u32[]{:S(2)}, u32[]{:S(2)}) collective-permute-start(bf16[2,144,768]{2,1,0:T(8,128)(2,1)S(1)} %pad_maximum_fusion.2), channel_id=1, source_target_pairs={{2,0},{4,2},{6,4},{3,1},{5,3},{7,5},{10,8},{12,10},{14,12},{11,9},... | collective-permute-start | bytes 1327112 | tf_op jit(solution)/shard_map/ppermute | solution.py:102
  50.0 5.1 %collective-permute-start.9 = (bf16[2,144,768]{2,1,0:T(8,128)(2,1)S(1)}, bf16[2,144,768]{2,1,0:T(8,128)(2,1)S(1)}, u32[]{:S(2)}, u32[]{:S(2)}) collective-permute-start(bf16[2,144,768]{2,1,0:T(8,128)(2,1)S(1)} %collective-permute-done.5), channel_id=1, source_target_pairs={{0,1},{1,0},{2,3},{3,2},{4,5},{5,4},{6,7},{7,6},{8,9},{9,8},{10,11... | collective-permute-start | bytes 1327112 | tf_op jit(solution)/shard_map/ppermute | solution.py:105
  50.6 7.1 %collective-permute-start.10 = (bf16[2,144,768]{2,1,0:T(8,128)(2,1)S(1)}, bf16[2,144,768]{2,1,0:T(8,128)(2,1)S(1)}, u32[]{:S(2)}, u32[]{:S(2)}) collective-permute-start(bf16[2,144,768]{2,1,0:T(8,128)(2,1)S(1)} %collective-permute-done.6), channel_id=1, source_target_pairs={{0,1},{1,0},{2,3},{3,2},{4,5},{5,4},{6,7},{7,6},{8,9},{9,8},{10,11... | collective-permute-start | bytes 1327112 | tf_op jit(solution)/shard_map/ppermute | solution.py:105
  51.1 10.4 %collective-permute-start.11 = (bf16[2,144,768]{2,1,0:T(8,128)(2,1)S(1)}, bf16[2,144,768]{2,1,0:T(8,128)(2,1)S(1)}, u32[]{:S(2)}, u32[]{:S(2)}) collective-permute-start(bf16[2,144,768]{2,1,0:T(8,128)(2,1)S(1)} %collective-permute-done.7), channel_id=1, source_target_pairs={{0,1},{1,0},{2,3},{3,2},{4,5},{5,4},{6,7},{7,6},{8,9},{9,8},{10,11... | collective-permute-start | bytes 1327112 | tf_op jit(solution)/shard_map/ppermute | solution.py:106
  51.2 12.2 %collective-permute-start.12 = (bf16[2,144,768]{2,1,0:T(8,128)(2,1)S(1)}, bf16[2,144,768]{2,1,0:T(8,128)(2,1)S(1)}, u32[]{:S(2)}, u32[]{:S(2)}) collective-permute-start(bf16[2,144,768]{2,1,0:T(8,128)(2,1)S(1)} %collective-permute-done.8), channel_id=1, source_target_pairs={{0,1},{1,0},{2,3},{3,2},{4,5},{5,4},{6,7},{7,6},{8,9},{9,8},{10,11... | collective-permute-start | bytes 1327112 | tf_op jit(solution)/shard_map/ppermute | solution.py:106
  51.6 14.3 %collective-permute-start.13 = (bf16[2,144,768]{2,1,0:T(8,128)(2,1)S(1)}, bf16[2,144,768]{2,1,0:T(8,128)(2,1)S(1)}, u32[]{:S(2)}, u32[]{:S(2)}) collective-permute-start(bf16[2,144,768]{2,1,0:T(8,128)(2,1)S(1)} %collective-permute-done.5), channel_id=1, source_target_pairs={{0,2},{2,4},{4,6},{1,3},{3,5},{5,7},{8,10},{10,12},{12,14},{9,11},... | collective-permute-start | bytes 1327112 | tf_op jit(solution)/shard_map/ppermute | solution.py:101
  55.1 19.1 %collective-permute-start.14 = (bf16[2,144,768]{2,1,0:T(8,128)(2,1)S(1)}, bf16[2,144,768]{2,1,0:T(8,128)(2,1)S(1)}, u32[]{:S(2)}, u32[]{:S(2)}) collective-permute-start(bf16[2,144,768]{2,1,0:T(8,128)(2,1)S(1)} %collective-permute-done.6), channel_id=1, source_target_pairs={{0,2},{2,4},{4,6},{1,3},{3,5},{5,7},{8,10},{10,12},{12,14},{9,11},... | collective-permute-start | bytes 1327112 | tf_op jit(solution)/shard_map/ppermute | solution.py:101
  57.7 19.0 %collective-permute-start.15 = (bf16[2,144,768]{2,1,0:T(8,128)(2,1)S(1)}, bf16[2,144,768]{2,1,0:T(8,128)(2,1)S(1)}, u32[]{:S(2)}, u32[]{:S(2)}) collective-permute-start(bf16[2,144,768]{2,1,0:T(8,128)(2,1)S(1)} %collective-permute-done.7), channel_id=1, source_target_pairs={{2,0},{4,2},{6,4},{3,1},{5,3},{7,5},{10,8},{12,10},{14,12},{11,9},... | collective-permute-start | bytes 1327112 | tf_op jit(solution)/shard_map/ppermute | solution.py:102
  61.5 19.1 %collective-permute-start.16 = (bf16[2,144,768]{2,1,0:T(8,128)(2,1)S(1)}, bf16[2,144,768]{2,1,0:T(8,128)(2,1)S(1)}, u32[]{:S(2)}, u32[]{:S(2)}) collective-permute-start(bf16[2,144,768]{2,1,0:T(8,128)(2,1)S(1)} %collective-permute-done.8), channel_id=1, source_target_pairs={{2,0},{4,2},{6,4},{3,1},{5,3},{7,5},{10,8},{12,10},{14,12},{11,9},... | collective-permute-start | bytes 1327112 | tf_op jit(solution)/shard_map/ppermute | solution.py:102
  83.2 3.4 %collective-permute-start.17 = (bf16[2,144,768]{2,1,0:T(8,128)(2,1)S(1)}, bf16[2,144,768]{2,1,0:T(8,128)(2,1)S(1)}, u32[]{:S(2)}, u32[]{:S(2)}) collective-permute-start(bf16[2,144,768]{2,1,0:T(8,128)(2,1)S(1)} %collective-permute-done.13), channel_id=1, source_target_pairs={{0,1},{1,0},{2,3},{3,2},{4,5},{5,4},{6,7},{7,6},{8,9},{9,8},{10,11... | collective-permute-start | bytes 1327112 | tf_op jit(solution)/shard_map/ppermute | solution.py:105
  83.3 14.9 %collective-permute-start.21 = (bf16[2,144,768]{2,1,0:T(8,128)(2,1)S(1)}, bf16[2,144,768]{2,1,0:T(8,128)(2,1)S(1)}, u32[]{:S(2)}, u32[]{:S(2)}) collective-permute-start(bf16[2,144,768]{2,1,0:T(8,128)(2,1)S(1)} %broadcast_select_fusion.2), channel_id=1, source_target_pairs={{4,6},{2,0},{5,7},{3,1},{12,14},{10,8},{13,15},{11,9},{20,22},{18,... | collective-permute-start | bytes 1327112 | tf_op jit(solution)/shard_map/ppermute | solution.py:96
  84.6 22.6 %collective-permute-start.22 = (bf16[2,144,768]{2,1,0:T(8,128)(2,1)S(1)}, bf16[2,144,768]{2,1,0:T(8,128)(2,1)S(1)}, u32[]{:S(2)}, u32[]{:S(2)}) collective-permute-start(bf16[2,144,768]{2,1,0:T(8,128)(2,1)S(1)} %broadcast_select_fusion.1), channel_id=1, source_target_pairs={{4,6},{2,0},{5,7},{3,1},{12,14},{10,8},{13,15},{11,9},{20,22},{18,... | collective-permute-start | bytes 1327112 | tf_op jit(solution)/shard_map/ppermute | solution.py:96
  85.9 2.0 %collective-permute-start.18 = (bf16[2,144,768]{2,1,0:T(8,128)(2,1)S(1)}, bf16[2,144,768]{2,1,0:T(8,128)(2,1)S(1)}, u32[]{:S(2)}, u32[]{:S(2)}) collective-permute-start(bf16[2,144,768]{2,1,0:T(8,128)(2,1)S(1)} %collective-permute-done.14), channel_id=1, source_target_pairs={{0,1},{1,0},{2,3},{3,2},{4,5},{5,4},{6,7},{7,6},{8,9},{9,8},{10,11... | collective-permute-start | bytes 1327112 | tf_op jit(solution)/shard_map/ppermute | solution.py:105
  86.5 3.9 %collective-permute-start.19 = (bf16[2,144,768]{2,1,0:T(8,128)(2,1)S(1)}, bf16[2,144,768]{2,1,0:T(8,128)(2,1)S(1)}, u32[]{:S(2)}, u32[]{:S(2)}) collective-permute-start(bf16[2,144,768]{2,1,0:T(8,128)(2,1)S(1)} %collective-permute-done.15), channel_id=1, source_target_pairs={{0,1},{1,0},{2,3},{3,2},{4,5},{5,4},{6,7},{7,6},{8,9},{9,8},{10,11... | collective-permute-start | bytes 1327112 | tf_op jit(solution)/shard_map/ppermute | solution.py:106
  86.6 4.2 %collective-permute-start.20 = (bf16[2,144,768]{2,1,0:T(8,128)(2,1)S(1)}, bf16[2,144,768]{2,1,0:T(8,128)(2,1)S(1)}, u32[]{:S(2)}, u32[]{:S(2)}) collective-permute-start(bf16[2,144,768]{2,1,0:T(8,128)(2,1)S(1)} %collective-permute-done.16), channel_id=1, source_target_pairs={{0,1},{1,0},{2,3},{3,2},{4,5},{5,4},{6,7},{7,6},{8,9},{9,8},{10,11... | collective-permute-start | bytes 1327112 | tf_op jit(solution)/shard_map/ppermute | solution.py:106
  109.3 1.9 %collective-permute-start.23 = (bf16[2,144,768]{2,1,0:T(8,128)(2,1)S(1)}, bf16[2,144,768]{2,1,0:T(8,128)(2,1)S(1)}, u32[]{:S(2)}, u32[]{:S(2)}) collective-permute-start(bf16[2,144,768]{2,1,0:T(8,128)(2,1)S(1)} %collective-permute-done.21), channel_id=1, source_target_pairs={{0,1},{1,0},{2,3},{3,2},{4,5},{5,4},{6,7},{7,6},{8,9},{9,8},{10,11... | collective-permute-start | bytes 1327112 | tf_op jit(solution)/shard_map/ppermute | solution.py:99
  109.8 2.0 %collective-permute-start.24 = (bf16[2,144,768]{2,1,0:T(8,128)(2,1)S(1)}, bf16[2,144,768]{2,1,0:T(8,128)(2,1)S(1)}, u32[]{:S(2)}, u32[]{:S(2)}) collective-permute-start(bf16[2,144,768]{2,1,0:T(8,128)(2,1)S(1)} %collective-permute-done.22), channel_id=1, source_target_pairs={{0,1},{1,0},{2,3},{3,2},{4,5},{5,4},{6,7},{7,6},{8,9},{9,8},{10,11... | collective-permute-start | bytes 1327112 | tf_op jit(solution)/shard_map/ppermute | solution.py:99

commit v7 on v6

--- a/solution.py
+++ b/solution.py
@@ -46,8 +46,6 @@
     for m in range(1, buckets):
         outgoing = lax.dynamic_index_in_dim(packed, bucket ^ m, axis=0, keepdims=False)
         arrived.append(lax.ppermute(outgoing, "bucket", [(i, i ^ m) for i in range(buckets)]))
-    half = buckets // 2
-    halves = [jnp.stack(arrived[:half]), jnp.stack(arrived[half:])]
 
     own_data, live = split_pieces(jnp.stack(arrived), slot_rows)
     rows = own_data.shape[0]
@@ -105,10 +103,8 @@
             yield lax.ppermute(from_below, "core", swap), times_listed(chip - step, other_core)
             yield lax.ppermute(from_above, "core", swap), times_listed(chip + step, other_core)
 
-    first, second = relay(halves[0]), relay(halves[1])
-    for a, b in zip(first, second):
-        acc = add_pair(acc, *a)
-        acc = add_pair(acc, *b)
+    for got, weight in relay(jnp.stack(arrived)):
+        acc = add_pair(acc, got, weight)
         acc = lax.optimization_barrier(acc)
     summed, squares = acc
     result = summed * lax.rsqrt(squares)[:, None] * live[:, None]

time: 117 us -> 112 us (0.957)
  waiting for transfers between devices: 48.6 us -> 61.6 us
  starting transfers between devices: 28.4 us -> 18.1 us
  matrix products: 20.6 us -> 15.8 us
  other arithmetic: 15.1 us -> 11.4 us
  local copies, waits for them, and re-layouts: 1.85 us -> 3.34 us
    ppermute x4 -> x2, waiting for transfers between devices: 15.8 us -> 29 us  [relay(): from_below = lax.ppermute(from_below, 'chip', up)]
    ppermute x2 -> x1, waiting for transfers between devices: 13.5 us -> 18.7 us  [relay(): far = lax.ppermute(outgoing, 'chip', [(chips - 2, chips - 1), (1, 0)])]
    ppermute x4 -> x2, starting transfers between devices: 12.7 us -> 7.97 us  [relay(): from_below = lax.ppermute(from_below, 'chip', up)]
    ppermute x4 -> x2, waiting for transfers between devices: 8.38 us -> 3.81 us  [relay(): from_above = lax.ppermute(from_above, 'chip', down)]
    ppermute x4 -> x2, starting transfers between devices: 5.35 us -> 2.76 us  [relay(): from_above = lax.ppermute(from_above, 'chip', down)]
    dot_general x22 -> x11, matrix products: 9.12 us -> 6.67 us  [add_pair(): jnp.dot(weights.astype(jnp.bfloat16), got_data, preferred_element_type=jn...]
    dot_general x23 -> x12, matrix products: 10.9 us -> 8.53 us  [weigh(): scores = jnp.dot(unit_a, unit_b.T, preferred_element_type=jnp.float32)]
    reduce_sum x23 -> x12, other arithmetic: 3.86 us -> 2.78 us  [normalize(): jnp.sum(values * values, axis=-1, keepdims=True) + EPS]
  transfers between devices with their start and end apart: 25 -> 14, of which waited for: 12 -> 9; matrix products, arithmetic and copies ran while one was open for 20% -> 15% of each run, Pallas kernels for 0% -> 0%
where the time goes in v7:
time: 112 us; the launch traced here: 111 us
  waiting for transfers between devices  61.6 us (55%)
  starting transfers between devices  18.1 us (16%)
  matrix products  15.8 us (14%)
  other arithmetic  11.4 us (10%)
  local copies, waits for them, and re-layouts  3.34 us (3%)
    ppermute x2, waiting for transfers between devices, relay(): from_below = lax.ppermute(from_below, 'chip', up)  29 us
    ppermute x1, waiting for transfers between devices, relay(): far = lax.ppermute(outgoing, 'chip', [(chips - 2, chips - 1), (1, 0)])  18.7 us
    ppermute x3, waiting for transfers between devices, per_device(): lax.ppermute(outgoing, 'bucket', [(i, i ^ m) for i in range(buckets)])  9.29 us
    dot_general x12, matrix products, weigh(): scores = jnp.dot(unit_a, unit_b.T, preferred_element_type=jnp.float32)  8.53 us
    ppermute x2, starting transfers between devices, relay(): from_below = lax.ppermute(from_below, 'chip', up)  7.97 us
    dot_general x11, matrix products, add_pair(): jnp.dot(weights.astype(jnp.bfloat16), got_data, preferred_element_type=jn...  6.67 us
    ppermute x3, starting transfers between devices, per_device(): lax.ppermute(outgoing, 'bucket', [(i, i ^ m) for i in range(buckets)])  4.63 us
    ppermute x2, waiting for transfers between devices, relay(): from_above = lax.ppermute(from_above, 'chip', down)  3.81 us
  transfers between devices with their start and end apart: 14, of which 9 were waited for; matrix products, arithmetic and copies ran while one was open for 15% of the time, Pallas kernels for 0%

profile of v7, /device:TPU:0, one launch (start us, length us, event | category | flops | bytes accessed | tf_op | source)
XLA Modules:
  0.0 111.3 jit_solution(4779413492312619094)
XLA Ops:
  0.0 0.7 convert_bitcast_fusion.12
  0.8 1.2 %fusion.50 = bf16[4,144,768]{2,1,0:T(8,128)(2,1)S(1)} fusion(bf16[4,1,1]{2,1,0:T(2,128)(2,1)S(1)} %copy.5, bf16[4,128,768]{2,1,0:T(8,128)(2,1)} %bitcast.128), kind=kLoop, calls=%fused_computation.113 | loop fusion | flops 2654208 | bytes 1671176 | tf_op jit(solution)/shard_map/concatenate | solution.py:43
  2.1 4.0 %collective-permute-start.2 = (bf16[144,768]{1,0:T(8,128)(2,1)S(1)}, bf16[144,768]{1,0:T(8,128)(2,1)S(1)}, u32[]{:S(2)}, u32[]{:S(2)}) collective-permute-start(bf16[144,768]{1,0:T(8,128)(2,1)S(1)} %get-tuple-element.62), channel_id=1, source_target_pairs={{0,24},{8,16},{16,8},{24,0},{1,25},{9,17},{17,9},{25,1},{2,26},{10... | collective-permute-start | bytes 663560 | tf_op jit(solution)/shard_map/ppermute | solution.py:48
  6.0 0.5 collective-permute-start.1
  7.2 5.2 %collective-permute-done.2 = bf16[144,768]{1,0:T(8,128)(2,1)S(1)} collective-permute-done((bf16[144,768]{1,0:T(8,128)(2,1)S(1)}, bf16[144,768]{1,0:T(8,128)(2,1)S(1)}, u32[]{:S(2)}, u32[]{:S(2)}) %collective-permute-start.2) | collective-permute-done | bytes 221216 | tf_op jit(solution)/shard_map/ppermute | solution.py:48
  12.4 3.8 %collective-permute-done.1 = bf16[144,768]{1,0:T(8,128)(2,1)S(1)} collective-permute-done((bf16[144,768]{1,0:T(8,128)(2,1)S(1)}, bf16[144,768]{1,0:T(8,128)(2,1)S(1)}, u32[]{:S(2)}, u32[]{:S(2)}) %collective-permute-start.1) | collective-permute-done | bytes 221216 | tf_op jit(solution)/shard_map/ppermute | solution.py:48
  17.2 3.5 %collective-permute-start.4 = (bf16[4,144,768]{2,1,0:T(8,128)(2,1)S(1)}, bf16[4,144,768]{2,1,0:T(8,128)(2,1)S(1)}, u32[]{:S(2)}, u32[]{:S(2)}) collective-permute-start(bf16[4,144,768]{2,1,0:T(8,128)(2,1)S(1)} %pad_maximum_fusion), channel_id=1, source_target_pairs={{0,2},{2,4},{4,6},{1,3},{3,5},{5,7},{8,10},{10,12},{12,14},{9,11},... | collective-permute-start | bytes 2654216 | tf_op jit(solution)/shard_map/ppermute | solution.py:99
  20.7 1.3 %collective-permute-start.5 = (bf16[4,144,768]{2,1,0:T(8,128)(2,1)S(1)}, bf16[4,144,768]{2,1,0:T(8,128)(2,1)S(1)}, u32[]{:S(2)}, u32[]{:S(2)}) collective-permute-start(bf16[4,144,768]{2,1,0:T(8,128)(2,1)S(1)} %pad_maximum_fusion), channel_id=1, source_target_pairs={{2,0},{4,2},{6,4},{3,1},{5,3},{7,5},{10,8},{12,10},{14,12},{11,9},... | collective-permute-start | bytes 2654216 | tf_op jit(solution)/shard_map/ppermute | solution.py:100
  22.3 0.8 multiply_reduce_fusion.11
  23.1 0.6 fusion.62
  24.1 16.1 %collective-permute-done.4 = bf16[4,144,768]{2,1,0:T(8,128)(2,1)S(1)} collective-permute-done((bf16[4,144,768]{2,1,0:T(8,128)(2,1)S(1)}, bf16[4,144,768]{2,1,0:T(8,128)(2,1)S(1)}, u32[]{:S(2)}, u32[]{:S(2)}) %collective-permute-start.4) | collective-permute-done | bytes 884768 | tf_op jit(solution)/shard_map/ppermute | solution.py:99
  40.6 0.7 multiply_reduce_fusion.10
  41.4 0.6 multiply_add_fusion.10
  42.5 0.7 multiply_reduce_fusion.9
  43.2 0.4 slice-done
  43.6 0.6 multiply_add_fusion.9
  44.9 0.5 copy-done.1
  45.4 0.5 collective-permute-start.7
  46.1 0.7 multiply_reduce_fusion.8
  46.8 0.6 multiply_add_fusion.8
  47.5 4.4 %collective-permute-start.8 = (bf16[4,144,768]{2,1,0:T(8,128)(2,1)S(1)}, bf16[4,144,768]{2,1,0:T(8,128)(2,1)S(1)}, u32[]{:S(2)}, u32[]{:S(2)}) collective-permute-start(bf16[4,144,768]{2,1,0:T(8,128)(2,1)S(1)} %copy-done.1), channel_id=1, source_target_pairs={{0,2},{2,4},{4,6},{1,3},{3,5},{5,7},{8,10},{10,12},{12,14},{9,11},... | collective-permute-start | bytes 2654216 | tf_op jit(solution)/shard_map/ppermute | solution.py:99
  51.9 1.5 %collective-permute-start.9 = (bf16[4,144,768]{2,1,0:T(8,128)(2,1)S(1)}, bf16[4,144,768]{2,1,0:T(8,128)(2,1)S(1)}, u32[]{:S(2)}, u32[]{:S(2)}) collective-permute-start(bf16[4,144,768]{2,1,0:T(8,128)(2,1)S(1)} %collective-permute-done.5), channel_id=1, source_target_pairs={{2,0},{4,2},{6,4},{3,1},{5,3},{7,5},{10,8},{12,10},{14,12},{11,9},... | collective-permute-start | bytes 2654216 | tf_op jit(solution)/shard_map/ppermute | solution.py:100
  54.3 0.7 multiply_reduce_fusion.7
  55.1 0.6 multiply_add_fusion.7
  56.2 0.7 multiply_reduce_fusion.6
  56.9 0.4 slice-done.1
  57.3 0.6 multiply_add_fusion.6
  57.9 13.0 %collective-permute-done.8 = bf16[4,144,768]{2,1,0:T(8,128)(2,1)S(1)} collective-permute-done((bf16[4,144,768]{2,1,0:T(8,128)(2,1)S(1)}, bf16[4,144,768]{2,1,0:T(8,128)(2,1)S(1)}, u32[]{:S(2)}, u32[]{:S(2)}) %collective-permute-start.8) | collective-permute-done | bytes 884768 | tf_op jit(solution)/shard_map/ppermute | solution.py:99
  71.4 3.7 %collective-permute-done.9 = bf16[4,144,768]{2,1,0:T(8,128)(2,1)S(1)} collective-permute-done((bf16[4,144,768]{2,1,0:T(8,128)(2,1)S(1)}, bf16[4,144,768]{2,1,0:T(8,128)(2,1)S(1)}, u32[]{:S(2)}, u32[]{:S(2)}) %collective-permute-start.9) | collective-permute-done | bytes 884768 | tf_op jit(solution)/shard_map/ppermute | solution.py:100
  75.8 0.7 multiply_reduce_fusion.5
  76.7 0.7 multiply_reduce_fusion.4
  77.5 0.6 multiply_add_fusion.5
  78.2 0.6 multiply_add_fusion.4
  79.0 1.5 %collective-permute-start.12 = (bf16[4,144,768]{2,1,0:T(8,128)(2,1)S(1)}, bf16[4,144,768]{2,1,0:T(8,128)(2,1)S(1)}, u32[]{:S(2)}, u32[]{:S(2)}) collective-permute-start(bf16[4,144,768]{2,1,0:T(8,128)(2,1)S(1)} %broadcast_select_fusion), channel_id=1, source_target_pairs={{4,6},{2,0},{5,7},{3,1},{12,14},{10,8},{13,15},{11,9},{20,22},{18,... | collective-permute-start | bytes 2654216 | tf_op jit(solution)/shard_map/ppermute | solution.py:94
  80.5 0.5 collective-permute-start.11
  82.0 0.7 multiply_reduce_fusion.3
  82.7 0.4 slice-done.2
  83.1 0.6 multiply_add_fusion.3
  84.2 18.7 %collective-permute-done.12 = bf16[4,144,768]{2,1,0:T(8,128)(2,1)S(1)} collective-permute-done((bf16[4,144,768]{2,1,0:T(8,128)(2,1)S(1)}, bf16[4,144,768]{2,1,0:T(8,128)(2,1)S(1)}, u32[]{:S(2)}, u32[]{:S(2)}) %collective-permute-start.12) | collective-permute-done | bytes 884768 | tf_op jit(solution)/shard_map/ppermute | solution.py:94
  103.3 0.7 multiply_reduce_fusion.2
  104.1 0.6 multiply_add_fusion.2
  105.3 0.7 multiply_reduce_fusion.1
  106.0 0.6 multiply_add_fusion.1
  106.6 0.7 collective-permute-done.13
  108.1 0.7 multiply_reduce_fusion
  108.9 0.6 multiply_add_fusion
  109.7 0.6 gather_fusion
  110.3 1.0 broadcast_select_fusion.1
  (112 shorter events, 10.3 us)
Async XLA Ops:
  2.1 10.3 %collective-permute-start.2 = (bf16[144,768]{1,0:T(8,128)(2,1)S(1)}, bf16[144,768]{1,0:T(8,128)(2,1)S(1)}, u32[]{:S(2)}, u32[]{:S(2)}) collective-permute-start(bf16[144,768]{1,0:T(8,128)(2,1)S(1)} %get-tuple-element.62), channel_id=1, source_target_pairs={{0,24},{8,16},{16,8},{24,0},{1,25},{9,17},{17,9},{25,1},{2,26},{10... | collective-permute-start | bytes 663560 | tf_op jit(solution)/shard_map/ppermute | solution.py:48
  6.0 10.2 %collective-permute-start.1 = (bf16[144,768]{1,0:T(8,128)(2,1)S(1)}, bf16[144,768]{1,0:T(8,128)(2,1)S(1)}, u32[]{:S(2)}, u32[]{:S(2)}) collective-permute-start(bf16[144,768]{1,0:T(8,128)(2,1)S(1)} %get-tuple-element.63), channel_id=1, source_target_pairs={{0,16},{8,24},{16,0},{24,8},{1,17},{9,25},{17,1},{25,9},{2,18},{10... | collective-permute-start | bytes 663560 | tf_op jit(solution)/shard_map/ppermute | solution.py:48
  6.6 10.0 %collective-permute-start = (bf16[144,768]{1,0:T(8,128)(2,1)S(1)}, bf16[144,768]{1,0:T(8,128)(2,1)S(1)}, u32[]{:S(2)}, u32[]{:S(2)}) collective-permute-start(bf16[144,768]{1,0:T(8,128)(2,1)S(1)} %get-tuple-element.64), channel_id=1, source_target_pairs={{0,8},{8,0},{16,24},{24,16},{1,9},{9,1},{17,25},{25,17},{2,10},{10... | collective-permute-start | bytes 663560 | tf_op jit(solution)/shard_map/ppermute | solution.py:48
  17.1 6.6 %collective-permute-start.3 = (bf16[4,144,768]{2,1,0:T(8,128)(2,1)S(1)}, bf16[4,144,768]{2,1,0:T(8,128)(2,1)S(1)}, u32[]{:S(2)}, u32[]{:S(2)}) collective-permute-start(bf16[4,144,768]{2,1,0:T(8,128)(2,1)S(1)} %pad_maximum_fusion), channel_id=1, source_target_pairs={{0,1},{1,0},{2,3},{3,2},{4,5},{5,4},{6,7},{7,6},{8,9},{9,8},{10,11... | collective-permute-start | bytes 2654216 | tf_op jit(solution)/shard_map/ppermute | solution.py:89
  17.2 23.0 %collective-permute-start.4 = (bf16[4,144,768]{2,1,0:T(8,128)(2,1)S(1)}, bf16[4,144,768]{2,1,0:T(8,128)(2,1)S(1)}, u32[]{:S(2)}, u32[]{:S(2)}) collective-permute-start(bf16[4,144,768]{2,1,0:T(8,128)(2,1)S(1)} %pad_maximum_fusion), channel_id=1, source_target_pairs={{0,2},{2,4},{4,6},{1,3},{3,5},{5,7},{8,10},{10,12},{12,14},{9,11},... | collective-permute-start | bytes 2654216 | tf_op jit(solution)/shard_map/ppermute | solution.py:99
  20.7 23.7 %collective-permute-start.5 = (bf16[4,144,768]{2,1,0:T(8,128)(2,1)S(1)}, bf16[4,144,768]{2,1,0:T(8,128)(2,1)S(1)}, u32[]{:S(2)}, u32[]{:S(2)}) collective-permute-start(bf16[4,144,768]{2,1,0:T(8,128)(2,1)S(1)} %pad_maximum_fusion), channel_id=1, source_target_pairs={{2,0},{4,2},{6,4},{3,1},{5,3},{7,5},{10,8},{12,10},{14,12},{11,9},... | collective-permute-start | bytes 2654216 | tf_op jit(solution)/shard_map/ppermute | solution.py:100
  40.2 2.3 %copy-start = (bf16[4,144,768]{2,1,0:T(8,128)(2,1)}, bf16[4,144,768]{2,1,0:T(8,128)(2,1)S(1)}, u32[]{:S(2)}) copy-start(bf16[4,144,768]{2,1,0:T(8,128)(2,1)S(1)} %collective-permute-done.4) | copy-start | bytes 2654212
  42.5 1.1 %slice-start = ((bf16[4,144,768]{2,1,0:T(8,128)(2,1)}), bf16[4,128,768]{2,1,0:T(8,128)(2,1)S(1)}, s32[]{:S(2)}) async-start(bf16[4,144,768]{2,1,0:T(8,128)(2,1)} %copy-done), calls=%async_computation | async-start | bytes 1572864 | tf_op jit(solution)/shard_map/slice | solution.py:29
  44.2 1.2 %copy-start.1 = (bf16[4,144,768]{2,1,0:T(8,128)(2,1)S(1)}, bf16[4,144,768]{2,1,0:T(8,128)(2,1)}, u32[]{:S(2)}) copy-start(bf16[4,144,768]{2,1,0:T(8,128)(2,1)} %copy-done) | copy-start | bytes 2654212
  45.4 8.0 %collective-permute-start.6 = (bf16[4,144,768]{2,1,0:T(8,128)(2,1)S(1)}, bf16[4,144,768]{2,1,0:T(8,128)(2,1)S(1)}, u32[]{:S(2)}, u32[]{:S(2)}) collective-permute-start(bf16[4,144,768]{2,1,0:T(8,128)(2,1)S(1)} %copy-done.1), channel_id=1, source_target_pairs={{0,1},{1,0},{2,3},{3,2},{4,5},{5,4},{6,7},{7,6},{8,9},{9,8},{10,11... | collective-permute-start | bytes 2654216 | tf_op jit(solution)/shard_map/ppermute | solution.py:103
  45.4 8.5 %collective-permute-start.7 = (bf16[4,144,768]{2,1,0:T(8,128)(2,1)S(1)}, bf16[4,144,768]{2,1,0:T(8,128)(2,1)S(1)}, u32[]{:S(2)}, u32[]{:S(2)}) collective-permute-start(bf16[4,144,768]{2,1,0:T(8,128)(2,1)S(1)} %collective-permute-done.5), channel_id=1, source_target_pairs={{0,1},{1,0},{2,3},{3,2},{4,5},{5,4},{6,7},{7,6},{8,9},{9,8},{10,11... | collective-permute-start | bytes 2654216 | tf_op jit(solution)/shard_map/ppermute | solution.py:104
  47.5 23.4 %collective-permute-start.8 = (bf16[4,144,768]{2,1,0:T(8,128)(2,1)S(1)}, bf16[4,144,768]{2,1,0:T(8,128)(2,1)S(1)}, u32[]{:S(2)}, u32[]{:S(2)}) collective-permute-start(bf16[4,144,768]{2,1,0:T(8,128)(2,1)S(1)} %copy-done.1), channel_id=1, source_target_pairs={{0,2},{2,4},{4,6},{1,3},{3,5},{5,7},{8,10},{10,12},{12,14},{9,11},... | collective-permute-start | bytes 2654216 | tf_op jit(solution)/shard_map/ppermute | solution.py:99
  51.9 23.2 %collective-permute-start.9 = (bf16[4,144,768]{2,1,0:T(8,128)(2,1)S(1)}, bf16[4,144,768]{2,1,0:T(8,128)(2,1)S(1)}, u32[]{:S(2)}, u32[]{:S(2)}) collective-permute-start(bf16[4,144,768]{2,1,0:T(8,128)(2,1)S(1)} %collective-permute-done.5), channel_id=1, source_target_pairs={{2,0},{4,2},{6,4},{3,1},{5,3},{7,5},{10,8},{12,10},{14,12},{11,9},... | collective-permute-start | bytes 2654216 | tf_op jit(solution)/shard_map/ppermute | solution.py:100
  53.9 2.3 %copy-start.2 = (bf16[4,144,768]{2,1,0:T(8,128)(2,1)}, bf16[4,144,768]{2,1,0:T(8,128)(2,1)S(1)}, u32[]{:S(2)}) copy-start(bf16[4,144,768]{2,1,0:T(8,128)(2,1)S(1)} %collective-permute-done.7) | copy-start | bytes 2654212
  56.2 1.1 %slice-start.1 = ((bf16[4,144,768]{2,1,0:T(8,128)(2,1)}), bf16[4,128,768]{2,1,0:T(8,128)(2,1)S(1)}, s32[]{:S(2)}) async-start(bf16[4,144,768]{2,1,0:T(8,128)(2,1)} %copy-done.2), calls=%async_computation.1 | async-start | bytes 1572864 | tf_op jit(solution)/shard_map/slice | solution.py:29
  78.1 3.0 %collective-permute-start.10 = (bf16[4,144,768]{2,1,0:T(8,128)(2,1)S(1)}, bf16[4,144,768]{2,1,0:T(8,128)(2,1)S(1)}, u32[]{:S(2)}, u32[]{:S(2)}) collective-permute-start(bf16[4,144,768]{2,1,0:T(8,128)(2,1)S(1)} %collective-permute-done.8), channel_id=1, source_target_pairs={{0,1},{1,0},{2,3},{3,2},{4,5},{5,4},{6,7},{7,6},{8,9},{9,8},{10,11... | collective-permute-start | bytes 2654216 | tf_op jit(solution)/shard_map/ppermute | solution.py:103
  79.0 23.9 %collective-permute-start.12 = (bf16[4,144,768]{2,1,0:T(8,128)(2,1)S(1)}, bf16[4,144,768]{2,1,0:T(8,128)(2,1)S(1)}, u32[]{:S(2)}, u32[]{:S(2)}) collective-permute-start(bf16[4,144,768]{2,1,0:T(8,128)(2,1)S(1)} %broadcast_select_fusion), channel_id=1, source_target_pairs={{4,6},{2,0},{5,7},{3,1},{12,14},{10,8},{13,15},{11,9},{20,22},{18,... | collective-permute-start | bytes 2654216 | tf_op jit(solution)/shard_map/ppermute | solution.py:94
  80.5 3.2 %collective-permute-start.11 = (bf16[4,144,768]{2,1,0:T(8,128)(2,1)S(1)}, bf16[4,144,768]{2,1,0:T(8,128)(2,1)S(1)}, u32[]{:S(2)}, u32[]{:S(2)}) collective-permute-start(bf16[4,144,768]{2,1,0:T(8,128)(2,1)S(1)} %collective-permute-done.9), channel_id=1, source_target_pairs={{0,1},{1,0},{2,3},{3,2},{4,5},{5,4},{6,7},{7,6},{8,9},{9,8},{10,11... | collective-permute-start | bytes 2654216 | tf_op jit(solution)/shard_map/ppermute | solution.py:104
  81.0 0.9 copy-start.3
  82.0 1.1 %slice-start.2 = ((bf16[4,144,768]{2,1,0:T(8,128)(2,1)}), bf16[4,128,768]{2,1,0:T(8,128)(2,1)S(1)}, s32[]{:S(2)}) async-start(bf16[4,144,768]{2,1,0:T(8,128)(2,1)} %copy-done.3), calls=%async_computation.2 | async-start | bytes 1572864 | tf_op jit(solution)/shard_map/slice | solution.py:29
  104.9 2.5 %collective-permute-start.13 = (bf16[4,144,768]{2,1,0:T(8,128)(2,1)S(1)}, bf16[4,144,768]{2,1,0:T(8,128)(2,1)S(1)}, u32[]{:S(2)}, u32[]{:S(2)}) collective-permute-start(bf16[4,144,768]{2,1,0:T(8,128)(2,1)S(1)} %collective-permute-done.12), channel_id=1, source_target_pairs={{0,1},{1,0},{2,3},{3,2},{4,5},{5,4},{6,7},{7,6},{8,9},{9,8},{10,11... | collective-permute-start | bytes 2654216 | tf_op jit(solution)/shard_map/ppermute | solution.py:97

commit v8 on v5

--- a/solution.py
+++ b/solution.py
@@ -30,16 +30,22 @@
 
 
 def per_device(embeddings, counts):
+    buckets = lax.axis_size("bucket")
+    bucket = lax.axis_index("bucket")
     slot_rows = embeddings.shape[3]
     width = embeddings.shape[4]
-    count_rows = jnp.zeros(embeddings.shape[:3] + (16, width), jnp.bfloat16)
-    count_rows = count_rows.at[:, :, :, 0, 0].set(counts[..., 0].astype(jnp.bfloat16))
-    packed = jnp.concatenate([embeddings, count_rows], axis=3)
-    slabs = lax.all_to_all(packed, "bucket", split_axis=2, concat_axis=0, tiled=True)
+    count_rows = jnp.zeros(embeddings.shape[2:3] + (16, width), jnp.bfloat16)
+    count_rows = count_rows.at[:, 0, 0].set(counts[0, 0, :, 0].astype(jnp.bfloat16))
+    packed = jnp.concatenate([embeddings[0, 0], count_rows], axis=1)
+    arrived = [lax.dynamic_index_in_dim(packed, bucket, axis=0, keepdims=False)]
+    for m in range(1, buckets):
+        outgoing = lax.dynamic_index_in_dim(packed, bucket ^ m, axis=0, keepdims=False)
+        arrived.append(lax.ppermute(outgoing, "bucket", [(i, i ^ m) for i in range(buckets)]))
+    slabs = jnp.stack(arrived)
     sources = slabs.shape[0]
     rows = sources * slot_rows
-    data = slabs[:, :, :, :slot_rows].reshape(rows, width)
-    own_counts = slabs[:, 0, 0, slot_rows, 0].astype(jnp.int32)
+    data = slabs[:, :slot_rows].reshape(rows, width)
+    own_counts = slabs[:, slot_rows, 0].astype(jnp.int32)
     live = live_of(own_counts, slot_rows)
     chips = lax.axis_size("chip")
     cores = lax.axis_size("core")
@@ -110,7 +116,9 @@
         acc = add_pair(acc, above_swapped, times_listed(chip + step, other_core))
     summed, squares = acc
     result = summed * lax.rsqrt(squares)[:, None] * live[:, None]
-    return result.astype(jnp.bfloat16).reshape(1, 1, rows, width)
+    result = result.astype(jnp.bfloat16).reshape(sources, slot_rows, width)
+    order = jnp.arange(sources, dtype=jnp.int32) ^ bucket
+    return jnp.take(result, order, axis=0).reshape(1, 1, rows, width)
 
 
 def solution(mesh):

time: 101 us -> 99.3 us (0.983)
  waiting for transfers between devices: 57.8 us -> 52.1 us
  other arithmetic: 7.31 us -> 10.2 us
    all_to_all x1 -> x0, waiting for transfers between devices: 11.9 us -> none  [per_device(): lax.all_to_all(packed, 'bucket', split_axis=2, concat_axis=0, tiled=True)]
    ppermute x0 -> x3, waiting for transfers between devices: none -> 9.29 us  [per_device(): lax.ppermute(outgoing, 'bucket', [(i, i ^ m) for i in range(buckets)])]
    all_to_all x1 -> x0, starting transfers between devices: 5.19 us -> none  [per_device(): lax.all_to_all(packed, 'bucket', split_axis=2, concat_axis=0, tiled=True)]
    ppermute x0 -> x3, starting transfers between devices: none -> 4.63 us  [per_device(): lax.ppermute(outgoing, 'bucket', [(i, i ^ m) for i in range(buckets)])]
    ppermute x1, waiting for transfers between devices: 12.9 us -> 9.87 us  [per_device(): lax.ppermute(mine, 'chip', up)]
    convert_element_type x2, other arithmetic: 0.42 us -> 2.19 us  [normalize(): (values * lax.rsqrt(jnp.sum(values * values, axis=-1, keepdims=True) + EP...]
    dot_general x12, matrix products: 8.75 us -> 10.1 us  [weigh(): scores = jnp.dot(unit_a, unit_b.T, preferred_element_type=jnp.float32)]
    select_n x0 -> x2, other arithmetic: none -> 1.03 us  [per_device(): return jnp.take(result, order, axis=0).reshape(1, 1, rows, width)]
  transfers between devices with their start and end apart: 12 -> 14, of which waited for: 7 -> 9; matrix products, arithmetic and copies ran while one was open for 18% -> 22% of each run, Pallas kernels for 0% -> 0%
where the time goes in v8:
time: 99.3 us; the launch traced here: 98.9 us
  waiting for transfers between devices  52.1 us (52%)
  matrix products  17.8 us (18%)
  starting transfers between devices  16.9 us (17%)
  other arithmetic  10.2 us (10%)
  local copies, waits for them, and re-layouts  1.1 us (1%)
    ppermute x1, waiting for transfers between devices, per_device(): last = lax.ppermute(outgoing, 'chip', ends)  14.2 us
    dot_general x12, matrix products, weigh(): scores = jnp.dot(unit_a, unit_b.T, preferred_element_type=jnp.float32)  10.1 us
    ppermute x1, waiting for transfers between devices, per_device(): lax.ppermute(mine, 'chip', up)  9.87 us
    ppermute x1, waiting for transfers between devices, per_device(): lax.ppermute(from_below, 'chip', up)  9.83 us
    ppermute x3, waiting for transfers between devices, per_device(): lax.ppermute(outgoing, 'bucket', [(i, i ^ m) for i in range(buckets)])  9.29 us
    dot_general x11, matrix products, pair_terms(): jnp.dot(weights.astype(jnp.bfloat16), got_data, preferred_element_type=jn...  7.14 us
    ppermute x3, starting transfers between devices, per_device(): lax.ppermute(outgoing, 'bucket', [(i, i ^ m) for i in range(buckets)])  4.63 us
    ppermute x1, waiting for transfers between devices, per_device(): lax.ppermute(from_above, 'chip', down)  4.16 us
  transfers between devices with their start and end apart: 14, of which 9 were waited for; matrix products, arithmetic and copies ran while one was open for 22% of the time, Pallas kernels for 0%

profile of v8, /device:TPU:0, one launch (start us, length us, event | category | flops | bytes accessed | tf_op | source)
XLA Modules:
  0.0 98.9 jit_solution(2214394281233511679)
XLA Ops:
  0.0 0.7 convert_bitcast_fusion.12
  0.8 1.2 %fusion.51 = bf16[4,144,768]{2,1,0:T(8,128)(2,1)S(1)} fusion(bf16[4,1,1]{2,1,0:T(2,128)(2,1)S(1)} %copy.5, bf16[4,128,768]{2,1,0:T(8,128)(2,1)} %bitcast.129), kind=kLoop, calls=%fused_computation.108 | loop fusion | flops 2654208 | bytes 1671176 | tf_op jit(solution)/shard_map/concatenate | solution.py:39
  2.1 4.0 %collective-permute-start.2 = (bf16[144,768]{1,0:T(8,128)(2,1)S(1)}, bf16[144,768]{1,0:T(8,128)(2,1)S(1)}, u32[]{:S(2)}, u32[]{:S(2)}) collective-permute-start(bf16[144,768]{1,0:T(8,128)(2,1)S(1)} %get-tuple-element.54), channel_id=1, source_target_pairs={{0,24},{8,16},{16,8},{24,0},{1,25},{9,17},{17,9},{25,1},{2,26},{10... | collective-permute-start | bytes 663560 | tf_op jit(solution)/shard_map/ppermute | solution.py:43
  6.0 0.5 collective-permute-start.1
  7.2 5.2 %collective-permute-done.2 = bf16[144,768]{1,0:T(8,128)(2,1)S(1)} collective-permute-done((bf16[144,768]{1,0:T(8,128)(2,1)S(1)}, bf16[144,768]{1,0:T(8,128)(2,1)S(1)}, u32[]{:S(2)}, u32[]{:S(2)}) %collective-permute-start.2) | collective-permute-done | bytes 221216 | tf_op jit(solution)/shard_map/ppermute | solution.py:43
  12.4 3.8 %collective-permute-done.1 = bf16[144,768]{1,0:T(8,128)(2,1)S(1)} collective-permute-done((bf16[144,768]{1,0:T(8,128)(2,1)S(1)}, bf16[144,768]{1,0:T(8,128)(2,1)S(1)}, u32[]{:S(2)}, u32[]{:S(2)}) %collective-permute-start.1) | collective-permute-done | bytes 221216 | tf_op jit(solution)/shard_map/ppermute | solution.py:43
  17.0 0.9 fusion.52
  18.0 3.5 %collective-permute-start.4 = (bf16[528,768]{1,0:T(8,128)(2,1)}, bf16[528,768]{1,0:T(8,128)(2,1)S(1)}, u32[]{:S(2)}, u32[]{:S(2)}) collective-permute-start(bf16[528,768]{1,0:T(8,128)(2,1)} %fusion.52), channel_id=1, source_target_pairs={{0,2},{2,4},{4,6},{1,3},{3,5},{5,7},{8,10},{10,12},{12,14},{9,11},... | collective-permute-start | bytes 2433032 | tf_op jit(solution)/shard_map/ppermute | solution.py:90
  21.5 1.3 %collective-permute-start.5 = (bf16[528,768]{1,0:T(8,128)(2,1)}, bf16[528,768]{1,0:T(8,128)(2,1)S(1)}, u32[]{:S(2)}, u32[]{:S(2)}) collective-permute-start(bf16[528,768]{1,0:T(8,128)(2,1)} %fusion.52), channel_id=1, source_target_pairs={{2,0},{4,2},{6,4},{3,1},{5,3},{7,5},{10,8},{12,10},{14,12},{11,9},... | collective-permute-start | bytes 2433032 | tf_op jit(solution)/shard_map/ppermute | solution.py:90
  22.8 1.1 %fusion.3 = bf16[4,128,768]{2,1,0:T(8,128)(2,1)} fusion(f32[4,128]{1,0:T(4,128)S(1)} %get-tuple-element.58, bf16[4,144,768]{2,1,0:T(8,128)(2,1)S(1)} %pad_maximum_fusion), kind=kLoop, calls=%fused_computation.30 | loop fusion | flops 1179648 | bytes 1574912 | tf_op jit(solution)/shard_map/convert_element_type | solution.py:16
  23.9 1.1 %multiply_convert_fusion.1 = bf16[512,768]{1,0:T(8,128)(2,1)} fusion(f32[512]{0:T(512)S(1)} %get-tuple-element.57, bf16[4,128,768]{2,1,0:T(8,128)(2,1)S(1)} %slice.133), kind=kLoop, calls=%fused_computation.57 | loop fusion | flops 1179648 | bytes 1574912 | tf_op jit(solution)/shard_map/convert_element_type | solution.py:16
  25.2 2.1 %multiply_reduce_fusion.11 = (f32[512]{0:T(512)S(1)}, bf16[512,512]{0,1:T(8,128)(2,1)S(1)}) fusion(f32[512]{0:T(512)S(1)} %convert_bitcast_fusion.11, bf16[512,768]{1,0:T(8,128)(2,1)} %bitcast.130), kind=kOutput, calls=%fused_computation.106 | convolution fusion | flops 405011968 | bytes 1314816 | tf_op jit(solution)/shard_map/dot_general | solution.py:22
  27.4 0.6 fusion.115
  28.5 0.7 multiply_reduce_fusion.10
  29.3 0.6 multiply_add_fusion.2
  29.9 9.9 %collective-permute-done.4 = bf16[528,768]{1,0:T(8,128)(2,1)S(1)} collective-permute-done((bf16[528,768]{1,0:T(8,128)(2,1)}, bf16[528,768]{1,0:T(8,128)(2,1)S(1)}, u32[]{:S(2)}, u32[]{:S(2)}) %collective-permute-start.4) | collective-permute-done | bytes 811040 | tf_op jit(solution)/shard_map/ppermute | solution.py:90
  39.8 4.1 %collective-permute-done.5 = bf16[528,768]{1,0:T(8,128)(2,1)S(1)} collective-permute-done((bf16[528,768]{1,0:T(8,128)(2,1)}, bf16[528,768]{1,0:T(8,128)(2,1)S(1)}, u32[]{:S(2)}, u32[]{:S(2)}) %collective-permute-start.5) | collective-permute-done | bytes 811040 | tf_op jit(solution)/shard_map/ppermute | solution.py:90
  44.2 0.6 collective-permute-start.7
  44.8 3.5 %collective-permute-start.8 = (bf16[528,768]{1,0:T(8,128)(2,1)S(1)}, bf16[528,768]{1,0:T(8,128)(2,1)S(1)}, u32[]{:S(2)}, u32[]{:S(2)}) collective-permute-start(bf16[528,768]{1,0:T(8,128)(2,1)S(1)} %collective-permute-done.4), channel_id=1, source_target_pairs={{0,2},{2,4},{4,6},{1,3},{3,5},{5,7},{8,10},{10,12},{12,14},{9,11},... | collective-permute-start | bytes 2433032 | tf_op jit(solution)/shard_map/ppermute | solution.py:97
  48.3 1.3 %collective-permute-start.9 = (bf16[528,768]{1,0:T(8,128)(2,1)S(1)}, bf16[528,768]{1,0:T(8,128)(2,1)S(1)}, u32[]{:S(2)}, u32[]{:S(2)}) collective-permute-start(bf16[528,768]{1,0:T(8,128)(2,1)S(1)} %collective-permute-done.5), channel_id=1, source_target_pairs={{2,0},{4,2},{6,4},{3,1},{5,3},{7,5},{10,8},{12,10},{14,12},{11,9},... | collective-permute-start | bytes 2433032 | tf_op jit(solution)/shard_map/ppermute | solution.py:97
  49.7 0.7 multiply_reduce_fusion.8
  50.4 0.7 multiply_reduce_fusion.9
  51.2 0.6 fusion.99
  51.8 0.6 fusion.102
  53.0 0.7 multiply_reduce_fusion.7
  53.7 0.7 multiply_reduce_fusion.6
  54.5 0.6 fusion.85
  55.1 0.8 multiply_add_fusion.1
  55.9 9.8 %collective-permute-done.8 = bf16[528,768]{1,0:T(8,128)(2,1)S(1)} collective-permute-done((bf16[528,768]{1,0:T(8,128)(2,1)S(1)}, bf16[528,768]{1,0:T(8,128)(2,1)S(1)}, u32[]{:S(2)}, u32[]{:S(2)}) %collective-permute-start.8) | collective-permute-done | bytes 811040 | tf_op jit(solution)/shard_map/ppermute | solution.py:97
  65.7 4.2 %collective-permute-done.9 = bf16[528,768]{1,0:T(8,128)(2,1)S(1)} collective-permute-done((bf16[528,768]{1,0:T(8,128)(2,1)S(1)}, bf16[528,768]{1,0:T(8,128)(2,1)S(1)}, u32[]{:S(2)}, u32[]{:S(2)}) %collective-permute-start.9) | collective-permute-done | bytes 811040 | tf_op jit(solution)/shard_map/ppermute | solution.py:97
  70.4 0.6 collective-permute-start.11
  71.2 1.5 %collective-permute-start.12 = (bf16[528,768]{1,0:T(8,128)(2,1)S(1)}, bf16[528,768]{1,0:T(8,128)(2,1)S(1)}, u32[]{:S(2)}, u32[]{:S(2)}) collective-permute-start(bf16[528,768]{1,0:T(8,128)(2,1)S(1)} %broadcast_select_fusion), channel_id=1, source_target_pairs={{4,6},{2,0},{5,7},{3,1},{12,14},{10,8},{13,15},{11,9},{20,22},{18,... | collective-permute-start | bytes 2433032 | tf_op jit(solution)/shard_map/ppermute | solution.py:101
  72.7 0.7 multiply_reduce_fusion.4
  73.4 0.7 multiply_reduce_fusion.5
  74.2 0.6 fusion.93
  74.8 0.6 fusion.96
  76.0 0.7 multiply_reduce_fusion.3
  76.8 0.7 multiply_reduce_fusion.2
  77.5 0.6 fusion.80
  78.1 0.8 multiply_add_fusion
  78.9 14.2 %collective-permute-done.12 = bf16[528,768]{1,0:T(8,128)(2,1)S(1)} collective-permute-done((bf16[528,768]{1,0:T(8,128)(2,1)S(1)}, bf16[528,768]{1,0:T(8,128)(2,1)S(1)}, u32[]{:S(2)}, u32[]{:S(2)}) %collective-permute-start.12) | collective-permute-done | bytes 811040 | tf_op jit(solution)/shard_map/ppermute | solution.py:101
  93.4 0.7 multiply_reduce_fusion.1
  94.2 0.6 fusion.90
  94.8 0.7 collective-permute-done.13
  95.8 0.7 multiply_reduce_fusion
  96.5 0.8 multiply_convert_fusion
  97.3 0.6 gather_fusion
  97.9 1.0 %broadcast_select_fusion.1 = bf16[1,1,512,768]{3,2,1,0:T(8,128)(2,1)} fusion(bf16[1,1,512,768]{3,2,1,0:T(8,128)(2,1)S(1)} %bitcast.122, pred[512]{0:T(512)(128)(4,1)S(1)} %broadcast_bitcast_fusion), kind=kLoop, calls=%fused_computation.123 | loop fusion | flops 393216 | bytes 1573376 | tf_op jit(solution)/shard_map/jit(_take)/select_n | solution.py:121
  (73 shorter events, 5.2 us)
Async XLA Ops:
  2.1 10.3 %collective-permute-start.2 = (bf16[144,768]{1,0:T(8,128)(2,1)S(1)}, bf16[144,768]{1,0:T(8,128)(2,1)S(1)}, u32[]{:S(2)}, u32[]{:S(2)}) collective-permute-start(bf16[144,768]{1,0:T(8,128)(2,1)S(1)} %get-tuple-element.54), channel_id=1, source_target_pairs={{0,24},{8,16},{16,8},{24,0},{1,25},{9,17},{17,9},{25,1},{2,26},{10... | collective-permute-start | bytes 663560 | tf_op jit(solution)/shard_map/ppermute | solution.py:43
  6.0 10.2 %collective-permute-start.1 = (bf16[144,768]{1,0:T(8,128)(2,1)S(1)}, bf16[144,768]{1,0:T(8,128)(2,1)S(1)}, u32[]{:S(2)}, u32[]{:S(2)}) collective-permute-start(bf16[144,768]{1,0:T(8,128)(2,1)S(1)} %get-tuple-element.55), channel_id=1, source_target_pairs={{0,16},{8,24},{16,0},{24,8},{1,17},{9,25},{17,1},{25,9},{2,18},{10... | collective-permute-start | bytes 663560 | tf_op jit(solution)/shard_map/ppermute | solution.py:43
  6.6 10.0 %collective-permute-start = (bf16[144,768]{1,0:T(8,128)(2,1)S(1)}, bf16[144,768]{1,0:T(8,128)(2,1)S(1)}, u32[]{:S(2)}, u32[]{:S(2)}) collective-permute-start(bf16[144,768]{1,0:T(8,128)(2,1)S(1)} %get-tuple-element.56), channel_id=1, source_target_pairs={{0,8},{8,0},{16,24},{24,16},{1,9},{9,1},{17,25},{25,17},{2,10},{10... | collective-permute-start | bytes 663560 | tf_op jit(solution)/shard_map/ppermute | solution.py:43
  18.0 10.0 %collective-permute-start.3 = (bf16[528,768]{1,0:T(8,128)(2,1)}, bf16[528,768]{1,0:T(8,128)(2,1)S(1)}, u32[]{:S(2)}, u32[]{:S(2)}) collective-permute-start(bf16[528,768]{1,0:T(8,128)(2,1)} %fusion.52), channel_id=1, source_target_pairs={{0,1},{1,0},{2,3},{3,2},{4,5},{5,4},{6,7},{7,6},{8,9},{9,8},{10,11... | collective-permute-start | bytes 2433032 | tf_op jit(solution)/shard_map/ppermute | solution.py:91
  18.0 21.8 %collective-permute-start.4 = (bf16[528,768]{1,0:T(8,128)(2,1)}, bf16[528,768]{1,0:T(8,128)(2,1)S(1)}, u32[]{:S(2)}, u32[]{:S(2)}) collective-permute-start(bf16[528,768]{1,0:T(8,128)(2,1)} %fusion.52), channel_id=1, source_target_pairs={{0,2},{2,4},{4,6},{1,3},{3,5},{5,7},{8,10},{10,12},{12,14},{9,11},... | collective-permute-start | bytes 2433032 | tf_op jit(solution)/shard_map/ppermute | solution.py:90
  21.5 22.3 %collective-permute-start.5 = (bf16[528,768]{1,0:T(8,128)(2,1)}, bf16[528,768]{1,0:T(8,128)(2,1)S(1)}, u32[]{:S(2)}, u32[]{:S(2)}) collective-permute-start(bf16[528,768]{1,0:T(8,128)(2,1)} %fusion.52), channel_id=1, source_target_pairs={{2,0},{4,2},{6,4},{3,1},{5,3},{7,5},{10,8},{12,10},{14,12},{11,9},... | collective-permute-start | bytes 2433032 | tf_op jit(solution)/shard_map/ppermute | solution.py:90
  27.4 1.1 %copy-start = (bf16[512,768]{1,0:T(8,128)(2,1)S(1)}, bf16[512,768]{1,0:T(8,128)(2,1)}, u32[]{:S(2)}) copy-start(bf16[512,768]{1,0:T(8,128)(2,1)} %multiply_convert_fusion.1) | copy-start | bytes 2359300
  43.8 8.6 %collective-permute-start.6 = (bf16[528,768]{1,0:T(8,128)(2,1)S(1)}, bf16[528,768]{1,0:T(8,128)(2,1)S(1)}, u32[]{:S(2)}, u32[]{:S(2)}) collective-permute-start(bf16[528,768]{1,0:T(8,128)(2,1)S(1)} %collective-permute-done.4), channel_id=1, source_target_pairs={{0,1},{1,0},{2,3},{3,2},{4,5},{5,4},{6,7},{7,6},{8,9},{9,8},{10,11... | collective-permute-start | bytes 2433032 | tf_op jit(solution)/shard_map/ppermute | solution.py:111
  44.2 8.5 %collective-permute-start.7 = (bf16[528,768]{1,0:T(8,128)(2,1)S(1)}, bf16[528,768]{1,0:T(8,128)(2,1)S(1)}, u32[]{:S(2)}, u32[]{:S(2)}) collective-permute-start(bf16[528,768]{1,0:T(8,128)(2,1)S(1)} %collective-permute-done.5), channel_id=1, source_target_pairs={{0,1},{1,0},{2,3},{3,2},{4,5},{5,4},{6,7},{7,6},{8,9},{9,8},{10,11... | collective-permute-start | bytes 2433032 | tf_op jit(solution)/shard_map/ppermute | solution.py:112
  44.8 20.9 %collective-permute-start.8 = (bf16[528,768]{1,0:T(8,128)(2,1)S(1)}, bf16[528,768]{1,0:T(8,128)(2,1)S(1)}, u32[]{:S(2)}, u32[]{:S(2)}) collective-permute-start(bf16[528,768]{1,0:T(8,128)(2,1)S(1)} %collective-permute-done.4), channel_id=1, source_target_pairs={{0,2},{2,4},{4,6},{1,3},{3,5},{5,7},{8,10},{10,12},{12,14},{9,11},... | collective-permute-start | bytes 2433032 | tf_op jit(solution)/shard_map/ppermute | solution.py:97
  48.3 21.6 %collective-permute-start.9 = (bf16[528,768]{1,0:T(8,128)(2,1)S(1)}, bf16[528,768]{1,0:T(8,128)(2,1)S(1)}, u32[]{:S(2)}, u32[]{:S(2)}) collective-permute-start(bf16[528,768]{1,0:T(8,128)(2,1)S(1)} %collective-permute-done.5), channel_id=1, source_target_pairs={{2,0},{4,2},{6,4},{3,1},{5,3},{7,5},{10,8},{12,10},{14,12},{11,9},... | collective-permute-start | bytes 2433032 | tf_op jit(solution)/shard_map/ppermute | solution.py:97
  70.1 5.3 %collective-permute-start.10 = (bf16[528,768]{1,0:T(8,128)(2,1)S(1)}, bf16[528,768]{1,0:T(8,128)(2,1)S(1)}, u32[]{:S(2)}, u32[]{:S(2)}) collective-permute-start(bf16[528,768]{1,0:T(8,128)(2,1)S(1)} %collective-permute-done.8), channel_id=1, source_target_pairs={{0,1},{1,0},{2,3},{3,2},{4,5},{5,4},{6,7},{7,6},{8,9},{9,8},{10,11... | collective-permute-start | bytes 2433032 | tf_op jit(solution)/shard_map/ppermute | solution.py:111
  70.4 5.3 %collective-permute-start.11 = (bf16[528,768]{1,0:T(8,128)(2,1)S(1)}, bf16[528,768]{1,0:T(8,128)(2,1)S(1)}, u32[]{:S(2)}, u32[]{:S(2)}) collective-permute-start(bf16[528,768]{1,0:T(8,128)(2,1)S(1)} %collective-permute-done.9), channel_id=1, source_target_pairs={{0,1},{1,0},{2,3},{3,2},{4,5},{5,4},{6,7},{7,6},{8,9},{9,8},{10,11... | collective-permute-start | bytes 2433032 | tf_op jit(solution)/shard_map/ppermute | solution.py:112
  71.2 21.9 %collective-permute-start.12 = (bf16[528,768]{1,0:T(8,128)(2,1)S(1)}, bf16[528,768]{1,0:T(8,128)(2,1)S(1)}, u32[]{:S(2)}, u32[]{:S(2)}) collective-permute-start(bf16[528,768]{1,0:T(8,128)(2,1)S(1)} %broadcast_select_fusion), channel_id=1, source_target_pairs={{4,6},{2,0},{5,7},{3,1},{12,14},{10,8},{13,15},{11,9},{20,22},{18,... | collective-permute-start | bytes 2433032 | tf_op jit(solution)/shard_map/ppermute | solution.py:101
  93.1 2.3 %collective-permute-start.13 = (bf16[528,768]{1,0:T(8,128)(2,1)S(1)}, bf16[528,768]{1,0:T(8,128)(2,1)S(1)}, u32[]{:S(2)}, u32[]{:S(2)}) collective-permute-start(bf16[528,768]{1,0:T(8,128)(2,1)S(1)} %collective-permute-done.12), channel_id=1, source_target_pairs={{0,1},{1,0},{2,3},{3,2},{4,5},{5,4},{6,7},{7,6},{8,9},{9,8},{10,11... | collective-permute-start | bytes 2433032 | tf_op jit(solution)/shard_map/ppermute | solution.py:107

commit v9 on v8

--- a/solution.py
+++ b/solution.py
@@ -87,7 +87,22 @@
     tail = jnp.zeros((16, width), jnp.bfloat16).at[0, :sources].set(own_counts.astype(jnp.bfloat16))
     mine = jnp.concatenate([data, tail], axis=0)
     other_core = (core + 1) % cores
-    received = (lax.ppermute(mine, "chip", up), lax.ppermute(mine, "chip", down))
+    early = arrived[0]
+    late_rows = jnp.concatenate([a[:slot_rows] for a in arrived[1:]], axis=0)
+    late_tail = jnp.zeros((16, width), jnp.bfloat16).at[0, : sources - 1].set(
+        own_counts[1:].astype(jnp.bfloat16)
+    )
+    late = jnp.concatenate([late_rows, late_tail], axis=0)
+
+    def joined(first, rest):
+        tail = jnp.zeros((16, width), jnp.bfloat16).at[0, 0].set(first[slot_rows, 0])
+        tail = tail.at[0, 1:sources].set(rest[rows - slot_rows, : sources - 1])
+        return jnp.concatenate([first[:slot_rows], rest[: rows - slot_rows], tail], axis=0)
+
+    received = (
+        joined(lax.ppermute(early, "chip", up), lax.ppermute(late, "chip", up)),
+        joined(lax.ppermute(early, "chip", down), lax.ppermute(late, "chip", down)),
+    )
     swapped = lax.ppermute(mine, "core", swap)
     acc = add_pair(acc, swapped, times_listed(chip, other_core))
     for step in range(1, chips):

time: 99.3 us -> 106 us (1.067)
  local copies, waits for them, and re-layouts: 1.1 us -> 10.4 us
  waiting for transfers between devices: 52.1 us -> 44.9 us
  starting transfers between devices: 16.9 us -> 23.1 us
  matrix products: 17.8 us -> 16.5 us
    ppermute x2 -> x4, starting transfers between devices: 4.81 us -> 11.8 us  [the longest x1 4.97 us: per_device(): lax.ppermute(early, 'chip', up)]
    ppermute x2 -> x4, waiting for transfers between devices: 13.9 us -> 7.8 us  [the longest x1 5.97 us: per_device(): lax.ppermute(late, 'chip', up)]
    scatter x0 -> x4, local copies, waits for them, and re-layouts: none -> 4.24 us  [the longest x2 2.94 us: joined(): tail = tail.at[0, 1:sources].set(rest[rows - slot_rows, :sources - 1])]
    slice x0 -> x15, local copies, waits for them, and re-layouts: none -> 3.17 us  [the longest x3 1.21 us: joined(): rest[:rows - slot_rows]]
    unnamed x3 -> x9, local copies, waits for them, and re-layouts: 0.31 us -> 1.68 us
    dot_general x12, matrix products: 10.1 us -> 8.72 us  [weigh(): scores = jnp.dot(unit_a, unit_b.T, preferred_element_type=jnp.float32)]
    ppermute x3, starting transfers between devices: 4.63 us -> 3.55 us  [per_device(): lax.ppermute(outgoing, 'bucket', [(i, i ^ m) for i in range(buckets)])]
  transfers between devices with their start and end apart: 14 -> 16, of which waited for: 9 -> 9; matrix products, arithmetic and copies ran while one was open for 22% -> 27% of each run, Pallas kernels for 0% -> 0%
where the time goes in v9:
time: 106 us
  waiting for transfers between devices  44.9 us (42%)
  starting transfers between devices  23.1 us (22%)
  matrix products  16.5 us (16%)
  local copies, waits for them, and re-layouts  10.4 us (10%)
  other arithmetic  10.3 us (10%)
    ppermute x1, waiting for transfers between devices, per_device(): last = lax.ppermute(outgoing, 'chip', ends)  14.2 us
    ppermute x1, waiting for transfers between devices, per_device(): lax.ppermute(from_below, 'chip', up)  9.6 us
    dot_general x12, matrix products, weigh(): scores = jnp.dot(unit_a, unit_b.T, preferred_element_type=jnp.float32)  8.72 us
    ppermute x3, waiting for transfers between devices, per_device(): lax.ppermute(outgoing, 'bucket', [(i, i ^ m) for i in range(buckets)])  8.45 us
    dot_general x11, matrix products, pair_terms(): jnp.dot(weights.astype(jnp.bfloat16), got_data, preferred_element_type=jn...  7.18 us
    ppermute x1, waiting for transfers between devices, per_device(): lax.ppermute(late, 'chip', up)  5.97 us
    ppermute x1, starting transfers between devices, per_device(): lax.ppermute(early, 'chip', up)  4.97 us
    ppermute x1, starting transfers between devices, per_device(): lax.ppermute(late, 'chip', up)  4.29 us
  transfers between devices with their start and end apart: 16, of which 9 were waited for; matrix products, arithmetic and copies ran while one was open for 27% of the time, Pallas kernels for 0%

profile of v9, /device:TPU:0, one launch (start us, length us, event | category | flops | bytes accessed | tf_op | source)
XLA Modules:
  0.0 105.8 jit_solution(13928466950118834230)
XLA Ops:
  0.0 0.7 convert_bitcast_fusion.12
  0.8 1.2 %fusion.52 = bf16[4,144,768]{2,1,0:T(8,128)(2,1)S(1)} fusion(bf16[4,1,1]{2,1,0:T(2,128)(2,1)S(1)} %copy.5, bf16[4,128,768]{2,1,0:T(8,128)(2,1)} %bitcast.135), kind=kLoop, calls=%fused_computation.110 | loop fusion | flops 2654208 | bytes 1671176 | tf_op jit(solution)/shard_map/concatenate | solution.py:39
  2.1 5.0 %collective-permute-start.4 = (bf16[144,768]{1,0:T(8,128)(2,1)S(1)}, bf16[144,768]{1,0:T(8,128)(2,1)S(1)}, u32[]{:S(2)}, u32[]{:S(2)}) collective-permute-start(bf16[144,768]{1,0:T(8,128)(2,1)S(1)} %bitcast.127), channel_id=1, source_target_pairs={{0,2},{2,4},{4,6},{1,3},{3,5},{5,7},{8,10},{10,12},{12,14},{9,11},... | collective-permute-start | bytes 663560 | tf_op jit(solution)/shard_map/ppermute | solution.py:103
  7.0 1.3 %collective-permute-start.6 = (bf16[144,768]{1,0:T(8,128)(2,1)S(1)}, bf16[144,768]{1,0:T(8,128)(2,1)S(1)}, u32[]{:S(2)}, u32[]{:S(2)}) collective-permute-start(bf16[144,768]{1,0:T(8,128)(2,1)S(1)} %bitcast.128), channel_id=1, source_target_pairs={{2,0},{4,2},{6,4},{3,1},{5,3},{7,5},{10,8},{12,10},{14,12},{11,9},... | collective-permute-start | bytes 663560 | tf_op jit(solution)/shard_map/ppermute | solution.py:104
  8.3 2.5 %collective-permute-start.2 = (bf16[144,768]{1,0:T(8,128)(2,1)S(1)}, bf16[144,768]{1,0:T(8,128)(2,1)S(1)}, u32[]{:S(2)}, u32[]{:S(2)}) collective-permute-start(bf16[144,768]{1,0:T(8,128)(2,1)S(1)} %get-tuple-element.114), channel_id=1, source_target_pairs={{0,24},{8,16},{16,8},{24,0},{1,25},{9,17},{17,9},{25,1},{2,26},{10... | collective-permute-start | bytes 663560 | tf_op jit(solution)/shard_map/ppermute | solution.py:43
  12.6 5.1 %collective-permute-done.2 = bf16[144,768]{1,0:T(8,128)(2,1)S(1)} collective-permute-done((bf16[144,768]{1,0:T(8,128)(2,1)S(1)}, bf16[144,768]{1,0:T(8,128)(2,1)S(1)}, u32[]{:S(2)}, u32[]{:S(2)}) %collective-permute-start.2) | collective-permute-done | bytes 221216 | tf_op jit(solution)/shard_map/ppermute | solution.py:43
  17.6 3.3 %collective-permute-done.1 = bf16[144,768]{1,0:T(8,128)(2,1)S(1)} collective-permute-done((bf16[144,768]{1,0:T(8,128)(2,1)S(1)}, bf16[144,768]{1,0:T(8,128)(2,1)S(1)}, u32[]{:S(2)}, u32[]{:S(2)}) %collective-permute-start.1) | collective-permute-done | bytes 221216 | tf_op jit(solution)/shard_map/ppermute | solution.py:43
  21.9 0.9 fusion.76
  22.8 4.3 %collective-permute-start.5 = (bf16[400,768]{1,0:T(8,128)(2,1)}, bf16[400,768]{1,0:T(8,128)(2,1)S(1)}, u32[]{:S(2)}, u32[]{:S(2)}) collective-permute-start(bf16[400,768]{1,0:T(8,128)(2,1)} %fusion.76), channel_id=1, source_target_pairs={{0,2},{2,4},{4,6},{1,3},{3,5},{5,7},{8,10},{10,12},{12,14},{9,11},... | collective-permute-start | bytes 1843208 | tf_op jit(solution)/shard_map/ppermute | solution.py:103
  27.1 1.3 %collective-permute-start.7 = (bf16[400,768]{1,0:T(8,128)(2,1)}, bf16[400,768]{1,0:T(8,128)(2,1)}, u32[]{:S(2)}, u32[]{:S(2)}) collective-permute-start(bf16[400,768]{1,0:T(8,128)(2,1)} %fusion.76), channel_id=1, source_target_pairs={{2,0},{4,2},{6,4},{3,1},{5,3},{7,5},{10,8},{12,10},{14,12},{11,9},... | collective-permute-start | bytes 1843208 | tf_op jit(solution)/shard_map/ppermute | solution.py:104
  28.7 0.9 fusion.53
  29.6 0.7 multiply_reduce_fusion.11
  31.0 0.6 scatter.29
  32.2 0.6 scatter.31
  32.8 1.1 %multiply_convert_fusion.1 = bf16[512,768]{1,0:T(8,128)(2,1)} fusion(f32[512]{0:T(512)S(1)} %get-tuple-element.117, bf16[4,128,768]{2,1,0:T(8,128)(2,1)S(1)} %slice.270), kind=kLoop, calls=%fused_computation.57 | loop fusion | flops 1179648 | bytes 1574912 | tf_op jit(solution)/shard_map/convert_element_type | solution.py:16
  34.0 0.6 fusion.117
  34.6 6.0 %collective-permute-done.5 = bf16[400,768]{1,0:T(8,128)(2,1)S(1)} collective-permute-done((bf16[400,768]{1,0:T(8,128)(2,1)}, bf16[400,768]{1,0:T(8,128)(2,1)S(1)}, u32[]{:S(2)}, u32[]{:S(2)}) %collective-permute-start.5) | collective-permute-done | bytes 614432 | tf_op jit(solution)/shard_map/ppermute | solution.py:103
  40.5 0.8 copy-done
  41.4 1.5 %scatter.30 = bf16[16,768]{1,0:T(8,128)(2,1)S(1)} dynamic-update-slice(bf16[16,768]{1,0:T(8,128)(2,1)S(1)} %scatter.29, bf16[1,3]{1,0:T(2,128)(2,1)S(1)} %slice.280, s32[]{:T(128)} %bitcast.16, s32[]{:T(128)} %bitcast.17) | dynamic-update-slice | bytes 16 | tf_op jit(solution)/shard_map/scatter | solution.py:99
  42.9 1.8 %collective-permute-done.7 = bf16[400,768]{1,0:T(8,128)(2,1)} collective-permute-done((bf16[400,768]{1,0:T(8,128)(2,1)}, bf16[400,768]{1,0:T(8,128)(2,1)}, u32[]{:S(2)}, u32[]{:S(2)}) %collective-permute-start.7) | collective-permute-done | bytes 614432 | tf_op jit(solution)/shard_map/ppermute | solution.py:104
  44.7 0.7 slice.284
  45.4 1.4 %scatter.34 = bf16[16,768]{1,0:T(8,128)(2,1)S(1)} dynamic-update-slice(bf16[16,768]{1,0:T(8,128)(2,1)S(1)} %scatter.31, bf16[1,3]{1,0:T(2,128)(2,1)S(1)} %slice.284, s32[]{:T(128)} %bitcast.16, s32[]{:T(128)} %bitcast.17) | dynamic-update-slice | bytes 16 | tf_op jit(solution)/shard_map/scatter | solution.py:99
  46.9 1.2 %slice.282 = bf16[384,768]{1,0:T(8,128)(2,1)S(1)} slice(bf16[400,768]{1,0:T(8,128)(2,1)} %collective-permute-done.7), slice={[0:384], [0:768]} | slice | bytes 1179648 | tf_op jit(solution)/shard_map/slice | solution.py:100
  48.5 0.7 copy-done.3
  49.3 0.7 multiply_reduce_fusion.10
  50.0 0.6 multiply_add_fusion.2
  51.7 3.5 %collective-permute-start.10 = (bf16[528,768]{1,0:T(8,128)(2,1)S(1)}, bf16[528,768]{1,0:T(8,128)(2,1)S(1)}, u32[]{:S(2)}, u32[]{:S(2)}) collective-permute-start(bf16[528,768]{1,0:T(8,128)(2,1)S(1)} %pad_maximum_fusion.1), channel_id=1, source_target_pairs={{0,2},{2,4},{4,6},{1,3},{3,5},{5,7},{8,10},{10,12},{12,14},{9,11},... | collective-permute-start | bytes 2433032 | tf_op jit(solution)/shard_map/ppermute | solution.py:112
  55.1 1.5 %collective-permute-start.11 = (bf16[528,768]{1,0:T(8,128)(2,1)S(1)}, bf16[528,768]{1,0:T(8,128)(2,1)S(1)}, u32[]{:S(2)}, u32[]{:S(2)}) collective-permute-start(bf16[528,768]{1,0:T(8,128)(2,1)S(1)} %pad_maximum_fusion.2), channel_id=1, source_target_pairs={{2,0},{4,2},{6,4},{3,1},{5,3},{7,5},{10,8},{12,10},{14,12},{11,9},... | collective-permute-start | bytes 2433032 | tf_op jit(solution)/shard_map/ppermute | solution.py:112
  56.8 0.7 multiply_reduce_fusion.8
  57.5 0.7 multiply_reduce_fusion.9
  60.1 0.7 multiply_reduce_fusion.7
  60.8 0.7 multiply_reduce_fusion.6
  62.2 0.8 multiply_add_fusion.1
  63.0 9.6 %collective-permute-done.10 = bf16[528,768]{1,0:T(8,128)(2,1)S(1)} collective-permute-done((bf16[528,768]{1,0:T(8,128)(2,1)S(1)}, bf16[528,768]{1,0:T(8,128)(2,1)S(1)}, u32[]{:S(2)}, u32[]{:S(2)}) %collective-permute-start.10) | collective-permute-done | bytes 811040 | tf_op jit(solution)/shard_map/ppermute | solution.py:112
  72.6 4.2 %collective-permute-done.11 = bf16[528,768]{1,0:T(8,128)(2,1)S(1)} collective-permute-done((bf16[528,768]{1,0:T(8,128)(2,1)S(1)}, bf16[528,768]{1,0:T(8,128)(2,1)S(1)}, u32[]{:S(2)}, u32[]{:S(2)}) %collective-permute-start.11) | collective-permute-done | bytes 811040 | tf_op jit(solution)/shard_map/ppermute | solution.py:112
  78.1 1.5 %collective-permute-start.14 = (bf16[528,768]{1,0:T(8,128)(2,1)S(1)}, bf16[528,768]{1,0:T(8,128)(2,1)S(1)}, u32[]{:S(2)}, u32[]{:S(2)}) collective-permute-start(bf16[528,768]{1,0:T(8,128)(2,1)S(1)} %broadcast_select_fusion), channel_id=1, source_target_pairs={{4,6},{2,0},{5,7},{3,1},{12,14},{10,8},{13,15},{11,9},{20,22},{18,... | collective-permute-start | bytes 2433032 | tf_op jit(solution)/shard_map/ppermute | solution.py:116
  79.6 0.7 multiply_reduce_fusion.4
  80.4 0.7 multiply_reduce_fusion.5
  82.9 0.7 multiply_reduce_fusion.3
  83.7 0.7 multiply_reduce_fusion.2
  84.4 0.6 fusion.82
  85.0 0.8 multiply_add_fusion
  85.8 14.2 %collective-permute-done.14 = bf16[528,768]{1,0:T(8,128)(2,1)S(1)} collective-permute-done((bf16[528,768]{1,0:T(8,128)(2,1)S(1)}, bf16[528,768]{1,0:T(8,128)(2,1)S(1)}, u32[]{:S(2)}, u32[]{:S(2)}) %collective-permute-start.14) | collective-permute-done | bytes 811040 | tf_op jit(solution)/shard_map/ppermute | solution.py:116
  100.3 0.7 multiply_reduce_fusion.1
  101.7 0.7 collective-permute-done.15
  102.7 0.7 multiply_reduce_fusion
  103.4 0.8 multiply_convert_fusion
  104.8 1.0 broadcast_select_fusion.1
  (108 shorter events, 13.3 us)
Async XLA Ops:
  2.1 28.3 %collective-permute-start.4 = (bf16[144,768]{1,0:T(8,128)(2,1)S(1)}, bf16[144,768]{1,0:T(8,128)(2,1)S(1)}, u32[]{:S(2)}, u32[]{:S(2)}) collective-permute-start(bf16[144,768]{1,0:T(8,128)(2,1)S(1)} %bitcast.127), channel_id=1, source_target_pairs={{0,2},{2,4},{4,6},{1,3},{3,5},{5,7},{8,10},{10,12},{12,14},{9,11},... | collective-permute-start | bytes 663560 | tf_op jit(solution)/shard_map/ppermute | solution.py:103
  7.0 24.6 %collective-permute-start.6 = (bf16[144,768]{1,0:T(8,128)(2,1)S(1)}, bf16[144,768]{1,0:T(8,128)(2,1)S(1)}, u32[]{:S(2)}, u32[]{:S(2)}) collective-permute-start(bf16[144,768]{1,0:T(8,128)(2,1)S(1)} %bitcast.128), channel_id=1, source_target_pairs={{2,0},{4,2},{6,4},{3,1},{5,3},{7,5},{10,8},{12,10},{14,12},{11,9},... | collective-permute-start | bytes 663560 | tf_op jit(solution)/shard_map/ppermute | solution.py:104
  8.3 9.3 %collective-permute-start.2 = (bf16[144,768]{1,0:T(8,128)(2,1)S(1)}, bf16[144,768]{1,0:T(8,128)(2,1)S(1)}, u32[]{:S(2)}, u32[]{:S(2)}) collective-permute-start(bf16[144,768]{1,0:T(8,128)(2,1)S(1)} %get-tuple-element.114), channel_id=1, source_target_pairs={{0,24},{8,16},{16,8},{24,0},{1,25},{9,17},{17,9},{25,1},{2,26},{10... | collective-permute-start | bytes 663560 | tf_op jit(solution)/shard_map/ppermute | solution.py:43
  10.9 10.1 %collective-permute-start.1 = (bf16[144,768]{1,0:T(8,128)(2,1)S(1)}, bf16[144,768]{1,0:T(8,128)(2,1)S(1)}, u32[]{:S(2)}, u32[]{:S(2)}) collective-permute-start(bf16[144,768]{1,0:T(8,128)(2,1)S(1)} %get-tuple-element.115), channel_id=1, source_target_pairs={{0,16},{8,24},{16,0},{24,8},{1,17},{9,25},{17,1},{25,9},{2,18},{10... | collective-permute-start | bytes 663560 | tf_op jit(solution)/shard_map/ppermute | solution.py:43
  11.4 9.7 %collective-permute-start = (bf16[144,768]{1,0:T(8,128)(2,1)S(1)}, bf16[144,768]{1,0:T(8,128)(2,1)S(1)}, u32[]{:S(2)}, u32[]{:S(2)}) collective-permute-start(bf16[144,768]{1,0:T(8,128)(2,1)S(1)} %get-tuple-element.116), channel_id=1, source_target_pairs={{0,8},{8,0},{16,24},{24,16},{1,9},{9,1},{17,25},{25,17},{2,10},{10... | collective-permute-start | bytes 663560 | tf_op jit(solution)/shard_map/ppermute | solution.py:43
  22.8 17.7 %collective-permute-start.5 = (bf16[400,768]{1,0:T(8,128)(2,1)}, bf16[400,768]{1,0:T(8,128)(2,1)S(1)}, u32[]{:S(2)}, u32[]{:S(2)}) collective-permute-start(bf16[400,768]{1,0:T(8,128)(2,1)} %fusion.76), channel_id=1, source_target_pairs={{0,2},{2,4},{4,6},{1,3},{3,5},{5,7},{8,10},{10,12},{12,14},{9,11},... | collective-permute-start | bytes 1843208 | tf_op jit(solution)/shard_map/ppermute | solution.py:103
  27.1 17.6 %collective-permute-start.7 = (bf16[400,768]{1,0:T(8,128)(2,1)}, bf16[400,768]{1,0:T(8,128)(2,1)}, u32[]{:S(2)}, u32[]{:S(2)}) collective-permute-start(bf16[400,768]{1,0:T(8,128)(2,1)} %fusion.76), channel_id=1, source_target_pairs={{2,0},{4,2},{6,4},{3,1},{5,3},{7,5},{10,8},{12,10},{14,12},{11,9},... | collective-permute-start | bytes 1843208 | tf_op jit(solution)/shard_map/ppermute | solution.py:104
  29.6 18.6 %collective-permute-start.3 = (bf16[528,768]{1,0:T(8,128)(2,1)}, bf16[528,768]{1,0:T(8,128)(2,1)S(1)}, u32[]{:S(2)}, u32[]{:S(2)}) collective-permute-start(bf16[528,768]{1,0:T(8,128)(2,1)} %fusion.53), channel_id=1, source_target_pairs={{0,1},{1,0},{2,3},{3,2},{4,5},{5,4},{6,7},{7,6},{8,9},{9,8},{10,11... | collective-permute-start | bytes 2433032 | tf_op jit(solution)/shard_map/ppermute | solution.py:106
  30.4 3.6 %copy-start.2 = (bf16[144,768]{1,0:T(8,128)(2,1)}, bf16[144,768]{1,0:T(8,128)(2,1)S(1)}, u32[]{:S(2)}) copy-start(bf16[144,768]{1,0:T(8,128)(2,1)S(1)} %collective-permute-done.4) | copy-start | bytes 663556
  31.6 2.9 %copy-start.1 = (bf16[144,768]{1,0:T(8,128)(2,1)}, bf16[144,768]{1,0:T(8,128)(2,1)S(1)}, u32[]{:S(2)}) copy-start(bf16[144,768]{1,0:T(8,128)(2,1)S(1)} %collective-permute-done.6) | copy-start | bytes 663556
  40.5 0.8 copy-start
  41.4 6.7 %slice-start.2 = ((bf16[144,768]{1,0:T(8,128)(2,1)}), bf16[128,768]{1,0:T(8,128)(2,1)S(1)}, s32[]{:S(2)}) async-start(bf16[144,768]{1,0:T(8,128)(2,1)} %copy-done.2), calls=%async_computation.2 | async-start | bytes 393216 | tf_op jit(solution)/shard_map/slice | solution.py:100
  46.8 1.2 %slice-start = ((bf16[400,768]{1,0:T(8,128)(2,1)}), bf16[384,768]{1,0:T(8,128)(2,1)S(1)}, s32[]{:S(2)}) async-start(bf16[400,768]{1,0:T(8,128)(2,1)} %copy-done), calls=%async_computation | async-start | bytes 1179648 | tf_op jit(solution)/shard_map/slice | solution.py:100
  46.8 1.3 %slice-start.1 = ((bf16[144,768]{1,0:T(8,128)(2,1)}), bf16[128,768]{1,0:T(8,128)(2,1)S(1)}, s32[]{:S(2)}) async-start(bf16[144,768]{1,0:T(8,128)(2,1)} %copy-done.1), calls=%async_computation.1 | async-start | bytes 393216 | tf_op jit(solution)/shard_map/slice | solution.py:100
  48.1 1.1 %copy-start.3 = (bf16[512,768]{1,0:T(8,128)(2,1)S(1)}, bf16[512,768]{1,0:T(8,128)(2,1)}, u32[]{:S(2)}) copy-start(bf16[512,768]{1,0:T(8,128)(2,1)} %multiply_convert_fusion.1) | copy-start | bytes 2359300
  50.6 8.8 %collective-permute-start.8 = (bf16[528,768]{1,0:T(8,128)(2,1)S(1)}, bf16[528,768]{1,0:T(8,128)(2,1)S(1)}, u32[]{:S(2)}, u32[]{:S(2)}) collective-permute-start(bf16[528,768]{1,0:T(8,128)(2,1)S(1)} %pad_maximum_fusion.1), channel_id=1, source_target_pairs={{0,1},{1,0},{2,3},{3,2},{4,5},{5,4},{6,7},{7,6},{8,9},{9,8},{10,11... | collective-permute-start | bytes 2433032 | tf_op jit(solution)/shard_map/ppermute | solution.py:126
  51.1 8.7 %collective-permute-start.9 = (bf16[528,768]{1,0:T(8,128)(2,1)S(1)}, bf16[528,768]{1,0:T(8,128)(2,1)S(1)}, u32[]{:S(2)}, u32[]{:S(2)}) collective-permute-start(bf16[528,768]{1,0:T(8,128)(2,1)S(1)} %pad_maximum_fusion.2), channel_id=1, source_target_pairs={{0,1},{1,0},{2,3},{3,2},{4,5},{5,4},{6,7},{7,6},{8,9},{9,8},{10,11... | collective-permute-start | bytes 2433032 | tf_op jit(solution)/shard_map/ppermute | solution.py:127
  51.7 20.9 %collective-permute-start.10 = (bf16[528,768]{1,0:T(8,128)(2,1)S(1)}, bf16[528,768]{1,0:T(8,128)(2,1)S(1)}, u32[]{:S(2)}, u32[]{:S(2)}) collective-permute-start(bf16[528,768]{1,0:T(8,128)(2,1)S(1)} %pad_maximum_fusion.1), channel_id=1, source_target_pairs={{0,2},{2,4},{4,6},{1,3},{3,5},{5,7},{8,10},{10,12},{12,14},{9,11},... | collective-permute-start | bytes 2433032 | tf_op jit(solution)/shard_map/ppermute | solution.py:112
  55.1 21.6 %collective-permute-start.11 = (bf16[528,768]{1,0:T(8,128)(2,1)S(1)}, bf16[528,768]{1,0:T(8,128)(2,1)S(1)}, u32[]{:S(2)}, u32[]{:S(2)}) collective-permute-start(bf16[528,768]{1,0:T(8,128)(2,1)S(1)} %pad_maximum_fusion.2), channel_id=1, source_target_pairs={{2,0},{4,2},{6,4},{3,1},{5,3},{7,5},{10,8},{12,10},{14,12},{11,9},... | collective-permute-start | bytes 2433032 | tf_op jit(solution)/shard_map/ppermute | solution.py:112
  77.0 5.3 %collective-permute-start.12 = (bf16[528,768]{1,0:T(8,128)(2,1)S(1)}, bf16[528,768]{1,0:T(8,128)(2,1)S(1)}, u32[]{:S(2)}, u32[]{:S(2)}) collective-permute-start(bf16[528,768]{1,0:T(8,128)(2,1)S(1)} %collective-permute-done.10), channel_id=1, source_target_pairs={{0,1},{1,0},{2,3},{3,2},{4,5},{5,4},{6,7},{7,6},{8,9},{9,8},{10,11... | collective-permute-start | bytes 2433032 | tf_op jit(solution)/shard_map/ppermute | solution.py:126
  77.3 5.3 %collective-permute-start.13 = (bf16[528,768]{1,0:T(8,128)(2,1)S(1)}, bf16[528,768]{1,0:T(8,128)(2,1)S(1)}, u32[]{:S(2)}, u32[]{:S(2)}) collective-permute-start(bf16[528,768]{1,0:T(8,128)(2,1)S(1)} %collective-permute-done.11), channel_id=1, source_target_pairs={{0,1},{1,0},{2,3},{3,2},{4,5},{5,4},{6,7},{7,6},{8,9},{9,8},{10,11... | collective-permute-start | bytes 2433032 | tf_op jit(solution)/shard_map/ppermute | solution.py:127
  78.1 21.9 %collective-permute-start.14 = (bf16[528,768]{1,0:T(8,128)(2,1)S(1)}, bf16[528,768]{1,0:T(8,128)(2,1)S(1)}, u32[]{:S(2)}, u32[]{:S(2)}) collective-permute-start(bf16[528,768]{1,0:T(8,128)(2,1)S(1)} %broadcast_select_fusion), channel_id=1, source_target_pairs={{4,6},{2,0},{5,7},{3,1},{12,14},{10,8},{13,15},{11,9},{20,22},{18,... | collective-permute-start | bytes 2433032 | tf_op jit(solution)/shard_map/ppermute | solution.py:116
  100.0 2.3 %collective-permute-start.15 = (bf16[528,768]{1,0:T(8,128)(2,1)S(1)}, bf16[528,768]{1,0:T(8,128)(2,1)S(1)}, u32[]{:S(2)}, u32[]{:S(2)}) collective-permute-start(bf16[528,768]{1,0:T(8,128)(2,1)S(1)} %collective-permute-done.14), channel_id=1, source_target_pairs={{0,1},{1,0},{2,3},{3,2},{4,5},{5,4},{6,7},{7,6},{8,9},{9,8},{10,11... | collective-permute-start | bytes 2433032 | tf_op jit(solution)/shard_map/ppermute | solution.py:122

commit v10 on v8

--- a/solution.py
+++ b/solution.py
@@ -71,8 +71,8 @@
 
     def pair_terms(acc, got, weight):
         summed, squares = acc
-        got_data = got[:rows]
-        got_counts = got[rows, :sources].astype(jnp.int32)
+        got_data = got[:, :slot_rows].reshape(-1, width)
+        got_counts = got[:, slot_rows, 0].astype(jnp.int32)
         weights = weigh(unit, normalize(got_data), live_of(got_counts, slot_rows), 1.0)
         part = jnp.dot(weights.astype(jnp.bfloat16), got_data, preferred_element_type=jnp.float32)
         return (summed + weight * part, squares + weight * jnp.sum(weights * weights, axis=1))
@@ -80,40 +80,25 @@
     def add_pair(acc, got, weight):
         return pair_terms(acc, got, weight)
 
-    swap = [(c, (c + 1) % cores) for c in range(cores)]
-    up = [(c, c + 1) for c in range(chips - 1)]
-    down = [(c + 1, c) for c in range(chips - 1)]
     acc = (summed, squares)
-    tail = jnp.zeros((16, width), jnp.bfloat16).at[0, :sources].set(own_counts.astype(jnp.bfloat16))
-    mine = jnp.concatenate([data, tail], axis=0)
-    other_core = (core + 1) % cores
-    received = (lax.ppermute(mine, "chip", up), lax.ppermute(mine, "chip", down))
-    swapped = lax.ppermute(mine, "core", swap)
-    acc = add_pair(acc, swapped, times_listed(chip, other_core))
-    for step in range(1, chips):
-        acc, received = lax.optimization_barrier((acc, received))
-        from_below, from_above = received
-        if step + 2 < chips:
-            received = (lax.ppermute(from_below, "chip", up), lax.ppermute(from_above, "chip", down))
-        elif step + 2 == chips and chips >= 4:
-            ends = [(chips - 2, chips - 1), (1, 0)]
-            outgoing = jnp.where(chip == chips - 2, from_below, from_above)
-            last = lax.ppermute(outgoing, "chip", ends)
-            received = (last, last)
-        elif step + 2 == chips:
-            received = (lax.ppermute(from_below, "chip", up), lax.ppermute(from_above, "chip", down))
-        if step + 1 == chips and chips >= 4:
-            far_chip = jnp.where(chip == 0, chips - 1, jnp.where(chip == chips - 1, 0, -1))
-            far_swapped = lax.ppermute(from_below, "core", swap)
-            acc = add_pair(acc, from_below, times_listed(far_chip, core))
-            acc = add_pair(acc, far_swapped, times_listed(far_chip, other_core))
-            continue
-        below_swapped = lax.ppermute(from_below, "core", swap)
-        above_swapped = lax.ppermute(from_above, "core", swap)
-        acc = add_pair(acc, from_below, times_listed(chip - step, core))
-        acc = add_pair(acc, from_above, times_listed(chip + step, core))
-        acc = add_pair(acc, below_swapped, times_listed(chip - step, other_core))
-        acc = add_pair(acc, above_swapped, times_listed(chip + step, other_core))
+    half = sources // 2
+    halves = [jnp.stack(arrived[:half]), jnp.stack(arrived[half:])]
+    gathered = []
+    for piece in halves:
+        if gathered:
+            piece, gathered[-1] = lax.optimization_barrier((piece, gathered[-1]))
+        along = lax.all_gather(piece, "chip", axis=0, tiled=False)
+        gathered.append(lax.all_gather(along, "core", axis=1, tiled=False))
+    for index in range(len(gathered)):
+        if index:
+            acc, got_all = lax.optimization_barrier((acc, gathered[index]))
+        else:
+            got_all = gathered[index]
+        for other_chip in range(chips):
+            for other in range(cores):
+                weight = times_listed(jnp.int32(other_chip), jnp.int32(other))
+                acc = add_pair(acc, got_all[other_chip, other], weight)
+                acc = lax.optimization_barrier(acc)
     summed, squares = acc
     result = summed * lax.rsqrt(squares)[:, None] * live[:, None]
     result = result.astype(jnp.bfloat16).reshape(sources, slot_rows, width)

time: 99.3 us -> 160 us (1.61)
  waiting for transfers between devices: 52.1 us -> 99.6 us
  between operations: 0.78 us -> 13.9 us
  starting transfers between devices: 16.9 us -> 6.33 us
  local copies, waits for them, and re-layouts: 1.1 us -> 9.19 us
  other arithmetic: 10.2 us -> 13.7 us
    all_gather x0 -> x4, waiting for transfers between devices: none -> 84.7 us  [the longest x2 75.3 us: per_device(): along = lax.all_gather(piece, 'chip', axis=0, tiled=False)]
    ppermute x11 -> x0, waiting for transfers between devices: 42.9 us -> none  [the longest x1 14.2 us: per_device(): last = lax.ppermute(outgoing, 'chip', ends)]
    ppermute x11 -> x0, starting transfers between devices: 12.2 us -> none  [the longest x1 3.52 us: per_device(): lax.ppermute(mine, 'chip', up)]
    ppermute x3, waiting for transfers between devices: 9.29 us -> 14.8 us  [per_device(): lax.ppermute(outgoing, 'bucket', [(i, i ^ m) for i in range(buckets)])]
    squeeze x0 -> x2, local copies, waits for them, and re-layouts: none -> 4.35 us  [per_device(): acc = add_pair(acc, got_all[other_chip, other], weight)]
    slice x0 -> x16, local copies, waits for them, and re-layouts: none -> 1.93 us  [pair_terms(): got_data = got[:, :slot_rows].reshape(-1, width)]
    another operation x0 -> x2, other arithmetic: none -> 1.73 us  [per_device(): halves = [jnp.stack(arrived[:half]), jnp.stack(arrived[half:])]]
    convert_element_type x11 -> x13, other arithmetic: 0.17 us -> 1.82 us  [the longest x12 1.6 us: pair_terms(): got_counts = got[:, slot_rows, 0].astype(jnp.int32)]
  transfers between devices with their start and end apart: 14 -> 7, of which waited for: 9 -> 6; matrix products, arithmetic and copies ran while one was open for 22% -> 7% of each run, Pallas kernels for 0% -> 0%
where the time goes in v10:
time: 160 us; the launch traced here: 159 us
  waiting for transfers between devices  99.6 us (62%)
  matrix products  16.6 us (10%)
  between operations  13.9 us (9%)
  other arithmetic  13.7 us (9%)
  local copies, waits for them, and re-layouts  9.19 us (6%)
  starting transfers between devices  6.33 us (4%)
    all_gather x2, waiting for transfers between devices, per_device(): along = lax.all_gather(piece, 'chip', axis=0, tiled=False)  75.3 us
    ppermute x3, waiting for transfers between devices, per_device(): lax.ppermute(outgoing, 'bucket', [(i, i ^ m) for i in range(buckets)])  14.8 us
    dot_general x17, matrix products, weigh(): scores = jnp.dot(unit_a, unit_b.T, preferred_element_type=jnp.float32)  9.44 us
    all_gather x2, waiting for transfers between devices, per_device(): gathered.append(lax.all_gather(along, 'core', axis=1, tiled=False))  9.38 us
    dot_general x16, matrix products, pair_terms(): jnp.dot(weights.astype(jnp.bfloat16), got_data, preferred_element_type=jn...  6.54 us
    ppermute x3, starting transfers between devices, per_device(): lax.ppermute(outgoing, 'bucket', [(i, i ^ m) for i in range(buckets)])  6.03 us
    squeeze x2, local copies, waits for them, and re-layouts, per_device(): acc = add_pair(acc, got_all[other_chip, other], weight)  4.35 us
  transfers between devices with their start and end apart: 7, of which 6 were waited for; matrix products, arithmetic and copies ran while one was open for 7% of the time, Pallas kernels for 0%

profile of v10, /device:TPU:0, one launch (start us, length us, event | category | flops | bytes accessed | tf_op | source)
XLA Modules:
  0.0 159.3 jit_solution(2180678459166494269)
XLA Ops:
  6.5 0.7 convert_bitcast_fusion.1
  7.3 1.2 fusion.38
  8.6 3.0 %collective-permute-start = (bf16[144,768]{1,0:T(8,128)(2,1)S(1)}, bf16[144,768]{1,0:T(8,128)(2,1)S(1)}, u32[]{:S(2)}, u32[]{:S(2)}) collective-permute-start(bf16[144,768]{1,0:T(8,128)(2,1)S(1)} %get-tuple-element.110), channel_id=1, source_target_pairs={{0,8},{8,0},{16,24},{24,16},{1,9},{9,1},{17,25},{25,17},{2,10},{10... | collective-permute-start | bytes 663560 | tf_op jit(solution)/shard_map/ppermute | solution.py:43
  11.6 5.4 %collective-permute-done = bf16[144,768]{1,0:T(8,128)(2,1)S(1)} collective-permute-done((bf16[144,768]{1,0:T(8,128)(2,1)S(1)}, bf16[144,768]{1,0:T(8,128)(2,1)S(1)}, u32[]{:S(2)}, u32[]{:S(2)}) %collective-permute-start) | collective-permute-done | bytes 221216 | tf_op jit(solution)/shard_map/ppermute | solution.py:43
  17.1 0.8 pad_maximum_fusion.2
  17.9 41.9 %all-gather.9.cloned.1.call-done = bf16[8,144,768]{2,1,0:T(8,128)(2,1)} async-done(((bf16[2,144,768]{2,1,0:T(8,128)(2,1)}), bf16[8,144,768]{2,1,0:T(8,128)(2,1)}) %all-gather.9.cloned.1.call-update) | async-done | bytes 1769488 | tf_op jit(solution)/shard_map/all_gather | solution.py:90
  59.9 2.4 %collective-permute-start.2 = (bf16[144,768]{1,0:T(8,128)(2,1)S(1)}, bf16[144,768]{1,0:T(8,128)(2,1)S(1)}, u32[]{:S(2)}, u32[]{:S(2)}) collective-permute-start(bf16[144,768]{1,0:T(8,128)(2,1)S(1)} %get-tuple-element.108), channel_id=1, source_target_pairs={{0,24},{8,16},{16,8},{24,0},{1,25},{9,17},{17,9},{25,1},{2,26},{10... | collective-permute-start | bytes 663560 | tf_op jit(solution)/shard_map/ppermute | solution.py:43
  62.3 0.6 collective-permute-start.1
  63.0 4.8 %collective-permute-done.2 = bf16[144,768]{1,0:T(8,128)(2,1)S(1)} collective-permute-done((bf16[144,768]{1,0:T(8,128)(2,1)S(1)}, bf16[144,768]{1,0:T(8,128)(2,1)S(1)}, u32[]{:S(2)}, u32[]{:S(2)}) %collective-permute-start.2) | collective-permute-done | bytes 221216 | tf_op jit(solution)/shard_map/ppermute | solution.py:43
  67.7 4.6 %collective-permute-done.1 = bf16[144,768]{1,0:T(8,128)(2,1)S(1)} collective-permute-done((bf16[144,768]{1,0:T(8,128)(2,1)S(1)}, bf16[144,768]{1,0:T(8,128)(2,1)S(1)}, u32[]{:S(2)}, u32[]{:S(2)}) %collective-permute-start.1) | collective-permute-done | bytes 221216 | tf_op jit(solution)/shard_map/ppermute | solution.py:43
  72.7 0.9 pad_maximum_fusion.1
  74.1 0.9 copy-done.3
  75.0 0.7 multiply_reduce_fusion
  75.8 2.2 %slice_bitcast_fusion.8 = (bf16[2,144,768]{2,1,0:T(8,128)(2,1)S(1)}, bf16[2,144,768]{2,1,0:T(8,128)(2,1)S(1)}, bf16[2,144,768]{2,1,0:T(8,128)(2,1)S(1)}, bf16[2,...) fusion(bf16[4,2,2,144,768]{4,3,2,1,0:T(8,128)(2,1)} %bitcast.191), kind=kLoop, calls=%fused_computation.172 | loop fusion | bytes 7077888 | tf_op jit(solution)/shard_map/squeeze | solution.py:100
  78.9 0.8 slice.228
  79.9 0.5 multiply_reduce_fusion.16
  80.8 0.7 slice-done
  81.5 0.6 multiply_add_fusion.15
  82.3 0.5 multiply_reduce_fusion.15
  82.8 0.4 multiply_add_fusion.14
  83.4 0.5 multiply_reduce_fusion.14
  83.9 0.4 multiply_add_fusion.13
  84.4 0.9 fusion.46
  85.5 1.7 %multiply_reduce_fusion.13 = (f32[512]{0:T(512)S(1)}, bf16[512,256]{0,1:T(8,128)(2,1)S(1)}) fusion(f32[256]{0:T(256)S(1)} %fusion.93, bf16[512,768]{1,0:T(8,128)(2,1)} %bitcast.224, bf16[256,768]{1,0:T(8,128)(2,1)} %bitcast.240), kind=kOutput, calls=%fused_computation.157 | convolution fusion | flops 201981440 | bytes 1444864 | tf_op jit(solution)/shard_map/dot_general | solution.py:22
  87.3 0.4 multiply_add_fusion.12
  87.9 0.8 slice.232
  89.2 0.5 multiply_reduce_fusion.12
  89.6 0.4 multiply_add_fusion.11
  90.3 0.5 multiply_reduce_fusion.11
  90.8 33.4 %all-gather.13.cloned.1.call-done = bf16[8,144,768]{2,1,0:T(8,128)(2,1)} async-done(((bf16[2,144,768]{2,1,0:T(8,128)(2,1)}), bf16[8,144,768]{2,1,0:T(8,128)(2,1)}) %all-gather.13.cloned.1.call-update) | async-done | bytes 1769488 | tf_op jit(solution)/shard_map/all_gather | solution.py:90
  125.4 0.4 copy-done.6
  125.8 0.5 multiply_reduce_fusion.10
  126.3 0.4 multiply_add_fusion.9
  126.9 0.5 multiply_reduce_fusion.9
  127.8 9.4 %all-gather.15.cloned.1.call-done = bf16[4,4,144,768]{3,2,1,0:T(8,128)(2,1)} async-done(((bf16[4,2,144,768]{3,2,1,0:T(8,128)(2,1)}), bf16[4,4,144,768]{3,2,1,0:T(8,128)(2,1)}) %all-gather.15.cloned.1.call-update) | async-done | bytes 3538960 | tf_op jit(solution)/shard_map/all_gather | solution.py:91
  137.2 2.2 %slice_bitcast_fusion = (bf16[2,144,768]{2,1,0:T(8,128)(2,1)S(1)}, bf16[2,144,768]{2,1,0:T(8,128)(2,1)S(1)}, bf16[2,144,768]{2,1,0:T(8,128)(2,1)S(1)}, bf16[2,14...) fusion(bf16[4,2,2,144,768]{4,3,2,1,0:T(8,128)(2,1)} %bitcast.192), kind=kLoop, calls=%fused_computation.164 | loop fusion | bytes 7077888 | tf_op jit(solution)/shard_map/squeeze | solution.py:100
  142.2 0.5 multiply_reduce_fusion.8
  142.6 0.4 multiply_add_fusion.7
  143.3 0.5 multiply_reduce_fusion.7
  144.4 0.5 multiply_reduce_fusion.6
  144.9 0.4 multiply_add_fusion.5
  145.5 0.5 multiply_reduce_fusion.5
  146.6 0.5 multiply_reduce_fusion.4
  147.7 0.5 multiply_reduce_fusion.3
  148.9 0.5 multiply_reduce_fusion.2
  150.0 0.5 multiply_reduce_fusion.1
  151.1 0.6 gather_fusion
  151.7 1.0 broadcast_select_fusion
  (146 shorter events, 12.9 us)
Async XLA Ops:
  6.5 53.3 %all-gather.9.cloned.1.call-start = ((), (), s32[]{:S(2)}) async-start(), calls=%async_computation | async-start | bytes 2211840 | tf_op jit(solution)/shard_map/all_gather | solution.py:90
  8.6 8.5 %collective-permute-start = (bf16[144,768]{1,0:T(8,128)(2,1)S(1)}, bf16[144,768]{1,0:T(8,128)(2,1)S(1)}, u32[]{:S(2)}, u32[]{:S(2)}) collective-permute-start(bf16[144,768]{1,0:T(8,128)(2,1)S(1)} %get-tuple-element.110), channel_id=1, source_target_pairs={{0,8},{8,0},{16,24},{24,16},{1,9},{9,1},{17,25},{25,17},{2,10},{10... | collective-permute-start | bytes 663560 | tf_op jit(solution)/shard_map/ppermute | solution.py:43
  17.9 57.9 %all-gather.11.cloned.1.call-start = ((), (), s32[]{:S(2)}) async-start(), calls=%async_computation.1 | async-start | bytes 5308416 | tf_op jit(solution)/shard_map/all_gather | solution.py:91
  59.8 64.4 %all-gather.13.cloned.1.call-start = ((), (), s32[]{:S(2)}) async-start(), calls=%async_computation.2 | async-start | bytes 2211840 | tf_op jit(solution)/shard_map/all_gather | solution.py:90
  59.9 7.9 %collective-permute-start.2 = (bf16[144,768]{1,0:T(8,128)(2,1)S(1)}, bf16[144,768]{1,0:T(8,128)(2,1)S(1)}, u32[]{:S(2)}, u32[]{:S(2)}) collective-permute-start(bf16[144,768]{1,0:T(8,128)(2,1)S(1)} %get-tuple-element.108), channel_id=1, source_target_pairs={{0,24},{8,16},{16,8},{24,0},{1,25},{9,17},{17,9},{25,1},{2,26},{10... | collective-permute-start | bytes 663560 | tf_op jit(solution)/shard_map/ppermute | solution.py:43
  62.3 10.1 %collective-permute-start.1 = (bf16[144,768]{1,0:T(8,128)(2,1)S(1)}, bf16[144,768]{1,0:T(8,128)(2,1)S(1)}, u32[]{:S(2)}, u32[]{:S(2)}) collective-permute-start(bf16[144,768]{1,0:T(8,128)(2,1)S(1)} %get-tuple-element.109), channel_id=1, source_target_pairs={{0,16},{8,24},{16,0},{24,8},{1,17},{9,25},{17,1},{25,9},{2,18},{10... | collective-permute-start | bytes 663560 | tf_op jit(solution)/shard_map/ppermute | solution.py:43
  72.5 1.4 copy-start
  74.1 0.9 copy-start.3
  78.4 1.4 copy-start.4
  80.3 1.1 slice-start
  85.3 51.9 %all-gather.15.cloned.1.call-start = ((), (), s32[]{:S(2)}) async-start(), calls=%async_computation.3 | async-start | bytes 5308416 | tf_op jit(solution)/shard_map/all_gather | solution.py:91
  85.5 1.8 %copy-start.1 = (bf16[2,128,768]{2,1,0:T(8,128)(2,1)S(1)}, bf16[2,128,768]{2,1,0:T(8,128)(2,1)}, u32[]{:S(2)}) copy-start(bf16[2,128,768]{2,1,0:T(8,128)(2,1)} %slice.228) | copy-start | bytes 1179652
  87.9 1.3 copy-start.5
  90.3 33.9 %copy-start.2 = (bf16[2,128,768]{2,1,0:T(8,128)(2,1)S(1)}, bf16[2,128,768]{2,1,0:T(8,128)(2,1)}, u32[]{:S(2)}) copy-start(bf16[2,128,768]{2,1,0:T(8,128)(2,1)} %slice.232) | copy-start | bytes 1179652
  124.7 1.1 copy-start.6
Sparse Core Ops, SparseCore 0:
  18.0 41.7 all-gather.8
  61.3 11.5 all-gather.10
  85.4 38.7 all-gather.12
  125.6 11.5 all-gather.14

commit v11 on v8

--- a/solution.py
+++ b/solution.py
@@ -91,7 +91,6 @@
     swapped = lax.ppermute(mine, "core", swap)
     acc = add_pair(acc, swapped, times_listed(chip, other_core))
     for step in range(1, chips):
-        acc, received = lax.optimization_barrier((acc, received))
         from_below, from_above = received
         if step + 2 < chips:
             received = (lax.ppermute(from_below, "chip", up), lax.ppermute(from_above, "chip", down))

time: 99.3 us -> 96.6 us (0.973)
  starting transfers between devices: 16.9 us -> 19.5 us
  other arithmetic: 10.2 us -> 7.61 us
  waiting for transfers between devices: 52.1 us -> 49.8 us
    ppermute x1, waiting for transfers between devices: 9.87 us -> 1.1 us  [per_device(): lax.ppermute(mine, 'chip', up)]
    ppermute x1, waiting for transfers between devices: 4.06 us -> 12.8 us  [per_device(): lax.ppermute(mine, 'chip', down)]
    ppermute x1, waiting for transfers between devices: 4.16 us -> 0.01 us  [per_device(): lax.ppermute(from_above, 'chip', down)]
    ppermute x1, waiting for transfers between devices: 9.83 us -> 13.1 us  [per_device(): lax.ppermute(from_below, 'chip', up)]
    convert_element_type x2, other arithmetic: 2.19 us -> 0.42 us  [normalize(): (values * lax.rsqrt(jnp.sum(values * values, axis=-1, keepdims=True) + EP...]
    ppermute x1, starting transfers between devices: 3.47 us -> 5.05 us  [per_device(): lax.ppermute(from_below, 'chip', up)]
    dot_general x12, matrix products: 10.1 us -> 8.67 us  [weigh(): scores = jnp.dot(unit_a, unit_b.T, preferred_element_type=jnp.float32)]
    ppermute x1, starting transfers between devices: 3.52 us -> 4.6 us  [per_device(): lax.ppermute(mine, 'chip', up)]
  transfers between devices with their start and end apart: 14 -> 14, of which waited for: 9 -> 6; matrix products, arithmetic and copies ran while one was open for 22% -> 17% of each run, Pallas kernels for 0% -> 0%
where the time goes in v11:
time: 96.6 us; the launch traced here: 95.9 us
  waiting for transfers between devices  49.8 us (52%)
  starting transfers between devices  19.5 us (20%)
  matrix products  17.3 us (18%)
  other arithmetic  7.61 us (8%)
    ppermute x1, waiting for transfers between devices, per_device(): last = lax.ppermute(outgoing, 'chip', ends)  13.2 us
    ppermute x1, waiting for transfers between devices, per_device(): lax.ppermute(from_below, 'chip', up)  13.1 us
    ppermute x1, waiting for transfers between devices, per_device(): lax.ppermute(mine, 'chip', down)  12.8 us
    ppermute x3, waiting for transfers between devices, per_device(): lax.ppermute(outgoing, 'bucket', [(i, i ^ m) for i in range(buckets)])  9.57 us
    dot_general x12, matrix products, weigh(): scores = jnp.dot(unit_a, unit_b.T, preferred_element_type=jnp.float32)  8.67 us
    dot_general x11, matrix products, pair_terms(): jnp.dot(weights.astype(jnp.bfloat16), got_data, preferred_element_type=jn...  8.01 us
    ppermute x1, starting transfers between devices, per_device(): lax.ppermute(from_below, 'chip', up)  5.05 us
    ppermute x1, starting transfers between devices, per_device(): lax.ppermute(mine, 'chip', up)  4.6 us
  transfers between devices with their start and end apart: 14, of which 6 were waited for; matrix products, arithmetic and copies ran while one was open for 17% of the time, Pallas kernels for 0%

profile of v11, /device:TPU:0, one launch (start us, length us, event | category | flops | bytes accessed | tf_op | source)
XLA Modules:
  0.0 95.9 jit_solution(12978203122115576138)
XLA Ops:
  0.0 0.7 convert_bitcast_fusion.12
  0.8 1.2 %fusion.51 = bf16[4,144,768]{2,1,0:T(8,128)(2,1)S(1)} fusion(bf16[4,1,1]{2,1,0:T(2,128)(2,1)S(1)} %copy.5, bf16[4,128,768]{2,1,0:T(8,128)(2,1)} %bitcast.139), kind=kLoop, calls=%fused_computation.105 | loop fusion | flops 2654208 | bytes 1671176 | tf_op jit(solution)/shard_map/concatenate | solution.py:39
  2.0 3.0 %collective-permute-start = (bf16[144,768]{1,0:T(8,128)(2,1)S(1)}, bf16[144,768]{1,0:T(8,128)(2,1)S(1)}, u32[]{:S(2)}, u32[]{:S(2)}) collective-permute-start(bf16[144,768]{1,0:T(8,128)(2,1)S(1)} %get-tuple-element.34), channel_id=1, source_target_pairs={{0,8},{8,0},{16,24},{24,16},{1,9},{9,1},{17,25},{25,17},{2,10},{10... | collective-permute-start | bytes 663560 | tf_op jit(solution)/shard_map/ppermute | solution.py:43
  5.1 1.5 %collective-permute-start.1 = (bf16[144,768]{1,0:T(8,128)(2,1)S(1)}, bf16[144,768]{1,0:T(8,128)(2,1)S(1)}, u32[]{:S(2)}, u32[]{:S(2)}) collective-permute-start(bf16[144,768]{1,0:T(8,128)(2,1)S(1)} %get-tuple-element.33), channel_id=1, source_target_pairs={{0,16},{8,24},{16,0},{24,8},{1,17},{9,25},{17,1},{25,9},{2,18},{10... | collective-permute-start | bytes 663560 | tf_op jit(solution)/shard_map/ppermute | solution.py:43
  7.1 4.2 %collective-permute-done = bf16[144,768]{1,0:T(8,128)(2,1)S(1)} collective-permute-done((bf16[144,768]{1,0:T(8,128)(2,1)S(1)}, bf16[144,768]{1,0:T(8,128)(2,1)S(1)}, u32[]{:S(2)}, u32[]{:S(2)}) %collective-permute-start) | collective-permute-done | bytes 221216 | tf_op jit(solution)/shard_map/ppermute | solution.py:43
  11.4 5.3 %collective-permute-done.1 = bf16[144,768]{1,0:T(8,128)(2,1)S(1)} collective-permute-done((bf16[144,768]{1,0:T(8,128)(2,1)S(1)}, bf16[144,768]{1,0:T(8,128)(2,1)S(1)}, u32[]{:S(2)}, u32[]{:S(2)}) %collective-permute-start.1) | collective-permute-done | bytes 221216 | tf_op jit(solution)/shard_map/ppermute | solution.py:43
  16.9 0.2 fusion.2
  17.5 1.3 %collective-permute-start.5 = (bf16[528,768]{1,0:T(8,128)(2,1)S(1)}, bf16[528,768]{1,0:T(8,128)(2,1)S(1)}, u32[]{:S(2)}, u32[]{:S(2)}) collective-permute-start(bf16[528,768]{1,0:T(8,128)(2,1)S(1)} %fusion.52), channel_id=1, source_target_pairs={{2,0},{4,2},{6,4},{3,1},{5,3},{7,5},{10,8},{12,10},{14,12},{11,9},... | collective-permute-start | bytes 2433032 | tf_op jit(solution)/shard_map/ppermute | solution.py:90
  18.8 4.6 %collective-permute-start.4 = (bf16[528,768]{1,0:T(8,128)(2,1)S(1)}, bf16[528,768]{1,0:T(8,128)(2,1)S(1)}, u32[]{:S(2)}, u32[]{:S(2)}) collective-permute-start(bf16[528,768]{1,0:T(8,128)(2,1)S(1)} %fusion.52), channel_id=1, source_target_pairs={{0,2},{2,4},{4,6},{1,3},{3,5},{5,7},{8,10},{10,12},{12,14},{9,11},... | collective-permute-start | bytes 2433032 | tf_op jit(solution)/shard_map/ppermute | solution.py:90
  23.7 0.7 multiply_reduce_fusion.11
  24.7 0.6 fusion.118
  25.3 12.8 %collective-permute-done.5 = bf16[528,768]{1,0:T(8,128)(2,1)S(1)} collective-permute-done((bf16[528,768]{1,0:T(8,128)(2,1)S(1)}, bf16[528,768]{1,0:T(8,128)(2,1)S(1)}, u32[]{:S(2)}, u32[]{:S(2)}) %collective-permute-start.5) | collective-permute-done | bytes 811040 | tf_op jit(solution)/shard_map/ppermute | solution.py:90
  38.2 1.1 %collective-permute-done.4 = bf16[528,768]{1,0:T(8,128)(2,1)S(1)} collective-permute-done((bf16[528,768]{1,0:T(8,128)(2,1)S(1)}, bf16[528,768]{1,0:T(8,128)(2,1)S(1)}, u32[]{:S(2)}, u32[]{:S(2)}) %collective-permute-start.4) | collective-permute-done | bytes 811040 | tf_op jit(solution)/shard_map/ppermute | solution.py:90
  39.6 0.2 fusion.4
  39.9 1.3 %collective-permute-start.9 = (bf16[528,768]{1,0:T(8,128)(2,1)S(1)}, bf16[528,768]{1,0:T(8,128)(2,1)S(1)}, u32[]{:S(2)}, u32[]{:S(2)}) collective-permute-start(bf16[528,768]{1,0:T(8,128)(2,1)S(1)} %collective-permute-done.5), channel_id=1, source_target_pairs={{2,0},{4,2},{6,4},{3,1},{5,3},{7,5},{10,8},{12,10},{14,12},{11,9},... | collective-permute-start | bytes 2433032 | tf_op jit(solution)/shard_map/ppermute | solution.py:96
  41.3 0.5 collective-permute-start.7
  41.8 5.1 %collective-permute-start.8 = (bf16[528,768]{1,0:T(8,128)(2,1)S(1)}, bf16[528,768]{1,0:T(8,128)(2,1)S(1)}, u32[]{:S(2)}, u32[]{:S(2)}) collective-permute-start(bf16[528,768]{1,0:T(8,128)(2,1)S(1)} %collective-permute-done.4), channel_id=1, source_target_pairs={{0,2},{2,4},{4,6},{1,3},{3,5},{5,7},{8,10},{10,12},{12,14},{9,11},... | collective-permute-start | bytes 2433032 | tf_op jit(solution)/shard_map/ppermute | solution.py:96
  46.9 0.7 multiply_reduce_fusion.10
  47.6 0.6 fusion.105
  48.2 0.7 multiply_reduce_fusion.9
  48.9 0.6 fusion.102
  49.5 0.2 fusion.8
  49.7 0.7 multiply_reduce_fusion.8
  50.5 0.6 fusion.99
  51.2 13.1 %collective-permute-done.8 = bf16[528,768]{1,0:T(8,128)(2,1)S(1)} collective-permute-done((bf16[528,768]{1,0:T(8,128)(2,1)S(1)}, bf16[528,768]{1,0:T(8,128)(2,1)S(1)}, u32[]{:S(2)}, u32[]{:S(2)}) %collective-permute-start.8) | collective-permute-done | bytes 811040 | tf_op jit(solution)/shard_map/ppermute | solution.py:96
  64.9 0.2 fusion.14
  65.2 0.2 fusion.16
  65.6 1.5 %collective-permute-start.12 = (bf16[528,768]{1,0:T(8,128)(2,1)S(1)}, bf16[528,768]{1,0:T(8,128)(2,1)S(1)}, u32[]{:S(2)}, u32[]{:S(2)}) collective-permute-start(bf16[528,768]{1,0:T(8,128)(2,1)S(1)} %broadcast_select_fusion), channel_id=1, source_target_pairs={{4,6},{2,0},{5,7},{3,1},{12,14},{10,8},{13,15},{11,9},{20,22},{18,... | collective-permute-start | bytes 2433032 | tf_op jit(solution)/shard_map/ppermute | solution.py:100
  67.2 0.5 collective-permute-start.10
  67.7 0.7 multiply_reduce_fusion.7
  68.4 0.6 fusion.96
  69.0 0.7 multiply_reduce_fusion.6
  69.7 0.6 fusion.93
  70.3 0.7 multiply_reduce_fusion.5
  71.0 0.7 multiply_reduce_fusion.4
  71.8 0.6 fusion.90
  72.3 0.6 fusion.87
  73.6 13.2 %collective-permute-done.12 = bf16[528,768]{1,0:T(8,128)(2,1)S(1)} collective-permute-done((bf16[528,768]{1,0:T(8,128)(2,1)S(1)}, bf16[528,768]{1,0:T(8,128)(2,1)S(1)}, u32[]{:S(2)}, u32[]{:S(2)}) %collective-permute-start.12) | collective-permute-done | bytes 811040 | tf_op jit(solution)/shard_map/ppermute | solution.py:100
  87.2 0.7 multiply_reduce_fusion.2
  87.9 0.7 multiply_reduce_fusion.3
  88.6 0.7 multiply_reduce_fusion.1
  89.3 0.6 fusion.84
  89.9 0.6 fusion.79
  90.9 0.7 multiply_reduce_fusion
  91.6 0.6 fusion.76
  92.2 2.0 %multiply_convert_fusion = bf16[512,768]{1,0:T(8,128)(2,1)S(1)} fusion(f32[512,768]{1,0:T(8,128)S(1)} %fusion.76, f32[512,768]{1,0:T(8,128)S(1)} %fusion.79, f32[512,768]{1,0:T(8,128)S(1)} %fusion.84, f32[512,768]{1,0:T(8,128)S(1)} %fusion.87, f32[512,768]{1,0:T(8,128)S(1)} %fusion.90, f32[512,768]{1,0:T(8,128)S(1)} %fusion.93, f32[512,768]{1,0:T(8,128)S(1)} %fusion.96, ...), kind=kOutput, calls=%fused_computation.53 | convolution fusion | flops 412483584 | bytes 19402796 | tf_op jit(solution)/shard_map/dot_general | solution.py:77
  94.3 0.6 gather_fusion
  94.9 1.0 %broadcast_select_fusion.1 = bf16[1,1,512,768]{3,2,1,0:T(8,128)(2,1)} fusion(bf16[1,1,512,768]{3,2,1,0:T(8,128)(2,1)S(1)} %bitcast.131, pred[512]{0:T(512)(128)(4,1)S(1)} %broadcast_bitcast_fusion), kind=kLoop, calls=%fused_computation.120 | loop fusion | flops 393216 | bytes 1573376 | tf_op jit(solution)/shard_map/jit(_take)/select_n | solution.py:120
  (70 shorter events, 4.2 us)
Async XLA Ops:
  2.0 9.3 %collective-permute-start = (bf16[144,768]{1,0:T(8,128)(2,1)S(1)}, bf16[144,768]{1,0:T(8,128)(2,1)S(1)}, u32[]{:S(2)}, u32[]{:S(2)}) collective-permute-start(bf16[144,768]{1,0:T(8,128)(2,1)S(1)} %get-tuple-element.34), channel_id=1, source_target_pairs={{0,8},{8,0},{16,24},{24,16},{1,9},{9,1},{17,25},{25,17},{2,10},{10... | collective-permute-start | bytes 663560 | tf_op jit(solution)/shard_map/ppermute | solution.py:43
  5.1 11.6 %collective-permute-start.1 = (bf16[144,768]{1,0:T(8,128)(2,1)S(1)}, bf16[144,768]{1,0:T(8,128)(2,1)S(1)}, u32[]{:S(2)}, u32[]{:S(2)}) collective-permute-start(bf16[144,768]{1,0:T(8,128)(2,1)S(1)} %get-tuple-element.33), channel_id=1, source_target_pairs={{0,16},{8,24},{16,0},{24,8},{1,17},{9,25},{17,1},{25,9},{2,18},{10... | collective-permute-start | bytes 663560 | tf_op jit(solution)/shard_map/ppermute | solution.py:43
  6.6 10.1 %collective-permute-start.2 = (bf16[144,768]{1,0:T(8,128)(2,1)S(1)}, bf16[144,768]{1,0:T(8,128)(2,1)S(1)}, u32[]{:S(2)}, u32[]{:S(2)}) collective-permute-start(bf16[144,768]{1,0:T(8,128)(2,1)S(1)} %get-tuple-element.32), channel_id=1, source_target_pairs={{0,24},{8,16},{16,8},{24,0},{1,25},{9,17},{17,9},{25,1},{2,26},{10... | collective-permute-start | bytes 663560 | tf_op jit(solution)/shard_map/ppermute | solution.py:43
  17.5 20.6 %collective-permute-start.5 = (bf16[528,768]{1,0:T(8,128)(2,1)S(1)}, bf16[528,768]{1,0:T(8,128)(2,1)S(1)}, u32[]{:S(2)}, u32[]{:S(2)}) collective-permute-start(bf16[528,768]{1,0:T(8,128)(2,1)S(1)} %fusion.52), channel_id=1, source_target_pairs={{2,0},{4,2},{6,4},{3,1},{5,3},{7,5},{10,8},{12,10},{14,12},{11,9},... | collective-permute-start | bytes 2433032 | tf_op jit(solution)/shard_map/ppermute | solution.py:90
  18.8 20.5 %collective-permute-start.4 = (bf16[528,768]{1,0:T(8,128)(2,1)S(1)}, bf16[528,768]{1,0:T(8,128)(2,1)S(1)}, u32[]{:S(2)}, u32[]{:S(2)}) collective-permute-start(bf16[528,768]{1,0:T(8,128)(2,1)S(1)} %fusion.52), channel_id=1, source_target_pairs={{0,2},{2,4},{4,6},{1,3},{3,5},{5,7},{8,10},{10,12},{12,14},{9,11},... | collective-permute-start | bytes 2433032 | tf_op jit(solution)/shard_map/ppermute | solution.py:90
  23.4 16.2 %collective-permute-start.3 = (bf16[528,768]{1,0:T(8,128)(2,1)S(1)}, bf16[528,768]{1,0:T(8,128)(2,1)S(1)}, u32[]{:S(2)}, u32[]{:S(2)}) collective-permute-start(bf16[528,768]{1,0:T(8,128)(2,1)S(1)} %fusion.52), channel_id=1, source_target_pairs={{0,1},{1,0},{2,3},{3,2},{4,5},{5,4},{6,7},{7,6},{8,9},{9,8},{10,11... | collective-permute-start | bytes 2433032 | tf_op jit(solution)/shard_map/ppermute | solution.py:91
  39.9 25.2 %collective-permute-start.9 = (bf16[528,768]{1,0:T(8,128)(2,1)S(1)}, bf16[528,768]{1,0:T(8,128)(2,1)S(1)}, u32[]{:S(2)}, u32[]{:S(2)}) collective-permute-start(bf16[528,768]{1,0:T(8,128)(2,1)S(1)} %collective-permute-done.5), channel_id=1, source_target_pairs={{2,0},{4,2},{6,4},{3,1},{5,3},{7,5},{10,8},{12,10},{14,12},{11,9},... | collective-permute-start | bytes 2433032 | tf_op jit(solution)/shard_map/ppermute | solution.py:96
  41.2 9.9 %collective-permute-start.6 = (bf16[528,768]{1,0:T(8,128)(2,1)S(1)}, bf16[528,768]{1,0:T(8,128)(2,1)S(1)}, u32[]{:S(2)}, u32[]{:S(2)}) collective-permute-start(bf16[528,768]{1,0:T(8,128)(2,1)S(1)} %collective-permute-done.4), channel_id=1, source_target_pairs={{0,1},{1,0},{2,3},{3,2},{4,5},{5,4},{6,7},{7,6},{8,9},{9,8},{10,11... | collective-permute-start | bytes 2433032 | tf_op jit(solution)/shard_map/ppermute | solution.py:110
  41.3 9.9 %collective-permute-start.7 = (bf16[528,768]{1,0:T(8,128)(2,1)S(1)}, bf16[528,768]{1,0:T(8,128)(2,1)S(1)}, u32[]{:S(2)}, u32[]{:S(2)}) collective-permute-start(bf16[528,768]{1,0:T(8,128)(2,1)S(1)} %collective-permute-done.5), channel_id=1, source_target_pairs={{0,1},{1,0},{2,3},{3,2},{4,5},{5,4},{6,7},{7,6},{8,9},{9,8},{10,11... | collective-permute-start | bytes 2433032 | tf_op jit(solution)/shard_map/ppermute | solution.py:111
  41.8 22.6 %collective-permute-start.8 = (bf16[528,768]{1,0:T(8,128)(2,1)S(1)}, bf16[528,768]{1,0:T(8,128)(2,1)S(1)}, u32[]{:S(2)}, u32[]{:S(2)}) collective-permute-start(bf16[528,768]{1,0:T(8,128)(2,1)S(1)} %collective-permute-done.4), channel_id=1, source_target_pairs={{0,2},{2,4},{4,6},{1,3},{3,5},{5,7},{8,10},{10,12},{12,14},{9,11},... | collective-permute-start | bytes 2433032 | tf_op jit(solution)/shard_map/ppermute | solution.py:96
  65.6 21.2 %collective-permute-start.12 = (bf16[528,768]{1,0:T(8,128)(2,1)S(1)}, bf16[528,768]{1,0:T(8,128)(2,1)S(1)}, u32[]{:S(2)}, u32[]{:S(2)}) collective-permute-start(bf16[528,768]{1,0:T(8,128)(2,1)S(1)} %broadcast_select_fusion), channel_id=1, source_target_pairs={{4,6},{2,0},{5,7},{3,1},{12,14},{10,8},{13,15},{11,9},{20,22},{18,... | collective-permute-start | bytes 2433032 | tf_op jit(solution)/shard_map/ppermute | solution.py:100
  67.1 5.9 %collective-permute-start.11 = (bf16[528,768]{1,0:T(8,128)(2,1)S(1)}, bf16[528,768]{1,0:T(8,128)(2,1)S(1)}, u32[]{:S(2)}, u32[]{:S(2)}) collective-permute-start(bf16[528,768]{1,0:T(8,128)(2,1)S(1)} %collective-permute-done.9), channel_id=1, source_target_pairs={{0,1},{1,0},{2,3},{3,2},{4,5},{5,4},{6,7},{7,6},{8,9},{9,8},{10,11... | collective-permute-start | bytes 2433032 | tf_op jit(solution)/shard_map/ppermute | solution.py:111
  67.2 6.1 %collective-permute-start.10 = (bf16[528,768]{1,0:T(8,128)(2,1)S(1)}, bf16[528,768]{1,0:T(8,128)(2,1)S(1)}, u32[]{:S(2)}, u32[]{:S(2)}) collective-permute-start(bf16[528,768]{1,0:T(8,128)(2,1)S(1)} %collective-permute-done.8), channel_id=1, source_target_pairs={{0,1},{1,0},{2,3},{3,2},{4,5},{5,4},{6,7},{7,6},{8,9},{9,8},{10,11... | collective-permute-start | bytes 2433032 | tf_op jit(solution)/shard_map/ppermute | solution.py:110
  87.1 3.4 %collective-permute-start.13 = (bf16[528,768]{1,0:T(8,128)(2,1)S(1)}, bf16[528,768]{1,0:T(8,128)(2,1)S(1)}, u32[]{:S(2)}, u32[]{:S(2)}) collective-permute-start(bf16[528,768]{1,0:T(8,128)(2,1)S(1)} %collective-permute-done.12), channel_id=1, source_target_pairs={{0,1},{1,0},{2,3},{3,2},{4,5},{5,4},{6,7},{7,6},{8,9},{9,8},{10,11... | collective-permute-start | bytes 2433032 | tf_op jit(solution)/shard_map/ppermute | solution.py:106

commit v12 on v11

--- a/solution.py
+++ b/solution.py
@@ -8,6 +8,7 @@
 
 EPS = 1e-06
 TEMP = 12.0
+DEAD = 1000.0
 CORES = 2
 
 
@@ -23,10 +24,8 @@
     return jnp.exp(TEMP * scores) * live_b[None, :] * extra
 
 
-def live_of(block_counts, slot_rows):
-    sources = block_counts.shape[0]
-    slot_index = lax.broadcasted_iota(jnp.int32, (sources, slot_rows), 1)
-    return (slot_index < block_counts.reshape(sources, 1)).astype(jnp.float32).reshape(-1)
+def live_of(block):
+    return (block[:, 0] < DEAD / 2).astype(jnp.float32)
 
 
 def per_device(embeddings, counts):
@@ -34,19 +33,19 @@
     bucket = lax.axis_index("bucket")
     slot_rows = embeddings.shape[3]
     width = embeddings.shape[4]
-    count_rows = jnp.zeros(embeddings.shape[2:3] + (16, width), jnp.bfloat16)
-    count_rows = count_rows.at[:, 0, 0].set(counts[0, 0, :, 0].astype(jnp.bfloat16))
-    packed = jnp.concatenate([embeddings[0, 0], count_rows], axis=1)
-    arrived = [lax.dynamic_index_in_dim(packed, bucket, axis=0, keepdims=False)]
+    pieces = embeddings[0, 0]
+    slot_index = lax.broadcasted_iota(jnp.int32, pieces.shape, 1)
+    lane_index = lax.broadcasted_iota(jnp.int32, pieces.shape, 2)
+    dead = (slot_index >= counts[0, 0, :, :, None]) & (lane_index == 0)
+    marked = jnp.where(dead, jnp.bfloat16(DEAD), pieces)
+    arrived = [lax.dynamic_index_in_dim(marked, bucket, axis=0, keepdims=False)]
     for m in range(1, buckets):
-        outgoing = lax.dynamic_index_in_dim(packed, bucket ^ m, axis=0, keepdims=False)
+        outgoing = lax.dynamic_index_in_dim(marked, bucket ^ m, axis=0, keepdims=False)
         arrived.append(lax.ppermute(outgoing, "bucket", [(i, i ^ m) for i in range(buckets)]))
-    slabs = jnp.stack(arrived)
-    sources = slabs.shape[0]
+    sources = buckets
     rows = sources * slot_rows
-    data = slabs[:, :slot_rows].reshape(rows, width)
-    own_counts = slabs[:, slot_rows, 0].astype(jnp.int32)
-    live = live_of(own_counts, slot_rows)
+    data = jnp.concatenate(arrived, axis=0)
+    live = live_of(data)
     chips = lax.axis_size("chip")
     cores = lax.axis_size("core")
     blocks = chips * cores
@@ -71,10 +70,8 @@
 
     def pair_terms(acc, got, weight):
         summed, squares = acc
-        got_data = got[:rows]
-        got_counts = got[rows, :sources].astype(jnp.int32)
-        weights = weigh(unit, normalize(got_data), live_of(got_counts, slot_rows), 1.0)
-        part = jnp.dot(weights.astype(jnp.bfloat16), got_data, preferred_element_type=jnp.float32)
+        weights = weigh(unit, normalize(got), live_of(got), 1.0)
+        part = jnp.dot(weights.astype(jnp.bfloat16), got, preferred_element_type=jnp.float32)
         return (summed + weight * part, squares + weight * jnp.sum(weights * weights, axis=1))
 
     def add_pair(acc, got, weight):
@@ -84,8 +81,7 @@
     up = [(c, c + 1) for c in range(chips - 1)]
     down = [(c + 1, c) for c in range(chips - 1)]
     acc = (summed, squares)
-    tail = jnp.zeros((16, width), jnp.bfloat16).at[0, :sources].set(own_counts.astype(jnp.bfloat16))
-    mine = jnp.concatenate([data, tail], axis=0)
+    mine = data
     other_core = (core + 1) % cores
     received = (lax.ppermute(mine, "chip", up), lax.ppermute(mine, "chip", down))
     swapped = lax.ppermute(mine, "core", swap)

time: 96.6 us -> 90.3 us (0.935)
  waiting for transfers between devices: 49.8 us -> 44.2 us
  matrix products: 17.3 us -> 18.4 us
    ppermute x1, waiting for transfers between devices: 13.1 us -> 11.2 us  [per_device(): lax.ppermute(from_below, 'chip', up)]
    select_n x0 -> x1, other arithmetic: none -> 1.5 us  [per_device(): marked = jnp.where(dead, jnp.bfloat16(DEAD), pieces)]
    ppermute x1, waiting for transfers between devices: 13.2 us -> 11.9 us  [per_device(): last = lax.ppermute(outgoing, 'chip', ends)]
    concatenate x2 -> x0, other arithmetic: 1.25 us -> none  [the longest x1 1.19 us: per_device(): packed = jnp.concatenate([embeddings[0, 0], count_rows], axis=1)]
    ppermute x1, waiting for transfers between devices: 1.1 us -> 0.01 us  [per_device(): lax.ppermute(mine, 'chip', up)]
    dot_general x12, matrix products: 8.67 us -> 9.73 us  [weigh(): scores = jnp.dot(unit_a, unit_b.T, preferred_element_type=jnp.float32)]
    ppermute x3, waiting for transfers between devices: 9.57 us -> 8.51 us  [per_device(): lax.ppermute(outgoing, 'bucket', [(i, i ^ m) for i in range(buckets)])]
    convert_element_type x28 -> x12, other arithmetic: 2.28 us -> 1.44 us  [live_of(): return (block[:, 0] < DEAD / 2).astype(jnp.float32)]
  transfers between devices with their start and end apart: 14 -> 14, of which waited for: 6 -> 5; matrix products, arithmetic and copies ran while one was open for 17% -> 20% of each run, Pallas kernels for 0% -> 0%
where the time goes in v12:
time: 90.3 us; the launch traced here: 90.1 us
  waiting for transfers between devices  44.2 us (49%)
  starting transfers between devices  19.1 us (21%)
  matrix products  18.4 us (20%)
  other arithmetic  6.9 us (8%)
    ppermute x1, waiting for transfers between devices, per_device(): lax.ppermute(mine, 'chip', down)  12.6 us
    ppermute x1, waiting for transfers between devices, per_device(): last = lax.ppermute(outgoing, 'chip', ends)  11.9 us
    ppermute x1, waiting for transfers between devices, per_device(): lax.ppermute(from_below, 'chip', up)  11.2 us
    dot_general x12, matrix products, weigh(): scores = jnp.dot(unit_a, unit_b.T, preferred_element_type=jnp.float32)  9.73 us
    ppermute x3, waiting for transfers between devices, per_device(): lax.ppermute(outgoing, 'bucket', [(i, i ^ m) for i in range(buckets)])  8.51 us
    dot_general x11, matrix products, pair_terms(): jnp.dot(weights.astype(jnp.bfloat16), got, preferred_element_type=jnp.flo...  8.04 us
    ppermute x1, starting transfers between devices, per_device(): lax.ppermute(mine, 'chip', up)  4.6 us
    ppermute x1, starting transfers between devices, per_device(): lax.ppermute(from_below, 'chip', up)  4.58 us
  transfers between devices with their start and end apart: 14, of which 5 were waited for; matrix products, arithmetic and copies ran while one was open for 20% of the time, Pallas kernels for 0%

profile of v12, /device:TPU:0, one launch (start us, length us, event | category | flops | bytes accessed | tf_op | source)
XLA Modules:
  0.0 90.1 jit_solution(11359599506380721922)
XLA Ops:
  0.0 1.5 %fusion.25 = bf16[4,128,768]{2,1,0:T(8,128)(2,1)S(1)} fusion(bf16[1,1,4,128,768]{4,3,2,1,0:T(8,128)(2,1)} %param.2, s32[4]{0:T(128)} %bitcast.43, pred[768]{0:T(1024)(128)(4,1)S(1)} %iota_compare_fusion.2), kind=kLoop, calls=%fused_computation.52 | loop fusion | flops 1179648 | bytes 1573648 | tf_op jit(solution)/shard_map/jit(_where)/select_n | solution.py:40
  1.6 3.0 %collective-permute-start = (bf16[128,768]{1,0:T(8,128)(2,1)S(1)}, bf16[128,768]{1,0:T(8,128)(2,1)S(1)}, u32[]{:S(2)}, u32[]{:S(2)}) collective-permute-start(bf16[128,768]{1,0:T(8,128)(2,1)S(1)} %get-tuple-element.10), channel_id=1, source_target_pairs={{0,8},{8,0},{16,24},{24,16},{1,9},{9,1},{17,25},{25,17},{2,10},{10... | collective-permute-start | bytes 589832 | tf_op jit(solution)/shard_map/ppermute | solution.py:44
  4.6 1.5 %collective-permute-start.1 = (bf16[128,768]{1,0:T(8,128)(2,1)S(1)}, bf16[128,768]{1,0:T(8,128)(2,1)S(1)}, u32[]{:S(2)}, u32[]{:S(2)}) collective-permute-start(bf16[128,768]{1,0:T(8,128)(2,1)S(1)} %get-tuple-element.9), channel_id=1, source_target_pairs={{0,16},{8,24},{16,0},{24,8},{1,17},{9,25},{17,1},{25,9},{2,18},{10... | collective-permute-start | bytes 589832 | tf_op jit(solution)/shard_map/ppermute | solution.py:44
  6.7 3.7 %collective-permute-done = bf16[128,768]{1,0:T(8,128)(2,1)S(1)} collective-permute-done((bf16[128,768]{1,0:T(8,128)(2,1)S(1)}, bf16[128,768]{1,0:T(8,128)(2,1)S(1)}, u32[]{:S(2)}, u32[]{:S(2)}) %collective-permute-start) | collective-permute-done | bytes 196640 | tf_op jit(solution)/shard_map/ppermute | solution.py:44
  10.4 4.8 %collective-permute-done.1 = bf16[128,768]{1,0:T(8,128)(2,1)S(1)} collective-permute-done((bf16[128,768]{1,0:T(8,128)(2,1)S(1)}, bf16[128,768]{1,0:T(8,128)(2,1)S(1)}, u32[]{:S(2)}, u32[]{:S(2)}) %collective-permute-start.1) | collective-permute-done | bytes 196640 | tf_op jit(solution)/shard_map/ppermute | solution.py:44
  15.4 1.3 %collective-permute-start.5 = (bf16[512,768]{1,0:T(8,128)(2,1)S(1)}, bf16[512,768]{1,0:T(8,128)(2,1)S(1)}, u32[]{:S(2)}, u32[]{:S(2)}) collective-permute-start(bf16[512,768]{1,0:T(8,128)(2,1)S(1)} %get-tuple-element.6), channel_id=1, source_target_pairs={{2,0},{4,2},{6,4},{3,1},{5,3},{7,5},{10,8},{12,10},{14,12},{11,9},... | collective-permute-start | bytes 2359304 | tf_op jit(solution)/shard_map/ppermute | solution.py:86
  16.7 4.6 %collective-permute-start.4 = (bf16[512,768]{1,0:T(8,128)(2,1)S(1)}, bf16[512,768]{1,0:T(8,128)(2,1)S(1)}, u32[]{:S(2)}, u32[]{:S(2)}) collective-permute-start(bf16[512,768]{1,0:T(8,128)(2,1)S(1)} %get-tuple-element.6), channel_id=1, source_target_pairs={{0,2},{2,4},{4,6},{1,3},{3,5},{5,7},{8,10},{10,12},{12,14},{9,11},... | collective-permute-start | bytes 2359304 | tf_op jit(solution)/shard_map/ppermute | solution.py:86
  21.5 0.8 multiply_reduce_fusion.11
  22.4 0.6 fusion.94
  23.0 12.6 %collective-permute-done.5 = bf16[512,768]{1,0:T(8,128)(2,1)S(1)} collective-permute-done((bf16[512,768]{1,0:T(8,128)(2,1)S(1)}, bf16[512,768]{1,0:T(8,128)(2,1)S(1)}, u32[]{:S(2)}, u32[]{:S(2)}) %collective-permute-start.5) | collective-permute-done | bytes 786464 | tf_op jit(solution)/shard_map/ppermute | solution.py:86
  35.5 1.3 %collective-permute-start.9 = (bf16[512,768]{1,0:T(8,128)(2,1)S(1)}, bf16[512,768]{1,0:T(8,128)(2,1)S(1)}, u32[]{:S(2)}, u32[]{:S(2)}) collective-permute-start(bf16[512,768]{1,0:T(8,128)(2,1)S(1)} %collective-permute-done.5), channel_id=1, source_target_pairs={{2,0},{4,2},{6,4},{3,1},{5,3},{7,5},{10,8},{12,10},{14,12},{11,9},... | collective-permute-start | bytes 2359304 | tf_op jit(solution)/shard_map/ppermute | solution.py:92
  36.9 0.5 collective-permute-start.6
  37.4 4.6 %collective-permute-start.8 = (bf16[512,768]{1,0:T(8,128)(2,1)S(1)}, bf16[512,768]{1,0:T(8,128)(2,1)S(1)}, u32[]{:S(2)}, u32[]{:S(2)}) collective-permute-start(bf16[512,768]{1,0:T(8,128)(2,1)S(1)} %collective-permute-done.4), channel_id=1, source_target_pairs={{0,2},{2,4},{4,6},{1,3},{3,5},{5,7},{8,10},{10,12},{12,14},{9,11},... | collective-permute-start | bytes 2359304 | tf_op jit(solution)/shard_map/ppermute | solution.py:92
  42.2 0.2 fusion.6
  42.7 0.2 fusion.2
  43.0 0.8 multiply_reduce_fusion.8
  43.8 0.6 fusion.88
  44.4 0.8 multiply_reduce_fusion.9
  45.2 0.6 fusion.90
  45.9 0.8 multiply_reduce_fusion.10
  46.7 0.6 fusion.92
  47.3 0.2 fusion.10
  47.6 0.2 fusion.8
  47.8 11.2 %collective-permute-done.8 = bf16[512,768]{1,0:T(8,128)(2,1)S(1)} collective-permute-done((bf16[512,768]{1,0:T(8,128)(2,1)S(1)}, bf16[512,768]{1,0:T(8,128)(2,1)S(1)}, u32[]{:S(2)}, u32[]{:S(2)}) %collective-permute-start.8) | collective-permute-done | bytes 786464 | tf_op jit(solution)/shard_map/ppermute | solution.py:92
  59.2 0.2 fusion.14
  59.6 1.5 %collective-permute-start.12 = (bf16[512,768]{1,0:T(8,128)(2,1)S(1)}, bf16[512,768]{1,0:T(8,128)(2,1)S(1)}, u32[]{:S(2)}, u32[]{:S(2)}) collective-permute-start(bf16[512,768]{1,0:T(8,128)(2,1)S(1)} %broadcast_select_fusion.1), channel_id=1, source_target_pairs={{4,6},{2,0},{5,7},{3,1},{12,14},{10,8},{13,15},{11,9},{20,22},{18,... | collective-permute-start | bytes 2359304 | tf_op jit(solution)/shard_map/ppermute | solution.py:96
  61.6 0.6 collective-permute-start.10
  62.2 0.8 multiply_reduce_fusion.7
  63.0 0.6 fusion.86
  63.6 0.8 multiply_reduce_fusion.6
  64.4 0.6 fusion.84
  65.0 0.8 multiply_reduce_fusion.5
  65.8 0.8 multiply_reduce_fusion.4
  66.6 0.6 fusion.82
  67.2 0.6 fusion.80
  67.9 0.2 fusion.18
  68.3 11.9 %collective-permute-done.12 = bf16[512,768]{1,0:T(8,128)(2,1)S(1)} collective-permute-done((bf16[512,768]{1,0:T(8,128)(2,1)S(1)}, bf16[512,768]{1,0:T(8,128)(2,1)S(1)}, u32[]{:S(2)}, u32[]{:S(2)}) %collective-permute-start.12) | collective-permute-done | bytes 786464 | tf_op jit(solution)/shard_map/ppermute | solution.py:96
  81.0 0.8 multiply_reduce_fusion.2
  81.8 0.8 multiply_reduce_fusion.3
  82.6 0.8 multiply_reduce_fusion.1
  83.4 0.6 fusion.78
  84.0 0.6 fusion.75
  84.6 0.2 fusion.22
  85.0 0.8 multiply_reduce_fusion
  85.8 0.6 fusion.73
  86.4 2.1 %multiply_convert_fusion = bf16[512,768]{1,0:T(8,128)(2,1)S(1)} fusion(f32[512,768]{1,0:T(8,128)S(1)} %fusion.73, f32[512,768]{1,0:T(8,128)S(1)} %fusion.75, f32[512,768]{1,0:T(8,128)S(1)} %fusion.78, f32[512,768]{1,0:T(8,128)S(1)} %fusion.80, f32[512,768]{1,0:T(8,128)S(1)} %fusion.82, f32[512,768]{1,0:T(8,128)S(1)} %fusion.84, f32[512,768]{1,0:T(8,128)S(1)} %fusion.86, ...), kind=kOutput, calls=%fused_computation.49 | convolution fusion | flops 412483584 | bytes 19402796 | tf_op jit(solution)/shard_map/dot_general | solution.py:74
  88.5 0.6 gather_fusion
  89.1 1.0 %broadcast_select_fusion = bf16[1,1,512,768]{3,2,1,0:T(8,128)(2,1)} fusion(bf16[1,1,512,768]{3,2,1,0:T(8,128)(2,1)S(1)} %bitcast.41, pred[512]{0:T(512)(128)(4,1)S(1)} %broadcast_bitcast_fusion), kind=kLoop, calls=%fused_computation.115 | loop fusion | flops 393216 | bytes 1573376 | tf_op jit(solution)/shard_map/jit(_take)/select_n | solution.py:116
  (51 shorter events, 3.2 us)
Async XLA Ops:
  1.6 8.8 %collective-permute-start = (bf16[128,768]{1,0:T(8,128)(2,1)S(1)}, bf16[128,768]{1,0:T(8,128)(2,1)S(1)}, u32[]{:S(2)}, u32[]{:S(2)}) collective-permute-start(bf16[128,768]{1,0:T(8,128)(2,1)S(1)} %get-tuple-element.10), channel_id=1, source_target_pairs={{0,8},{8,0},{16,24},{24,16},{1,9},{9,1},{17,25},{25,17},{2,10},{10... | collective-permute-start | bytes 589832 | tf_op jit(solution)/shard_map/ppermute | solution.py:44
  4.6 10.6 %collective-permute-start.1 = (bf16[128,768]{1,0:T(8,128)(2,1)S(1)}, bf16[128,768]{1,0:T(8,128)(2,1)S(1)}, u32[]{:S(2)}, u32[]{:S(2)}) collective-permute-start(bf16[128,768]{1,0:T(8,128)(2,1)S(1)} %get-tuple-element.9), channel_id=1, source_target_pairs={{0,16},{8,24},{16,0},{24,8},{1,17},{9,25},{17,1},{25,9},{2,18},{10... | collective-permute-start | bytes 589832 | tf_op jit(solution)/shard_map/ppermute | solution.py:44
  6.1 9.1 %collective-permute-start.2 = (bf16[128,768]{1,0:T(8,128)(2,1)S(1)}, bf16[128,768]{1,0:T(8,128)(2,1)S(1)}, u32[]{:S(2)}, u32[]{:S(2)}) collective-permute-start(bf16[128,768]{1,0:T(8,128)(2,1)S(1)} %get-tuple-element.8), channel_id=1, source_target_pairs={{0,24},{8,16},{16,8},{24,0},{1,25},{9,17},{17,9},{25,1},{2,26},{10... | collective-permute-start | bytes 589832 | tf_op jit(solution)/shard_map/ppermute | solution.py:44
  15.4 20.1 %collective-permute-start.5 = (bf16[512,768]{1,0:T(8,128)(2,1)S(1)}, bf16[512,768]{1,0:T(8,128)(2,1)S(1)}, u32[]{:S(2)}, u32[]{:S(2)}) collective-permute-start(bf16[512,768]{1,0:T(8,128)(2,1)S(1)} %get-tuple-element.6), channel_id=1, source_target_pairs={{2,0},{4,2},{6,4},{3,1},{5,3},{7,5},{10,8},{12,10},{14,12},{11,9},... | collective-permute-start | bytes 2359304 | tf_op jit(solution)/shard_map/ppermute | solution.py:86
  16.7 20.2 %collective-permute-start.4 = (bf16[512,768]{1,0:T(8,128)(2,1)S(1)}, bf16[512,768]{1,0:T(8,128)(2,1)S(1)}, u32[]{:S(2)}, u32[]{:S(2)}) collective-permute-start(bf16[512,768]{1,0:T(8,128)(2,1)S(1)} %get-tuple-element.6), channel_id=1, source_target_pairs={{0,2},{2,4},{4,6},{1,3},{3,5},{5,7},{8,10},{10,12},{12,14},{9,11},... | collective-permute-start | bytes 2359304 | tf_op jit(solution)/shard_map/ppermute | solution.py:86
  21.3 21.4 %collective-permute-start.3 = (bf16[512,768]{1,0:T(8,128)(2,1)S(1)}, bf16[512,768]{1,0:T(8,128)(2,1)S(1)}, u32[]{:S(2)}, u32[]{:S(2)}) collective-permute-start(bf16[512,768]{1,0:T(8,128)(2,1)S(1)} %get-tuple-element.6), channel_id=1, source_target_pairs={{0,1},{1,0},{2,3},{3,2},{4,5},{5,4},{6,7},{7,6},{8,9},{9,8},{10,11... | collective-permute-start | bytes 2359304 | tf_op jit(solution)/shard_map/ppermute | solution.py:87
  35.5 23.7 %collective-permute-start.9 = (bf16[512,768]{1,0:T(8,128)(2,1)S(1)}, bf16[512,768]{1,0:T(8,128)(2,1)S(1)}, u32[]{:S(2)}, u32[]{:S(2)}) collective-permute-start(bf16[512,768]{1,0:T(8,128)(2,1)S(1)} %collective-permute-done.5), channel_id=1, source_target_pairs={{2,0},{4,2},{6,4},{3,1},{5,3},{7,5},{10,8},{12,10},{14,12},{11,9},... | collective-permute-start | bytes 2359304 | tf_op jit(solution)/shard_map/ppermute | solution.py:92
  36.8 10.5 %collective-permute-start.7 = (bf16[512,768]{1,0:T(8,128)(2,1)S(1)}, bf16[512,768]{1,0:T(8,128)(2,1)S(1)}, u32[]{:S(2)}, u32[]{:S(2)}) collective-permute-start(bf16[512,768]{1,0:T(8,128)(2,1)S(1)} %collective-permute-done.5), channel_id=1, source_target_pairs={{0,1},{1,0},{2,3},{3,2},{4,5},{5,4},{6,7},{7,6},{8,9},{9,8},{10,11... | collective-permute-start | bytes 2359304 | tf_op jit(solution)/shard_map/ppermute | solution.py:107
  36.9 10.7 %collective-permute-start.6 = (bf16[512,768]{1,0:T(8,128)(2,1)S(1)}, bf16[512,768]{1,0:T(8,128)(2,1)S(1)}, u32[]{:S(2)}, u32[]{:S(2)}) collective-permute-start(bf16[512,768]{1,0:T(8,128)(2,1)S(1)} %collective-permute-done.4), channel_id=1, source_target_pairs={{0,1},{1,0},{2,3},{3,2},{4,5},{5,4},{6,7},{7,6},{8,9},{9,8},{10,11... | collective-permute-start | bytes 2359304 | tf_op jit(solution)/shard_map/ppermute | solution.py:106
  37.4 21.6 %collective-permute-start.8 = (bf16[512,768]{1,0:T(8,128)(2,1)S(1)}, bf16[512,768]{1,0:T(8,128)(2,1)S(1)}, u32[]{:S(2)}, u32[]{:S(2)}) collective-permute-start(bf16[512,768]{1,0:T(8,128)(2,1)S(1)} %collective-permute-done.4), channel_id=1, source_target_pairs={{0,2},{2,4},{4,6},{1,3},{3,5},{5,7},{8,10},{10,12},{12,14},{9,11},... | collective-permute-start | bytes 2359304 | tf_op jit(solution)/shard_map/ppermute | solution.py:92
  59.6 20.7 %collective-permute-start.12 = (bf16[512,768]{1,0:T(8,128)(2,1)S(1)}, bf16[512,768]{1,0:T(8,128)(2,1)S(1)}, u32[]{:S(2)}, u32[]{:S(2)}) collective-permute-start(bf16[512,768]{1,0:T(8,128)(2,1)S(1)} %broadcast_select_fusion.1), channel_id=1, source_target_pairs={{4,6},{2,0},{5,7},{3,1},{12,14},{10,8},{13,15},{11,9},{20,22},{18,... | collective-permute-start | bytes 2359304 | tf_op jit(solution)/shard_map/ppermute | solution.py:96
  61.1 6.8 %collective-permute-start.11 = (bf16[512,768]{1,0:T(8,128)(2,1)S(1)}, bf16[512,768]{1,0:T(8,128)(2,1)S(1)}, u32[]{:S(2)}, u32[]{:S(2)}) collective-permute-start(bf16[512,768]{1,0:T(8,128)(2,1)S(1)} %collective-permute-done.9), channel_id=1, source_target_pairs={{0,1},{1,0},{2,3},{3,2},{4,5},{5,4},{6,7},{7,6},{8,9},{9,8},{10,11... | collective-permute-start | bytes 2359304 | tf_op jit(solution)/shard_map/ppermute | solution.py:107
  61.6 6.5 %collective-permute-start.10 = (bf16[512,768]{1,0:T(8,128)(2,1)S(1)}, bf16[512,768]{1,0:T(8,128)(2,1)S(1)}, u32[]{:S(2)}, u32[]{:S(2)}) collective-permute-start(bf16[512,768]{1,0:T(8,128)(2,1)S(1)} %collective-permute-done.8), channel_id=1, source_target_pairs={{0,1},{1,0},{2,3},{3,2},{4,5},{5,4},{6,7},{7,6},{8,9},{9,8},{10,11... | collective-permute-start | bytes 2359304 | tf_op jit(solution)/shard_map/ppermute | solution.py:106
  80.9 3.7 %collective-permute-start.13 = (bf16[512,768]{1,0:T(8,128)(2,1)S(1)}, bf16[512,768]{1,0:T(8,128)(2,1)S(1)}, u32[]{:S(2)}, u32[]{:S(2)}) collective-permute-start(bf16[512,768]{1,0:T(8,128)(2,1)S(1)} %collective-permute-done.12), channel_id=1, source_target_pairs={{0,1},{1,0},{2,3},{3,2},{4,5},{5,4},{6,7},{7,6},{8,9},{9,8},{10,11... | collective-permute-start | bytes 2359304 | tf_op jit(solution)/shard_map/ppermute | solution.py:102

commit v13 on v12

--- a/solution.py
+++ b/solution.py
@@ -87,6 +87,8 @@
     swapped = lax.ppermute(mine, "core", swap)
     acc = add_pair(acc, swapped, times_listed(chip, other_core))
     for step in range(1, chips):
+        if step + 1 == chips:
+            acc, received = lax.optimization_barrier((acc, received))
         from_below, from_above = received
         if step + 2 < chips:
             received = (lax.ppermute(from_below, "chip", up), lax.ppermute(from_above, "chip", down))
@@ -113,7 +115,7 @@
     result = summed * lax.rsqrt(squares)[:, None] * live[:, None]
     result = result.astype(jnp.bfloat16).reshape(sources, slot_rows, width)
     order = jnp.arange(sources, dtype=jnp.int32) ^ bucket
-    return jnp.take(result, order, axis=0).reshape(1, 1, rows, width)
+    return jnp.take(result, order, axis=0, mode="clip").reshape(1, 1, rows, width)
 
 
 def solution(mesh):

time: 90.3 us -> 89.2 us (0.988)
  waiting for transfers between devices: 44.2 us -> 46.7 us
  starting transfers between devices: 19.1 us -> 17 us
  other arithmetic: 6.9 us -> 5.88 us
    ppermute x1, waiting for transfers between devices: 11.9 us -> 5.59 us  [per_device(): last = lax.ppermute(outgoing, 'chip', ends)]
    ppermute x1, waiting for transfers between devices: 12.6 us -> 18 us  [per_device(): lax.ppermute(mine, 'chip', down)]
    ppermute x1, waiting for transfers between devices: 0.01 us -> 4.16 us  [per_device(): lax.ppermute(from_above, 'chip', down)]
    ppermute x1, waiting for transfers between devices: 11.2 us -> 9.24 us  [per_device(): lax.ppermute(from_below, 'chip', up)]
    ppermute x1, starting transfers between devices: 4.58 us -> 3.48 us  [per_device(): lax.ppermute(from_below, 'chip', up)]
    ppermute x1, starting transfers between devices: 4.6 us -> 3.52 us  [per_device(): lax.ppermute(mine, 'chip', up)]
    select_n x2 -> x0, other arithmetic: 1.03 us -> none  [per_device(): return jnp.take(result, order, axis=0).reshape(1, 1, rows, width)]
  transfers between devices with their start and end apart: 14 -> 14, of which waited for: 5 -> 8; matrix products, arithmetic and copies ran while one was open for 20% -> 22% of each run, Pallas kernels for 0% -> 0%
where the time goes in v13:
time: 89.2 us; the launch traced here: 89 us
  waiting for transfers between devices  46.7 us (52%)
  matrix products  17.6 us (20%)
  starting transfers between devices  17 us (19%)
  other arithmetic  5.88 us (7%)
  local copies, waits for them, and re-layouts  1.54 us (2%)
    ppermute x1, waiting for transfers between devices, per_device(): lax.ppermute(mine, 'chip', down)  18 us
    dot_general x12, matrix products, weigh(): scores = jnp.dot(unit_a, unit_b.T, preferred_element_type=jnp.float32)  9.6 us
    ppermute x1, waiting for transfers between devices, per_device(): lax.ppermute(from_below, 'chip', up)  9.24 us
    ppermute x3, waiting for transfers between devices, per_device(): lax.ppermute(outgoing, 'bucket', [(i, i ^ m) for i in range(buckets)])  8.75 us
    dot_general x11, matrix products, pair_terms(): jnp.dot(weights.astype(jnp.bfloat16), got, preferred_element_type=jnp.flo...  7.36 us
    ppermute x1, waiting for transfers between devices, per_device(): last = lax.ppermute(outgoing, 'chip', ends)  5.59 us
    ppermute x3, starting transfers between devices, per_device(): lax.ppermute(outgoing, 'bucket', [(i, i ^ m) for i in range(buckets)])  4.63 us
    ppermute x1, waiting for transfers between devices, per_device(): lax.ppermute(from_above, 'chip', down)  4.16 us
  transfers between devices with their start and end apart: 14, of which 8 were waited for; matrix products, arithmetic and copies ran while one was open for 22% of the time, Pallas kernels for 0%

profile of v13, /device:TPU:0, one launch (start us, length us, event | category | flops | bytes accessed | tf_op | source)
XLA Modules:
  0.0 89.0 jit_solution(6712825708446183657)
XLA Ops:
  0.0 1.5 %fusion.25 = bf16[4,128,768]{2,1,0:T(8,128)(2,1)S(1)} fusion(bf16[1,1,4,128,768]{4,3,2,1,0:T(8,128)(2,1)} %param.2, s32[4]{0:T(128)} %bitcast.40, pred[768]{0:T(1024)(128)(4,1)S(1)} %iota_compare_fusion.2), kind=kLoop, calls=%fused_computation.53 | loop fusion | flops 1179648 | bytes 1573648 | tf_op jit(solution)/shard_map/jit(_where)/select_n | solution.py:40
  1.6 4.0 %collective-permute-start.2 = (bf16[128,768]{1,0:T(8,128)(2,1)S(1)}, bf16[128,768]{1,0:T(8,128)(2,1)S(1)}, u32[]{:S(2)}, u32[]{:S(2)}) collective-permute-start(bf16[128,768]{1,0:T(8,128)(2,1)S(1)} %get-tuple-element.14), channel_id=1, source_target_pairs={{0,24},{8,16},{16,8},{24,0},{1,25},{9,17},{17,9},{25,1},{2,26},{10... | collective-permute-start | bytes 589832 | tf_op jit(solution)/shard_map/ppermute | solution.py:44
  5.6 0.5 collective-permute-start.1
  6.2 5.1 %collective-permute-done.2 = bf16[128,768]{1,0:T(8,128)(2,1)S(1)} collective-permute-done((bf16[128,768]{1,0:T(8,128)(2,1)S(1)}, bf16[128,768]{1,0:T(8,128)(2,1)S(1)}, u32[]{:S(2)}, u32[]{:S(2)}) %collective-permute-start.2) | collective-permute-done | bytes 196640 | tf_op jit(solution)/shard_map/ppermute | solution.py:44
  11.4 3.3 %collective-permute-done.1 = bf16[128,768]{1,0:T(8,128)(2,1)S(1)} collective-permute-done((bf16[128,768]{1,0:T(8,128)(2,1)S(1)}, bf16[128,768]{1,0:T(8,128)(2,1)S(1)}, u32[]{:S(2)}, u32[]{:S(2)}) %collective-permute-start.1) | collective-permute-done | bytes 196640 | tf_op jit(solution)/shard_map/ppermute | solution.py:44
  14.7 0.3 collective-permute-done
  15.2 3.5 %collective-permute-start.4 = (bf16[512,768]{1,0:T(8,128)(2,1)S(1)}, bf16[512,768]{1,0:T(8,128)(2,1)S(1)}, u32[]{:S(2)}, u32[]{:S(2)}) collective-permute-start(bf16[512,768]{1,0:T(8,128)(2,1)S(1)} %get-tuple-element.12), channel_id=1, source_target_pairs={{0,2},{2,4},{4,6},{1,3},{3,5},{5,7},{8,10},{10,12},{12,14},{9,11},... | collective-permute-start | bytes 2359304 | tf_op jit(solution)/shard_map/ppermute | solution.py:86
  18.7 1.3 %collective-permute-start.5 = (bf16[512,768]{1,0:T(8,128)(2,1)S(1)}, bf16[512,768]{1,0:T(8,128)(2,1)S(1)}, u32[]{:S(2)}, u32[]{:S(2)}) collective-permute-start(bf16[512,768]{1,0:T(8,128)(2,1)S(1)} %get-tuple-element.12), channel_id=1, source_target_pairs={{2,0},{4,2},{6,4},{3,1},{5,3},{7,5},{10,8},{12,10},{14,12},{11,9},... | collective-permute-start | bytes 2359304 | tf_op jit(solution)/shard_map/ppermute | solution.py:86
  20.3 0.8 multiply_reduce_fusion.11
  21.1 0.6 fusion.93
  21.7 18.0 %collective-permute-done.5 = bf16[512,768]{1,0:T(8,128)(2,1)S(1)} collective-permute-done((bf16[512,768]{1,0:T(8,128)(2,1)S(1)}, bf16[512,768]{1,0:T(8,128)(2,1)S(1)}, u32[]{:S(2)}, u32[]{:S(2)}) %collective-permute-start.5) | collective-permute-done | bytes 786464 | tf_op jit(solution)/shard_map/ppermute | solution.py:86
  40.0 0.2 fusion.4
  40.2 0.2 fusion.2
  40.5 3.5 %collective-permute-start.8 = (bf16[512,768]{1,0:T(8,128)(2,1)S(1)}, bf16[512,768]{1,0:T(8,128)(2,1)S(1)}, u32[]{:S(2)}, u32[]{:S(2)}) collective-permute-start(bf16[512,768]{1,0:T(8,128)(2,1)S(1)} %collective-permute-done.4), channel_id=1, source_target_pairs={{0,2},{2,4},{4,6},{1,3},{3,5},{5,7},{8,10},{10,12},{12,14},{9,11},... | collective-permute-start | bytes 2359304 | tf_op jit(solution)/shard_map/ppermute | solution.py:94
  44.0 1.3 %collective-permute-start.9 = (bf16[512,768]{1,0:T(8,128)(2,1)S(1)}, bf16[512,768]{1,0:T(8,128)(2,1)S(1)}, u32[]{:S(2)}, u32[]{:S(2)}) collective-permute-start(bf16[512,768]{1,0:T(8,128)(2,1)S(1)} %collective-permute-done.5), channel_id=1, source_target_pairs={{2,0},{4,2},{6,4},{3,1},{5,3},{7,5},{10,8},{12,10},{14,12},{11,9},... | collective-permute-start | bytes 2359304 | tf_op jit(solution)/shard_map/ppermute | solution.py:94
  45.3 0.5 collective-permute-start.6
  46.2 0.8 multiply_reduce_fusion.8
  47.0 0.6 fusion.87
  47.6 0.8 multiply_reduce_fusion.9
  48.4 0.8 multiply_reduce_fusion.10
  49.2 0.6 fusion.89
  49.8 0.6 fusion.91
  50.4 9.2 %collective-permute-done.8 = bf16[512,768]{1,0:T(8,128)(2,1)S(1)} collective-permute-done((bf16[512,768]{1,0:T(8,128)(2,1)S(1)}, bf16[512,768]{1,0:T(8,128)(2,1)S(1)}, u32[]{:S(2)}, u32[]{:S(2)}) %collective-permute-start.8) | collective-permute-done | bytes 786464 | tf_op jit(solution)/shard_map/ppermute | solution.py:94
  59.6 4.2 %collective-permute-done.9 = bf16[512,768]{1,0:T(8,128)(2,1)S(1)} collective-permute-done((bf16[512,768]{1,0:T(8,128)(2,1)S(1)}, bf16[512,768]{1,0:T(8,128)(2,1)S(1)}, u32[]{:S(2)}, u32[]{:S(2)}) %collective-permute-start.9) | collective-permute-done | bytes 786464 | tf_op jit(solution)/shard_map/ppermute | solution.py:94
  63.9 1.5 %collective-permute-start.12 = (bf16[512,768]{1,0:T(8,128)(2,1)S(1)}, bf16[512,768]{1,0:T(8,128)(2,1)S(1)}, u32[]{:S(2)}, u32[]{:S(2)}) collective-permute-start(bf16[512,768]{1,0:T(8,128)(2,1)S(1)} %broadcast_select_fusion), channel_id=1, source_target_pairs={{4,6},{2,0},{5,7},{3,1},{12,14},{10,8},{13,15},{11,9},{20,22},{18,... | collective-permute-start | bytes 2359304 | tf_op jit(solution)/shard_map/ppermute | solution.py:98
  65.7 0.2 fusion.14
  66.2 0.2 fusion.10
  66.7 0.2 fusion.8
  66.9 0.6 collective-permute-start.11
  67.5 0.8 multiply_reduce_fusion.4
  68.3 0.6 fusion.79
  68.9 0.8 multiply_reduce_fusion.5
  69.7 0.6 fusion.81
  70.3 0.8 multiply_reduce_fusion.6
  71.1 0.6 fusion.83
  71.7 0.8 multiply_reduce_fusion.7
  72.5 0.6 fusion.85
  73.8 0.8 multiply_reduce_fusion.3
  74.6 0.6 fusion.77
  75.2 0.8 multiply_reduce_fusion.2
  76.1 1.2 %multiply_add_fusion = f32[512,768]{1,0:T(8,128)S(1)} fusion(f32[512,768]{1,0:T(8,128)S(1)} %fusion.77, f32[512,768]{1,0:T(8,128)S(1)} %fusion.79, f32[512,768]{1,0:T(8,128)S(1)} %fusion.81, f32[512,768]{1,0:T(8,128)S(1)} %fusion.83, f32[512,768]{1,0:T(8,128)S(1)} %fusion.85, f32[512,768]{1,0:T(8,128)S(1)} %fusion.87, f32[512,768]{1,0:T(8,128)S(1)} %fusion.89, ...), kind=kOutput, calls=%fused_computation.50 | convolution fusion | flops 409731072 | bytes 17039396 | tf_op jit(solution)/shard_map/dot_general | solution.py:74
  77.3 5.6 %collective-permute-done.12 = bf16[512,768]{1,0:T(8,128)(2,1)S(1)} collective-permute-done((bf16[512,768]{1,0:T(8,128)(2,1)S(1)}, bf16[512,768]{1,0:T(8,128)(2,1)S(1)}, u32[]{:S(2)}, u32[]{:S(2)}) %collective-permute-start.12) | collective-permute-done | bytes 786464 | tf_op jit(solution)/shard_map/ppermute | solution.py:98
  83.3 0.8 multiply_reduce_fusion.1
  84.1 0.6 fusion.74
  84.7 0.9 collective-permute-done.13
  85.9 0.8 multiply_reduce_fusion
  86.8 0.8 multiply_convert_fusion
  87.5 1.5 %gather_fusion = bf16[4,128,768]{2,1,0:T(8,128)(2,1)} fusion(bf16[4,128,768]{2,1,0:T(8,128)(2,1)S(1)} %bitcast.39, s32[1024]{0:T(1024)S(1)} %pad_clamp_fusion), kind=kCustom, calls=%fused_computation | custom fusion | bytes 1572880 | tf_op jit(solution)/shard_map/jit(_take)/gather | solution.py:118
  (49 shorter events, 3.7 us)
Async XLA Ops:
  1.6 9.8 %collective-permute-start.2 = (bf16[128,768]{1,0:T(8,128)(2,1)S(1)}, bf16[128,768]{1,0:T(8,128)(2,1)S(1)}, u32[]{:S(2)}, u32[]{:S(2)}) collective-permute-start(bf16[128,768]{1,0:T(8,128)(2,1)S(1)} %get-tuple-element.14), channel_id=1, source_target_pairs={{0,24},{8,16},{16,8},{24,0},{1,25},{9,17},{17,9},{25,1},{2,26},{10... | collective-permute-start | bytes 589832 | tf_op jit(solution)/shard_map/ppermute | solution.py:44
  5.6 9.1 %collective-permute-start.1 = (bf16[128,768]{1,0:T(8,128)(2,1)S(1)}, bf16[128,768]{1,0:T(8,128)(2,1)S(1)}, u32[]{:S(2)}, u32[]{:S(2)}) collective-permute-start(bf16[128,768]{1,0:T(8,128)(2,1)S(1)} %get-tuple-element.15), channel_id=1, source_target_pairs={{0,16},{8,24},{16,0},{24,8},{1,17},{9,25},{17,1},{25,9},{2,18},{10... | collective-permute-start | bytes 589832 | tf_op jit(solution)/shard_map/ppermute | solution.py:44
  6.1 8.9 %collective-permute-start = (bf16[128,768]{1,0:T(8,128)(2,1)S(1)}, bf16[128,768]{1,0:T(8,128)(2,1)S(1)}, u32[]{:S(2)}, u32[]{:S(2)}) collective-permute-start(bf16[128,768]{1,0:T(8,128)(2,1)S(1)} %get-tuple-element.16), channel_id=1, source_target_pairs={{0,8},{8,0},{16,24},{24,16},{1,9},{9,1},{17,25},{25,17},{2,10},{10... | collective-permute-start | bytes 589832 | tf_op jit(solution)/shard_map/ppermute | solution.py:44
  15.2 24.7 %collective-permute-start.4 = (bf16[512,768]{1,0:T(8,128)(2,1)S(1)}, bf16[512,768]{1,0:T(8,128)(2,1)S(1)}, u32[]{:S(2)}, u32[]{:S(2)}) collective-permute-start(bf16[512,768]{1,0:T(8,128)(2,1)S(1)} %get-tuple-element.12), channel_id=1, source_target_pairs={{0,2},{2,4},{4,6},{1,3},{3,5},{5,7},{8,10},{10,12},{12,14},{9,11},... | collective-permute-start | bytes 2359304 | tf_op jit(solution)/shard_map/ppermute | solution.py:86
  18.7 21.0 %collective-permute-start.5 = (bf16[512,768]{1,0:T(8,128)(2,1)S(1)}, bf16[512,768]{1,0:T(8,128)(2,1)S(1)}, u32[]{:S(2)}, u32[]{:S(2)}) collective-permute-start(bf16[512,768]{1,0:T(8,128)(2,1)S(1)} %get-tuple-element.12), channel_id=1, source_target_pairs={{2,0},{4,2},{6,4},{3,1},{5,3},{7,5},{10,8},{12,10},{14,12},{11,9},... | collective-permute-start | bytes 2359304 | tf_op jit(solution)/shard_map/ppermute | solution.py:86
  20.0 20.2 %collective-permute-start.3 = (bf16[512,768]{1,0:T(8,128)(2,1)S(1)}, bf16[512,768]{1,0:T(8,128)(2,1)S(1)}, u32[]{:S(2)}, u32[]{:S(2)}) collective-permute-start(bf16[512,768]{1,0:T(8,128)(2,1)S(1)} %get-tuple-element.12), channel_id=1, source_target_pairs={{0,1},{1,0},{2,3},{3,2},{4,5},{5,4},{6,7},{7,6},{8,9},{9,8},{10,11... | collective-permute-start | bytes 2359304 | tf_op jit(solution)/shard_map/ppermute | solution.py:87
  40.5 19.2 %collective-permute-start.8 = (bf16[512,768]{1,0:T(8,128)(2,1)S(1)}, bf16[512,768]{1,0:T(8,128)(2,1)S(1)}, u32[]{:S(2)}, u32[]{:S(2)}) collective-permute-start(bf16[512,768]{1,0:T(8,128)(2,1)S(1)} %collective-permute-done.4), channel_id=1, source_target_pairs={{0,2},{2,4},{4,6},{1,3},{3,5},{5,7},{8,10},{10,12},{12,14},{9,11},... | collective-permute-start | bytes 2359304 | tf_op jit(solution)/shard_map/ppermute | solution.py:94
  44.0 19.8 %collective-permute-start.9 = (bf16[512,768]{1,0:T(8,128)(2,1)S(1)}, bf16[512,768]{1,0:T(8,128)(2,1)S(1)}, u32[]{:S(2)}, u32[]{:S(2)}) collective-permute-start(bf16[512,768]{1,0:T(8,128)(2,1)S(1)} %collective-permute-done.5), channel_id=1, source_target_pairs={{2,0},{4,2},{6,4},{3,1},{5,3},{7,5},{10,8},{12,10},{14,12},{11,9},... | collective-permute-start | bytes 2359304 | tf_op jit(solution)/shard_map/ppermute | solution.py:94
  45.3 20.9 %collective-permute-start.7 = (bf16[512,768]{1,0:T(8,128)(2,1)S(1)}, bf16[512,768]{1,0:T(8,128)(2,1)S(1)}, u32[]{:S(2)}, u32[]{:S(2)}) collective-permute-start(bf16[512,768]{1,0:T(8,128)(2,1)S(1)} %collective-permute-done.5), channel_id=1, source_target_pairs={{0,1},{1,0},{2,3},{3,2},{4,5},{5,4},{6,7},{7,6},{8,9},{9,8},{10,11... | collective-permute-start | bytes 2359304 | tf_op jit(solution)/shard_map/ppermute | solution.py:109
  45.3 21.2 %collective-permute-start.6 = (bf16[512,768]{1,0:T(8,128)(2,1)S(1)}, bf16[512,768]{1,0:T(8,128)(2,1)S(1)}, u32[]{:S(2)}, u32[]{:S(2)}) collective-permute-start(bf16[512,768]{1,0:T(8,128)(2,1)S(1)} %collective-permute-done.4), channel_id=1, source_target_pairs={{0,1},{1,0},{2,3},{3,2},{4,5},{5,4},{6,7},{7,6},{8,9},{9,8},{10,11... | collective-permute-start | bytes 2359304 | tf_op jit(solution)/shard_map/ppermute | solution.py:108
  63.9 19.0 %collective-permute-start.12 = (bf16[512,768]{1,0:T(8,128)(2,1)S(1)}, bf16[512,768]{1,0:T(8,128)(2,1)S(1)}, u32[]{:S(2)}, u32[]{:S(2)}) collective-permute-start(bf16[512,768]{1,0:T(8,128)(2,1)S(1)} %broadcast_select_fusion), channel_id=1, source_target_pairs={{4,6},{2,0},{5,7},{3,1},{12,14},{10,8},{13,15},{11,9},{20,22},{18,... | collective-permute-start | bytes 2359304 | tf_op jit(solution)/shard_map/ppermute | solution.py:98
  65.4 7.7 %collective-permute-start.10 = (bf16[512,768]{1,0:T(8,128)(2,1)S(1)}, bf16[512,768]{1,0:T(8,128)(2,1)S(1)}, u32[]{:S(2)}, u32[]{:S(2)}) collective-permute-start(bf16[512,768]{1,0:T(8,128)(2,1)S(1)} %collective-permute-done.8), channel_id=1, source_target_pairs={{0,1},{1,0},{2,3},{3,2},{4,5},{5,4},{6,7},{7,6},{8,9},{9,8},{10,11... | collective-permute-start | bytes 2359304 | tf_op jit(solution)/shard_map/ppermute | solution.py:108
  66.9 6.4 %collective-permute-start.11 = (bf16[512,768]{1,0:T(8,128)(2,1)S(1)}, bf16[512,768]{1,0:T(8,128)(2,1)S(1)}, u32[]{:S(2)}, u32[]{:S(2)}) collective-permute-start(bf16[512,768]{1,0:T(8,128)(2,1)S(1)} %collective-permute-done.9), channel_id=1, source_target_pairs={{0,1},{1,0},{2,3},{3,2},{4,5},{5,4},{6,7},{7,6},{8,9},{9,8},{10,11... | collective-permute-start | bytes 2359304 | tf_op jit(solution)/shard_map/ppermute | solution.py:109
  83.2 2.4 %collective-permute-start.13 = (bf16[512,768]{1,0:T(8,128)(2,1)S(1)}, bf16[512,768]{1,0:T(8,128)(2,1)S(1)}, u32[]{:S(2)}, u32[]{:S(2)}) collective-permute-start(bf16[512,768]{1,0:T(8,128)(2,1)S(1)} %collective-permute-done.12), channel_id=1, source_target_pairs={{0,1},{1,0},{2,3},{3,2},{4,5},{5,4},{6,7},{7,6},{8,9},{9,8},{10,11... | collective-permute-start | bytes 2359304 | tf_op jit(solution)/shard_map/ppermute | solution.py:104

commit v14 on v13

--- a/solution.py
+++ b/solution.py
@@ -44,7 +44,9 @@
         arrived.append(lax.ppermute(outgoing, "bucket", [(i, i ^ m) for i in range(buckets)]))
     sources = buckets
     rows = sources * slot_rows
-    data = jnp.concatenate(arrived, axis=0)
+    data = jnp.zeros((rows, width), jnp.bfloat16)
+    for m, piece in enumerate(arrived):
+        data = lax.dynamic_update_slice_in_dim(data, piece, (bucket ^ m) * slot_rows, axis=0)
     live = live_of(data)
     chips = lax.axis_size("chip")
     cores = lax.axis_size("core")
@@ -113,9 +115,7 @@
         acc = add_pair(acc, above_swapped, times_listed(chip + step, other_core))
     summed, squares = acc
     result = summed * lax.rsqrt(squares)[:, None] * live[:, None]
-    result = result.astype(jnp.bfloat16).reshape(sources, slot_rows, width)
-    order = jnp.arange(sources, dtype=jnp.int32) ^ bucket
-    return jnp.take(result, order, axis=0, mode="clip").reshape(1, 1, rows, width)
+    return result.astype(jnp.bfloat16).reshape(1, 1, rows, width)
 
 
 def solution(mesh):

time: 89.2 us -> 84.2 us (0.944)
  waiting for transfers between devices: 46.7 us -> 43 us
  other arithmetic: 5.88 us -> 4.34 us
    ppermute x1, waiting for transfers between devices: 18 us -> 16.5 us  [per_device(): lax.ppermute(mine, 'chip', down)]
    gather x1 -> x0, local copies, waits for them, and re-layouts: 1.48 us -> none  [per_device(): jnp.take(result, order, axis=0, mode='clip').reshape(1, 1, rows, width)]
    convert_element_type x12, other arithmetic: 1.44 us -> 0.07 us  [live_of(): return (block[:, 0] < DEAD / 2).astype(jnp.float32)]
    dot_general x11, matrix products: 7.36 us -> 8.48 us  [pair_terms(): jnp.dot(weights.astype(jnp.bfloat16), got, preferred_element_type=jnp.flo...]
    ppermute x1, waiting for transfers between devices: 9.24 us -> 8.25 us  [per_device(): lax.ppermute(from_below, 'chip', up)]
  transfers between devices with their start and end apart: 14 -> 14, of which waited for: 8 -> 7; matrix products, arithmetic and copies ran while one was open for 22% -> 22% of each run, Pallas kernels for 0% -> 0%
where the time goes in v14:
time: 84.2 us; the launch traced here: 84 us
  waiting for transfers between devices  43 us (51%)
  matrix products  18 us (21%)
  starting transfers between devices  16.9 us (20%)
  other arithmetic  4.34 us (5%)
  local copies, waits for them, and re-layouts  0.97 us (1%)
    ppermute x1, waiting for transfers between devices, per_device(): lax.ppermute(mine, 'chip', down)  16.5 us
    dot_general x12, matrix products, weigh(): scores = jnp.dot(unit_a, unit_b.T, preferred_element_type=jnp.float32)  8.85 us
    dot_general x11, matrix products, pair_terms(): jnp.dot(weights.astype(jnp.bfloat16), got, preferred_element_type=jnp.flo...  8.48 us
    ppermute x1, waiting for transfers between devices, per_device(): lax.ppermute(from_below, 'chip', up)  8.25 us
    ppermute x3, waiting for transfers between devices, per_device(): lax.ppermute(outgoing, 'bucket', [(i, i ^ m) for i in range(buckets)])  8.15 us
    ppermute x1, waiting for transfers between devices, per_device(): last = lax.ppermute(outgoing, 'chip', ends)  5.23 us
    ppermute x3, starting transfers between devices, per_device(): lax.ppermute(outgoing, 'bucket', [(i, i ^ m) for i in range(buckets)])  4.57 us
    ppermute x1, waiting for transfers between devices, per_device(): lax.ppermute(from_above, 'chip', down)  4.16 us
  transfers between devices with their start and end apart: 14, of which 7 were waited for; matrix products, arithmetic and copies ran while one was open for 22% of the time, Pallas kernels for 0%

profile of v14, /device:TPU:0, one launch (start us, length us, event | category | flops | bytes accessed | tf_op | source)
XLA Modules:
  0.0 84.0 jit_solution(4456390724796847068)
XLA Ops:
  0.0 1.5 %fusion.25 = bf16[4,128,768]{2,1,0:T(8,128)(2,1)S(1)} fusion(bf16[1,1,4,128,768]{4,3,2,1,0:T(8,128)(2,1)} %param.2, s32[4]{0:T(128)} %bitcast.62, pred[768]{0:T(1024)(128)(4,1)S(1)} %iota_compare_fusion.2), kind=kLoop, calls=%fused_computation.52 | loop fusion | flops 1179648 | bytes 1573648 | tf_op jit(solution)/shard_map/jit(_where)/select_n | solution.py:40
  1.6 3.0 %collective-permute-start = (bf16[128,768]{1,0:T(8,128)(2,1)S(1)}, bf16[128,768]{1,0:T(8,128)(2,1)S(1)}, u32[]{:S(2)}, u32[]{:S(2)}) collective-permute-start(bf16[128,768]{1,0:T(8,128)(2,1)S(1)} %get-tuple-element.13), channel_id=1, source_target_pairs={{0,8},{8,0},{16,24},{24,16},{1,9},{9,1},{17,25},{25,17},{2,10},{10... | collective-permute-start | bytes 589832 | tf_op jit(solution)/shard_map/ppermute | solution.py:44
  4.6 1.5 %collective-permute-start.1 = (bf16[128,768]{1,0:T(8,128)(2,1)S(1)}, bf16[128,768]{1,0:T(8,128)(2,1)S(1)}, u32[]{:S(2)}, u32[]{:S(2)}) collective-permute-start(bf16[128,768]{1,0:T(8,128)(2,1)S(1)} %get-tuple-element.12), channel_id=1, source_target_pairs={{0,16},{8,24},{16,0},{24,8},{1,17},{9,25},{17,1},{25,9},{2,18},{10... | collective-permute-start | bytes 589832 | tf_op jit(solution)/shard_map/ppermute | solution.py:44
  6.9 3.5 %collective-permute-done = bf16[128,768]{1,0:T(8,128)(2,1)S(1)} collective-permute-done((bf16[128,768]{1,0:T(8,128)(2,1)S(1)}, bf16[128,768]{1,0:T(8,128)(2,1)S(1)}, u32[]{:S(2)}, u32[]{:S(2)}) %collective-permute-start) | collective-permute-done | bytes 196640 | tf_op jit(solution)/shard_map/ppermute | solution.py:44
  10.5 4.7 %collective-permute-done.1 = bf16[128,768]{1,0:T(8,128)(2,1)S(1)} collective-permute-done((bf16[128,768]{1,0:T(8,128)(2,1)S(1)}, bf16[128,768]{1,0:T(8,128)(2,1)S(1)}, u32[]{:S(2)}, u32[]{:S(2)}) %collective-permute-start.1) | collective-permute-done | bytes 196640 | tf_op jit(solution)/shard_map/ppermute | solution.py:44
  15.7 3.5 %collective-permute-start.4 = (bf16[512,768]{0,1:T(8,128)(2,1)S(1)}, bf16[512,768]{0,1:T(8,128)(2,1)S(1)}, u32[]{:S(2)}, u32[]{:S(2)}) collective-permute-start(bf16[512,768]{0,1:T(8,128)(2,1)S(1)} %constant_dynamic-update-slice_fusion), channel_id=1, source_target_pairs={{0,2},{2,4},{4,6},{1,3},{3,5},{5,7},{8,10},{10,12},{12,14},{9,11},... | collective-permute-start | bytes 2359304 | tf_op jit(solution)/shard_map/ppermute | solution.py:88
  19.3 1.3 %collective-permute-start.5 = (bf16[512,768]{0,1:T(8,128)(2,1)S(1)}, bf16[512,768]{0,1:T(8,128)(2,1)S(1)}, u32[]{:S(2)}, u32[]{:S(2)}) collective-permute-start(bf16[512,768]{0,1:T(8,128)(2,1)S(1)} %constant_dynamic-update-slice_fusion), channel_id=1, source_target_pairs={{2,0},{4,2},{6,4},{3,1},{5,3},{7,5},{10,8},{12,10},{14,12},{11,9},... | collective-permute-start | bytes 2359304 | tf_op jit(solution)/shard_map/ppermute | solution.py:88
  20.6 0.2 fusion
  20.9 0.8 multiply_reduce_fusion.11
  21.6 0.6 fusion.94
  22.3 16.5 %collective-permute-done.5 = bf16[512,768]{0,1:T(8,128)(2,1)S(1)} collective-permute-done((bf16[512,768]{0,1:T(8,128)(2,1)S(1)}, bf16[512,768]{0,1:T(8,128)(2,1)S(1)}, u32[]{:S(2)}, u32[]{:S(2)}) %collective-permute-start.5) | collective-permute-done | bytes 786464 | tf_op jit(solution)/shard_map/ppermute | solution.py:88
  39.5 3.5 %collective-permute-start.8 = (bf16[512,768]{0,1:T(8,128)(2,1)S(1)}, bf16[512,768]{0,1:T(8,128)(2,1)S(1)}, u32[]{:S(2)}, u32[]{:S(2)}) collective-permute-start(bf16[512,768]{0,1:T(8,128)(2,1)S(1)} %collective-permute-done.4), channel_id=1, source_target_pairs={{0,2},{2,4},{4,6},{1,3},{3,5},{5,7},{8,10},{10,12},{12,14},{9,11},... | collective-permute-start | bytes 2359304 | tf_op jit(solution)/shard_map/ppermute | solution.py:96
  43.0 1.3 %collective-permute-start.9 = (bf16[512,768]{0,1:T(8,128)(2,1)S(1)}, bf16[512,768]{0,1:T(8,128)(2,1)S(1)}, u32[]{:S(2)}, u32[]{:S(2)}) collective-permute-start(bf16[512,768]{0,1:T(8,128)(2,1)S(1)} %collective-permute-done.5), channel_id=1, source_target_pairs={{2,0},{4,2},{6,4},{3,1},{5,3},{7,5},{10,8},{12,10},{14,12},{11,9},... | collective-permute-start | bytes 2359304 | tf_op jit(solution)/shard_map/ppermute | solution.py:96
  44.3 0.5 collective-permute-start.6
  44.9 0.7 multiply_reduce_fusion.8
  45.6 0.6 fusion.88
  46.2 0.7 multiply_reduce_fusion.9
  47.0 0.7 multiply_reduce_fusion.10
  47.7 0.6 fusion.90
  48.3 0.6 fusion.92
  48.9 8.2 %collective-permute-done.8 = bf16[512,768]{0,1:T(8,128)(2,1)S(1)} collective-permute-done((bf16[512,768]{0,1:T(8,128)(2,1)S(1)}, bf16[512,768]{0,1:T(8,128)(2,1)S(1)}, u32[]{:S(2)}, u32[]{:S(2)}) %collective-permute-start.8) | collective-permute-done | bytes 786464 | tf_op jit(solution)/shard_map/ppermute | solution.py:96
  57.2 4.2 %collective-permute-done.9 = bf16[512,768]{0,1:T(8,128)(2,1)S(1)} collective-permute-done((bf16[512,768]{0,1:T(8,128)(2,1)S(1)}, bf16[512,768]{0,1:T(8,128)(2,1)S(1)}, u32[]{:S(2)}, u32[]{:S(2)}) %collective-permute-start.9) | collective-permute-done | bytes 786464 | tf_op jit(solution)/shard_map/ppermute | solution.py:96
  61.4 1.5 %collective-permute-start.12 = (bf16[512,768]{0,1:T(8,128)(2,1)S(1)}, bf16[512,768]{0,1:T(8,128)(2,1)S(1)}, u32[]{:S(2)}, u32[]{:S(2)}) collective-permute-start(bf16[512,768]{0,1:T(8,128)(2,1)S(1)} %broadcast_select_fusion), channel_id=1, source_target_pairs={{4,6},{2,0},{5,7},{3,1},{12,14},{10,8},{13,15},{11,9},{20,22},{18,... | collective-permute-start | bytes 2359304 | tf_op jit(solution)/shard_map/ppermute | solution.py:100
  63.0 0.2 fusion.14
  63.5 0.2 fusion.10
  63.7 0.2 fusion.8
  63.9 0.6 collective-permute-start.11
  64.5 0.7 multiply_reduce_fusion.4
  65.2 0.6 fusion.80
  65.9 0.7 multiply_reduce_fusion.5
  66.6 0.6 fusion.82
  67.2 0.7 multiply_reduce_fusion.6
  68.0 0.6 fusion.84
  68.6 0.7 multiply_reduce_fusion.7
  69.3 0.6 fusion.86
  70.0 0.2 fusion.16
  70.2 0.2 fusion.18
  70.4 0.7 multiply_reduce_fusion.3
  71.2 0.6 fusion.78
  71.8 0.7 multiply_reduce_fusion.2
  72.6 1.2 %multiply_add_fusion = f32[512,768]{1,0:T(8,128)S(1)} fusion(f32[512,768]{1,0:T(8,128)S(1)} %fusion.78, f32[512,768]{1,0:T(8,128)S(1)} %fusion.80, f32[512,768]{1,0:T(8,128)S(1)} %fusion.82, f32[512,768]{1,0:T(8,128)S(1)} %fusion.84, f32[512,768]{1,0:T(8,128)S(1)} %fusion.86, f32[512,768]{1,0:T(8,128)S(1)} %fusion.88, f32[512,768]{1,0:T(8,128)S(1)} %fusion.90, ...), kind=kOutput, calls=%fused_computation.49 | convolution fusion | flops 409731072 | bytes 17039396 | tf_op jit(solution)/shard_map/dot_general | solution.py:76
  73.7 5.2 %collective-permute-done.12 = bf16[512,768]{0,1:T(8,128)(2,1)S(1)} collective-permute-done((bf16[512,768]{0,1:T(8,128)(2,1)S(1)}, bf16[512,768]{0,1:T(8,128)(2,1)S(1)}, u32[]{:S(2)}, u32[]{:S(2)}) %collective-permute-start.12) | collective-permute-done | bytes 786464 | tf_op jit(solution)/shard_map/ppermute | solution.py:100
  79.0 0.2 fusion.20
  79.2 0.7 multiply_reduce_fusion.1
  79.9 0.6 fusion.75
  80.6 0.7 collective-permute-done.13
  81.5 0.7 multiply_reduce_fusion
  82.2 1.7 %fusion.51 = bf16[1,1,512,768]{3,2,1,0:T(8,128)(2,1)} fusion(bf16[512,768]{0,1:T(8,128)(2,1)S(1)} %collective-permute-done.13, f32[512,768]{1,0:T(8,128)S(1)} %multiply_add_fusion, f32[512,768]{1,0:T(8,128)S(1)} %fusion.75, f32[512]{0:T(512)S(1)} %bitcast.50, f32[512]{0:T(512)S(1)} %add_rsqrt_fusion, f32[]{:T(128)S(6)} %convert_element_type.686, ...), kind=kOutput, calls=%fused_computation.90 | convolution fusion | flops 405405696 | bytes 5246984 | tf_op jit(solution)/shard_map/dot_general | solution.py:76
  (55 shorter events, 2.5 us)
Async XLA Ops:
  1.6 8.8 %collective-permute-start = (bf16[128,768]{1,0:T(8,128)(2,1)S(1)}, bf16[128,768]{1,0:T(8,128)(2,1)S(1)}, u32[]{:S(2)}, u32[]{:S(2)}) collective-permute-start(bf16[128,768]{1,0:T(8,128)(2,1)S(1)} %get-tuple-element.13), channel_id=1, source_target_pairs={{0,8},{8,0},{16,24},{24,16},{1,9},{9,1},{17,25},{25,17},{2,10},{10... | collective-permute-start | bytes 589832 | tf_op jit(solution)/shard_map/ppermute | solution.py:44
  4.6 10.6 %collective-permute-start.1 = (bf16[128,768]{1,0:T(8,128)(2,1)S(1)}, bf16[128,768]{1,0:T(8,128)(2,1)S(1)}, u32[]{:S(2)}, u32[]{:S(2)}) collective-permute-start(bf16[128,768]{1,0:T(8,128)(2,1)S(1)} %get-tuple-element.12), channel_id=1, source_target_pairs={{0,16},{8,24},{16,0},{24,8},{1,17},{9,25},{17,1},{25,9},{2,18},{10... | collective-permute-start | bytes 589832 | tf_op jit(solution)/shard_map/ppermute | solution.py:44
  6.1 9.3 %collective-permute-start.2 = (bf16[128,768]{1,0:T(8,128)(2,1)S(1)}, bf16[128,768]{1,0:T(8,128)(2,1)S(1)}, u32[]{:S(2)}, u32[]{:S(2)}) collective-permute-start(bf16[128,768]{1,0:T(8,128)(2,1)S(1)} %get-tuple-element.11), channel_id=1, source_target_pairs={{0,24},{8,16},{16,8},{24,0},{1,25},{9,17},{17,9},{25,1},{2,26},{10... | collective-permute-start | bytes 589832 | tf_op jit(solution)/shard_map/ppermute | solution.py:44
  15.7 23.3 %collective-permute-start.4 = (bf16[512,768]{0,1:T(8,128)(2,1)S(1)}, bf16[512,768]{0,1:T(8,128)(2,1)S(1)}, u32[]{:S(2)}, u32[]{:S(2)}) collective-permute-start(bf16[512,768]{0,1:T(8,128)(2,1)S(1)} %constant_dynamic-update-slice_fusion), channel_id=1, source_target_pairs={{0,2},{2,4},{4,6},{1,3},{3,5},{5,7},{8,10},{10,12},{12,14},{9,11},... | collective-permute-start | bytes 2359304 | tf_op jit(solution)/shard_map/ppermute | solution.py:88
  19.3 19.5 %collective-permute-start.5 = (bf16[512,768]{0,1:T(8,128)(2,1)S(1)}, bf16[512,768]{0,1:T(8,128)(2,1)S(1)}, u32[]{:S(2)}, u32[]{:S(2)}) collective-permute-start(bf16[512,768]{0,1:T(8,128)(2,1)S(1)} %constant_dynamic-update-slice_fusion), channel_id=1, source_target_pairs={{2,0},{4,2},{6,4},{3,1},{5,3},{7,5},{10,8},{12,10},{14,12},{11,9},... | collective-permute-start | bytes 2359304 | tf_op jit(solution)/shard_map/ppermute | solution.py:88
  20.8 18.5 %collective-permute-start.3 = (bf16[512,768]{0,1:T(8,128)(2,1)S(1)}, bf16[512,768]{0,1:T(8,128)(2,1)S(1)}, u32[]{:S(2)}, u32[]{:S(2)}) collective-permute-start(bf16[512,768]{0,1:T(8,128)(2,1)S(1)} %constant_dynamic-update-slice_fusion), channel_id=1, source_target_pairs={{0,1},{1,0},{2,3},{3,2},{4,5},{5,4},{6,7},{7,6},{8,9},{9,8},{10,11... | collective-permute-start | bytes 2359304 | tf_op jit(solution)/shard_map/ppermute | solution.py:89
  39.5 17.7 %collective-permute-start.8 = (bf16[512,768]{0,1:T(8,128)(2,1)S(1)}, bf16[512,768]{0,1:T(8,128)(2,1)S(1)}, u32[]{:S(2)}, u32[]{:S(2)}) collective-permute-start(bf16[512,768]{0,1:T(8,128)(2,1)S(1)} %collective-permute-done.4), channel_id=1, source_target_pairs={{0,2},{2,4},{4,6},{1,3},{3,5},{5,7},{8,10},{10,12},{12,14},{9,11},... | collective-permute-start | bytes 2359304 | tf_op jit(solution)/shard_map/ppermute | solution.py:96
  43.0 18.4 %collective-permute-start.9 = (bf16[512,768]{0,1:T(8,128)(2,1)S(1)}, bf16[512,768]{0,1:T(8,128)(2,1)S(1)}, u32[]{:S(2)}, u32[]{:S(2)}) collective-permute-start(bf16[512,768]{0,1:T(8,128)(2,1)S(1)} %collective-permute-done.5), channel_id=1, source_target_pairs={{2,0},{4,2},{6,4},{3,1},{5,3},{7,5},{10,8},{12,10},{14,12},{11,9},... | collective-permute-start | bytes 2359304 | tf_op jit(solution)/shard_map/ppermute | solution.py:96
  44.3 19.2 %collective-permute-start.7 = (bf16[512,768]{0,1:T(8,128)(2,1)S(1)}, bf16[512,768]{0,1:T(8,128)(2,1)S(1)}, u32[]{:S(2)}, u32[]{:S(2)}) collective-permute-start(bf16[512,768]{0,1:T(8,128)(2,1)S(1)} %collective-permute-done.5), channel_id=1, source_target_pairs={{0,1},{1,0},{2,3},{3,2},{4,5},{5,4},{6,7},{7,6},{8,9},{9,8},{10,11... | collective-permute-start | bytes 2359304 | tf_op jit(solution)/shard_map/ppermute | solution.py:111
  44.3 19.4 %collective-permute-start.6 = (bf16[512,768]{0,1:T(8,128)(2,1)S(1)}, bf16[512,768]{0,1:T(8,128)(2,1)S(1)}, u32[]{:S(2)}, u32[]{:S(2)}) collective-permute-start(bf16[512,768]{0,1:T(8,128)(2,1)S(1)} %collective-permute-done.4), channel_id=1, source_target_pairs={{0,1},{1,0},{2,3},{3,2},{4,5},{5,4},{6,7},{7,6},{8,9},{9,8},{10,11... | collective-permute-start | bytes 2359304 | tf_op jit(solution)/shard_map/ppermute | solution.py:110
  61.4 17.5 %collective-permute-start.12 = (bf16[512,768]{0,1:T(8,128)(2,1)S(1)}, bf16[512,768]{0,1:T(8,128)(2,1)S(1)}, u32[]{:S(2)}, u32[]{:S(2)}) collective-permute-start(bf16[512,768]{0,1:T(8,128)(2,1)S(1)} %broadcast_select_fusion), channel_id=1, source_target_pairs={{4,6},{2,0},{5,7},{3,1},{12,14},{10,8},{13,15},{11,9},{20,22},{18,... | collective-permute-start | bytes 2359304 | tf_op jit(solution)/shard_map/ppermute | solution.py:100
  62.9 7.0 %collective-permute-start.10 = (bf16[512,768]{0,1:T(8,128)(2,1)S(1)}, bf16[512,768]{0,1:T(8,128)(2,1)S(1)}, u32[]{:S(2)}, u32[]{:S(2)}) collective-permute-start(bf16[512,768]{0,1:T(8,128)(2,1)S(1)} %collective-permute-done.8), channel_id=1, source_target_pairs={{0,1},{1,0},{2,3},{3,2},{4,5},{5,4},{6,7},{7,6},{8,9},{9,8},{10,11... | collective-permute-start | bytes 2359304 | tf_op jit(solution)/shard_map/ppermute | solution.py:110
  63.9 6.2 %collective-permute-start.11 = (bf16[512,768]{0,1:T(8,128)(2,1)S(1)}, bf16[512,768]{0,1:T(8,128)(2,1)S(1)}, u32[]{:S(2)}, u32[]{:S(2)}) collective-permute-start(bf16[512,768]{0,1:T(8,128)(2,1)S(1)} %collective-permute-done.9), channel_id=1, source_target_pairs={{0,1},{1,0},{2,3},{3,2},{4,5},{5,4},{6,7},{7,6},{8,9},{9,8},{10,11... | collective-permute-start | bytes 2359304 | tf_op jit(solution)/shard_map/ppermute | solution.py:111
  79.0 2.3 %collective-permute-start.13 = (bf16[512,768]{0,1:T(8,128)(2,1)S(1)}, bf16[512,768]{0,1:T(8,128)(2,1)S(1)}, u32[]{:S(2)}, u32[]{:S(2)}) collective-permute-start(bf16[512,768]{0,1:T(8,128)(2,1)S(1)} %collective-permute-done.12), channel_id=1, source_target_pairs={{0,1},{1,0},{2,3},{3,2},{4,5},{5,4},{6,7},{7,6},{8,9},{9,8},{10,11... | collective-permute-start | bytes 2359304 | tf_op jit(solution)/shard_map/ppermute | solution.py:106

commit v15 on v14

--- a/solution.py
+++ b/solution.py
@@ -80,39 +80,39 @@
         return pair_terms(acc, got, weight)
 
     swap = [(c, (c + 1) % cores) for c in range(cores)]
-    up = [(c, c + 1) for c in range(chips - 1)]
-    down = [(c + 1, c) for c in range(chips - 1)]
+    exchange = [(z, z + 1) if z % 2 == 0 else (z, z - 1) for z in range(chips) if z % 2 or z + 1 < chips]
+    across = [(z, z - 1) if z % 2 == 0 else (z, z + 1) for z in range(chips) if (z % 2 == 0 and z >= 2) or (z % 2 and z + 1 < chips)]
+    upward = 1 - 2 * (chip % 2)
     acc = (summed, squares)
     mine = data
     other_core = (core + 1) % cores
-    received = (lax.ppermute(mine, "chip", up), lax.ppermute(mine, "chip", down))
+    received = (lax.ppermute(mine, "chip", exchange), lax.ppermute(mine, "chip", across))
     swapped = lax.ppermute(mine, "core", swap)
     acc = add_pair(acc, swapped, times_listed(chip, other_core))
     for step in range(1, chips):
         if step + 1 == chips:
             acc, received = lax.optimization_barrier((acc, received))
-        from_below, from_above = received
-        if step + 2 < chips:
-            received = (lax.ppermute(from_below, "chip", up), lax.ppermute(from_above, "chip", down))
-        elif step + 2 == chips and chips >= 4:
-            ends = [(chips - 2, chips - 1), (1, 0)]
-            outgoing = jnp.where(chip == chips - 2, from_below, from_above)
-            last = lax.ppermute(outgoing, "chip", ends)
+        by_exchange, by_across = received
+        if step + 2 < chips or (step + 2 == chips and chips < 4):
+            received = (lax.ppermute(by_across, "chip", exchange), lax.ppermute(by_exchange, "chip", across))
+        elif step + 2 == chips:
+            last = lax.ppermute(by_across, "chip", [(chips - 2, chips - 1), (1, 0)])
             received = (last, last)
-        elif step + 2 == chips:
-            received = (lax.ppermute(from_below, "chip", up), lax.ppermute(from_above, "chip", down))
         if step + 1 == chips and chips >= 4:
             far_chip = jnp.where(chip == 0, chips - 1, jnp.where(chip == chips - 1, 0, -1))
-            far_swapped = lax.ppermute(from_below, "core", swap)
-            acc = add_pair(acc, from_below, times_listed(far_chip, core))
+            far = by_exchange
+            far_swapped = lax.ppermute(far, "core", swap)
+            acc = add_pair(acc, far, times_listed(far_chip, core))
             acc = add_pair(acc, far_swapped, times_listed(far_chip, other_core))
             continue
-        below_swapped = lax.ppermute(from_below, "core", swap)
-        above_swapped = lax.ppermute(from_above, "core", swap)
-        acc = add_pair(acc, from_below, times_listed(chip - step, core))
-        acc = add_pair(acc, from_above, times_listed(chip + step, core))
-        acc = add_pair(acc, below_swapped, times_listed(chip - step, other_core))
-        acc = add_pair(acc, above_swapped, times_listed(chip + step, other_core))
+        exchange_chip = chip + upward * step
+        across_chip = chip - upward * step
+        exchange_swapped = lax.ppermute(by_exchange, "core", swap)
+        across_swapped = lax.ppermute(by_across, "core", swap)
+        acc = add_pair(acc, by_exchange, times_listed(exchange_chip, core))
+        acc = add_pair(acc, by_across, times_listed(across_chip, core))
+        acc = add_pair(acc, exchange_swapped, times_listed(exchange_chip, other_core))
+        acc = add_pair(acc, across_swapped, times_listed(across_chip, other_core))
     summed, squares = acc
     result = summed * lax.rsqrt(squares)[:, None] * live[:, None]
     return result.astype(jnp.bfloat16).reshape(1, 1, rows, width)

time: 84.2 us -> 83.8 us (level)
  starting transfers between devices: 16.9 us -> 14.8 us
  waiting for transfers between devices: 43 us -> 44.7 us
  other arithmetic: 4.34 us -> 5.51 us
  matrix products: 18 us -> 16.9 us
    ppermute x10, starting transfers between devices: 12.3 us -> 10.2 us  [the longest x1 4.41 us: per_device(): lax.ppermute(mine, 'chip', exchange)]
    ppermute x10, waiting for transfers between devices: 34.9 us -> 36.5 us  [the longest x1 14.3 us: per_device(): lax.ppermute(mine, 'chip', exchange)]
    reshape x0 -> x1, other arithmetic: none -> 1.26 us  [per_device(): return result.astype(jnp.bfloat16).reshape(1, 1, rows, width)]
    dot_general x11, matrix products: 8.48 us -> 7.37 us  [pair_terms(): jnp.dot(weights.astype(jnp.bfloat16), got, preferred_element_type=jnp.flo...]
  transfers between devices with their start and end apart: 14 -> 14, of which waited for: 7 -> 6; matrix products, arithmetic and copies ran while one was open for 22% -> 22% of each run, Pallas kernels for 0% -> 0%
where the time goes in v15:
time: 83.8 us; the launch traced here: 83.6 us
  waiting for transfers between devices  44.7 us (53%)
  matrix products  16.9 us (20%)
  starting transfers between devices  14.8 us (18%)
  other arithmetic  5.51 us (7%)
  local copies, waits for them, and re-layouts  0.97 us (1%)
    ppermute x1, waiting for transfers between devices, per_device(): lax.ppermute(mine, 'chip', exchange)  14.3 us
    ppermute x1, waiting for transfers between devices, per_device(): last = lax.ppermute(by_across, 'chip', [(chips - 2, chips - 1), (1, 0)])  11.6 us
    ppermute x1, waiting for transfers between devices, per_device(): lax.ppermute(by_across, 'chip', exchange)  9.92 us
    dot_general x12, matrix products, weigh(): scores = jnp.dot(unit_a, unit_b.T, preferred_element_type=jnp.float32)  8.86 us
    ppermute x3, waiting for transfers between devices, per_device(): lax.ppermute(outgoing, 'bucket', [(i, i ^ m) for i in range(buckets)])  8.15 us
    dot_general x11, matrix products, pair_terms(): jnp.dot(weights.astype(jnp.bfloat16), got, preferred_element_type=jnp.flo...  7.37 us
    ppermute x3, starting transfers between devices, per_device(): lax.ppermute(outgoing, 'bucket', [(i, i ^ m) for i in range(buckets)])  4.57 us
    ppermute x1, starting transfers between devices, per_device(): lax.ppermute(mine, 'chip', exchange)  4.41 us
  transfers between devices with their start and end apart: 14, of which 6 were waited for; matrix products, arithmetic and copies ran while one was open for 22% of the time, Pallas kernels for 0%

profile of v15, /device:TPU:0, one launch (start us, length us, event | category | flops | bytes accessed | tf_op | source)
XLA Modules:
  0.0 83.6 jit_solution(5128033374590526167)
XLA Ops:
  0.0 1.5 %fusion.25 = bf16[4,128,768]{2,1,0:T(8,128)(2,1)S(1)} fusion(bf16[1,1,4,128,768]{4,3,2,1,0:T(8,128)(2,1)} %param.2, s32[4]{0:T(128)} %bitcast.62, pred[768]{0:T(1024)(128)(4,1)S(1)} %iota_compare_fusion.2), kind=kLoop, calls=%fused_computation.52 | loop fusion | flops 1179648 | bytes 1573648 | tf_op jit(solution)/shard_map/jit(_where)/select_n | solution.py:40
  1.6 3.0 %collective-permute-start = (bf16[128,768]{1,0:T(8,128)(2,1)S(1)}, bf16[128,768]{1,0:T(8,128)(2,1)S(1)}, u32[]{:S(2)}, u32[]{:S(2)}) collective-permute-start(bf16[128,768]{1,0:T(8,128)(2,1)S(1)} %get-tuple-element.13), channel_id=1, source_target_pairs={{0,8},{8,0},{16,24},{24,16},{1,9},{9,1},{17,25},{25,17},{2,10},{10... | collective-permute-start | bytes 589832 | tf_op jit(solution)/shard_map/ppermute | solution.py:44
  4.6 1.5 %collective-permute-start.1 = (bf16[128,768]{1,0:T(8,128)(2,1)S(1)}, bf16[128,768]{1,0:T(8,128)(2,1)S(1)}, u32[]{:S(2)}, u32[]{:S(2)}) collective-permute-start(bf16[128,768]{1,0:T(8,128)(2,1)S(1)} %get-tuple-element.12), channel_id=1, source_target_pairs={{0,16},{8,24},{16,0},{24,8},{1,17},{9,25},{17,1},{25,9},{2,18},{10... | collective-permute-start | bytes 589832 | tf_op jit(solution)/shard_map/ppermute | solution.py:44
  6.9 3.5 %collective-permute-done = bf16[128,768]{1,0:T(8,128)(2,1)S(1)} collective-permute-done((bf16[128,768]{1,0:T(8,128)(2,1)S(1)}, bf16[128,768]{1,0:T(8,128)(2,1)S(1)}, u32[]{:S(2)}, u32[]{:S(2)}) %collective-permute-start) | collective-permute-done | bytes 196640 | tf_op jit(solution)/shard_map/ppermute | solution.py:44
  10.5 4.7 %collective-permute-done.1 = bf16[128,768]{1,0:T(8,128)(2,1)S(1)} collective-permute-done((bf16[128,768]{1,0:T(8,128)(2,1)S(1)}, bf16[128,768]{1,0:T(8,128)(2,1)S(1)}, u32[]{:S(2)}, u32[]{:S(2)}) %collective-permute-start.1) | collective-permute-done | bytes 196640 | tf_op jit(solution)/shard_map/ppermute | solution.py:44
  15.7 0.7 collective-permute-start.5
  16.4 0.2 fusion
  16.6 4.4 %collective-permute-start.4 = (bf16[512,768]{0,1:T(8,128)(2,1)S(1)}, bf16[512,768]{0,1:T(8,128)(2,1)S(1)}, u32[]{:S(2)}, u32[]{:S(2)}) collective-permute-start(bf16[512,768]{0,1:T(8,128)(2,1)S(1)} %constant_dynamic-update-slice_fusion), channel_id=1, source_target_pairs={{0,2},{2,0},{4,6},{6,4},{1,3},{3,1},{5,7},{7,5},{8,10},{10,8},{12,... | collective-permute-start | bytes 2359304 | tf_op jit(solution)/shard_map/ppermute | solution.py:89
  21.1 0.8 multiply_reduce_fusion.11
  21.9 0.6 fusion.95
  22.5 0.2 fusion.6
  22.7 14.3 %collective-permute-done.4 = bf16[512,768]{0,1:T(8,128)(2,1)S(1)} collective-permute-done((bf16[512,768]{0,1:T(8,128)(2,1)S(1)}, bf16[512,768]{0,1:T(8,128)(2,1)S(1)}, u32[]{:S(2)}, u32[]{:S(2)}) %collective-permute-start.4) | collective-permute-done | bytes 786464 | tf_op jit(solution)/shard_map/ppermute | solution.py:89
  37.2 0.2 fusion.2
  37.4 1.8 %collective-permute-start.8 = (bf16[512,768]{0,1:T(8,128)(2,1)S(1)}, bf16[512,768]{0,1:T(8,128)(2,1)S(1)}, u32[]{:S(2)}, u32[]{:S(2)}) collective-permute-start(bf16[512,768]{0,1:T(8,128)(2,1)S(1)} %collective-permute-done.5), channel_id=1, source_target_pairs={{0,2},{2,0},{4,6},{6,4},{1,3},{3,1},{5,7},{7,5},{8,10},{10,8},{12,... | collective-permute-start | bytes 2359304 | tf_op jit(solution)/shard_map/ppermute | solution.py:97
  39.2 0.7 collective-permute-start.9
  40.0 0.5 collective-permute-start.6
  40.5 0.7 multiply_reduce_fusion.8
  41.3 0.6 fusion.89
  41.9 0.7 multiply_reduce_fusion.9
  42.6 0.7 multiply_reduce_fusion.10
  43.4 0.6 fusion.91
  44.0 0.6 fusion.93
  44.6 9.9 %collective-permute-done.8 = bf16[512,768]{0,1:T(8,128)(2,1)S(1)} collective-permute-done((bf16[512,768]{0,1:T(8,128)(2,1)S(1)}, bf16[512,768]{0,1:T(8,128)(2,1)S(1)}, u32[]{:S(2)}, u32[]{:S(2)}) %collective-permute-start.8) | collective-permute-done | bytes 786464 | tf_op jit(solution)/shard_map/ppermute | solution.py:97
  55.0 0.2 fusion.10
  55.3 0.2 fusion.8
  55.5 0.6 collective-permute-start.11
  56.1 1.5 %collective-permute-start.12 = (bf16[512,768]{0,1:T(8,128)(2,1)S(1)}, bf16[512,768]{0,1:T(8,128)(2,1)S(1)}, u32[]{:S(2)}, u32[]{:S(2)}) collective-permute-start(bf16[512,768]{0,1:T(8,128)(2,1)S(1)} %collective-permute-done.9), channel_id=1, source_target_pairs={{4,6},{2,0},{5,7},{3,1},{12,14},{10,8},{13,15},{11,9},{20,22},{18,... | collective-permute-start | bytes 2359304 | tf_op jit(solution)/shard_map/ppermute | solution.py:99
  57.5 0.7 multiply_reduce_fusion.4
  58.3 0.6 fusion.81
  58.9 0.7 multiply_reduce_fusion.5
  59.6 0.6 fusion.83
  60.3 0.7 multiply_reduce_fusion.6
  61.0 0.6 fusion.85
  61.6 0.7 multiply_reduce_fusion.7
  62.4 0.6 fusion.87
  63.0 0.2 fusion.16
  63.2 0.2 fusion.18
  63.5 0.7 multiply_reduce_fusion.3
  64.2 0.6 fusion.79
  64.8 0.7 multiply_reduce_fusion.2
  65.6 1.2 %multiply_add_fusion = f32[512,768]{1,0:T(8,128)S(1)} fusion(f32[512,768]{1,0:T(8,128)S(1)} %fusion.79, f32[512,768]{1,0:T(8,128)S(1)} %fusion.81, f32[512,768]{1,0:T(8,128)S(1)} %fusion.83, f32[512,768]{1,0:T(8,128)S(1)} %fusion.85, f32[512,768]{1,0:T(8,128)S(1)} %fusion.87, f32[512,768]{1,0:T(8,128)S(1)} %fusion.89, f32[512,768]{1,0:T(8,128)S(1)} %fusion.91, ...), kind=kOutput, calls=%fused_computation.49 | convolution fusion | flops 409731072 | bytes 17039396 | tf_op jit(solution)/shard_map/dot_general | solution.py:76
  66.8 11.6 %collective-permute-done.12 = bf16[512,768]{0,1:T(8,128)(2,1)S(1)} collective-permute-done((bf16[512,768]{0,1:T(8,128)(2,1)S(1)}, bf16[512,768]{0,1:T(8,128)(2,1)S(1)}, u32[]{:S(2)}, u32[]{:S(2)}) %collective-permute-start.12) | collective-permute-done | bytes 786464 | tf_op jit(solution)/shard_map/ppermute | solution.py:99
  78.7 0.7 multiply_reduce_fusion.1
  79.4 0.6 fusion.76
  80.0 0.7 collective-permute-done.13
  81.0 0.7 multiply_reduce_fusion
  81.7 0.6 fusion.74
  82.3 1.3 %fusion.51 = bf16[1,1,512,768]{3,2,1,0:T(8,128)(2,1)} fusion(f32[512,768]{1,0:T(8,128)S(1)} %fusion.74, f32[512,768]{1,0:T(8,128)S(1)} %multiply_add_fusion, f32[512,768]{1,0:T(8,128)S(1)} %fusion.76, f32[512]{0:T(512)S(1)} %bitcast.50, f32[512]{0:T(512)S(1)} %add_rsqrt_fusion, f32[]{:T(128)S(6)} %convert_element_type.686, f32[]{:T(128)S(6)} %convert_element_type.672), kind=kLoop, calls=%fused_computation.103 | loop fusion | flops 2752512 | bytes 5509128 | tf_op jit(solution)/shard_map/reshape | solution.py:118
  (55 shorter events, 2.3 us)
Async XLA Ops:
  1.6 8.8 %collective-permute-start = (bf16[128,768]{1,0:T(8,128)(2,1)S(1)}, bf16[128,768]{1,0:T(8,128)(2,1)S(1)}, u32[]{:S(2)}, u32[]{:S(2)}) collective-permute-start(bf16[128,768]{1,0:T(8,128)(2,1)S(1)} %get-tuple-element.13), channel_id=1, source_target_pairs={{0,8},{8,0},{16,24},{24,16},{1,9},{9,1},{17,25},{25,17},{2,10},{10... | collective-permute-start | bytes 589832 | tf_op jit(solution)/shard_map/ppermute | solution.py:44
  4.6 10.6 %collective-permute-start.1 = (bf16[128,768]{1,0:T(8,128)(2,1)S(1)}, bf16[128,768]{1,0:T(8,128)(2,1)S(1)}, u32[]{:S(2)}, u32[]{:S(2)}) collective-permute-start(bf16[128,768]{1,0:T(8,128)(2,1)S(1)} %get-tuple-element.12), channel_id=1, source_target_pairs={{0,16},{8,24},{16,0},{24,8},{1,17},{9,25},{17,1},{25,9},{2,18},{10... | collective-permute-start | bytes 589832 | tf_op jit(solution)/shard_map/ppermute | solution.py:44
  6.1 9.3 %collective-permute-start.2 = (bf16[128,768]{1,0:T(8,128)(2,1)S(1)}, bf16[128,768]{1,0:T(8,128)(2,1)S(1)}, u32[]{:S(2)}, u32[]{:S(2)}) collective-permute-start(bf16[128,768]{1,0:T(8,128)(2,1)S(1)} %get-tuple-element.11), channel_id=1, source_target_pairs={{0,24},{8,16},{16,8},{24,0},{1,25},{9,17},{17,9},{25,1},{2,26},{10... | collective-permute-start | bytes 589832 | tf_op jit(solution)/shard_map/ppermute | solution.py:44
  15.7 6.8 %collective-permute-start.5 = (bf16[512,768]{0,1:T(8,128)(2,1)S(1)}, bf16[512,768]{0,1:T(8,128)(2,1)S(1)}, u32[]{:S(2)}, u32[]{:S(2)}) collective-permute-start(bf16[512,768]{0,1:T(8,128)(2,1)S(1)} %constant_dynamic-update-slice_fusion), channel_id=1, source_target_pairs={{2,4},{4,2},{3,5},{5,3},{10,12},{12,10},{11,13},{13,11},{18,20},{2... | collective-permute-start | bytes 2359304 | tf_op jit(solution)/shard_map/ppermute | solution.py:89
  16.6 20.3 %collective-permute-start.4 = (bf16[512,768]{0,1:T(8,128)(2,1)S(1)}, bf16[512,768]{0,1:T(8,128)(2,1)S(1)}, u32[]{:S(2)}, u32[]{:S(2)}) collective-permute-start(bf16[512,768]{0,1:T(8,128)(2,1)S(1)} %constant_dynamic-update-slice_fusion), channel_id=1, source_target_pairs={{0,2},{2,0},{4,6},{6,4},{1,3},{3,1},{5,7},{7,5},{8,10},{10,8},{12,... | collective-permute-start | bytes 2359304 | tf_op jit(solution)/shard_map/ppermute | solution.py:89
  21.1 16.1 %collective-permute-start.3 = (bf16[512,768]{0,1:T(8,128)(2,1)S(1)}, bf16[512,768]{0,1:T(8,128)(2,1)S(1)}, u32[]{:S(2)}, u32[]{:S(2)}) collective-permute-start(bf16[512,768]{0,1:T(8,128)(2,1)S(1)} %constant_dynamic-update-slice_fusion), channel_id=1, source_target_pairs={{0,1},{1,0},{2,3},{3,2},{4,5},{5,4},{6,7},{7,6},{8,9},{9,8},{10,11... | collective-permute-start | bytes 2359304 | tf_op jit(solution)/shard_map/ppermute | solution.py:90
  37.4 17.1 %collective-permute-start.8 = (bf16[512,768]{0,1:T(8,128)(2,1)S(1)}, bf16[512,768]{0,1:T(8,128)(2,1)S(1)}, u32[]{:S(2)}, u32[]{:S(2)}) collective-permute-start(bf16[512,768]{0,1:T(8,128)(2,1)S(1)} %collective-permute-done.5), channel_id=1, source_target_pairs={{0,2},{2,0},{4,6},{6,4},{1,3},{3,1},{5,7},{7,5},{8,10},{10,8},{12,... | collective-permute-start | bytes 2359304 | tf_op jit(solution)/shard_map/ppermute | solution.py:97
  39.2 15.5 %collective-permute-start.9 = (bf16[512,768]{0,1:T(8,128)(2,1)S(1)}, bf16[512,768]{0,1:T(8,128)(2,1)S(1)}, u32[]{:S(2)}, u32[]{:S(2)}) collective-permute-start(bf16[512,768]{0,1:T(8,128)(2,1)S(1)} %collective-permute-done.4), channel_id=1, source_target_pairs={{2,4},{4,2},{3,5},{5,3},{10,12},{12,10},{11,13},{13,11},{18,20},{2... | collective-permute-start | bytes 2359304 | tf_op jit(solution)/shard_map/ppermute | solution.py:97
  39.9 15.1 %collective-permute-start.7 = (bf16[512,768]{0,1:T(8,128)(2,1)S(1)}, bf16[512,768]{0,1:T(8,128)(2,1)S(1)}, u32[]{:S(2)}, u32[]{:S(2)}) collective-permute-start(bf16[512,768]{0,1:T(8,128)(2,1)S(1)} %collective-permute-done.5), channel_id=1, source_target_pairs={{0,1},{1,0},{2,3},{3,2},{4,5},{5,4},{6,7},{7,6},{8,9},{9,8},{10,11... | collective-permute-start | bytes 2359304 | tf_op jit(solution)/shard_map/ppermute | solution.py:111
  40.0 15.3 %collective-permute-start.6 = (bf16[512,768]{0,1:T(8,128)(2,1)S(1)}, bf16[512,768]{0,1:T(8,128)(2,1)S(1)}, u32[]{:S(2)}, u32[]{:S(2)}) collective-permute-start(bf16[512,768]{0,1:T(8,128)(2,1)S(1)} %collective-permute-done.4), channel_id=1, source_target_pairs={{0,1},{1,0},{2,3},{3,2},{4,5},{5,4},{6,7},{7,6},{8,9},{9,8},{10,11... | collective-permute-start | bytes 2359304 | tf_op jit(solution)/shard_map/ppermute | solution.py:110
  54.5 8.5 %collective-permute-start.10 = (bf16[512,768]{0,1:T(8,128)(2,1)S(1)}, bf16[512,768]{0,1:T(8,128)(2,1)S(1)}, u32[]{:S(2)}, u32[]{:S(2)}) collective-permute-start(bf16[512,768]{0,1:T(8,128)(2,1)S(1)} %collective-permute-done.8), channel_id=1, source_target_pairs={{0,1},{1,0},{2,3},{3,2},{4,5},{5,4},{6,7},{7,6},{8,9},{9,8},{10,11... | collective-permute-start | bytes 2359304 | tf_op jit(solution)/shard_map/ppermute | solution.py:110
  55.5 7.7 %collective-permute-start.11 = (bf16[512,768]{0,1:T(8,128)(2,1)S(1)}, bf16[512,768]{0,1:T(8,128)(2,1)S(1)}, u32[]{:S(2)}, u32[]{:S(2)}) collective-permute-start(bf16[512,768]{0,1:T(8,128)(2,1)S(1)} %collective-permute-done.9), channel_id=1, source_target_pairs={{0,1},{1,0},{2,3},{3,2},{4,5},{5,4},{6,7},{7,6},{8,9},{9,8},{10,11... | collective-permute-start | bytes 2359304 | tf_op jit(solution)/shard_map/ppermute | solution.py:111
  56.1 22.4 %collective-permute-start.12 = (bf16[512,768]{0,1:T(8,128)(2,1)S(1)}, bf16[512,768]{0,1:T(8,128)(2,1)S(1)}, u32[]{:S(2)}, u32[]{:S(2)}) collective-permute-start(bf16[512,768]{0,1:T(8,128)(2,1)S(1)} %collective-permute-done.9), channel_id=1, source_target_pairs={{4,6},{2,0},{5,7},{3,1},{12,14},{10,8},{13,15},{11,9},{20,22},{18,... | collective-permute-start | bytes 2359304 | tf_op jit(solution)/shard_map/ppermute | solution.py:99
  78.4 2.3 %collective-permute-start.13 = (bf16[512,768]{0,1:T(8,128)(2,1)S(1)}, bf16[512,768]{0,1:T(8,128)(2,1)S(1)}, u32[]{:S(2)}, u32[]{:S(2)}) collective-permute-start(bf16[512,768]{0,1:T(8,128)(2,1)S(1)} %collective-permute-done.12), channel_id=1, source_target_pairs={{0,1},{1,0},{2,3},{3,2},{4,5},{5,4},{6,7},{7,6},{8,9},{9,8},{10,11... | collective-permute-start | bytes 2359304 | tf_op jit(solution)/shard_map/ppermute | solution.py:104

commit v16 on v15

--- a/solution.py
+++ b/solution.py
@@ -34,13 +34,17 @@
     slot_rows = embeddings.shape[3]
     width = embeddings.shape[4]
     pieces = embeddings[0, 0]
-    slot_index = lax.broadcasted_iota(jnp.int32, pieces.shape, 1)
-    lane_index = lax.broadcasted_iota(jnp.int32, pieces.shape, 2)
-    dead = (slot_index >= counts[0, 0, :, :, None]) & (lane_index == 0)
-    marked = jnp.where(dead, jnp.bfloat16(DEAD), pieces)
-    arrived = [lax.dynamic_index_in_dim(marked, bucket, axis=0, keepdims=False)]
+    slot_index = lax.broadcasted_iota(jnp.int32, pieces.shape[1:], 0)
+    lane_index = lax.broadcasted_iota(jnp.int32, pieces.shape[1:], 1)
+
+    def marked(dest):
+        piece = lax.dynamic_index_in_dim(pieces, dest, axis=0, keepdims=False)
+        count = lax.dynamic_index_in_dim(counts[0, 0, :, 0], dest, axis=0, keepdims=False)
+        return jnp.where((slot_index >= count) & (lane_index == 0), jnp.bfloat16(DEAD), piece)
+
+    arrived = [marked(bucket)]
     for m in range(1, buckets):
-        outgoing = lax.dynamic_index_in_dim(marked, bucket ^ m, axis=0, keepdims=False)
+        outgoing = marked(bucket ^ m)
         arrived.append(lax.ppermute(outgoing, "bucket", [(i, i ^ m) for i in range(buckets)]))
     sources = buckets
     rows = sources * slot_rows

time: 83.8 us -> 87.8 us (1.048)
  other arithmetic: 5.51 us -> 8.07 us
  local copies, waits for them, and re-layouts: 0.97 us -> 2.37 us
    ge x0 -> x2, other arithmetic: none -> 2.53 us  [marked(): slot_index >= count]
    dynamic_slice x0 -> x1, local copies, waits for them, and re-layouts: none -> 1.47 us  [marked(): lax.dynamic_index_in_dim(counts[0, 0, :, 0], dest, axis=0, keepdims=False)]
  transfers between devices with their start and end apart: 14 -> 14, of which waited for: 6 -> 6; matrix products, arithmetic and copies ran while one was open for 22% -> 21% of each run, Pallas kernels for 0% -> 0%
where the time goes in v16:
time: 87.8 us; the launch traced here: 87.6 us
  waiting for transfers between devices  44.7 us (51%)
  matrix products  16.9 us (19%)
  starting transfers between devices  14.8 us (17%)
  other arithmetic  8.07 us (9%)
  local copies, waits for them, and re-layouts  2.37 us (3%)
    ppermute x1, waiting for transfers between devices, per_device(): lax.ppermute(mine, 'chip', exchange)  14.3 us
    ppermute x1, waiting for transfers between devices, per_device(): last = lax.ppermute(by_across, 'chip', [(chips - 2, chips - 1), (1, 0)])  11.6 us
    ppermute x1, waiting for transfers between devices, per_device(): lax.ppermute(by_across, 'chip', exchange)  9.92 us
    dot_general x12, matrix products, weigh(): scores = jnp.dot(unit_a, unit_b.T, preferred_element_type=jnp.float32)  8.86 us
    ppermute x3, waiting for transfers between devices, per_device(): lax.ppermute(outgoing, 'bucket', [(i, i ^ m) for i in range(buckets)])  8.15 us
    dot_general x11, matrix products, pair_terms(): jnp.dot(weights.astype(jnp.bfloat16), got, preferred_element_type=jnp.flo...  7.38 us
    ppermute x3, starting transfers between devices, per_device(): lax.ppermute(outgoing, 'bucket', [(i, i ^ m) for i in range(buckets)])  4.57 us
    ppermute x1, starting transfers between devices, per_device(): lax.ppermute(mine, 'chip', exchange)  4.41 us
  transfers between devices with their start and end apart: 14, of which 6 were waited for; matrix products, arithmetic and copies ran while one was open for 21% of the time, Pallas kernels for 0%

profile of v16, /device:TPU:0, one launch (start us, length us, event | category | flops | bytes accessed | tf_op | source)
XLA Modules:
  0.0 87.6 jit_solution(12922876918966639829)
XLA Ops:
  0.0 1.5 %constant_dynamic-slice_fusion = (s32[1,1,1,1]{2,3,1,0:T(1,128)}, s32[1,1,1,1]{2,3,1,0:T(1,128)}, s32[1,1,1,1]{2,3,1,0:T(1,128)}, s32[1,1,1,1]{2,3,1,0:T(1,128)}) fusion(s32[1,1,4,1]{2,3,1,0:T(1,128)} %param.3, s32[]{:T(128)S(6)} %select_n.297, s32[]{:T(128)S(6)} %select_n.291, s32[]{:T(128)S(6)} %select_n.288, s32[]{:T(128)S(6)} %select_n.294), kind=kLoop, calls=%fused_computation.153 | loop fusion | bytes 48 | tf_op jit(solution)/shard_map/jit(dynamic_index_in_dim)/dynamic_slice | solution.py:42
  1.5 1.3 %iota_compare_fusion.2 = (pred[128]{0:T(512)(128)(4,1)S(1)}, pred[128]{0:T(512)(128)(4,1)S(1)}) fusion(s32[]{:T(128)} %bitcast.6, s32[]{:T(128)} %bitcast.4), kind=kLoop, calls=%fused_computation.174 | loop fusion | flops 256 | bytes 264 | tf_op jit(solution)/shard_map/ge | solution.py:43
  2.8 1.3 %iota_compare_fusion.4 = (pred[128]{0:T(512)(128)(4,1)S(1)}, pred[128]{0:T(512)(128)(4,1)S(1)}) fusion(s32[]{:T(128)} %bitcast.2, s32[]{:T(128)} %bitcast), kind=kLoop, calls=%fused_computation.176 | loop fusion | flops 256 | bytes 264 | tf_op jit(solution)/shard_map/ge | solution.py:43
  4.0 1.5 %and_select_fusion = (bf16[128,768]{1,0:T(8,128)(2,1)S(1)}, bf16[128,768]{1,0:T(8,128)(2,1)S(1)}, bf16[128,768]{1,0:T(8,128)(2,1)S(1)}, bf16[128,768]{1,0:T(8,128)(2,1)S(1)}) fusion(bf16[1,1,4,128,768]{4,3,2,1,0:T(8,128)(2,1)} %param.2, s32[]{:T(128)S(6)} %select_n.297, pred[768]{0:T(1024)(128)(4,1)S(1)} %iota_compare_fusion.1, ...), kind=kLoop, calls=%fused_computation.135 | loop fusion | flops 786432 | bytes 1574160 | tf_op jit(solution)/shard_map/jit(_where)/select_n | solution.py:43
  5.6 3.0 %collective-permute-start = (bf16[128,768]{1,0:T(8,128)(2,1)S(1)}, bf16[128,768]{1,0:T(8,128)(2,1)S(1)}, u32[]{:S(2)}, u32[]{:S(2)}) collective-permute-start(bf16[128,768]{1,0:T(8,128)(2,1)S(1)} %get-tuple-element.12), channel_id=1, source_target_pairs={{0,8},{8,0},{16,24},{24,16},{1,9},{9,1},{17,25},{25,17},{2,10},{10... | collective-permute-start | bytes 589832 | tf_op jit(solution)/shard_map/ppermute | solution.py:48
  8.6 1.5 %collective-permute-start.1 = (bf16[128,768]{1,0:T(8,128)(2,1)S(1)}, bf16[128,768]{1,0:T(8,128)(2,1)S(1)}, u32[]{:S(2)}, u32[]{:S(2)}) collective-permute-start(bf16[128,768]{1,0:T(8,128)(2,1)S(1)} %get-tuple-element.14), channel_id=1, source_target_pairs={{0,16},{8,24},{16,0},{24,8},{1,17},{9,25},{17,1},{25,9},{2,18},{10... | collective-permute-start | bytes 589832 | tf_op jit(solution)/shard_map/ppermute | solution.py:48
  10.8 3.5 %collective-permute-done = bf16[128,768]{1,0:T(8,128)(2,1)S(1)} collective-permute-done((bf16[128,768]{1,0:T(8,128)(2,1)S(1)}, bf16[128,768]{1,0:T(8,128)(2,1)S(1)}, u32[]{:S(2)}, u32[]{:S(2)}) %collective-permute-start) | collective-permute-done | bytes 196640 | tf_op jit(solution)/shard_map/ppermute | solution.py:48
  14.5 4.7 %collective-permute-done.1 = bf16[128,768]{1,0:T(8,128)(2,1)S(1)} collective-permute-done((bf16[128,768]{1,0:T(8,128)(2,1)S(1)}, bf16[128,768]{1,0:T(8,128)(2,1)S(1)}, u32[]{:S(2)}, u32[]{:S(2)}) %collective-permute-start.1) | collective-permute-done | bytes 196640 | tf_op jit(solution)/shard_map/ppermute | solution.py:48
  19.7 0.7 collective-permute-start.5
  20.4 0.2 fusion
  20.6 4.4 %collective-permute-start.4 = (bf16[512,768]{0,1:T(8,128)(2,1)S(1)}, bf16[512,768]{0,1:T(8,128)(2,1)S(1)}, u32[]{:S(2)}, u32[]{:S(2)}) collective-permute-start(bf16[512,768]{0,1:T(8,128)(2,1)S(1)} %constant_dynamic-update-slice_fusion), channel_id=1, source_target_pairs={{0,2},{2,0},{4,6},{6,4},{1,3},{3,1},{5,7},{7,5},{8,10},{10,8},{12,... | collective-permute-start | bytes 2359304 | tf_op jit(solution)/shard_map/ppermute | solution.py:93
  25.0 0.8 multiply_reduce_fusion.11
  25.8 0.6 fusion.93
  26.5 0.2 fusion.6
  26.7 14.3 %collective-permute-done.4 = bf16[512,768]{0,1:T(8,128)(2,1)S(1)} collective-permute-done((bf16[512,768]{0,1:T(8,128)(2,1)S(1)}, bf16[512,768]{0,1:T(8,128)(2,1)S(1)}, u32[]{:S(2)}, u32[]{:S(2)}) %collective-permute-start.4) | collective-permute-done | bytes 786464 | tf_op jit(solution)/shard_map/ppermute | solution.py:93
  41.2 0.2 fusion.2
  41.4 1.8 %collective-permute-start.8 = (bf16[512,768]{0,1:T(8,128)(2,1)S(1)}, bf16[512,768]{0,1:T(8,128)(2,1)S(1)}, u32[]{:S(2)}, u32[]{:S(2)}) collective-permute-start(bf16[512,768]{0,1:T(8,128)(2,1)S(1)} %collective-permute-done.5), channel_id=1, source_target_pairs={{0,2},{2,0},{4,6},{6,4},{1,3},{3,1},{5,7},{7,5},{8,10},{10,8},{12,... | collective-permute-start | bytes 2359304 | tf_op jit(solution)/shard_map/ppermute | solution.py:101
  43.2 0.7 collective-permute-start.9
  44.0 0.5 collective-permute-start.6
  44.5 0.7 multiply_reduce_fusion.8
  45.2 0.6 fusion.87
  45.9 0.7 multiply_reduce_fusion.9
  46.6 0.7 multiply_reduce_fusion.10
  47.3 0.6 fusion.89
  48.0 0.6 fusion.91
  48.6 9.9 %collective-permute-done.8 = bf16[512,768]{0,1:T(8,128)(2,1)S(1)} collective-permute-done((bf16[512,768]{0,1:T(8,128)(2,1)S(1)}, bf16[512,768]{0,1:T(8,128)(2,1)S(1)}, u32[]{:S(2)}, u32[]{:S(2)}) %collective-permute-start.8) | collective-permute-done | bytes 786464 | tf_op jit(solution)/shard_map/ppermute | solution.py:101
  59.0 0.2 fusion.10
  59.5 0.6 collective-permute-start.11
  60.0 1.5 %collective-permute-start.12 = (bf16[512,768]{0,1:T(8,128)(2,1)S(1)}, bf16[512,768]{0,1:T(8,128)(2,1)S(1)}, u32[]{:S(2)}, u32[]{:S(2)}) collective-permute-start(bf16[512,768]{0,1:T(8,128)(2,1)S(1)} %collective-permute-done.9), channel_id=1, source_target_pairs={{4,6},{2,0},{5,7},{3,1},{12,14},{10,8},{13,15},{11,9},{20,22},{18,... | collective-permute-start | bytes 2359304 | tf_op jit(solution)/shard_map/ppermute | solution.py:103
  61.5 0.7 multiply_reduce_fusion.4
  62.2 0.6 fusion.79
  62.9 0.7 multiply_reduce_fusion.5
  63.6 0.6 fusion.81
  64.2 0.7 multiply_reduce_fusion.6
  65.0 0.6 fusion.83
  65.6 0.7 multiply_reduce_fusion.7
  66.3 0.6 fusion.85
  67.4 0.7 multiply_reduce_fusion.3
  68.2 0.6 fusion.77
  68.8 0.7 multiply_reduce_fusion.2
  69.6 1.2 %multiply_add_fusion = f32[512,768]{1,0:T(8,128)S(1)} fusion(f32[512,768]{1,0:T(8,128)S(1)} %fusion.77, f32[512,768]{1,0:T(8,128)S(1)} %fusion.79, f32[512,768]{1,0:T(8,128)S(1)} %fusion.81, f32[512,768]{1,0:T(8,128)S(1)} %fusion.83, f32[512,768]{1,0:T(8,128)S(1)} %fusion.85, f32[512,768]{1,0:T(8,128)S(1)} %fusion.87, f32[512,768]{1,0:T(8,128)S(1)} %fusion.89, ...), kind=kOutput, calls=%fused_computation.49 | convolution fusion | flops 409731072 | bytes 17039396 | tf_op jit(solution)/shard_map/dot_general | solution.py:80
  70.8 11.6 %collective-permute-done.12 = bf16[512,768]{0,1:T(8,128)(2,1)S(1)} collective-permute-done((bf16[512,768]{0,1:T(8,128)(2,1)S(1)}, bf16[512,768]{0,1:T(8,128)(2,1)S(1)}, u32[]{:S(2)}, u32[]{:S(2)}) %collective-permute-start.12) | collective-permute-done | bytes 786464 | tf_op jit(solution)/shard_map/ppermute | solution.py:103
  82.6 0.7 multiply_reduce_fusion.1
  83.4 0.6 fusion.74
  84.0 0.7 collective-permute-done.13
  84.9 0.7 multiply_reduce_fusion
  85.7 0.6 fusion.72
  86.3 1.3 %fusion.49 = bf16[1,1,512,768]{3,2,1,0:T(8,128)(2,1)} fusion(f32[512,768]{1,0:T(8,128)S(1)} %fusion.72, f32[512,768]{1,0:T(8,128)S(1)} %multiply_add_fusion, f32[512,768]{1,0:T(8,128)S(1)} %fusion.74, f32[512]{0:T(512)S(1)} %bitcast.51, f32[512]{0:T(512)S(1)} %add_rsqrt_fusion, f32[]{:T(128)S(6)} %convert_element_type.686, f32[]{:T(128)S(6)} %convert_element_type.672), kind=kLoop, calls=%fused_computation.100 | loop fusion | flops 2752512 | bytes 5509128 | tf_op jit(solution)/shard_map/reshape | solution.py:122
  (57 shorter events, 2.9 us)
Async XLA Ops:
  5.6 8.8 %collective-permute-start = (bf16[128,768]{1,0:T(8,128)(2,1)S(1)}, bf16[128,768]{1,0:T(8,128)(2,1)S(1)}, u32[]{:S(2)}, u32[]{:S(2)}) collective-permute-start(bf16[128,768]{1,0:T(8,128)(2,1)S(1)} %get-tuple-element.12), channel_id=1, source_target_pairs={{0,8},{8,0},{16,24},{24,16},{1,9},{9,1},{17,25},{25,17},{2,10},{10... | collective-permute-start | bytes 589832 | tf_op jit(solution)/shard_map/ppermute | solution.py:48
  8.6 10.6 %collective-permute-start.1 = (bf16[128,768]{1,0:T(8,128)(2,1)S(1)}, bf16[128,768]{1,0:T(8,128)(2,1)S(1)}, u32[]{:S(2)}, u32[]{:S(2)}) collective-permute-start(bf16[128,768]{1,0:T(8,128)(2,1)S(1)} %get-tuple-element.14), channel_id=1, source_target_pairs={{0,16},{8,24},{16,0},{24,8},{1,17},{9,25},{17,1},{25,9},{2,18},{10... | collective-permute-start | bytes 589832 | tf_op jit(solution)/shard_map/ppermute | solution.py:48
  10.1 9.3 %collective-permute-start.2 = (bf16[128,768]{1,0:T(8,128)(2,1)S(1)}, bf16[128,768]{1,0:T(8,128)(2,1)S(1)}, u32[]{:S(2)}, u32[]{:S(2)}) collective-permute-start(bf16[128,768]{1,0:T(8,128)(2,1)S(1)} %get-tuple-element.11), channel_id=1, source_target_pairs={{0,24},{8,16},{16,8},{24,0},{1,25},{9,17},{17,9},{25,1},{2,26},{10... | collective-permute-start | bytes 589832 | tf_op jit(solution)/shard_map/ppermute | solution.py:48
  19.7 6.8 %collective-permute-start.5 = (bf16[512,768]{0,1:T(8,128)(2,1)S(1)}, bf16[512,768]{0,1:T(8,128)(2,1)S(1)}, u32[]{:S(2)}, u32[]{:S(2)}) collective-permute-start(bf16[512,768]{0,1:T(8,128)(2,1)S(1)} %constant_dynamic-update-slice_fusion), channel_id=1, source_target_pairs={{2,4},{4,2},{3,5},{5,3},{10,12},{12,10},{11,13},{13,11},{18,20},{2... | collective-permute-start | bytes 2359304 | tf_op jit(solution)/shard_map/ppermute | solution.py:93
  20.6 20.3 %collective-permute-start.4 = (bf16[512,768]{0,1:T(8,128)(2,1)S(1)}, bf16[512,768]{0,1:T(8,128)(2,1)S(1)}, u32[]{:S(2)}, u32[]{:S(2)}) collective-permute-start(bf16[512,768]{0,1:T(8,128)(2,1)S(1)} %constant_dynamic-update-slice_fusion), channel_id=1, source_target_pairs={{0,2},{2,0},{4,6},{6,4},{1,3},{3,1},{5,7},{7,5},{8,10},{10,8},{12,... | collective-permute-start | bytes 2359304 | tf_op jit(solution)/shard_map/ppermute | solution.py:93
  25.0 16.1 %collective-permute-start.3 = (bf16[512,768]{0,1:T(8,128)(2,1)S(1)}, bf16[512,768]{0,1:T(8,128)(2,1)S(1)}, u32[]{:S(2)}, u32[]{:S(2)}) collective-permute-start(bf16[512,768]{0,1:T(8,128)(2,1)S(1)} %constant_dynamic-update-slice_fusion), channel_id=1, source_target_pairs={{0,1},{1,0},{2,3},{3,2},{4,5},{5,4},{6,7},{7,6},{8,9},{9,8},{10,11... | collective-permute-start | bytes 2359304 | tf_op jit(solution)/shard_map/ppermute | solution.py:94
  41.4 17.1 %collective-permute-start.8 = (bf16[512,768]{0,1:T(8,128)(2,1)S(1)}, bf16[512,768]{0,1:T(8,128)(2,1)S(1)}, u32[]{:S(2)}, u32[]{:S(2)}) collective-permute-start(bf16[512,768]{0,1:T(8,128)(2,1)S(1)} %collective-permute-done.5), channel_id=1, source_target_pairs={{0,2},{2,0},{4,6},{6,4},{1,3},{3,1},{5,7},{7,5},{8,10},{10,8},{12,... | collective-permute-start | bytes 2359304 | tf_op jit(solution)/shard_map/ppermute | solution.py:101
  43.2 15.5 %collective-permute-start.9 = (bf16[512,768]{0,1:T(8,128)(2,1)S(1)}, bf16[512,768]{0,1:T(8,128)(2,1)S(1)}, u32[]{:S(2)}, u32[]{:S(2)}) collective-permute-start(bf16[512,768]{0,1:T(8,128)(2,1)S(1)} %collective-permute-done.4), channel_id=1, source_target_pairs={{2,4},{4,2},{3,5},{5,3},{10,12},{12,10},{11,13},{13,11},{18,20},{2... | collective-permute-start | bytes 2359304 | tf_op jit(solution)/shard_map/ppermute | solution.py:101
  43.9 15.1 %collective-permute-start.7 = (bf16[512,768]{0,1:T(8,128)(2,1)S(1)}, bf16[512,768]{0,1:T(8,128)(2,1)S(1)}, u32[]{:S(2)}, u32[]{:S(2)}) collective-permute-start(bf16[512,768]{0,1:T(8,128)(2,1)S(1)} %collective-permute-done.5), channel_id=1, source_target_pairs={{0,1},{1,0},{2,3},{3,2},{4,5},{5,4},{6,7},{7,6},{8,9},{9,8},{10,11... | collective-permute-start | bytes 2359304 | tf_op jit(solution)/shard_map/ppermute | solution.py:115
  44.0 15.3 %collective-permute-start.6 = (bf16[512,768]{0,1:T(8,128)(2,1)S(1)}, bf16[512,768]{0,1:T(8,128)(2,1)S(1)}, u32[]{:S(2)}, u32[]{:S(2)}) collective-permute-start(bf16[512,768]{0,1:T(8,128)(2,1)S(1)} %collective-permute-done.4), channel_id=1, source_target_pairs={{0,1},{1,0},{2,3},{3,2},{4,5},{5,4},{6,7},{7,6},{8,9},{9,8},{10,11... | collective-permute-start | bytes 2359304 | tf_op jit(solution)/shard_map/ppermute | solution.py:114
  58.5 8.5 %collective-permute-start.10 = (bf16[512,768]{0,1:T(8,128)(2,1)S(1)}, bf16[512,768]{0,1:T(8,128)(2,1)S(1)}, u32[]{:S(2)}, u32[]{:S(2)}) collective-permute-start(bf16[512,768]{0,1:T(8,128)(2,1)S(1)} %collective-permute-done.8), channel_id=1, source_target_pairs={{0,1},{1,0},{2,3},{3,2},{4,5},{5,4},{6,7},{7,6},{8,9},{9,8},{10,11... | collective-permute-start | bytes 2359304 | tf_op jit(solution)/shard_map/ppermute | solution.py:114
  59.5 7.7 %collective-permute-start.11 = (bf16[512,768]{0,1:T(8,128)(2,1)S(1)}, bf16[512,768]{0,1:T(8,128)(2,1)S(1)}, u32[]{:S(2)}, u32[]{:S(2)}) collective-permute-start(bf16[512,768]{0,1:T(8,128)(2,1)S(1)} %collective-permute-done.9), channel_id=1, source_target_pairs={{0,1},{1,0},{2,3},{3,2},{4,5},{5,4},{6,7},{7,6},{8,9},{9,8},{10,11... | collective-permute-start | bytes 2359304 | tf_op jit(solution)/shard_map/ppermute | solution.py:115
  60.0 22.4 %collective-permute-start.12 = (bf16[512,768]{0,1:T(8,128)(2,1)S(1)}, bf16[512,768]{0,1:T(8,128)(2,1)S(1)}, u32[]{:S(2)}, u32[]{:S(2)}) collective-permute-start(bf16[512,768]{0,1:T(8,128)(2,1)S(1)} %collective-permute-done.9), channel_id=1, source_target_pairs={{4,6},{2,0},{5,7},{3,1},{12,14},{10,8},{13,15},{11,9},{20,22},{18,... | collective-permute-start | bytes 2359304 | tf_op jit(solution)/shard_map/ppermute | solution.py:103
  82.4 2.3 %collective-permute-start.13 = (bf16[512,768]{0,1:T(8,128)(2,1)S(1)}, bf16[512,768]{0,1:T(8,128)(2,1)S(1)}, u32[]{:S(2)}, u32[]{:S(2)}) collective-permute-start(bf16[512,768]{0,1:T(8,128)(2,1)S(1)} %collective-permute-done.12), channel_id=1, source_target_pairs={{0,1},{1,0},{2,3},{3,2},{4,5},{5,4},{6,7},{7,6},{8,9},{9,8},{10,11... | collective-permute-start | bytes 2359304 | tf_op jit(solution)/shard_map/ppermute | solution.py:108

commit v17 on v15

--- a/solution.py
+++ b/solution.py
@@ -90,7 +90,7 @@
     swapped = lax.ppermute(mine, "core", swap)
     acc = add_pair(acc, swapped, times_listed(chip, other_core))
     for step in range(1, chips):
-        if step + 1 == chips:
+        if step > 1:
             acc, received = lax.optimization_barrier((acc, received))
         by_exchange, by_across = received
         if step + 2 < chips or (step + 2 == chips and chips < 4):

time: 83.8 us -> 86.3 us (1.030)
  waiting for transfers between devices: 44.7 us -> 46.8 us
  other arithmetic: 5.51 us -> 4.17 us
  matrix products: 16.9 us -> 17.8 us
    ppermute x1, starting transfers between devices: 1.8 us -> 5.11 us  [per_device(): lax.ppermute(by_across, 'chip', exchange)]
    ppermute x1, waiting for transfers between devices: 11.6 us -> 14.9 us  [per_device(): last = lax.ppermute(by_across, 'chip', [(chips - 2, chips - 1), (1, 0)])]
    ppermute x1, starting transfers between devices: 4.41 us -> 1.64 us  [per_device(): lax.ppermute(mine, 'chip', exchange)]
    reshape x1 -> x0, other arithmetic: 1.26 us -> none  [per_device(): return result.astype(jnp.bfloat16).reshape(1, 1, rows, width)]
    dot_general x11, matrix products: 7.37 us -> 8.38 us  [pair_terms(): jnp.dot(weights.astype(jnp.bfloat16), got, preferred_element_type=jnp.flo...]
    reduce_sum x12 -> x11, other arithmetic: 2.57 us -> 2.48 us  [normalize(): jnp.sum(values * values, axis=-1, keepdims=True) + EPS]
  transfers between devices with their start and end apart: 14 -> 14, of which waited for: 6 -> 6; matrix products, arithmetic and copies ran while one was open for 22% -> 21% of each run, Pallas kernels for 0% -> 0%
where the time goes in v17:
time: 86.3 us; the launch traced here: 86.1 us
  waiting for transfers between devices  46.8 us (54%)
  matrix products  17.8 us (21%)
  starting transfers between devices  15.6 us (18%)
  other arithmetic  4.17 us (5%)
  local copies, waits for them, and re-layouts  0.97 us (1%)
    ppermute x1, waiting for transfers between devices, per_device(): last = lax.ppermute(by_across, 'chip', [(chips - 2, chips - 1), (1, 0)])  14.9 us
    ppermute x1, waiting for transfers between devices, per_device(): lax.ppermute(mine, 'chip', exchange)  13.7 us
    ppermute x1, waiting for transfers between devices, per_device(): lax.ppermute(by_across, 'chip', exchange)  9.38 us
    dot_general x12, matrix products, weigh(): scores = jnp.dot(unit_a, unit_b.T, preferred_element_type=jnp.float32)  8.85 us
    dot_general x11, matrix products, pair_terms(): jnp.dot(weights.astype(jnp.bfloat16), got, preferred_element_type=jnp.flo...  8.38 us
    ppermute x3, waiting for transfers between devices, per_device(): lax.ppermute(outgoing, 'bucket', [(i, i ^ m) for i in range(buckets)])  8.15 us
    ppermute x1, starting transfers between devices, per_device(): lax.ppermute(by_across, 'chip', exchange)  5.11 us
    ppermute x3, starting transfers between devices, per_device(): lax.ppermute(outgoing, 'bucket', [(i, i ^ m) for i in range(buckets)])  4.57 us
  transfers between devices with their start and end apart: 14, of which 6 were waited for; matrix products, arithmetic and copies ran while one was open for 21% of the time, Pallas kernels for 0%

profile of v17, /device:TPU:0, one launch (start us, length us, event | category | flops | bytes accessed | tf_op | source)
XLA Modules:
  0.0 86.1 jit_solution(2083965710471627920)
XLA Ops:
  0.0 1.5 %fusion.25 = bf16[4,128,768]{2,1,0:T(8,128)(2,1)S(1)} fusion(bf16[1,1,4,128,768]{4,3,2,1,0:T(8,128)(2,1)} %param.2, s32[4]{0:T(128)} %bitcast.62, pred[768]{0:T(1024)(128)(4,1)S(1)} %iota_compare_fusion.2), kind=kLoop, calls=%fused_computation.53 | loop fusion | flops 1179648 | bytes 1573648 | tf_op jit(solution)/shard_map/jit(_where)/select_n | solution.py:40
  1.6 3.0 %collective-permute-start = (bf16[128,768]{1,0:T(8,128)(2,1)S(1)}, bf16[128,768]{1,0:T(8,128)(2,1)S(1)}, u32[]{:S(2)}, u32[]{:S(2)}) collective-permute-start(bf16[128,768]{1,0:T(8,128)(2,1)S(1)} %get-tuple-element.21), channel_id=1, source_target_pairs={{0,8},{8,0},{16,24},{24,16},{1,9},{9,1},{17,25},{25,17},{2,10},{10... | collective-permute-start | bytes 589832 | tf_op jit(solution)/shard_map/ppermute | solution.py:44
  4.6 1.5 %collective-permute-start.1 = (bf16[128,768]{1,0:T(8,128)(2,1)S(1)}, bf16[128,768]{1,0:T(8,128)(2,1)S(1)}, u32[]{:S(2)}, u32[]{:S(2)}) collective-permute-start(bf16[128,768]{1,0:T(8,128)(2,1)S(1)} %get-tuple-element.20), channel_id=1, source_target_pairs={{0,16},{8,24},{16,0},{24,8},{1,17},{9,25},{17,1},{25,9},{2,18},{10... | collective-permute-start | bytes 589832 | tf_op jit(solution)/shard_map/ppermute | solution.py:44
  6.9 3.5 %collective-permute-done = bf16[128,768]{1,0:T(8,128)(2,1)S(1)} collective-permute-done((bf16[128,768]{1,0:T(8,128)(2,1)S(1)}, bf16[128,768]{1,0:T(8,128)(2,1)S(1)}, u32[]{:S(2)}, u32[]{:S(2)}) %collective-permute-start) | collective-permute-done | bytes 196640 | tf_op jit(solution)/shard_map/ppermute | solution.py:44
  10.5 4.7 %collective-permute-done.1 = bf16[128,768]{1,0:T(8,128)(2,1)S(1)} collective-permute-done((bf16[128,768]{1,0:T(8,128)(2,1)S(1)}, bf16[128,768]{1,0:T(8,128)(2,1)S(1)}, u32[]{:S(2)}, u32[]{:S(2)}) %collective-permute-start.1) | collective-permute-done | bytes 196640 | tf_op jit(solution)/shard_map/ppermute | solution.py:44
  15.7 1.6 %collective-permute-start.4 = (bf16[512,768]{0,1:T(8,128)(2,1)S(1)}, bf16[512,768]{0,1:T(8,128)(2,1)S(1)}, u32[]{:S(2)}, u32[]{:S(2)}) collective-permute-start(bf16[512,768]{0,1:T(8,128)(2,1)S(1)} %constant_dynamic-update-slice_fusion), channel_id=1, source_target_pairs={{0,2},{2,0},{4,6},{6,4},{1,3},{3,1},{5,7},{7,5},{8,10},{10,8},{12,... | collective-permute-start | bytes 2359304 | tf_op jit(solution)/shard_map/ppermute | solution.py:89
  17.6 0.7 collective-permute-start.5
  18.4 0.8 multiply_reduce_fusion.11
  19.2 0.6 fusion.93
  19.8 0.2 fusion.6
  20.0 13.7 %collective-permute-done.4 = bf16[512,768]{0,1:T(8,128)(2,1)S(1)} collective-permute-done((bf16[512,768]{0,1:T(8,128)(2,1)S(1)}, bf16[512,768]{0,1:T(8,128)(2,1)S(1)}, u32[]{:S(2)}, u32[]{:S(2)}) %collective-permute-start.4) | collective-permute-done | bytes 786464 | tf_op jit(solution)/shard_map/ppermute | solution.py:89
  34.0 0.2 fusion.2
  34.2 0.6 collective-permute-start.7
  34.7 5.1 %collective-permute-start.8 = (bf16[512,768]{0,1:T(8,128)(2,1)S(1)}, bf16[512,768]{0,1:T(8,128)(2,1)S(1)}, u32[]{:S(2)}, u32[]{:S(2)}) collective-permute-start(bf16[512,768]{0,1:T(8,128)(2,1)S(1)} %collective-permute-done.5), channel_id=1, source_target_pairs={{0,2},{2,0},{4,6},{6,4},{1,3},{3,1},{5,7},{7,5},{8,10},{10,8},{12,... | collective-permute-start | bytes 2359304 | tf_op jit(solution)/shard_map/ppermute | solution.py:97
  39.9 0.9 %collective-permute-start.9 = (bf16[512,768]{0,1:T(8,128)(2,1)S(1)}, bf16[512,768]{0,1:T(8,128)(2,1)S(1)}, u32[]{:S(2)}, u32[]{:S(2)}) collective-permute-start(bf16[512,768]{0,1:T(8,128)(2,1)S(1)} %collective-permute-done.4), channel_id=1, source_target_pairs={{2,4},{4,2},{3,5},{5,3},{10,12},{12,10},{11,13},{13,11},{18,20},{2... | collective-permute-start | bytes 2359304 | tf_op jit(solution)/shard_map/ppermute | solution.py:97
  40.7 0.7 multiply_reduce_fusion.8
  41.5 0.6 fusion.87
  42.1 0.7 multiply_reduce_fusion.9
  42.8 0.6 fusion.89
  43.5 0.7 multiply_reduce_fusion.10
  44.2 0.6 fusion.91
  44.8 0.2 fusion.8
  45.1 0.2 fusion.10
  45.3 0.7 multiply_reduce_fusion.7
  46.1 0.7 multiply_reduce_fusion.6
  46.8 0.6 fusion.85
  47.4 0.8 multiply_add_fusion.1
  48.3 9.4 %collective-permute-done.8 = bf16[512,768]{0,1:T(8,128)(2,1)S(1)} collective-permute-done((bf16[512,768]{0,1:T(8,128)(2,1)S(1)}, bf16[512,768]{0,1:T(8,128)(2,1)S(1)}, u32[]{:S(2)}, u32[]{:S(2)}) %collective-permute-start.8) | collective-permute-done | bytes 786464 | tf_op jit(solution)/shard_map/ppermute | solution.py:97
  57.6 0.5 collective-permute-start.10
  58.2 0.3 fusion.12
  58.5 1.5 %collective-permute-start.12 = (bf16[512,768]{0,1:T(8,128)(2,1)S(1)}, bf16[512,768]{0,1:T(8,128)(2,1)S(1)}, u32[]{:S(2)}, u32[]{:S(2)}) collective-permute-start(bf16[512,768]{0,1:T(8,128)(2,1)S(1)} %collective-permute-done.9), channel_id=1, source_target_pairs={{4,6},{2,0},{5,7},{3,1},{12,14},{10,8},{13,15},{11,9},{20,22},{18,... | collective-permute-start | bytes 2359304 | tf_op jit(solution)/shard_map/ppermute | solution.py:99
  60.0 0.7 multiply_reduce_fusion.5
  60.8 0.7 multiply_reduce_fusion.4
  61.5 0.6 fusion.82
  62.1 0.2 fusion.18
  62.4 0.2 fusion.16
  62.6 0.7 multiply_reduce_fusion.2
  63.4 0.6 fusion.77
  64.0 0.7 multiply_reduce_fusion.3
  64.7 0.6 fusion.79
  65.4 0.9 multiply_add_fusion
  66.2 14.9 %collective-permute-done.12 = bf16[512,768]{0,1:T(8,128)(2,1)S(1)} collective-permute-done((bf16[512,768]{0,1:T(8,128)(2,1)S(1)}, bf16[512,768]{0,1:T(8,128)(2,1)S(1)}, u32[]{:S(2)}, u32[]{:S(2)}) %collective-permute-start.12) | collective-permute-done | bytes 786464 | tf_op jit(solution)/shard_map/ppermute | solution.py:99
  81.1 0.2 fusion.20
  81.4 0.7 multiply_reduce_fusion.1
  82.1 0.6 fusion.75
  82.7 0.7 collective-permute-done.13
  83.6 0.7 multiply_reduce_fusion
  84.4 1.8 %fusion.51 = bf16[1,1,512,768]{3,2,1,0:T(8,128)(2,1)} fusion(bf16[512,768]{0,1:T(8,128)(2,1)S(1)} %collective-permute-done.13, f32[512,768]{1,0:T(8,128)S(1)} %multiply_add_fusion, f32[512,768]{1,0:T(8,128)S(1)} %fusion.75, f32[512]{0:T(512)S(1)} %bitcast.50, f32[512]{0:T(512)S(1)} %add_rsqrt_fusion, f32[]{:T(128)S(6)} %convert_element_type.686, ...), kind=kOutput, calls=%fused_computation.91 | convolution fusion | flops 405405696 | bytes 5246984 | tf_op jit(solution)/shard_map/dot_general | solution.py:76
  (53 shorter events, 1.9 us)
Async XLA Ops:
  1.6 8.8 %collective-permute-start = (bf16[128,768]{1,0:T(8,128)(2,1)S(1)}, bf16[128,768]{1,0:T(8,128)(2,1)S(1)}, u32[]{:S(2)}, u32[]{:S(2)}) collective-permute-start(bf16[128,768]{1,0:T(8,128)(2,1)S(1)} %get-tuple-element.21), channel_id=1, source_target_pairs={{0,8},{8,0},{16,24},{24,16},{1,9},{9,1},{17,25},{25,17},{2,10},{10... | collective-permute-start | bytes 589832 | tf_op jit(solution)/shard_map/ppermute | solution.py:44
  4.6 10.6 %collective-permute-start.1 = (bf16[128,768]{1,0:T(8,128)(2,1)S(1)}, bf16[128,768]{1,0:T(8,128)(2,1)S(1)}, u32[]{:S(2)}, u32[]{:S(2)}) collective-permute-start(bf16[128,768]{1,0:T(8,128)(2,1)S(1)} %get-tuple-element.20), channel_id=1, source_target_pairs={{0,16},{8,24},{16,0},{24,8},{1,17},{9,25},{17,1},{25,9},{2,18},{10... | collective-permute-start | bytes 589832 | tf_op jit(solution)/shard_map/ppermute | solution.py:44
  6.1 9.3 %collective-permute-start.2 = (bf16[128,768]{1,0:T(8,128)(2,1)S(1)}, bf16[128,768]{1,0:T(8,128)(2,1)S(1)}, u32[]{:S(2)}, u32[]{:S(2)}) collective-permute-start(bf16[128,768]{1,0:T(8,128)(2,1)S(1)} %get-tuple-element.19), channel_id=1, source_target_pairs={{0,24},{8,16},{16,8},{24,0},{1,25},{9,17},{17,9},{25,1},{2,26},{10... | collective-permute-start | bytes 589832 | tf_op jit(solution)/shard_map/ppermute | solution.py:44
  15.7 18.0 %collective-permute-start.4 = (bf16[512,768]{0,1:T(8,128)(2,1)S(1)}, bf16[512,768]{0,1:T(8,128)(2,1)S(1)}, u32[]{:S(2)}, u32[]{:S(2)}) collective-permute-start(bf16[512,768]{0,1:T(8,128)(2,1)S(1)} %constant_dynamic-update-slice_fusion), channel_id=1, source_target_pairs={{0,2},{2,0},{4,6},{6,4},{1,3},{3,1},{5,7},{7,5},{8,10},{10,8},{12,... | collective-permute-start | bytes 2359304 | tf_op jit(solution)/shard_map/ppermute | solution.py:89
  17.6 2.2 %collective-permute-start.5 = (bf16[512,768]{0,1:T(8,128)(2,1)S(1)}, bf16[512,768]{0,1:T(8,128)(2,1)S(1)}, u32[]{:S(2)}, u32[]{:S(2)}) collective-permute-start(bf16[512,768]{0,1:T(8,128)(2,1)S(1)} %constant_dynamic-update-slice_fusion), channel_id=1, source_target_pairs={{2,4},{4,2},{3,5},{5,3},{10,12},{12,10},{11,13},{13,11},{18,20},{2... | collective-permute-start | bytes 2359304 | tf_op jit(solution)/shard_map/ppermute | solution.py:89
  18.3 15.7 %collective-permute-start.3 = (bf16[512,768]{0,1:T(8,128)(2,1)S(1)}, bf16[512,768]{0,1:T(8,128)(2,1)S(1)}, u32[]{:S(2)}, u32[]{:S(2)}) collective-permute-start(bf16[512,768]{0,1:T(8,128)(2,1)S(1)} %constant_dynamic-update-slice_fusion), channel_id=1, source_target_pairs={{0,1},{1,0},{2,3},{3,2},{4,5},{5,4},{6,7},{7,6},{8,9},{9,8},{10,11... | collective-permute-start | bytes 2359304 | tf_op jit(solution)/shard_map/ppermute | solution.py:90
  33.7 11.1 %collective-permute-start.6 = (bf16[512,768]{0,1:T(8,128)(2,1)S(1)}, bf16[512,768]{0,1:T(8,128)(2,1)S(1)}, u32[]{:S(2)}, u32[]{:S(2)}) collective-permute-start(bf16[512,768]{0,1:T(8,128)(2,1)S(1)} %collective-permute-done.4), channel_id=1, source_target_pairs={{0,1},{1,0},{2,3},{3,2},{4,5},{5,4},{6,7},{7,6},{8,9},{9,8},{10,11... | collective-permute-start | bytes 2359304 | tf_op jit(solution)/shard_map/ppermute | solution.py:110
  34.2 10.9 %collective-permute-start.7 = (bf16[512,768]{0,1:T(8,128)(2,1)S(1)}, bf16[512,768]{0,1:T(8,128)(2,1)S(1)}, u32[]{:S(2)}, u32[]{:S(2)}) collective-permute-start(bf16[512,768]{0,1:T(8,128)(2,1)S(1)} %collective-permute-done.5), channel_id=1, source_target_pairs={{0,1},{1,0},{2,3},{3,2},{4,5},{5,4},{6,7},{7,6},{8,9},{9,8},{10,11... | collective-permute-start | bytes 2359304 | tf_op jit(solution)/shard_map/ppermute | solution.py:111
  34.7 22.9 %collective-permute-start.8 = (bf16[512,768]{0,1:T(8,128)(2,1)S(1)}, bf16[512,768]{0,1:T(8,128)(2,1)S(1)}, u32[]{:S(2)}, u32[]{:S(2)}) collective-permute-start(bf16[512,768]{0,1:T(8,128)(2,1)S(1)} %collective-permute-done.5), channel_id=1, source_target_pairs={{0,2},{2,0},{4,6},{6,4},{1,3},{3,1},{5,7},{7,5},{8,10},{10,8},{12,... | collective-permute-start | bytes 2359304 | tf_op jit(solution)/shard_map/ppermute | solution.py:97
  39.9 17.8 %collective-permute-start.9 = (bf16[512,768]{0,1:T(8,128)(2,1)S(1)}, bf16[512,768]{0,1:T(8,128)(2,1)S(1)}, u32[]{:S(2)}, u32[]{:S(2)}) collective-permute-start(bf16[512,768]{0,1:T(8,128)(2,1)S(1)} %collective-permute-done.4), channel_id=1, source_target_pairs={{2,4},{4,2},{3,5},{5,3},{10,12},{12,10},{11,13},{13,11},{18,20},{2... | collective-permute-start | bytes 2359304 | tf_op jit(solution)/shard_map/ppermute | solution.py:97
  57.6 4.5 %collective-permute-start.11 = (bf16[512,768]{0,1:T(8,128)(2,1)S(1)}, bf16[512,768]{0,1:T(8,128)(2,1)S(1)}, u32[]{:S(2)}, u32[]{:S(2)}) collective-permute-start(bf16[512,768]{0,1:T(8,128)(2,1)S(1)} %collective-permute-done.9), channel_id=1, source_target_pairs={{0,1},{1,0},{2,3},{3,2},{4,5},{5,4},{6,7},{7,6},{8,9},{9,8},{10,11... | collective-permute-start | bytes 2359304 | tf_op jit(solution)/shard_map/ppermute | solution.py:111
  57.6 4.7 %collective-permute-start.10 = (bf16[512,768]{0,1:T(8,128)(2,1)S(1)}, bf16[512,768]{0,1:T(8,128)(2,1)S(1)}, u32[]{:S(2)}, u32[]{:S(2)}) collective-permute-start(bf16[512,768]{0,1:T(8,128)(2,1)S(1)} %collective-permute-done.8), channel_id=1, source_target_pairs={{0,1},{1,0},{2,3},{3,2},{4,5},{5,4},{6,7},{7,6},{8,9},{9,8},{10,11... | collective-permute-start | bytes 2359304 | tf_op jit(solution)/shard_map/ppermute | solution.py:110
  58.5 22.6 %collective-permute-start.12 = (bf16[512,768]{0,1:T(8,128)(2,1)S(1)}, bf16[512,768]{0,1:T(8,128)(2,1)S(1)}, u32[]{:S(2)}, u32[]{:S(2)}) collective-permute-start(bf16[512,768]{0,1:T(8,128)(2,1)S(1)} %collective-permute-done.9), channel_id=1, source_target_pairs={{4,6},{2,0},{5,7},{3,1},{12,14},{10,8},{13,15},{11,9},{20,22},{18,... | collective-permute-start | bytes 2359304 | tf_op jit(solution)/shard_map/ppermute | solution.py:99
  81.1 2.3 %collective-permute-start.13 = (bf16[512,768]{0,1:T(8,128)(2,1)S(1)}, bf16[512,768]{0,1:T(8,128)(2,1)S(1)}, u32[]{:S(2)}, u32[]{:S(2)}) collective-permute-start(bf16[512,768]{0,1:T(8,128)(2,1)S(1)} %collective-permute-done.12), channel_id=1, source_target_pairs={{0,1},{1,0},{2,3},{3,2},{4,5},{5,4},{6,7},{7,6},{8,9},{9,8},{10,11... | collective-permute-start | bytes 2359304 | tf_op jit(solution)/shard_map/ppermute | solution.py:104

commit v18 on v15

--- a/solution.py
+++ b/solution.py
@@ -96,14 +96,18 @@
         if step + 2 < chips or (step + 2 == chips and chips < 4):
             received = (lax.ppermute(by_across, "chip", exchange), lax.ppermute(by_exchange, "chip", across))
         elif step + 2 == chips:
-            last = lax.ppermute(by_across, "chip", [(chips - 2, chips - 1), (1, 0)])
-            received = (last, last)
+            ends = [(chips - 2, chips - 1), (1, 0)]
+            half = rows // 2
+            received = (
+                lax.ppermute(by_across[:half], "chip", ends),
+                lax.ppermute(by_across[half:], "chip", ends),
+            )
         if step + 1 == chips and chips >= 4:
             far_chip = jnp.where(chip == 0, chips - 1, jnp.where(chip == chips - 1, 0, -1))
-            far = by_exchange
-            far_swapped = lax.ppermute(far, "core", swap)
-            acc = add_pair(acc, far, times_listed(far_chip, core))
-            acc = add_pair(acc, far_swapped, times_listed(far_chip, other_core))
+            for far in received:
+                far_swapped = lax.ppermute(far, "core", swap)
+                acc = add_pair(acc, far, times_listed(far_chip, core))
+                acc = add_pair(acc, far_swapped, times_listed(far_chip, other_core))
             continue
         exchange_chip = chip + upward * step
         across_chip = chip - upward * step

time: 83.8 us -> 82 us (0.979)
  waiting for transfers between devices: 44.7 us -> 27.7 us
  starting transfers between devices: 14.8 us -> 29 us
  matrix products: 16.9 us -> 19 us
  other arithmetic: 5.51 us -> 4.3 us
    ppermute x1, waiting for transfers between devices: 14.3 us -> 1.01 us  [per_device(): lax.ppermute(mine, 'chip', exchange)]
    ppermute x1, starting transfers between devices: 1.8 us -> 14.6 us  [per_device(): lax.ppermute(by_across, 'chip', exchange)]
    ppermute x1, waiting for transfers between devices: 9.92 us -> 7.26 us  [per_device(): lax.ppermute(by_across, 'chip', exchange)]
    dot_general x11 -> x13, matrix products: 7.37 us -> 9.07 us  [pair_terms(): jnp.dot(weights.astype(jnp.bfloat16), got, preferred_element_type=jnp.flo...]
    ppermute x1 -> x2, starting transfers between devices: 1.46 us -> 2.76 us  [the longest x1 1.47 us: per_device(): lax.ppermute(by_across[half:], 'chip', ends)]
    reshape x1 -> x0, other arithmetic: 1.26 us -> none  [per_device(): return result.astype(jnp.bfloat16).reshape(1, 1, rows, width)]
    dot_general x12 -> x14, matrix products: 8.86 us -> 9.35 us  [weigh(): scores = jnp.dot(unit_a, unit_b.T, preferred_element_type=jnp.float32)]
    ppermute x1 -> x2, waiting for transfers between devices: 11.6 us -> 11.2 us  [the longest x1 5.89 us: per_device(): lax.ppermute(by_across[:half], 'chip', ends)]
  transfers between devices with their start and end apart: 14 -> 16, of which waited for: 6 -> 6; matrix products, arithmetic and copies ran while one was open for 22% -> 24% of each run, Pallas kernels for 0% -> 0%
where the time goes in v18:
time: 82 us; the launch traced here: 81.8 us
  starting transfers between devices  29 us (35%)
  waiting for transfers between devices  27.7 us (34%)
  matrix products  19 us (23%)
  other arithmetic  4.3 us (5%)
  local copies, waits for them, and re-layouts  1.03 us (1%)
  between operations  0.84 us (1%)
    ppermute x1, starting transfers between devices, per_device(): lax.ppermute(by_across, 'chip', exchange)  14.6 us
    dot_general x14, matrix products, weigh(): scores = jnp.dot(unit_a, unit_b.T, preferred_element_type=jnp.float32)  9.35 us
    dot_general x13, matrix products, pair_terms(): jnp.dot(weights.astype(jnp.bfloat16), got, preferred_element_type=jnp.flo...  9.07 us
    ppermute x3, waiting for transfers between devices, per_device(): lax.ppermute(outgoing, 'bucket', [(i, i ^ m) for i in range(buckets)])  8.15 us
    ppermute x1, waiting for transfers between devices, per_device(): lax.ppermute(by_across, 'chip', exchange)  7.26 us
    ppermute x1, waiting for transfers between devices, per_device(): lax.ppermute(by_across[:half], 'chip', ends)  5.89 us
    ppermute x1, waiting for transfers between devices, per_device(): lax.ppermute(by_across[half:], 'chip', ends)  5.33 us
    ppermute x3, starting transfers between devices, per_device(): lax.ppermute(outgoing, 'bucket', [(i, i ^ m) for i in range(buckets)])  4.57 us
  transfers between devices with their start and end apart: 16, of which 6 were waited for; matrix products, arithmetic and copies ran while one was open for 24% of the time, Pallas kernels for 0%

profile of v18, /device:TPU:0, one launch (start us, length us, event | category | flops | bytes accessed | tf_op | source)
XLA Modules:
  0.0 81.8 jit_solution(17991813937646415070)
XLA Ops:
  0.0 1.5 %fusion.21 = bf16[4,128,768]{2,1,0:T(8,128)(2,1)S(1)} fusion(bf16[1,1,4,128,768]{4,3,2,1,0:T(8,128)(2,1)} %param.2, s32[4]{0:T(128)} %bitcast.70, pred[768]{0:T(1024)(128)(4,1)S(1)} %iota_compare_fusion.2), kind=kLoop, calls=%fused_computation.44 | loop fusion | flops 1179648 | bytes 1573648 | tf_op jit(solution)/shard_map/jit(_where)/select_n | solution.py:40
  1.6 3.0 %collective-permute-start = (bf16[128,768]{1,0:T(8,128)(2,1)S(1)}, bf16[128,768]{1,0:T(8,128)(2,1)S(1)}, u32[]{:S(2)}, u32[]{:S(2)}) collective-permute-start(bf16[128,768]{1,0:T(8,128)(2,1)S(1)} %get-tuple-element.17), channel_id=1, source_target_pairs={{0,8},{8,0},{16,24},{24,16},{1,9},{9,1},{17,25},{25,17},{2,10},{10... | collective-permute-start | bytes 589832 | tf_op jit(solution)/shard_map/ppermute | solution.py:44
  4.6 1.5 %collective-permute-start.1 = (bf16[128,768]{1,0:T(8,128)(2,1)S(1)}, bf16[128,768]{1,0:T(8,128)(2,1)S(1)}, u32[]{:S(2)}, u32[]{:S(2)}) collective-permute-start(bf16[128,768]{1,0:T(8,128)(2,1)S(1)} %get-tuple-element.16), channel_id=1, source_target_pairs={{0,16},{8,24},{16,0},{24,8},{1,17},{9,25},{17,1},{25,9},{2,18},{10... | collective-permute-start | bytes 589832 | tf_op jit(solution)/shard_map/ppermute | solution.py:44
  6.9 3.5 %collective-permute-done = bf16[128,768]{1,0:T(8,128)(2,1)S(1)} collective-permute-done((bf16[128,768]{1,0:T(8,128)(2,1)S(1)}, bf16[128,768]{1,0:T(8,128)(2,1)S(1)}, u32[]{:S(2)}, u32[]{:S(2)}) %collective-permute-start) | collective-permute-done | bytes 196640 | tf_op jit(solution)/shard_map/ppermute | solution.py:44
  10.5 4.7 %collective-permute-done.1 = bf16[128,768]{1,0:T(8,128)(2,1)S(1)} collective-permute-done((bf16[128,768]{1,0:T(8,128)(2,1)S(1)}, bf16[128,768]{1,0:T(8,128)(2,1)S(1)}, u32[]{:S(2)}, u32[]{:S(2)}) %collective-permute-start.1) | collective-permute-done | bytes 196640 | tf_op jit(solution)/shard_map/ppermute | solution.py:44
  15.7 0.7 collective-permute-start.5
  16.6 4.4 %collective-permute-start.4 = (bf16[512,768]{0,1:T(8,128)(2,1)S(1)}, bf16[512,768]{0,1:T(8,128)(2,1)S(1)}, u32[]{:S(2)}, u32[]{:S(2)}) collective-permute-start(bf16[512,768]{0,1:T(8,128)(2,1)S(1)} %constant_dynamic-update-slice_fusion), channel_id=1, source_target_pairs={{0,2},{2,0},{4,6},{6,4},{1,3},{3,1},{5,7},{7,5},{8,10},{10,8},{12,... | collective-permute-start | bytes 2359304 | tf_op jit(solution)/shard_map/ppermute | solution.py:89
  21.1 0.8 multiply_reduce_fusion.9
  21.8 0.6 fusion.95
  22.5 14.6 %collective-permute-start.8 = (bf16[512,768]{0,1:T(8,128)(2,1)S(1)}, bf16[512,768]{0,1:T(8,128)(2,1)S(1)}, u32[]{:S(2)}, u32[]{:S(2)}) collective-permute-start(bf16[512,768]{0,1:T(8,128)(2,1)S(1)} %collective-permute-done.5), channel_id=1, source_target_pairs={{0,2},{2,0},{4,6},{6,4},{1,3},{3,1},{5,7},{7,5},{8,10},{10,8},{12,... | collective-permute-start | bytes 2359304 | tf_op jit(solution)/shard_map/ppermute | solution.py:97
  37.3 1.0 %collective-permute-done.4 = bf16[512,768]{0,1:T(8,128)(2,1)S(1)} collective-permute-done((bf16[512,768]{0,1:T(8,128)(2,1)S(1)}, bf16[512,768]{0,1:T(8,128)(2,1)S(1)}, u32[]{:S(2)}, u32[]{:S(2)}) %collective-permute-start.4) | collective-permute-done | bytes 786464 | tf_op jit(solution)/shard_map/ppermute | solution.py:89
  38.3 0.7 collective-permute-start.9
  39.1 0.2 fusion.4
  39.4 0.2 fusion.2
  39.6 0.7 multiply_reduce_fusion.6
  40.3 0.6 fusion.89
  41.0 0.7 multiply_reduce_fusion.7
  41.7 0.6 fusion.91
  42.3 0.7 multiply_reduce_fusion.8
  43.1 0.6 fusion.93
  43.8 1.3 %collective-permute-start.12 = (bf16[256,768]{0,1:T(8,128)(2,1)S(1)}, bf16[256,768]{0,1:T(8,128)(2,1)S(1)}, u32[]{:S(2)}, u32[]{:S(2)}) collective-permute-start(bf16[256,768]{0,1:T(8,128)(2,1)S(1)} %get-tuple-element.14), channel_id=1, source_target_pairs={{4,6},{2,0},{5,7},{3,1},{12,14},{10,8},{13,15},{11,9},{20,22},{18,... | collective-permute-start | bytes 1179656 | tf_op jit(solution)/shard_map/ppermute | solution.py:102
  45.1 1.5 %collective-permute-start.13 = (bf16[256,768]{0,1:T(8,128)(2,1)S(1)}, bf16[256,768]{0,1:T(8,128)(2,1)S(1)}, u32[]{:S(2)}, u32[]{:S(2)}) collective-permute-start(bf16[256,768]{0,1:T(8,128)(2,1)S(1)} %get-tuple-element.13), channel_id=1, source_target_pairs={{4,6},{2,0},{5,7},{3,1},{12,14},{10,8},{13,15},{11,9},{20,22},{18,... | collective-permute-start | bytes 1179656 | tf_op jit(solution)/shard_map/ppermute | solution.py:103
  46.5 7.3 %collective-permute-done.8 = bf16[512,768]{0,1:T(8,128)(2,1)S(1)} collective-permute-done((bf16[512,768]{0,1:T(8,128)(2,1)S(1)}, bf16[512,768]{0,1:T(8,128)(2,1)S(1)}, u32[]{:S(2)}, u32[]{:S(2)}) %collective-permute-start.8) | collective-permute-done | bytes 786464 | tf_op jit(solution)/shard_map/ppermute | solution.py:97
  54.5 0.2 fusion.8
  54.8 0.6 collective-permute-start.11
  55.3 0.7 multiply_reduce_fusion.2
  56.1 0.6 fusion.81
  56.7 0.7 multiply_reduce_fusion.3
  57.4 0.6 fusion.83
  58.0 0.7 multiply_reduce_fusion.4
  58.8 0.6 fusion.85
  59.4 0.7 multiply_reduce_fusion.5
  60.2 0.6 fusion.87
  61.3 0.7 multiply_reduce_fusion.1
  62.0 0.6 fusion.79
  62.6 0.7 multiply_reduce_fusion
  63.4 1.2 %multiply_add_fusion = f32[512,768]{1,0:T(8,128)S(1)} fusion(f32[512,768]{1,0:T(8,128)S(1)} %fusion.79, f32[512,768]{1,0:T(8,128)S(1)} %fusion.81, f32[512,768]{1,0:T(8,128)S(1)} %fusion.83, f32[512,768]{1,0:T(8,128)S(1)} %fusion.85, f32[512,768]{1,0:T(8,128)S(1)} %fusion.87, f32[512,768]{1,0:T(8,128)S(1)} %fusion.89, f32[512,768]{1,0:T(8,128)S(1)} %fusion.91, ...), kind=kOutput, calls=%fused_computation.41 | convolution fusion | flops 409731072 | bytes 17039396 | tf_op jit(solution)/shard_map/dot_general | solution.py:76
  64.6 5.9 %collective-permute-done.12 = bf16[256,768]{0,1:T(8,128)(2,1)S(1)} collective-permute-done((bf16[256,768]{0,1:T(8,128)(2,1)S(1)}, bf16[256,768]{0,1:T(8,128)(2,1)S(1)}, u32[]{:S(2)}, u32[]{:S(2)}) %collective-permute-start.12) | collective-permute-done | bytes 393248 | tf_op jit(solution)/shard_map/ppermute | solution.py:102
  70.5 5.3 %collective-permute-done.13 = bf16[256,768]{0,1:T(8,128)(2,1)S(1)} collective-permute-done((bf16[256,768]{0,1:T(8,128)(2,1)S(1)}, bf16[256,768]{0,1:T(8,128)(2,1)S(1)}, u32[]{:S(2)}, u32[]{:S(2)}) %collective-permute-start.13) | collective-permute-done | bytes 393248 | tf_op jit(solution)/shard_map/ppermute | solution.py:103
  76.0 0.6 collective-permute-start.14
  76.6 0.5 multiply_reduce_fusion.11
  77.1 0.4 fusion.106
  77.5 0.5 multiply_reduce_fusion.13
  78.0 0.4 fusion.110
  78.7 0.5 multiply_reduce_fusion.12
  79.2 0.5 multiply_reduce_fusion.10
  79.7 0.4 fusion.108
  80.2 1.7 %fusion.43 = bf16[1,1,512,768]{3,2,1,0:T(8,128)(2,1)} fusion(bf16[256,768]{0,1:T(8,128)(2,1)S(1)} %collective-permute-done.15, f32[512,768]{1,0:T(8,128)S(1)} %fusion.106, f32[512,768]{1,0:T(8,128)S(1)} %fusion.108, f32[512,768]{1,0:T(8,128)S(1)} %multiply_add_fusion, f32[512,768]{1,0:T(8,128)S(1)} %fusion.110, f32[512]{0:T(512)S(1)} %bitcast.56, ...), kind=kOutput, calls=%fused_computation.76 | convolution fusion | flops 205651968 | bytes 7737352 | tf_op jit(solution)/shard_map/dot_general | solution.py:76
  (67 shorter events, 3.3 us)
Async XLA Ops:
  1.6 8.8 %collective-permute-start = (bf16[128,768]{1,0:T(8,128)(2,1)S(1)}, bf16[128,768]{1,0:T(8,128)(2,1)S(1)}, u32[]{:S(2)}, u32[]{:S(2)}) collective-permute-start(bf16[128,768]{1,0:T(8,128)(2,1)S(1)} %get-tuple-element.17), channel_id=1, source_target_pairs={{0,8},{8,0},{16,24},{24,16},{1,9},{9,1},{17,25},{25,17},{2,10},{10... | collective-permute-start | bytes 589832 | tf_op jit(solution)/shard_map/ppermute | solution.py:44
  4.6 10.6 %collective-permute-start.1 = (bf16[128,768]{1,0:T(8,128)(2,1)S(1)}, bf16[128,768]{1,0:T(8,128)(2,1)S(1)}, u32[]{:S(2)}, u32[]{:S(2)}) collective-permute-start(bf16[128,768]{1,0:T(8,128)(2,1)S(1)} %get-tuple-element.16), channel_id=1, source_target_pairs={{0,16},{8,24},{16,0},{24,8},{1,17},{9,25},{17,1},{25,9},{2,18},{10... | collective-permute-start | bytes 589832 | tf_op jit(solution)/shard_map/ppermute | solution.py:44
  6.1 9.3 %collective-permute-start.2 = (bf16[128,768]{1,0:T(8,128)(2,1)S(1)}, bf16[128,768]{1,0:T(8,128)(2,1)S(1)}, u32[]{:S(2)}, u32[]{:S(2)}) collective-permute-start(bf16[128,768]{1,0:T(8,128)(2,1)S(1)} %get-tuple-element.15), channel_id=1, source_target_pairs={{0,24},{8,16},{16,8},{24,0},{1,25},{9,17},{17,9},{25,1},{2,26},{10... | collective-permute-start | bytes 589832 | tf_op jit(solution)/shard_map/ppermute | solution.py:44
  15.7 6.8 %collective-permute-start.5 = (bf16[512,768]{0,1:T(8,128)(2,1)S(1)}, bf16[512,768]{0,1:T(8,128)(2,1)S(1)}, u32[]{:S(2)}, u32[]{:S(2)}) collective-permute-start(bf16[512,768]{0,1:T(8,128)(2,1)S(1)} %constant_dynamic-update-slice_fusion), channel_id=1, source_target_pairs={{2,4},{4,2},{3,5},{5,3},{10,12},{12,10},{11,13},{13,11},{18,20},{2... | collective-permute-start | bytes 2359304 | tf_op jit(solution)/shard_map/ppermute | solution.py:89
  16.6 21.7 %collective-permute-start.4 = (bf16[512,768]{0,1:T(8,128)(2,1)S(1)}, bf16[512,768]{0,1:T(8,128)(2,1)S(1)}, u32[]{:S(2)}, u32[]{:S(2)}) collective-permute-start(bf16[512,768]{0,1:T(8,128)(2,1)S(1)} %constant_dynamic-update-slice_fusion), channel_id=1, source_target_pairs={{0,2},{2,0},{4,6},{6,4},{1,3},{3,1},{5,7},{7,5},{8,10},{10,8},{12,... | collective-permute-start | bytes 2359304 | tf_op jit(solution)/shard_map/ppermute | solution.py:89
  21.1 18.3 %collective-permute-start.3 = (bf16[512,768]{0,1:T(8,128)(2,1)S(1)}, bf16[512,768]{0,1:T(8,128)(2,1)S(1)}, u32[]{:S(2)}, u32[]{:S(2)}) collective-permute-start(bf16[512,768]{0,1:T(8,128)(2,1)S(1)} %constant_dynamic-update-slice_fusion), channel_id=1, source_target_pairs={{0,1},{1,0},{2,3},{3,2},{4,5},{5,4},{6,7},{7,6},{8,9},{9,8},{10,11... | collective-permute-start | bytes 2359304 | tf_op jit(solution)/shard_map/ppermute | solution.py:90
  22.5 31.3 %collective-permute-start.8 = (bf16[512,768]{0,1:T(8,128)(2,1)S(1)}, bf16[512,768]{0,1:T(8,128)(2,1)S(1)}, u32[]{:S(2)}, u32[]{:S(2)}) collective-permute-start(bf16[512,768]{0,1:T(8,128)(2,1)S(1)} %collective-permute-done.5), channel_id=1, source_target_pairs={{0,2},{2,0},{4,6},{6,4},{1,3},{3,1},{5,7},{7,5},{8,10},{10,8},{12,... | collective-permute-start | bytes 2359304 | tf_op jit(solution)/shard_map/ppermute | solution.py:97
  37.1 17.2 %collective-permute-start.7 = (bf16[512,768]{0,1:T(8,128)(2,1)S(1)}, bf16[512,768]{0,1:T(8,128)(2,1)S(1)}, u32[]{:S(2)}, u32[]{:S(2)}) collective-permute-start(bf16[512,768]{0,1:T(8,128)(2,1)S(1)} %collective-permute-done.5), channel_id=1, source_target_pairs={{0,1},{1,0},{2,3},{3,2},{4,5},{5,4},{6,7},{7,6},{8,9},{9,8},{10,11... | collective-permute-start | bytes 2359304 | tf_op jit(solution)/shard_map/ppermute | solution.py:115
  38.3 5.4 %collective-permute-start.9 = (bf16[512,768]{0,1:T(8,128)(2,1)S(1)}, bf16[512,768]{0,1:T(8,128)(2,1)S(1)}, u32[]{:S(2)}, u32[]{:S(2)}) collective-permute-start(bf16[512,768]{0,1:T(8,128)(2,1)S(1)} %collective-permute-done.4), channel_id=1, source_target_pairs={{2,4},{4,2},{3,5},{5,3},{10,12},{12,10},{11,13},{13,11},{18,20},{2... | collective-permute-start | bytes 2359304 | tf_op jit(solution)/shard_map/ppermute | solution.py:97
  39.0 15.5 %collective-permute-start.6 = (bf16[512,768]{0,1:T(8,128)(2,1)S(1)}, bf16[512,768]{0,1:T(8,128)(2,1)S(1)}, u32[]{:S(2)}, u32[]{:S(2)}) collective-permute-start(bf16[512,768]{0,1:T(8,128)(2,1)S(1)} %collective-permute-done.4), channel_id=1, source_target_pairs={{0,1},{1,0},{2,3},{3,2},{4,5},{5,4},{6,7},{7,6},{8,9},{9,8},{10,11... | collective-permute-start | bytes 2359304 | tf_op jit(solution)/shard_map/ppermute | solution.py:114
  43.8 26.7 %collective-permute-start.12 = (bf16[256,768]{0,1:T(8,128)(2,1)S(1)}, bf16[256,768]{0,1:T(8,128)(2,1)S(1)}, u32[]{:S(2)}, u32[]{:S(2)}) collective-permute-start(bf16[256,768]{0,1:T(8,128)(2,1)S(1)} %get-tuple-element.14), channel_id=1, source_target_pairs={{4,6},{2,0},{5,7},{3,1},{12,14},{10,8},{13,15},{11,9},{20,22},{18,... | collective-permute-start | bytes 1179656 | tf_op jit(solution)/shard_map/ppermute | solution.py:102
  45.1 30.7 %collective-permute-start.13 = (bf16[256,768]{0,1:T(8,128)(2,1)S(1)}, bf16[256,768]{0,1:T(8,128)(2,1)S(1)}, u32[]{:S(2)}, u32[]{:S(2)}) collective-permute-start(bf16[256,768]{0,1:T(8,128)(2,1)S(1)} %get-tuple-element.13), channel_id=1, source_target_pairs={{4,6},{2,0},{5,7},{3,1},{12,14},{10,8},{13,15},{11,9},{20,22},{18,... | collective-permute-start | bytes 1179656 | tf_op jit(solution)/shard_map/ppermute | solution.py:103
  53.8 7.0 %collective-permute-start.10 = (bf16[512,768]{0,1:T(8,128)(2,1)S(1)}, bf16[512,768]{0,1:T(8,128)(2,1)S(1)}, u32[]{:S(2)}, u32[]{:S(2)}) collective-permute-start(bf16[512,768]{0,1:T(8,128)(2,1)S(1)} %collective-permute-done.8), channel_id=1, source_target_pairs={{0,1},{1,0},{2,3},{3,2},{4,5},{5,4},{6,7},{7,6},{8,9},{9,8},{10,11... | collective-permute-start | bytes 2359304 | tf_op jit(solution)/shard_map/ppermute | solution.py:114
  54.8 6.3 %collective-permute-start.11 = (bf16[512,768]{0,1:T(8,128)(2,1)S(1)}, bf16[512,768]{0,1:T(8,128)(2,1)S(1)}, u32[]{:S(2)}, u32[]{:S(2)}) collective-permute-start(bf16[512,768]{0,1:T(8,128)(2,1)S(1)} %collective-permute-done.9), channel_id=1, source_target_pairs={{0,1},{1,0},{2,3},{3,2},{4,5},{5,4},{6,7},{7,6},{8,9},{9,8},{10,11... | collective-permute-start | bytes 2359304 | tf_op jit(solution)/shard_map/ppermute | solution.py:115
  75.8 2.8 %collective-permute-start.15 = (bf16[256,768]{0,1:T(8,128)(2,1)S(1)}, bf16[256,768]{0,1:T(8,128)(2,1)S(1)}, u32[]{:S(2)}, u32[]{:S(2)}) collective-permute-start(bf16[256,768]{0,1:T(8,128)(2,1)S(1)} %collective-permute-done.13), channel_id=1, source_target_pairs={{0,1},{1,0},{2,3},{3,2},{4,5},{5,4},{6,7},{7,6},{8,9},{9,8},{10,11... | collective-permute-start | bytes 1179656 | tf_op jit(solution)/shard_map/ppermute | solution.py:108
  76.0 2.4 %collective-permute-start.14 = (bf16[256,768]{0,1:T(8,128)(2,1)S(1)}, bf16[256,768]{0,1:T(8,128)(2,1)S(1)}, u32[]{:S(2)}, u32[]{:S(2)}) collective-permute-start(bf16[256,768]{0,1:T(8,128)(2,1)S(1)} %collective-permute-done.12), channel_id=1, source_target_pairs={{0,1},{1,0},{2,3},{3,2},{4,5},{5,4},{6,7},{7,6},{8,9},{9,8},{10,11... | collective-permute-start | bytes 1179656 | tf_op jit(solution)/shard_map/ppermute | solution.py:108

commit v19 on v15

--- a/solution.py
+++ b/solution.py
@@ -84,35 +84,45 @@
     across = [(z, z - 1) if z % 2 == 0 else (z, z + 1) for z in range(chips) if (z % 2 == 0 and z >= 2) or (z % 2 and z + 1 < chips)]
     upward = 1 - 2 * (chip % 2)
     acc = (summed, squares)
-    mine = data
+    half = rows // 2
+    mine = (data[:half], data[half:])
     other_core = (core + 1) % cores
-    received = (lax.ppermute(mine, "chip", exchange), lax.ppermute(mine, "chip", across))
-    swapped = lax.ppermute(mine, "core", swap)
-    acc = add_pair(acc, swapped, times_listed(chip, other_core))
+
+    def send(parts, pairs):
+        return tuple(lax.ppermute(part, "chip", pairs) for part in parts)
+
+    def add_all(acc, parts, weight):
+        for part in parts:
+            acc = add_pair(acc, part, weight)
+        return lax.optimization_barrier(acc)
+
+    def swapped(parts):
+        return tuple(lax.ppermute(part, "core", swap) for part in parts)
+
+    received = (send(mine, exchange), send(mine, across))
+    acc = add_all(acc, swapped(mine), times_listed(chip, other_core))
     for step in range(1, chips):
         if step + 1 == chips:
             acc, received = lax.optimization_barrier((acc, received))
         by_exchange, by_across = received
         if step + 2 < chips or (step + 2 == chips and chips < 4):
-            received = (lax.ppermute(by_across, "chip", exchange), lax.ppermute(by_exchange, "chip", across))
+            received = (send(by_across, exchange), send(by_exchange, across))
         elif step + 2 == chips:
-            last = lax.ppermute(by_across, "chip", [(chips - 2, chips - 1), (1, 0)])
-            received = (last, last)
+            far = send(by_across, [(chips - 2, chips - 1), (1, 0)])
+            received = (far, far)
         if step + 1 == chips and chips >= 4:
             far_chip = jnp.where(chip == 0, chips - 1, jnp.where(chip == chips - 1, 0, -1))
-            far = by_exchange
-            far_swapped = lax.ppermute(far, "core", swap)
-            acc = add_pair(acc, far, times_listed(far_chip, core))
-            acc = add_pair(acc, far_swapped, times_listed(far_chip, other_core))
+            acc = add_all(acc, by_exchange, times_listed(far_chip, core))
+            acc = add_all(acc, swapped(by_exchange), times_listed(far_chip, other_core))
             continue
         exchange_chip = chip + upward * step
         across_chip = chip - upward * step
-        exchange_swapped = lax.ppermute(by_exchange, "core", swap)
-        across_swapped = lax.ppermute(by_across, "core", swap)
-        acc = add_pair(acc, by_exchange, times_listed(exchange_chip, core))
-        acc = add_pair(acc, by_across, times_listed(across_chip, core))
-        acc = add_pair(acc, exchange_swapped, times_listed(exchange_chip, other_core))
-        acc = add_pair(acc, across_swapped, times_listed(across_chip, other_core))
+        exchange_swapped = swapped(by_exchange)
+        across_swapped = swapped(by_across)
+        acc = add_all(acc, by_exchange, times_listed(exchange_chip, core))
+        acc = add_all(acc, by_across, times_listed(across_chip, core))
+        acc = add_all(acc, exchange_swapped, times_listed(exchange_chip, other_core))
+        acc = add_all(acc, across_swapped, times_listed(across_chip, other_core))
     summed, squares = acc
     result = summed * lax.rsqrt(squares)[:, None] * live[:, None]
     return result.astype(jnp.bfloat16).reshape(1, 1, rows, width)

time: 83.8 us -> 96 us (1.15)
  matrix products: 16.9 us -> 21.7 us
  starting transfers between devices: 14.8 us -> 18.5 us
  waiting for transfers between devices: 44.7 us -> 47.3 us
    ppermute x11 -> x22, starting transfers between devices: 10.2 us -> 14 us  [the longest x10 10.9 us: send(): return tuple((lax.ppermute(part, 'chip', pairs) for part in parts))]
    dot_general x12 -> x23, matrix products: 8.86 us -> 11.7 us  [weigh(): scores = jnp.dot(unit_a, unit_b.T, preferred_element_type=jnp.float32)]
    ppermute x11 -> x22, waiting for transfers between devices: 36.5 us -> 39.1 us  [the longest x10 39.1 us: send(): return tuple((lax.ppermute(part, 'chip', pairs) for part in parts))]
    dot_general x11 -> x22, matrix products: 7.37 us -> 9.4 us  [pair_terms(): jnp.dot(weights.astype(jnp.bfloat16), got, preferred_element_type=jnp.flo...]
    reduce_sum x12 -> x22, other arithmetic: 2.57 us -> 3.13 us  [normalize(): jnp.sum(values * values, axis=-1, keepdims=True) + EPS]
  transfers between devices with their start and end apart: 14 -> 25, of which waited for: 6 -> 8; matrix products, arithmetic and copies ran while one was open for 22% -> 24% of each run, Pallas kernels for 0% -> 0%
where the time goes in v19:
time: 96 us; the launch traced here: 95.8 us
  waiting for transfers between devices  47.3 us (49%)
  matrix products  21.7 us (23%)
  starting transfers between devices  18.5 us (19%)
  other arithmetic  6.12 us (6%)
  between operations  1.11 us (1%)
  local copies, waits for them, and re-layouts  1.03 us (1%)
    ppermute x10, waiting for transfers between devices, send(): return tuple((lax.ppermute(part, 'chip', pairs) for part in parts))  39.1 us
    dot_general x23, matrix products, weigh(): scores = jnp.dot(unit_a, unit_b.T, preferred_element_type=jnp.float32)  11.7 us
    ppermute x10, starting transfers between devices, send(): return tuple((lax.ppermute(part, 'chip', pairs) for part in parts))  10.9 us
    dot_general x22, matrix products, pair_terms(): jnp.dot(weights.astype(jnp.bfloat16), got, preferred_element_type=jnp.flo...  9.4 us
    ppermute x3, waiting for transfers between devices, per_device(): lax.ppermute(outgoing, 'bucket', [(i, i ^ m) for i in range(buckets)])  8.15 us
    ppermute x3, starting transfers between devices, per_device(): lax.ppermute(outgoing, 'bucket', [(i, i ^ m) for i in range(buckets)])  4.57 us
    reduce_sum x22, other arithmetic, normalize(): jnp.sum(values * values, axis=-1, keepdims=True) + EPS  3.13 us
    ppermute x12, starting transfers between devices, swapped(): return tuple((lax.ppermute(part, 'core', swap) for part in parts))  3.07 us
  transfers between devices with their start and end apart: 25, of which 8 were waited for; matrix products, arithmetic and copies ran while one was open for 24% of the time, Pallas kernels for 0%

profile of v19, /device:TPU:0, one launch (start us, length us, event | category | flops | bytes accessed | tf_op | source)
XLA Modules:
  0.0 95.8 jit_solution(5907278655028469784)
XLA Ops:
  0.0 1.5 %fusion.3 = bf16[4,128,768]{2,1,0:T(8,128)(2,1)S(1)} fusion(bf16[1,1,4,128,768]{4,3,2,1,0:T(8,128)(2,1)} %param.2, s32[4]{0:T(128)} %bitcast.106, pred[768]{0:T(1024)(128)(4,1)S(1)} %iota_compare_fusion.2), kind=kLoop, calls=%fused_computation.18 | loop fusion | flops 1179648 | bytes 1573648 | tf_op jit(solution)/shard_map/jit(_where)/select_n | solution.py:40
  1.6 3.0 %collective-permute-start = (bf16[128,768]{1,0:T(8,128)(2,1)S(1)}, bf16[128,768]{1,0:T(8,128)(2,1)S(1)}, u32[]{:S(2)}, u32[]{:S(2)}) collective-permute-start(bf16[128,768]{1,0:T(8,128)(2,1)S(1)} %get-tuple-element.61), channel_id=1, source_target_pairs={{0,8},{8,0},{16,24},{24,16},{1,9},{9,1},{17,25},{25,17},{2,10},{10... | collective-permute-start | bytes 589832 | tf_op jit(solution)/shard_map/ppermute | solution.py:44
  4.6 1.5 %collective-permute-start.1 = (bf16[128,768]{1,0:T(8,128)(2,1)S(1)}, bf16[128,768]{1,0:T(8,128)(2,1)S(1)}, u32[]{:S(2)}, u32[]{:S(2)}) collective-permute-start(bf16[128,768]{1,0:T(8,128)(2,1)S(1)} %get-tuple-element.60), channel_id=1, source_target_pairs={{0,16},{8,24},{16,0},{24,8},{1,17},{9,25},{17,1},{25,9},{2,18},{10... | collective-permute-start | bytes 589832 | tf_op jit(solution)/shard_map/ppermute | solution.py:44
  6.9 3.5 %collective-permute-done = bf16[128,768]{1,0:T(8,128)(2,1)S(1)} collective-permute-done((bf16[128,768]{1,0:T(8,128)(2,1)S(1)}, bf16[128,768]{1,0:T(8,128)(2,1)S(1)}, u32[]{:S(2)}, u32[]{:S(2)}) %collective-permute-start) | collective-permute-done | bytes 196640 | tf_op jit(solution)/shard_map/ppermute | solution.py:44
  10.5 4.7 %collective-permute-done.1 = bf16[128,768]{1,0:T(8,128)(2,1)S(1)} collective-permute-done((bf16[128,768]{1,0:T(8,128)(2,1)S(1)}, bf16[128,768]{1,0:T(8,128)(2,1)S(1)}, u32[]{:S(2)}, u32[]{:S(2)}) %collective-permute-start.1) | collective-permute-done | bytes 196640 | tf_op jit(solution)/shard_map/ppermute | solution.py:44
  16.1 1.6 %collective-permute-start.5 = (bf16[256,768]{0,1:T(8,128)(2,1)S(1)}, bf16[256,768]{0,1:T(8,128)(2,1)S(1)}, u32[]{:S(2)}, u32[]{:S(2)}) collective-permute-start(bf16[256,768]{0,1:T(8,128)(2,1)S(1)} %get-tuple-element.58), channel_id=1, source_target_pairs={{0,2},{2,0},{4,6},{6,4},{1,3},{3,1},{5,7},{7,5},{8,10},{10,8},{12,... | collective-permute-start | bytes 1179656 | tf_op jit(solution)/shard_map/ppermute | solution.py:92
  18.3 0.7 collective-permute-start.7
  19.0 0.8 multiply_reduce_fusion
  19.8 0.6 fusion.96
  20.4 0.7 collective-permute-start.8
  21.4 0.5 multiply_reduce_fusion.22
  22.4 0.5 multiply_reduce_fusion.21
  23.3 4.8 %collective-permute-done.5 = bf16[256,768]{0,1:T(8,128)(2,1)S(1)} collective-permute-done((bf16[256,768]{0,1:T(8,128)(2,1)S(1)}, bf16[256,768]{0,1:T(8,128)(2,1)S(1)}, u32[]{:S(2)}, u32[]{:S(2)}) %collective-permute-start.5) | collective-permute-done | bytes 393248 | tf_op jit(solution)/shard_map/ppermute | solution.py:92
  28.3 7.7 %collective-permute-done.6 = bf16[256,768]{0,1:T(8,128)(2,1)S(1)} collective-permute-done((bf16[256,768]{0,1:T(8,128)(2,1)S(1)}, bf16[256,768]{0,1:T(8,128)(2,1)S(1)}, u32[]{:S(2)}, u32[]{:S(2)}) %collective-permute-start.6) | collective-permute-done | bytes 393248 | tf_op jit(solution)/shard_map/ppermute | solution.py:92
  36.2 0.5 multiply_reduce_fusion.20
  37.1 0.5 multiply_reduce_fusion.19
  38.5 0.5 collective-permute-start.10
  39.0 0.5 multiply_reduce_fusion.18
  39.9 0.5 multiply_reduce_fusion.17
  41.4 3.1 %collective-permute-start.13 = (bf16[256,768]{0,1:T(8,128)(2,1)S(1)}, bf16[256,768]{0,1:T(8,128)(2,1)S(1)}, u32[]{:S(2)}, u32[]{:S(2)}) collective-permute-start(bf16[256,768]{0,1:T(8,128)(2,1)S(1)} %collective-permute-done.7), channel_id=1, source_target_pairs={{0,2},{2,0},{4,6},{6,4},{1,3},{3,1},{5,7},{7,5},{8,10},{10,8},{12,... | collective-permute-start | bytes 1179656 | tf_op jit(solution)/shard_map/ppermute | solution.py:92
  44.7 0.9 collective-permute-start.15
  45.7 0.5 multiply_reduce_fusion.16
  46.6 0.5 multiply_reduce_fusion.15
  47.6 0.7 collective-permute-start.16
  48.6 0.5 multiply_reduce_fusion.14
  49.5 0.5 multiply_reduce_fusion.13
  50.5 4.0 %collective-permute-done.13 = bf16[256,768]{0,1:T(8,128)(2,1)S(1)} collective-permute-done((bf16[256,768]{0,1:T(8,128)(2,1)S(1)}, bf16[256,768]{0,1:T(8,128)(2,1)S(1)}, u32[]{:S(2)}, u32[]{:S(2)}) %collective-permute-start.13) | collective-permute-done | bytes 393248 | tf_op jit(solution)/shard_map/ppermute | solution.py:92
  54.6 7.7 %collective-permute-done.14 = bf16[256,768]{0,1:T(8,128)(2,1)S(1)} collective-permute-done((bf16[256,768]{0,1:T(8,128)(2,1)S(1)}, bf16[256,768]{0,1:T(8,128)(2,1)S(1)}, u32[]{:S(2)}, u32[]{:S(2)}) %collective-permute-start.14) | collective-permute-done | bytes 393248 | tf_op jit(solution)/shard_map/ppermute | solution.py:92
  62.4 0.5 multiply_reduce_fusion.12
  63.4 0.5 multiply_reduce_fusion.11
  64.7 0.5 collective-permute-start.18
  65.2 0.5 multiply_reduce_fusion.10
  66.1 0.5 multiply_reduce_fusion.9
  67.7 1.3 %collective-permute-start.21 = (bf16[256,768]{0,1:T(8,128)(2,1)S(1)}, bf16[256,768]{0,1:T(8,128)(2,1)S(1)}, u32[]{:S(2)}, u32[]{:S(2)}) collective-permute-start(bf16[256,768]{0,1:T(8,128)(2,1)S(1)} %collective-permute-done.15), channel_id=1, source_target_pairs={{4,6},{2,0},{5,7},{3,1},{12,14},{10,8},{13,15},{11,9},{20,22},{18,... | collective-permute-start | bytes 1179656 | tf_op jit(solution)/shard_map/ppermute | solution.py:92
  69.0 1.5 %collective-permute-start.22 = (bf16[256,768]{0,1:T(8,128)(2,1)S(1)}, bf16[256,768]{0,1:T(8,128)(2,1)S(1)}, u32[]{:S(2)}, u32[]{:S(2)}) collective-permute-start(bf16[256,768]{0,1:T(8,128)(2,1)S(1)} %collective-permute-done.16), channel_id=1, source_target_pairs={{4,6},{2,0},{5,7},{3,1},{12,14},{10,8},{13,15},{11,9},{20,22},{18,... | collective-permute-start | bytes 1179656 | tf_op jit(solution)/shard_map/ppermute | solution.py:92
  70.8 0.5 multiply_reduce_fusion.8
  71.7 0.5 multiply_reduce_fusion.7
  73.0 0.5 multiply_reduce_fusion.6
  73.9 0.5 multiply_reduce_fusion.5
  74.9 7.1 %collective-permute-done.21 = bf16[256,768]{0,1:T(8,128)(2,1)S(1)} collective-permute-done((bf16[256,768]{0,1:T(8,128)(2,1)S(1)}, bf16[256,768]{0,1:T(8,128)(2,1)S(1)}, u32[]{:S(2)}, u32[]{:S(2)}) %collective-permute-start.21) | collective-permute-done | bytes 393248 | tf_op jit(solution)/shard_map/ppermute | solution.py:92
  82.0 7.8 %collective-permute-done.22 = bf16[256,768]{0,1:T(8,128)(2,1)S(1)} collective-permute-done((bf16[256,768]{0,1:T(8,128)(2,1)S(1)}, bf16[256,768]{0,1:T(8,128)(2,1)S(1)}, u32[]{:S(2)}, u32[]{:S(2)}) %collective-permute-start.22) | collective-permute-done | bytes 393248 | tf_op jit(solution)/shard_map/ppermute | solution.py:92
  90.0 0.5 collective-permute-start.24
  90.5 0.5 multiply_reduce_fusion.4
  91.5 0.5 multiply_reduce_fusion.3
  92.8 0.5 multiply_reduce_fusion.2
  93.3 0.5 multiply_reduce_fusion.1
  94.2 0.5 multiply_add_fusion
  94.7 1.1 %fusion.95 = bf16[1,1,512,768]{3,2,1,0:T(8,128)(2,1)} fusion(f32[512,768]{1,0:T(8,128)S(1)} %multiply_add_fusion, f32[512]{0:T(512)S(1)} %bitcast.83, f32[512]{0:T(512)S(1)} %rsqrt.210), kind=kLoop, calls=%fused_computation.179 | loop fusion | flops 1179648 | bytes 2363392 | tf_op jit(solution)/shard_map/reshape | solution.py:128
  (141 shorter events, 15.6 us)
Async XLA Ops:
  1.6 8.8 %collective-permute-start = (bf16[128,768]{1,0:T(8,128)(2,1)S(1)}, bf16[128,768]{1,0:T(8,128)(2,1)S(1)}, u32[]{:S(2)}, u32[]{:S(2)}) collective-permute-start(bf16[128,768]{1,0:T(8,128)(2,1)S(1)} %get-tuple-element.61), channel_id=1, source_target_pairs={{0,8},{8,0},{16,24},{24,16},{1,9},{9,1},{17,25},{25,17},{2,10},{10... | collective-permute-start | bytes 589832 | tf_op jit(solution)/shard_map/ppermute | solution.py:44
  4.6 10.6 %collective-permute-start.1 = (bf16[128,768]{1,0:T(8,128)(2,1)S(1)}, bf16[128,768]{1,0:T(8,128)(2,1)S(1)}, u32[]{:S(2)}, u32[]{:S(2)}) collective-permute-start(bf16[128,768]{1,0:T(8,128)(2,1)S(1)} %get-tuple-element.60), channel_id=1, source_target_pairs={{0,16},{8,24},{16,0},{24,8},{1,17},{9,25},{17,1},{25,9},{2,18},{10... | collective-permute-start | bytes 589832 | tf_op jit(solution)/shard_map/ppermute | solution.py:44
  6.1 9.3 %collective-permute-start.2 = (bf16[128,768]{1,0:T(8,128)(2,1)S(1)}, bf16[128,768]{1,0:T(8,128)(2,1)S(1)}, u32[]{:S(2)}, u32[]{:S(2)}) collective-permute-start(bf16[128,768]{1,0:T(8,128)(2,1)S(1)} %get-tuple-element.59), channel_id=1, source_target_pairs={{0,24},{8,16},{16,8},{24,0},{1,25},{9,17},{17,9},{25,1},{2,26},{10... | collective-permute-start | bytes 589832 | tf_op jit(solution)/shard_map/ppermute | solution.py:44
  16.0 4.4 %collective-permute-start.3 = (bf16[256,768]{0,1:T(8,128)(2,1)S(1)}, bf16[256,768]{0,1:T(8,128)(2,1)S(1)}, u32[]{:S(2)}, u32[]{:S(2)}) collective-permute-start(bf16[256,768]{0,1:T(8,128)(2,1)S(1)} %get-tuple-element.58), channel_id=1, source_target_pairs={{0,1},{1,0},{2,3},{3,2},{4,5},{5,4},{6,7},{7,6},{8,9},{9,8},{10,11... | collective-permute-start | bytes 1179656 | tf_op jit(solution)/shard_map/ppermute | solution.py:100
  16.1 12.1 %collective-permute-start.5 = (bf16[256,768]{0,1:T(8,128)(2,1)S(1)}, bf16[256,768]{0,1:T(8,128)(2,1)S(1)}, u32[]{:S(2)}, u32[]{:S(2)}) collective-permute-start(bf16[256,768]{0,1:T(8,128)(2,1)S(1)} %get-tuple-element.58), channel_id=1, source_target_pairs={{0,2},{2,0},{4,6},{6,4},{1,3},{3,1},{5,7},{7,5},{8,10},{10,8},{12,... | collective-permute-start | bytes 1179656 | tf_op jit(solution)/shard_map/ppermute | solution.py:92
  17.7 3.5 %collective-permute-start.4 = (bf16[256,768]{0,1:T(8,128)(2,1)S(1)}, bf16[256,768]{0,1:T(8,128)(2,1)S(1)}, u32[]{:S(2)}, u32[]{:S(2)}) collective-permute-start(bf16[256,768]{0,1:T(8,128)(2,1)S(1)} %get-tuple-element.57), channel_id=1, source_target_pairs={{0,1},{1,0},{2,3},{3,2},{4,5},{5,4},{6,7},{7,6},{8,9},{9,8},{10,11... | collective-permute-start | bytes 1179656 | tf_op jit(solution)/shard_map/ppermute | solution.py:100
  17.9 18.1 %collective-permute-start.6 = (bf16[256,768]{0,1:T(8,128)(2,1)S(1)}, bf16[256,768]{0,1:T(8,128)(2,1)S(1)}, u32[]{:S(2)}, u32[]{:S(2)}) collective-permute-start(bf16[256,768]{0,1:T(8,128)(2,1)S(1)} %get-tuple-element.57), channel_id=1, source_target_pairs={{0,2},{2,0},{4,6},{6,4},{1,3},{3,1},{5,7},{7,5},{8,10},{10,8},{12,... | collective-permute-start | bytes 1179656 | tf_op jit(solution)/shard_map/ppermute | solution.py:92
  18.3 19.7 %collective-permute-start.7 = (bf16[256,768]{0,1:T(8,128)(2,1)S(1)}, bf16[256,768]{0,1:T(8,128)(2,1)S(1)}, u32[]{:S(2)}, u32[]{:S(2)}) collective-permute-start(bf16[256,768]{0,1:T(8,128)(2,1)S(1)} %get-tuple-element.58), channel_id=1, source_target_pairs={{2,4},{4,2},{3,5},{5,3},{10,12},{12,10},{11,13},{13,11},{18,20},{2... | collective-permute-start | bytes 1179656 | tf_op jit(solution)/shard_map/ppermute | solution.py:92
  20.4 17.8 %collective-permute-start.8 = (bf16[256,768]{0,1:T(8,128)(2,1)S(1)}, bf16[256,768]{0,1:T(8,128)(2,1)S(1)}, u32[]{:S(2)}, u32[]{:S(2)}) collective-permute-start(bf16[256,768]{0,1:T(8,128)(2,1)S(1)} %get-tuple-element.57), channel_id=1, source_target_pairs={{2,4},{4,2},{3,5},{5,3},{10,12},{12,10},{11,13},{13,11},{18,20},{2... | collective-permute-start | bytes 1179656 | tf_op jit(solution)/shard_map/ppermute | solution.py:92
  38.4 6.1 %collective-permute-start.9 = (bf16[256,768]{0,1:T(8,128)(2,1)S(1)}, bf16[256,768]{0,1:T(8,128)(2,1)S(1)}, u32[]{:S(2)}, u32[]{:S(2)}) collective-permute-start(bf16[256,768]{0,1:T(8,128)(2,1)S(1)} %collective-permute-done.5), channel_id=1, source_target_pairs={{0,1},{1,0},{2,3},{3,2},{4,5},{5,4},{6,7},{7,6},{8,9},{9,8},{10,11... | collective-permute-start | bytes 1179656 | tf_op jit(solution)/shard_map/ppermute | solution.py:100
  38.5 6.2 %collective-permute-start.10 = (bf16[256,768]{0,1:T(8,128)(2,1)S(1)}, bf16[256,768]{0,1:T(8,128)(2,1)S(1)}, u32[]{:S(2)}, u32[]{:S(2)}) collective-permute-start(bf16[256,768]{0,1:T(8,128)(2,1)S(1)} %collective-permute-done.6), channel_id=1, source_target_pairs={{0,1},{1,0},{2,3},{3,2},{4,5},{5,4},{6,7},{7,6},{8,9},{9,8},{10,11... | collective-permute-start | bytes 1179656 | tf_op jit(solution)/shard_map/ppermute | solution.py:100
  40.8 6.7 %collective-permute-start.11 = (bf16[256,768]{0,1:T(8,128)(2,1)S(1)}, bf16[256,768]{0,1:T(8,128)(2,1)S(1)}, u32[]{:S(2)}, u32[]{:S(2)}) collective-permute-start(bf16[256,768]{0,1:T(8,128)(2,1)S(1)} %collective-permute-done.7), channel_id=1, source_target_pairs={{0,1},{1,0},{2,3},{3,2},{4,5},{5,4},{6,7},{7,6},{8,9},{9,8},{10,11... | collective-permute-start | bytes 1179656 | tf_op jit(solution)/shard_map/ppermute | solution.py:100
  41.0 7.5 %collective-permute-start.12 = (bf16[256,768]{0,1:T(8,128)(2,1)S(1)}, bf16[256,768]{0,1:T(8,128)(2,1)S(1)}, u32[]{:S(2)}, u32[]{:S(2)}) collective-permute-start(bf16[256,768]{0,1:T(8,128)(2,1)S(1)} %collective-permute-done.8), channel_id=1, source_target_pairs={{0,1},{1,0},{2,3},{3,2},{4,5},{5,4},{6,7},{7,6},{8,9},{9,8},{10,11... | collective-permute-start | bytes 1179656 | tf_op jit(solution)/shard_map/ppermute | solution.py:100
  41.4 13.0 %collective-permute-start.13 = (bf16[256,768]{0,1:T(8,128)(2,1)S(1)}, bf16[256,768]{0,1:T(8,128)(2,1)S(1)}, u32[]{:S(2)}, u32[]{:S(2)}) collective-permute-start(bf16[256,768]{0,1:T(8,128)(2,1)S(1)} %collective-permute-done.7), channel_id=1, source_target_pairs={{0,2},{2,0},{4,6},{6,4},{1,3},{3,1},{5,7},{7,5},{8,10},{10,8},{12,... | collective-permute-start | bytes 1179656 | tf_op jit(solution)/shard_map/ppermute | solution.py:92
  44.5 17.8 %collective-permute-start.14 = (bf16[256,768]{0,1:T(8,128)(2,1)S(1)}, bf16[256,768]{0,1:T(8,128)(2,1)S(1)}, u32[]{:S(2)}, u32[]{:S(2)}) collective-permute-start(bf16[256,768]{0,1:T(8,128)(2,1)S(1)} %collective-permute-done.8), channel_id=1, source_target_pairs={{0,2},{2,0},{4,6},{6,4},{1,3},{3,1},{5,7},{7,5},{8,10},{10,8},{12,... | collective-permute-start | bytes 1179656 | tf_op jit(solution)/shard_map/ppermute | solution.py:92
  44.7 19.7 %collective-permute-start.15 = (bf16[256,768]{0,1:T(8,128)(2,1)S(1)}, bf16[256,768]{0,1:T(8,128)(2,1)S(1)}, u32[]{:S(2)}, u32[]{:S(2)}) collective-permute-start(bf16[256,768]{0,1:T(8,128)(2,1)S(1)} %collective-permute-done.5), channel_id=1, source_target_pairs={{2,4},{4,2},{3,5},{5,3},{10,12},{12,10},{11,13},{13,11},{18,20},{2... | collective-permute-start | bytes 1179656 | tf_op jit(solution)/shard_map/ppermute | solution.py:92
  47.6 16.9 %collective-permute-start.16 = (bf16[256,768]{0,1:T(8,128)(2,1)S(1)}, bf16[256,768]{0,1:T(8,128)(2,1)S(1)}, u32[]{:S(2)}, u32[]{:S(2)}) collective-permute-start(bf16[256,768]{0,1:T(8,128)(2,1)S(1)} %collective-permute-done.6), channel_id=1, source_target_pairs={{2,4},{4,2},{3,5},{5,3},{10,12},{12,10},{11,13},{13,11},{18,20},{2... | collective-permute-start | bytes 1179656 | tf_op jit(solution)/shard_map/ppermute | solution.py:92
  64.6 4.3 %collective-permute-start.17 = (bf16[256,768]{0,1:T(8,128)(2,1)S(1)}, bf16[256,768]{0,1:T(8,128)(2,1)S(1)}, u32[]{:S(2)}, u32[]{:S(2)}) collective-permute-start(bf16[256,768]{0,1:T(8,128)(2,1)S(1)} %collective-permute-done.13), channel_id=1, source_target_pairs={{0,1},{1,0},{2,3},{3,2},{4,5},{5,4},{6,7},{7,6},{8,9},{9,8},{10,11... | collective-permute-start | bytes 1179656 | tf_op jit(solution)/shard_map/ppermute | solution.py:100
  64.7 5.9 %collective-permute-start.18 = (bf16[256,768]{0,1:T(8,128)(2,1)S(1)}, bf16[256,768]{0,1:T(8,128)(2,1)S(1)}, u32[]{:S(2)}, u32[]{:S(2)}) collective-permute-start(bf16[256,768]{0,1:T(8,128)(2,1)S(1)} %collective-permute-done.14), channel_id=1, source_target_pairs={{0,1},{1,0},{2,3},{3,2},{4,5},{5,4},{6,7},{7,6},{8,9},{9,8},{10,11... | collective-permute-start | bytes 1179656 | tf_op jit(solution)/shard_map/ppermute | solution.py:100
  67.1 5.6 %collective-permute-start.19 = (bf16[256,768]{0,1:T(8,128)(2,1)S(1)}, bf16[256,768]{0,1:T(8,128)(2,1)S(1)}, u32[]{:S(2)}, u32[]{:S(2)}) collective-permute-start(bf16[256,768]{0,1:T(8,128)(2,1)S(1)} %collective-permute-done.15), channel_id=1, source_target_pairs={{0,1},{1,0},{2,3},{3,2},{4,5},{5,4},{6,7},{7,6},{8,9},{9,8},{10,11... | collective-permute-start | bytes 1179656 | tf_op jit(solution)/shard_map/ppermute | solution.py:100
  67.2 5.6 %collective-permute-start.20 = (bf16[256,768]{0,1:T(8,128)(2,1)S(1)}, bf16[256,768]{0,1:T(8,128)(2,1)S(1)}, u32[]{:S(2)}, u32[]{:S(2)}) collective-permute-start(bf16[256,768]{0,1:T(8,128)(2,1)S(1)} %collective-permute-done.16), channel_id=1, source_target_pairs={{0,1},{1,0},{2,3},{3,2},{4,5},{5,4},{6,7},{7,6},{8,9},{9,8},{10,11... | collective-permute-start | bytes 1179656 | tf_op jit(solution)/shard_map/ppermute | solution.py:100
  67.7 14.3 %collective-permute-start.21 = (bf16[256,768]{0,1:T(8,128)(2,1)S(1)}, bf16[256,768]{0,1:T(8,128)(2,1)S(1)}, u32[]{:S(2)}, u32[]{:S(2)}) collective-permute-start(bf16[256,768]{0,1:T(8,128)(2,1)S(1)} %collective-permute-done.15), channel_id=1, source_target_pairs={{4,6},{2,0},{5,7},{3,1},{12,14},{10,8},{13,15},{11,9},{20,22},{18,... | collective-permute-start | bytes 1179656 | tf_op jit(solution)/shard_map/ppermute | solution.py:92
  69.0 20.8 %collective-permute-start.22 = (bf16[256,768]{0,1:T(8,128)(2,1)S(1)}, bf16[256,768]{0,1:T(8,128)(2,1)S(1)}, u32[]{:S(2)}, u32[]{:S(2)}) collective-permute-start(bf16[256,768]{0,1:T(8,128)(2,1)S(1)} %collective-permute-done.16), channel_id=1, source_target_pairs={{4,6},{2,0},{5,7},{3,1},{12,14},{10,8},{13,15},{11,9},{20,22},{18,... | collective-permute-start | bytes 1179656 | tf_op jit(solution)/shard_map/ppermute | solution.py:92
  90.0 2.5 %collective-permute-start.23 = (bf16[256,768]{0,1:T(8,128)(2,1)S(1)}, bf16[256,768]{0,1:T(8,128)(2,1)S(1)}, u32[]{:S(2)}, u32[]{:S(2)}) collective-permute-start(bf16[256,768]{0,1:T(8,128)(2,1)S(1)} %collective-permute-done.21), channel_id=1, source_target_pairs={{0,1},{1,0},{2,3},{3,2},{4,5},{5,4},{6,7},{7,6},{8,9},{9,8},{10,11... | collective-permute-start | bytes 1179656 | tf_op jit(solution)/shard_map/ppermute | solution.py:100
  90.0 2.5 %collective-permute-start.24 = (bf16[256,768]{0,1:T(8,128)(2,1)S(1)}, bf16[256,768]{0,1:T(8,128)(2,1)S(1)}, u32[]{:S(2)}, u32[]{:S(2)}) collective-permute-start(bf16[256,768]{0,1:T(8,128)(2,1)S(1)} %collective-permute-done.22), channel_id=1, source_target_pairs={{0,1},{1,0},{2,3},{3,2},{4,5},{5,4},{6,7},{7,6},{8,9},{9,8},{10,11... | collective-permute-start | bytes 1179656 | tf_op jit(solution)/shard_map/ppermute | solution.py:100

commit v20 on v18

--- a/solution.py
+++ b/solution.py
@@ -10,6 +10,7 @@
 TEMP = 12.0
 DEAD = 1000.0
 CORES = 2
+LAST_PARTS = 4
 
 
 def normalize(block):
@@ -92,15 +93,14 @@
     for step in range(1, chips):
         if step + 1 == chips:
             acc, received = lax.optimization_barrier((acc, received))
-        by_exchange, by_across = received
+        by_exchange, by_across = received[0], received[-1]
         if step + 2 < chips or (step + 2 == chips and chips < 4):
             received = (lax.ppermute(by_across, "chip", exchange), lax.ppermute(by_exchange, "chip", across))
         elif step + 2 == chips:
             ends = [(chips - 2, chips - 1), (1, 0)]
-            half = rows // 2
-            received = (
-                lax.ppermute(by_across[:half], "chip", ends),
-                lax.ppermute(by_across[half:], "chip", ends),
+            part = rows // LAST_PARTS
+            received = tuple(
+                lax.ppermute(by_across[i * part : (i + 1) * part], "chip", ends) for i in range(LAST_PARTS)
             )
         if step + 1 == chips and chips >= 4:
             far_chip = jnp.where(chip == 0, chips - 1, jnp.where(chip == chips - 1, 0, -1))

time: 82 us -> 86.8 us (1.059)
  starting transfers between devices: 29 us -> 32.4 us
  matrix products: 19 us -> 21.8 us
  waiting for transfers between devices: 27.7 us -> 25.7 us
    ppermute x2 -> x4, starting transfers between devices: 2.76 us -> 5.56 us  [per_device(): lax.ppermute(by_across[i * part:(i + 1) * part], 'chip', ends)]
    ppermute x2 -> x4, waiting for transfers between devices: 11.2 us -> 9.41 us  [per_device(): lax.ppermute(by_across[i * part:(i + 1) * part], 'chip', ends)]
    dot_general x13 -> x17, matrix products: 9.07 us -> 10.9 us  [pair_terms(): jnp.dot(weights.astype(jnp.bfloat16), got, preferred_element_type=jnp.flo...]
    dot_general x14 -> x18, matrix products: 9.35 us -> 10.3 us  [weigh(): scores = jnp.dot(unit_a, unit_b.T, preferred_element_type=jnp.float32)]
    reduce_sum x13 -> x16, other arithmetic: 2.6 us -> 2.86 us  [normalize(): jnp.sum(values * values, axis=-1, keepdims=True) + EPS]
  transfers between devices with their start and end apart: 16 -> 20, of which waited for: 6 -> 7; matrix products, arithmetic and copies ran while one was open for 24% -> 24% of each run, Pallas kernels for 0% -> 0%
where the time goes in v20:
time: 86.8 us; the launch traced here: 86.6 us
  starting transfers between devices  32.4 us (37%)
  waiting for transfers between devices  25.7 us (30%)
  matrix products  21.8 us (25%)
  other arithmetic  4.6 us (5%)
  local copies, waits for them, and re-layouts  1.11 us (1%)
  between operations  0.95 us (1%)
    ppermute x1, starting transfers between devices, per_device(): lax.ppermute(by_across, 'chip', exchange)  14.6 us
    dot_general x17, matrix products, pair_terms(): jnp.dot(weights.astype(jnp.bfloat16), got, preferred_element_type=jnp.flo...  10.9 us
    dot_general x18, matrix products, weigh(): scores = jnp.dot(unit_a, unit_b.T, preferred_element_type=jnp.float32)  10.3 us
    ppermute x4, waiting for transfers between devices, per_device(): lax.ppermute(by_across[i * part:(i + 1) * part], 'chip', ends)  9.41 us
    ppermute x3, waiting for transfers between devices, per_device(): lax.ppermute(outgoing, 'bucket', [(i, i ^ m) for i in range(buckets)])  8.15 us
    ppermute x1, waiting for transfers between devices, per_device(): lax.ppermute(by_across, 'chip', exchange)  7.14 us
    ppermute x4, starting transfers between devices, per_device(): lax.ppermute(by_across[i * part:(i + 1) * part], 'chip', ends)  5.56 us
    ppermute x3, starting transfers between devices, per_device(): lax.ppermute(outgoing, 'bucket', [(i, i ^ m) for i in range(buckets)])  4.57 us
  transfers between devices with their start and end apart: 20, of which 7 were waited for; matrix products, arithmetic and copies ran while one was open for 24% of the time, Pallas kernels for 0%

profile of v20, /device:TPU:0, one launch (start us, length us, event | category | flops | bytes accessed | tf_op | source)
XLA Modules:
  0.0 86.6 jit_solution(12301142479505585555)
XLA Ops:
  0.0 1.5 %fusion.21 = bf16[4,128,768]{2,1,0:T(8,128)(2,1)S(1)} fusion(bf16[1,1,4,128,768]{4,3,2,1,0:T(8,128)(2,1)} %param.2, s32[4]{0:T(128)} %bitcast.86, pred[768]{0:T(1024)(128)(4,1)S(1)} %iota_compare_fusion.2), kind=kLoop, calls=%fused_computation.44 | loop fusion | flops 1179648 | bytes 1573648 | tf_op jit(solution)/shard_map/jit(_where)/select_n | solution.py:41
  1.6 3.0 %collective-permute-start = (bf16[128,768]{1,0:T(8,128)(2,1)S(1)}, bf16[128,768]{1,0:T(8,128)(2,1)S(1)}, u32[]{:S(2)}, u32[]{:S(2)}) collective-permute-start(bf16[128,768]{1,0:T(8,128)(2,1)S(1)} %get-tuple-element.23), channel_id=1, source_target_pairs={{0,8},{8,0},{16,24},{24,16},{1,9},{9,1},{17,25},{25,17},{2,10},{10... | collective-permute-start | bytes 589832 | tf_op jit(solution)/shard_map/ppermute | solution.py:45
  4.6 1.5 %collective-permute-start.1 = (bf16[128,768]{1,0:T(8,128)(2,1)S(1)}, bf16[128,768]{1,0:T(8,128)(2,1)S(1)}, u32[]{:S(2)}, u32[]{:S(2)}) collective-permute-start(bf16[128,768]{1,0:T(8,128)(2,1)S(1)} %get-tuple-element.22), channel_id=1, source_target_pairs={{0,16},{8,24},{16,0},{24,8},{1,17},{9,25},{17,1},{25,9},{2,18},{10... | collective-permute-start | bytes 589832 | tf_op jit(solution)/shard_map/ppermute | solution.py:45
  6.9 3.5 %collective-permute-done = bf16[128,768]{1,0:T(8,128)(2,1)S(1)} collective-permute-done((bf16[128,768]{1,0:T(8,128)(2,1)S(1)}, bf16[128,768]{1,0:T(8,128)(2,1)S(1)}, u32[]{:S(2)}, u32[]{:S(2)}) %collective-permute-start) | collective-permute-done | bytes 196640 | tf_op jit(solution)/shard_map/ppermute | solution.py:45
  10.5 4.7 %collective-permute-done.1 = bf16[128,768]{1,0:T(8,128)(2,1)S(1)} collective-permute-done((bf16[128,768]{1,0:T(8,128)(2,1)S(1)}, bf16[128,768]{1,0:T(8,128)(2,1)S(1)}, u32[]{:S(2)}, u32[]{:S(2)}) %collective-permute-start.1) | collective-permute-done | bytes 196640 | tf_op jit(solution)/shard_map/ppermute | solution.py:45
  15.7 0.7 collective-permute-start.5
  16.6 4.4 %collective-permute-start.4 = (bf16[512,768]{0,1:T(8,128)(2,1)S(1)}, bf16[512,768]{0,1:T(8,128)(2,1)S(1)}, u32[]{:S(2)}, u32[]{:S(2)}) collective-permute-start(bf16[512,768]{0,1:T(8,128)(2,1)S(1)} %constant_dynamic-update-slice_fusion), channel_id=1, source_target_pairs={{0,2},{2,0},{4,6},{6,4},{1,3},{3,1},{5,7},{7,5},{8,10},{10,8},{12,... | collective-permute-start | bytes 2359304 | tf_op jit(solution)/shard_map/ppermute | solution.py:90
  21.1 0.8 multiply_reduce_fusion.9
  21.8 0.6 fusion.95
  22.5 14.6 %collective-permute-start.8 = (bf16[512,768]{0,1:T(8,128)(2,1)S(1)}, bf16[512,768]{0,1:T(8,128)(2,1)S(1)}, u32[]{:S(2)}, u32[]{:S(2)}) collective-permute-start(bf16[512,768]{0,1:T(8,128)(2,1)S(1)} %collective-permute-done.5), channel_id=1, source_target_pairs={{0,2},{2,0},{4,6},{6,4},{1,3},{3,1},{5,7},{7,5},{8,10},{10,8},{12,... | collective-permute-start | bytes 2359304 | tf_op jit(solution)/shard_map/ppermute | solution.py:98
  37.3 1.0 %collective-permute-done.4 = bf16[512,768]{0,1:T(8,128)(2,1)S(1)} collective-permute-done((bf16[512,768]{0,1:T(8,128)(2,1)S(1)}, bf16[512,768]{0,1:T(8,128)(2,1)S(1)}, u32[]{:S(2)}, u32[]{:S(2)}) %collective-permute-start.4) | collective-permute-done | bytes 786464 | tf_op jit(solution)/shard_map/ppermute | solution.py:90
  38.3 0.7 collective-permute-start.9
  39.6 0.7 multiply_reduce_fusion.6
  40.3 0.6 fusion.89
  41.0 0.7 multiply_reduce_fusion.7
  41.7 0.6 fusion.91
  42.3 0.7 multiply_reduce_fusion.8
  43.1 0.6 fusion.93
  43.9 1.3 %collective-permute-start.12 = (bf16[128,768]{0,1:T(8,128)(2,1)S(1)}, bf16[128,768]{0,1:T(8,128)(2,1)S(1)}, u32[]{:S(2)}, u32[]{:S(2)}) collective-permute-start(bf16[128,768]{0,1:T(8,128)(2,1)S(1)} %get-tuple-element.20), channel_id=1, source_target_pairs={{4,6},{2,0},{5,7},{3,1},{12,14},{10,8},{13,15},{11,9},{20,22},{18,... | collective-permute-start | bytes 589832 | tf_op jit(solution)/shard_map/ppermute | solution.py:103
  45.2 1.3 %collective-permute-start.13 = (bf16[128,768]{0,1:T(8,128)(2,1)S(1)}, bf16[128,768]{0,1:T(8,128)(2,1)S(1)}, u32[]{:S(2)}, u32[]{:S(2)}) collective-permute-start(bf16[128,768]{0,1:T(8,128)(2,1)S(1)} %get-tuple-element.19), channel_id=1, source_target_pairs={{4,6},{2,0},{5,7},{3,1},{12,14},{10,8},{13,15},{11,9},{20,22},{18,... | collective-permute-start | bytes 589832 | tf_op jit(solution)/shard_map/ppermute | solution.py:103
  46.7 7.1 %collective-permute-done.8 = bf16[512,768]{0,1:T(8,128)(2,1)S(1)} collective-permute-done((bf16[512,768]{0,1:T(8,128)(2,1)S(1)}, bf16[512,768]{0,1:T(8,128)(2,1)S(1)}, u32[]{:S(2)}, u32[]{:S(2)}) %collective-permute-start.8) | collective-permute-done | bytes 786464 | tf_op jit(solution)/shard_map/ppermute | solution.py:98
  53.8 1.5 %collective-permute-start.14 = (bf16[128,768]{0,1:T(8,128)(2,1)S(1)}, bf16[128,768]{0,1:T(8,128)(2,1)S(1)}, u32[]{:S(2)}, u32[]{:S(2)}) collective-permute-start(bf16[128,768]{0,1:T(8,128)(2,1)S(1)} %get-tuple-element.18), channel_id=1, source_target_pairs={{4,6},{2,0},{5,7},{3,1},{12,14},{10,8},{13,15},{11,9},{20,22},{18,... | collective-permute-start | bytes 589832 | tf_op jit(solution)/shard_map/ppermute | solution.py:103
  56.1 0.6 collective-permute-start.11
  56.6 0.7 multiply_reduce_fusion.2
  57.4 0.6 fusion.81
  58.0 0.7 multiply_reduce_fusion.3
  58.7 0.6 fusion.83
  59.4 0.7 multiply_reduce_fusion.4
  60.1 0.6 fusion.85
  60.7 0.7 multiply_reduce_fusion.5
  61.5 0.6 fusion.87
  62.1 1.5 %collective-permute-start.15 = (bf16[128,768]{0,1:T(8,128)(2,1)S(1)}, bf16[128,768]{0,1:T(8,128)(2,1)S(1)}, u32[]{:S(2)}, u32[]{:S(2)}) collective-permute-start(bf16[128,768]{0,1:T(8,128)(2,1)S(1)} %get-tuple-element.17), channel_id=1, source_target_pairs={{4,6},{2,0},{5,7},{3,1},{12,14},{10,8},{13,15},{11,9},{20,22},{18,... | collective-permute-start | bytes 589832 | tf_op jit(solution)/shard_map/ppermute | solution.py:103
  64.1 0.7 multiply_reduce_fusion.1
  64.8 0.6 fusion.79
  65.5 0.7 multiply_reduce_fusion
  66.2 1.2 %multiply_add_fusion = f32[512,768]{1,0:T(8,128)S(1)} fusion(f32[512,768]{1,0:T(8,128)S(1)} %fusion.79, f32[512,768]{1,0:T(8,128)S(1)} %fusion.81, f32[512,768]{1,0:T(8,128)S(1)} %fusion.83, f32[512,768]{1,0:T(8,128)S(1)} %fusion.85, f32[512,768]{1,0:T(8,128)S(1)} %fusion.87, f32[512,768]{1,0:T(8,128)S(1)} %fusion.89, f32[512,768]{1,0:T(8,128)S(1)} %fusion.91, ...), kind=kOutput, calls=%fused_computation.41 | convolution fusion | flops 409731072 | bytes 17039396 | tf_op jit(solution)/shard_map/dot_general | solution.py:77
  67.4 2.1 %collective-permute-done.13 = bf16[128,768]{0,1:T(8,128)(2,1)S(1)} collective-permute-done((bf16[128,768]{0,1:T(8,128)(2,1)S(1)}, bf16[128,768]{0,1:T(8,128)(2,1)S(1)}, u32[]{:S(2)}, u32[]{:S(2)}) %collective-permute-start.13) | collective-permute-done | bytes 196640 | tf_op jit(solution)/shard_map/ppermute | solution.py:103
  69.6 2.1 %collective-permute-done.14 = bf16[128,768]{0,1:T(8,128)(2,1)S(1)} collective-permute-done((bf16[128,768]{0,1:T(8,128)(2,1)S(1)}, bf16[128,768]{0,1:T(8,128)(2,1)S(1)}, u32[]{:S(2)}, u32[]{:S(2)}) %collective-permute-start.14) | collective-permute-done | bytes 196640 | tf_op jit(solution)/shard_map/ppermute | solution.py:103
  71.7 5.2 %collective-permute-done.15 = bf16[128,768]{0,1:T(8,128)(2,1)S(1)} collective-permute-done((bf16[128,768]{0,1:T(8,128)(2,1)S(1)}, bf16[128,768]{0,1:T(8,128)(2,1)S(1)}, u32[]{:S(2)}, u32[]{:S(2)}) %collective-permute-start.15) | collective-permute-done | bytes 196640 | tf_op jit(solution)/shard_map/ppermute | solution.py:103
  77.0 0.6 collective-permute-start.18
  77.7 0.5 collective-permute-start.16
  78.6 0.4 fusion.130
  79.4 0.4 fusion.134
  81.0 0.4 fusion.142
  83.4 0.4 fusion.132
  83.8 0.4 fusion.136
  84.2 0.4 fusion.140
  84.6 2.0 %fusion.43 = bf16[1,1,512,768]{3,2,1,0:T(8,128)(2,1)} fusion(bf16[128,768]{0,1:T(8,128)(2,1)S(1)} %collective-permute-done.19, f32[512,768]{1,0:T(8,128)S(1)} %fusion.130, f32[512,768]{1,0:T(8,128)S(1)} %fusion.132, f32[512,768]{1,0:T(8,128)S(1)} %fusion.134, f32[512,768]{1,0:T(8,128)S(1)} %fusion.136, f32[512,768]{1,0:T(8,128)S(1)} %fusion.138, ...), kind=kOutput, calls=%fused_computation.76 | convolution fusion | flops 108134400 | bytes 13701128 | tf_op jit(solution)/shard_map/dot_general | solution.py:77
  (93 shorter events, 7.8 us)
Async XLA Ops:
  1.6 8.8 %collective-permute-start = (bf16[128,768]{1,0:T(8,128)(2,1)S(1)}, bf16[128,768]{1,0:T(8,128)(2,1)S(1)}, u32[]{:S(2)}, u32[]{:S(2)}) collective-permute-start(bf16[128,768]{1,0:T(8,128)(2,1)S(1)} %get-tuple-element.23), channel_id=1, source_target_pairs={{0,8},{8,0},{16,24},{24,16},{1,9},{9,1},{17,25},{25,17},{2,10},{10... | collective-permute-start | bytes 589832 | tf_op jit(solution)/shard_map/ppermute | solution.py:45
  4.6 10.6 %collective-permute-start.1 = (bf16[128,768]{1,0:T(8,128)(2,1)S(1)}, bf16[128,768]{1,0:T(8,128)(2,1)S(1)}, u32[]{:S(2)}, u32[]{:S(2)}) collective-permute-start(bf16[128,768]{1,0:T(8,128)(2,1)S(1)} %get-tuple-element.22), channel_id=1, source_target_pairs={{0,16},{8,24},{16,0},{24,8},{1,17},{9,25},{17,1},{25,9},{2,18},{10... | collective-permute-start | bytes 589832 | tf_op jit(solution)/shard_map/ppermute | solution.py:45
  6.1 9.3 %collective-permute-start.2 = (bf16[128,768]{1,0:T(8,128)(2,1)S(1)}, bf16[128,768]{1,0:T(8,128)(2,1)S(1)}, u32[]{:S(2)}, u32[]{:S(2)}) collective-permute-start(bf16[128,768]{1,0:T(8,128)(2,1)S(1)} %get-tuple-element.21), channel_id=1, source_target_pairs={{0,24},{8,16},{16,8},{24,0},{1,25},{9,17},{17,9},{25,1},{2,26},{10... | collective-permute-start | bytes 589832 | tf_op jit(solution)/shard_map/ppermute | solution.py:45
  15.7 6.8 %collective-permute-start.5 = (bf16[512,768]{0,1:T(8,128)(2,1)S(1)}, bf16[512,768]{0,1:T(8,128)(2,1)S(1)}, u32[]{:S(2)}, u32[]{:S(2)}) collective-permute-start(bf16[512,768]{0,1:T(8,128)(2,1)S(1)} %constant_dynamic-update-slice_fusion), channel_id=1, source_target_pairs={{2,4},{4,2},{3,5},{5,3},{10,12},{12,10},{11,13},{13,11},{18,20},{2... | collective-permute-start | bytes 2359304 | tf_op jit(solution)/shard_map/ppermute | solution.py:90
  16.6 21.7 %collective-permute-start.4 = (bf16[512,768]{0,1:T(8,128)(2,1)S(1)}, bf16[512,768]{0,1:T(8,128)(2,1)S(1)}, u32[]{:S(2)}, u32[]{:S(2)}) collective-permute-start(bf16[512,768]{0,1:T(8,128)(2,1)S(1)} %constant_dynamic-update-slice_fusion), channel_id=1, source_target_pairs={{0,2},{2,0},{4,6},{6,4},{1,3},{3,1},{5,7},{7,5},{8,10},{10,8},{12,... | collective-permute-start | bytes 2359304 | tf_op jit(solution)/shard_map/ppermute | solution.py:90
  21.1 18.3 %collective-permute-start.3 = (bf16[512,768]{0,1:T(8,128)(2,1)S(1)}, bf16[512,768]{0,1:T(8,128)(2,1)S(1)}, u32[]{:S(2)}, u32[]{:S(2)}) collective-permute-start(bf16[512,768]{0,1:T(8,128)(2,1)S(1)} %constant_dynamic-update-slice_fusion), channel_id=1, source_target_pairs={{0,1},{1,0},{2,3},{3,2},{4,5},{5,4},{6,7},{7,6},{8,9},{9,8},{10,11... | collective-permute-start | bytes 2359304 | tf_op jit(solution)/shard_map/ppermute | solution.py:91
  22.5 31.3 %collective-permute-start.8 = (bf16[512,768]{0,1:T(8,128)(2,1)S(1)}, bf16[512,768]{0,1:T(8,128)(2,1)S(1)}, u32[]{:S(2)}, u32[]{:S(2)}) collective-permute-start(bf16[512,768]{0,1:T(8,128)(2,1)S(1)} %collective-permute-done.5), channel_id=1, source_target_pairs={{0,2},{2,0},{4,6},{6,4},{1,3},{3,1},{5,7},{7,5},{8,10},{10,8},{12,... | collective-permute-start | bytes 2359304 | tf_op jit(solution)/shard_map/ppermute | solution.py:98
  37.1 18.4 %collective-permute-start.7 = (bf16[512,768]{0,1:T(8,128)(2,1)S(1)}, bf16[512,768]{0,1:T(8,128)(2,1)S(1)}, u32[]{:S(2)}, u32[]{:S(2)}) collective-permute-start(bf16[512,768]{0,1:T(8,128)(2,1)S(1)} %collective-permute-done.5), channel_id=1, source_target_pairs={{0,1},{1,0},{2,3},{3,2},{4,5},{5,4},{6,7},{7,6},{8,9},{9,8},{10,11... | collective-permute-start | bytes 2359304 | tf_op jit(solution)/shard_map/ppermute | solution.py:115
  38.3 5.4 %collective-permute-start.9 = (bf16[512,768]{0,1:T(8,128)(2,1)S(1)}, bf16[512,768]{0,1:T(8,128)(2,1)S(1)}, u32[]{:S(2)}, u32[]{:S(2)}) collective-permute-start(bf16[512,768]{0,1:T(8,128)(2,1)S(1)} %collective-permute-done.4), channel_id=1, source_target_pairs={{2,4},{4,2},{3,5},{5,3},{10,12},{12,10},{11,13},{13,11},{18,20},{2... | collective-permute-start | bytes 2359304 | tf_op jit(solution)/shard_map/ppermute | solution.py:98
  39.0 16.8 %collective-permute-start.6 = (bf16[512,768]{0,1:T(8,128)(2,1)S(1)}, bf16[512,768]{0,1:T(8,128)(2,1)S(1)}, u32[]{:S(2)}, u32[]{:S(2)}) collective-permute-start(bf16[512,768]{0,1:T(8,128)(2,1)S(1)} %collective-permute-done.4), channel_id=1, source_target_pairs={{0,1},{1,0},{2,3},{3,2},{4,5},{5,4},{6,7},{7,6},{8,9},{9,8},{10,11... | collective-permute-start | bytes 2359304 | tf_op jit(solution)/shard_map/ppermute | solution.py:114
  43.9 23.6 %collective-permute-start.12 = (bf16[128,768]{0,1:T(8,128)(2,1)S(1)}, bf16[128,768]{0,1:T(8,128)(2,1)S(1)}, u32[]{:S(2)}, u32[]{:S(2)}) collective-permute-start(bf16[128,768]{0,1:T(8,128)(2,1)S(1)} %get-tuple-element.20), channel_id=1, source_target_pairs={{4,6},{2,0},{5,7},{3,1},{12,14},{10,8},{13,15},{11,9},{20,22},{18,... | collective-permute-start | bytes 589832 | tf_op jit(solution)/shard_map/ppermute | solution.py:103
  45.2 24.4 %collective-permute-start.13 = (bf16[128,768]{0,1:T(8,128)(2,1)S(1)}, bf16[128,768]{0,1:T(8,128)(2,1)S(1)}, u32[]{:S(2)}, u32[]{:S(2)}) collective-permute-start(bf16[128,768]{0,1:T(8,128)(2,1)S(1)} %get-tuple-element.19), channel_id=1, source_target_pairs={{4,6},{2,0},{5,7},{3,1},{12,14},{10,8},{13,15},{11,9},{20,22},{18,... | collective-permute-start | bytes 589832 | tf_op jit(solution)/shard_map/ppermute | solution.py:103
  53.8 17.9 %collective-permute-start.14 = (bf16[128,768]{0,1:T(8,128)(2,1)S(1)}, bf16[128,768]{0,1:T(8,128)(2,1)S(1)}, u32[]{:S(2)}, u32[]{:S(2)}) collective-permute-start(bf16[128,768]{0,1:T(8,128)(2,1)S(1)} %get-tuple-element.18), channel_id=1, source_target_pairs={{4,6},{2,0},{5,7},{3,1},{12,14},{10,8},{13,15},{11,9},{20,22},{18,... | collective-permute-start | bytes 589832 | tf_op jit(solution)/shard_map/ppermute | solution.py:103
  55.5 6.6 %collective-permute-start.10 = (bf16[512,768]{0,1:T(8,128)(2,1)S(1)}, bf16[512,768]{0,1:T(8,128)(2,1)S(1)}, u32[]{:S(2)}, u32[]{:S(2)}) collective-permute-start(bf16[512,768]{0,1:T(8,128)(2,1)S(1)} %collective-permute-done.8), channel_id=1, source_target_pairs={{0,1},{1,0},{2,3},{3,2},{4,5},{5,4},{6,7},{7,6},{8,9},{9,8},{10,11... | collective-permute-start | bytes 2359304 | tf_op jit(solution)/shard_map/ppermute | solution.py:114
  56.1 7.8 %collective-permute-start.11 = (bf16[512,768]{0,1:T(8,128)(2,1)S(1)}, bf16[512,768]{0,1:T(8,128)(2,1)S(1)}, u32[]{:S(2)}, u32[]{:S(2)}) collective-permute-start(bf16[512,768]{0,1:T(8,128)(2,1)S(1)} %collective-permute-done.9), channel_id=1, source_target_pairs={{0,1},{1,0},{2,3},{3,2},{4,5},{5,4},{6,7},{7,6},{8,9},{9,8},{10,11... | collective-permute-start | bytes 2359304 | tf_op jit(solution)/shard_map/ppermute | solution.py:115
  62.1 14.7 %collective-permute-start.15 = (bf16[128,768]{0,1:T(8,128)(2,1)S(1)}, bf16[128,768]{0,1:T(8,128)(2,1)S(1)}, u32[]{:S(2)}, u32[]{:S(2)}) collective-permute-start(bf16[128,768]{0,1:T(8,128)(2,1)S(1)} %get-tuple-element.17), channel_id=1, source_target_pairs={{4,6},{2,0},{5,7},{3,1},{12,14},{10,8},{13,15},{11,9},{20,22},{18,... | collective-permute-start | bytes 589832 | tf_op jit(solution)/shard_map/ppermute | solution.py:103
  76.8 4.9 %collective-permute-start.19 = (bf16[128,768]{0,1:T(8,128)(2,1)S(1)}, bf16[128,768]{0,1:T(8,128)(2,1)S(1)}, u32[]{:S(2)}, u32[]{:S(2)}) collective-permute-start(bf16[128,768]{0,1:T(8,128)(2,1)S(1)} %collective-permute-done.15), channel_id=1, source_target_pairs={{0,1},{1,0},{2,3},{3,2},{4,5},{5,4},{6,7},{7,6},{8,9},{9,8},{10,11... | collective-permute-start | bytes 589832 | tf_op jit(solution)/shard_map/ppermute | solution.py:108
  77.0 4.4 %collective-permute-start.18 = (bf16[128,768]{0,1:T(8,128)(2,1)S(1)}, bf16[128,768]{0,1:T(8,128)(2,1)S(1)}, u32[]{:S(2)}, u32[]{:S(2)}) collective-permute-start(bf16[128,768]{0,1:T(8,128)(2,1)S(1)} %collective-permute-done.14), channel_id=1, source_target_pairs={{0,1},{1,0},{2,3},{3,2},{4,5},{5,4},{6,7},{7,6},{8,9},{9,8},{10,11... | collective-permute-start | bytes 589832 | tf_op jit(solution)/shard_map/ppermute | solution.py:108
  77.5 4.0 %collective-permute-start.17 = (bf16[128,768]{0,1:T(8,128)(2,1)S(1)}, bf16[128,768]{0,1:T(8,128)(2,1)S(1)}, u32[]{:S(2)}, u32[]{:S(2)}) collective-permute-start(bf16[128,768]{0,1:T(8,128)(2,1)S(1)} %collective-permute-done.13), channel_id=1, source_target_pairs={{0,1},{1,0},{2,3},{3,2},{4,5},{5,4},{6,7},{7,6},{8,9},{9,8},{10,11... | collective-permute-start | bytes 589832 | tf_op jit(solution)/shard_map/ppermute | solution.py:108
  77.7 3.9 %collective-permute-start.16 = (bf16[128,768]{0,1:T(8,128)(2,1)S(1)}, bf16[128,768]{0,1:T(8,128)(2,1)S(1)}, u32[]{:S(2)}, u32[]{:S(2)}) collective-permute-start(bf16[128,768]{0,1:T(8,128)(2,1)S(1)} %collective-permute-done.12), channel_id=1, source_target_pairs={{0,1},{1,0},{2,3},{3,2},{4,5},{5,4},{6,7},{7,6},{8,9},{9,8},{10,11... | collective-permute-start | bytes 589832 | tf_op jit(solution)/shard_map/ppermute | solution.py:108

commit v21 on v20

--- a/solution.py
+++ b/solution.py
@@ -10,7 +10,7 @@
 TEMP = 12.0
 DEAD = 1000.0
 CORES = 2
-LAST_PARTS = 4
+LAST_PARTS = 3
 
 
 def normalize(block):
@@ -98,9 +98,9 @@
             received = (lax.ppermute(by_across, "chip", exchange), lax.ppermute(by_exchange, "chip", across))
         elif step + 2 == chips:
             ends = [(chips - 2, chips - 1), (1, 0)]
-            part = rows // LAST_PARTS
+            bounds = [(rows * i // LAST_PARTS) // 16 * 16 for i in range(LAST_PARTS)] + [rows]
             received = tuple(
-                lax.ppermute(by_across[i * part : (i + 1) * part], "chip", ends) for i in range(LAST_PARTS)
+                lax.ppermute(by_across[bounds[i] : bounds[i + 1]], "chip", ends) for i in range(LAST_PARTS)
             )
         if step + 1 == chips and chips >= 4:
             far_chip = jnp.where(chip == 0, chips - 1, jnp.where(chip == chips - 1, 0, -1))

time: 86.8 us -> 92.7 us (1.068)
  waiting for transfers between devices: 25.7 us -> 34.4 us
  starting transfers between devices: 32.4 us -> 30.4 us
    ppermute x4 -> x3, waiting for transfers between devices: 9.41 us -> 18.3 us  [per_device(): lax.ppermute(by_across[bounds[i]:bounds[i + 1]], 'chip', ends)]
    ppermute x4 -> x3, starting transfers between devices: 5.56 us -> 4.05 us  [per_device(): lax.ppermute(by_across[bounds[i]:bounds[i + 1]], 'chip', ends)]
    dot_general x17 -> x15, matrix products: 10.9 us -> 10.3 us  [pair_terms(): jnp.dot(weights.astype(jnp.bfloat16), got, preferred_element_type=jnp.flo...]
    dot_general x18 -> x16, matrix products: 10.3 us -> 9.92 us  [weigh(): scores = jnp.dot(unit_a, unit_b.T, preferred_element_type=jnp.float32)]
    reduce_sum x16 -> x15, other arithmetic: 2.86 us -> 2.9 us  [normalize(): jnp.sum(values * values, axis=-1, keepdims=True) + EPS]
  transfers between devices with their start and end apart: 20 -> 18, of which waited for: 7 -> 7; matrix products, arithmetic and copies ran while one was open for 24% -> 23% of each run, Pallas kernels for 0% -> 0%
where the time goes in v21:
time: 92.7 us; the launch traced here: 92.5 us
  waiting for transfers between devices  34.4 us (37%)
  starting transfers between devices  30.4 us (33%)
  matrix products  20.9 us (23%)
  other arithmetic  4.62 us (5%)
  local copies, waits for them, and re-layouts  1.33 us (1%)
    ppermute x3, waiting for transfers between devices, per_device(): lax.ppermute(by_across[bounds[i]:bounds[i + 1]], 'chip', ends)  18.3 us
    ppermute x1, starting transfers between devices, per_device(): lax.ppermute(by_across, 'chip', exchange)  14.6 us
    dot_general x15, matrix products, pair_terms(): jnp.dot(weights.astype(jnp.bfloat16), got, preferred_element_type=jnp.flo...  10.3 us
    dot_general x16, matrix products, weigh(): scores = jnp.dot(unit_a, unit_b.T, preferred_element_type=jnp.float32)  9.92 us
    ppermute x3, waiting for transfers between devices, per_device(): lax.ppermute(outgoing, 'bucket', [(i, i ^ m) for i in range(buckets)])  8.15 us
    ppermute x1, waiting for transfers between devices, per_device(): lax.ppermute(by_across, 'chip', exchange)  6.91 us
    ppermute x3, starting transfers between devices, per_device(): lax.ppermute(outgoing, 'bucket', [(i, i ^ m) for i in range(buckets)])  4.57 us
    ppermute x1, starting transfers between devices, per_device(): lax.ppermute(mine, 'chip', exchange)  4.41 us
  transfers between devices with their start and end apart: 18, of which 7 were waited for; matrix products, arithmetic and copies ran while one was open for 23% of the time, Pallas kernels for 0%

profile of v21, /device:TPU:0, one launch (start us, length us, event | category | flops | bytes accessed | tf_op | source)
XLA Modules:
  0.0 92.5 jit_solution(7266377864340679427)
XLA Ops:
  0.0 1.5 %fusion.21 = bf16[4,128,768]{2,1,0:T(8,128)(2,1)S(1)} fusion(bf16[1,1,4,128,768]{4,3,2,1,0:T(8,128)(2,1)} %param.2, s32[4]{0:T(128)} %bitcast.78, pred[768]{0:T(1024)(128)(4,1)S(1)} %iota_compare_fusion.2), kind=kLoop, calls=%fused_computation.44 | loop fusion | flops 1179648 | bytes 1573648 | tf_op jit(solution)/shard_map/jit(_where)/select_n | solution.py:41
  1.6 3.0 %collective-permute-start = (bf16[128,768]{1,0:T(8,128)(2,1)S(1)}, bf16[128,768]{1,0:T(8,128)(2,1)S(1)}, u32[]{:S(2)}, u32[]{:S(2)}) collective-permute-start(bf16[128,768]{1,0:T(8,128)(2,1)S(1)} %get-tuple-element.19), channel_id=1, source_target_pairs={{0,8},{8,0},{16,24},{24,16},{1,9},{9,1},{17,25},{25,17},{2,10},{10... | collective-permute-start | bytes 589832 | tf_op jit(solution)/shard_map/ppermute | solution.py:45
  4.6 1.5 %collective-permute-start.1 = (bf16[128,768]{1,0:T(8,128)(2,1)S(1)}, bf16[128,768]{1,0:T(8,128)(2,1)S(1)}, u32[]{:S(2)}, u32[]{:S(2)}) collective-permute-start(bf16[128,768]{1,0:T(8,128)(2,1)S(1)} %get-tuple-element.18), channel_id=1, source_target_pairs={{0,16},{8,24},{16,0},{24,8},{1,17},{9,25},{17,1},{25,9},{2,18},{10... | collective-permute-start | bytes 589832 | tf_op jit(solution)/shard_map/ppermute | solution.py:45
  6.9 3.5 %collective-permute-done = bf16[128,768]{1,0:T(8,128)(2,1)S(1)} collective-permute-done((bf16[128,768]{1,0:T(8,128)(2,1)S(1)}, bf16[128,768]{1,0:T(8,128)(2,1)S(1)}, u32[]{:S(2)}, u32[]{:S(2)}) %collective-permute-start) | collective-permute-done | bytes 196640 | tf_op jit(solution)/shard_map/ppermute | solution.py:45
  10.5 4.7 %collective-permute-done.1 = bf16[128,768]{1,0:T(8,128)(2,1)S(1)} collective-permute-done((bf16[128,768]{1,0:T(8,128)(2,1)S(1)}, bf16[128,768]{1,0:T(8,128)(2,1)S(1)}, u32[]{:S(2)}, u32[]{:S(2)}) %collective-permute-start.1) | collective-permute-done | bytes 196640 | tf_op jit(solution)/shard_map/ppermute | solution.py:45
  15.7 0.7 collective-permute-start.5
  16.6 4.4 %collective-permute-start.4 = (bf16[512,768]{0,1:T(8,128)(2,1)S(1)}, bf16[512,768]{0,1:T(8,128)(2,1)S(1)}, u32[]{:S(2)}, u32[]{:S(2)}) collective-permute-start(bf16[512,768]{0,1:T(8,128)(2,1)S(1)} %constant_dynamic-update-slice_fusion), channel_id=1, source_target_pairs={{0,2},{2,0},{4,6},{6,4},{1,3},{3,1},{5,7},{7,5},{8,10},{10,8},{12,... | collective-permute-start | bytes 2359304 | tf_op jit(solution)/shard_map/ppermute | solution.py:90
  21.1 0.8 multiply_reduce_fusion.9
  21.8 0.6 fusion.103
  22.5 14.6 %collective-permute-start.8 = (bf16[512,768]{0,1:T(8,128)(2,1)S(1)}, bf16[512,768]{0,1:T(8,128)(2,1)S(1)}, u32[]{:S(2)}, u32[]{:S(2)}) collective-permute-start(bf16[512,768]{0,1:T(8,128)(2,1)S(1)} %collective-permute-done.5), channel_id=1, source_target_pairs={{0,2},{2,0},{4,6},{6,4},{1,3},{3,1},{5,7},{7,5},{8,10},{10,8},{12,... | collective-permute-start | bytes 2359304 | tf_op jit(solution)/shard_map/ppermute | solution.py:98
  37.3 1.0 %collective-permute-done.4 = bf16[512,768]{0,1:T(8,128)(2,1)S(1)} collective-permute-done((bf16[512,768]{0,1:T(8,128)(2,1)S(1)}, bf16[512,768]{0,1:T(8,128)(2,1)S(1)}, u32[]{:S(2)}, u32[]{:S(2)}) %collective-permute-start.4) | collective-permute-done | bytes 786464 | tf_op jit(solution)/shard_map/ppermute | solution.py:90
  38.3 0.7 collective-permute-start.9
  39.6 0.7 multiply_reduce_fusion.6
  40.3 0.6 fusion.97
  41.0 0.7 multiply_reduce_fusion.7
  41.7 0.6 fusion.99
  42.3 0.7 multiply_reduce_fusion.8
  43.1 0.6 fusion.101
  43.7 1.3 %collective-permute-start.12 = (bf16[160,768]{0,1:T(8,128)(2,1)S(1)}, bf16[160,768]{0,1:T(8,128)(2,1)S(1)}, u32[]{:S(2)}, u32[]{:S(2)}) collective-permute-start(bf16[160,768]{0,1:T(8,128)(2,1)S(1)} %slice.86), channel_id=1, source_target_pairs={{4,6},{2,0},{5,7},{3,1},{12,14},{10,8},{13,15},{11,9},{20,22},{18,... | collective-permute-start | bytes 737288 | tf_op jit(solution)/shard_map/ppermute | solution.py:103
  45.4 1.3 %collective-permute-start.13 = (bf16[176,768]{0,1:T(8,128)(2,1)S(1)}, bf16[176,768]{0,1:T(8,128)(2,1)S(1)}, u32[]{:S(2)}, u32[]{:S(2)}) collective-permute-start(bf16[176,768]{0,1:T(8,128)(2,1)S(1)} %get-tuple-element.16), channel_id=1, source_target_pairs={{4,6},{2,0},{5,7},{3,1},{12,14},{10,8},{13,15},{11,9},{20,22},{18,... | collective-permute-start | bytes 811016 | tf_op jit(solution)/shard_map/ppermute | solution.py:103
  46.9 6.9 %collective-permute-done.8 = bf16[512,768]{0,1:T(8,128)(2,1)S(1)} collective-permute-done((bf16[512,768]{0,1:T(8,128)(2,1)S(1)}, bf16[512,768]{0,1:T(8,128)(2,1)S(1)}, u32[]{:S(2)}, u32[]{:S(2)}) %collective-permute-start.8) | collective-permute-done | bytes 786464 | tf_op jit(solution)/shard_map/ppermute | solution.py:98
  53.8 1.5 %collective-permute-start.14 = (bf16[176,768]{0,1:T(8,128)(2,1)S(1)}, bf16[176,768]{0,1:T(8,128)(2,1)S(1)}, u32[]{:S(2)}, u32[]{:S(2)}) collective-permute-start(bf16[176,768]{0,1:T(8,128)(2,1)S(1)} %get-tuple-element.15), channel_id=1, source_target_pairs={{4,6},{2,0},{5,7},{3,1},{12,14},{10,8},{13,15},{11,9},{20,22},{18,... | collective-permute-start | bytes 811016 | tf_op jit(solution)/shard_map/ppermute | solution.py:103
  56.1 0.6 collective-permute-start.11
  56.6 0.7 multiply_reduce_fusion.2
  57.4 0.6 fusion.89
  58.0 0.7 multiply_reduce_fusion.3
  58.7 0.6 fusion.91
  59.4 0.7 multiply_reduce_fusion.4
  60.1 0.6 fusion.93
  60.7 0.7 multiply_reduce_fusion.5
  61.5 0.6 fusion.95
  62.6 0.7 multiply_reduce_fusion.1
  63.3 0.6 fusion.87
  63.9 0.7 multiply_reduce_fusion
  64.7 1.2 %multiply_add_fusion = f32[512,768]{1,0:T(8,128)S(1)} fusion(f32[512,768]{1,0:T(8,128)S(1)} %fusion.87, f32[512,768]{1,0:T(8,128)S(1)} %fusion.89, f32[512,768]{1,0:T(8,128)S(1)} %fusion.91, f32[512,768]{1,0:T(8,128)S(1)} %fusion.93, f32[512,768]{1,0:T(8,128)S(1)} %fusion.95, f32[512,768]{1,0:T(8,128)S(1)} %fusion.97, f32[512,768]{1,0:T(8,128)S(1)} %fusion.99, ...), kind=kOutput, calls=%fused_computation.41 | convolution fusion | flops 409731072 | bytes 17039396 | tf_op jit(solution)/shard_map/dot_general | solution.py:77
  65.9 4.6 %collective-permute-done.12 = bf16[160,768]{0,1:T(8,128)(2,1)S(1)} collective-permute-done((bf16[160,768]{0,1:T(8,128)(2,1)S(1)}, bf16[160,768]{0,1:T(8,128)(2,1)S(1)}, u32[]{:S(2)}, u32[]{:S(2)}) %collective-permute-start.12) | collective-permute-done | bytes 245792 | tf_op jit(solution)/shard_map/ppermute | solution.py:103
  70.5 8.4 %collective-permute-done.13 = bf16[176,768]{0,1:T(8,128)(2,1)S(1)} collective-permute-done((bf16[176,768]{0,1:T(8,128)(2,1)S(1)}, bf16[176,768]{0,1:T(8,128)(2,1)S(1)}, u32[]{:S(2)}, u32[]{:S(2)}) %collective-permute-start.13) | collective-permute-done | bytes 270368 | tf_op jit(solution)/shard_map/ppermute | solution.py:103
  78.9 5.3 %collective-permute-done.14 = bf16[176,768]{0,1:T(8,128)(2,1)S(1)} collective-permute-done((bf16[176,768]{0,1:T(8,128)(2,1)S(1)}, bf16[176,768]{0,1:T(8,128)(2,1)S(1)}, u32[]{:S(2)}, u32[]{:S(2)}) %collective-permute-start.14) | collective-permute-done | bytes 270368 | tf_op jit(solution)/shard_map/ppermute | solution.py:103
  84.4 0.6 collective-permute-start.16
  85.2 0.4 multiply_reduce_fusion.11
  86.1 0.4 multiply_reduce_fusion.13
  86.5 0.4 fusion.122
  87.3 0.7 fusion.126
  88.2 0.4 multiply_reduce_fusion.14
  88.6 0.4 fusion.124
  89.3 0.4 multiply_reduce_fusion.12
  89.8 0.4 multiply_reduce_fusion.10
  90.6 1.9 %fusion.43 = bf16[1,1,512,768]{3,2,1,0:T(8,128)(2,1)} fusion(bf16[176,768]{0,1:T(8,128)(2,1)S(1)} %collective-permute-done.17, f32[512,768]{1,0:T(8,128)S(1)} %fusion.118, f32[512,768]{1,0:T(8,128)S(1)} %fusion.120, f32[512,768]{1,0:T(8,128)S(1)} %fusion.122, f32[512,768]{1,0:T(8,128)S(1)} %fusion.124, f32[512,768]{1,0:T(8,128)S(1)} %multiply_add_fusion, ...), kind=kOutput, calls=%fused_computation.76 | convolution fusion | flops 144310272 | bytes 10678280 | tf_op jit(solution)/shard_map/dot_general | solution.py:77
  (82 shorter events, 6.0 us)
Async XLA Ops:
  1.6 8.8 %collective-permute-start = (bf16[128,768]{1,0:T(8,128)(2,1)S(1)}, bf16[128,768]{1,0:T(8,128)(2,1)S(1)}, u32[]{:S(2)}, u32[]{:S(2)}) collective-permute-start(bf16[128,768]{1,0:T(8,128)(2,1)S(1)} %get-tuple-element.19), channel_id=1, source_target_pairs={{0,8},{8,0},{16,24},{24,16},{1,9},{9,1},{17,25},{25,17},{2,10},{10... | collective-permute-start | bytes 589832 | tf_op jit(solution)/shard_map/ppermute | solution.py:45
  4.6 10.6 %collective-permute-start.1 = (bf16[128,768]{1,0:T(8,128)(2,1)S(1)}, bf16[128,768]{1,0:T(8,128)(2,1)S(1)}, u32[]{:S(2)}, u32[]{:S(2)}) collective-permute-start(bf16[128,768]{1,0:T(8,128)(2,1)S(1)} %get-tuple-element.18), channel_id=1, source_target_pairs={{0,16},{8,24},{16,0},{24,8},{1,17},{9,25},{17,1},{25,9},{2,18},{10... | collective-permute-start | bytes 589832 | tf_op jit(solution)/shard_map/ppermute | solution.py:45
  6.1 9.3 %collective-permute-start.2 = (bf16[128,768]{1,0:T(8,128)(2,1)S(1)}, bf16[128,768]{1,0:T(8,128)(2,1)S(1)}, u32[]{:S(2)}, u32[]{:S(2)}) collective-permute-start(bf16[128,768]{1,0:T(8,128)(2,1)S(1)} %get-tuple-element.17), channel_id=1, source_target_pairs={{0,24},{8,16},{16,8},{24,0},{1,25},{9,17},{17,9},{25,1},{2,26},{10... | collective-permute-start | bytes 589832 | tf_op jit(solution)/shard_map/ppermute | solution.py:45
  15.7 6.8 %collective-permute-start.5 = (bf16[512,768]{0,1:T(8,128)(2,1)S(1)}, bf16[512,768]{0,1:T(8,128)(2,1)S(1)}, u32[]{:S(2)}, u32[]{:S(2)}) collective-permute-start(bf16[512,768]{0,1:T(8,128)(2,1)S(1)} %constant_dynamic-update-slice_fusion), channel_id=1, source_target_pairs={{2,4},{4,2},{3,5},{5,3},{10,12},{12,10},{11,13},{13,11},{18,20},{2... | collective-permute-start | bytes 2359304 | tf_op jit(solution)/shard_map/ppermute | solution.py:90
  16.6 21.7 %collective-permute-start.4 = (bf16[512,768]{0,1:T(8,128)(2,1)S(1)}, bf16[512,768]{0,1:T(8,128)(2,1)S(1)}, u32[]{:S(2)}, u32[]{:S(2)}) collective-permute-start(bf16[512,768]{0,1:T(8,128)(2,1)S(1)} %constant_dynamic-update-slice_fusion), channel_id=1, source_target_pairs={{0,2},{2,0},{4,6},{6,4},{1,3},{3,1},{5,7},{7,5},{8,10},{10,8},{12,... | collective-permute-start | bytes 2359304 | tf_op jit(solution)/shard_map/ppermute | solution.py:90
  21.1 18.3 %collective-permute-start.3 = (bf16[512,768]{0,1:T(8,128)(2,1)S(1)}, bf16[512,768]{0,1:T(8,128)(2,1)S(1)}, u32[]{:S(2)}, u32[]{:S(2)}) collective-permute-start(bf16[512,768]{0,1:T(8,128)(2,1)S(1)} %constant_dynamic-update-slice_fusion), channel_id=1, source_target_pairs={{0,1},{1,0},{2,3},{3,2},{4,5},{5,4},{6,7},{7,6},{8,9},{9,8},{10,11... | collective-permute-start | bytes 2359304 | tf_op jit(solution)/shard_map/ppermute | solution.py:91
  22.5 31.3 %collective-permute-start.8 = (bf16[512,768]{0,1:T(8,128)(2,1)S(1)}, bf16[512,768]{0,1:T(8,128)(2,1)S(1)}, u32[]{:S(2)}, u32[]{:S(2)}) collective-permute-start(bf16[512,768]{0,1:T(8,128)(2,1)S(1)} %collective-permute-done.5), channel_id=1, source_target_pairs={{0,2},{2,0},{4,6},{6,4},{1,3},{3,1},{5,7},{7,5},{8,10},{10,8},{12,... | collective-permute-start | bytes 2359304 | tf_op jit(solution)/shard_map/ppermute | solution.py:98
  37.1 18.4 %collective-permute-start.7 = (bf16[512,768]{0,1:T(8,128)(2,1)S(1)}, bf16[512,768]{0,1:T(8,128)(2,1)S(1)}, u32[]{:S(2)}, u32[]{:S(2)}) collective-permute-start(bf16[512,768]{0,1:T(8,128)(2,1)S(1)} %collective-permute-done.5), channel_id=1, source_target_pairs={{0,1},{1,0},{2,3},{3,2},{4,5},{5,4},{6,7},{7,6},{8,9},{9,8},{10,11... | collective-permute-start | bytes 2359304 | tf_op jit(solution)/shard_map/ppermute | solution.py:115
  38.3 5.4 %collective-permute-start.9 = (bf16[512,768]{0,1:T(8,128)(2,1)S(1)}, bf16[512,768]{0,1:T(8,128)(2,1)S(1)}, u32[]{:S(2)}, u32[]{:S(2)}) collective-permute-start(bf16[512,768]{0,1:T(8,128)(2,1)S(1)} %collective-permute-done.4), channel_id=1, source_target_pairs={{2,4},{4,2},{3,5},{5,3},{10,12},{12,10},{11,13},{13,11},{18,20},{2... | collective-permute-start | bytes 2359304 | tf_op jit(solution)/shard_map/ppermute | solution.py:98
  39.0 16.8 %collective-permute-start.6 = (bf16[512,768]{0,1:T(8,128)(2,1)S(1)}, bf16[512,768]{0,1:T(8,128)(2,1)S(1)}, u32[]{:S(2)}, u32[]{:S(2)}) collective-permute-start(bf16[512,768]{0,1:T(8,128)(2,1)S(1)} %collective-permute-done.4), channel_id=1, source_target_pairs={{0,1},{1,0},{2,3},{3,2},{4,5},{5,4},{6,7},{7,6},{8,9},{9,8},{10,11... | collective-permute-start | bytes 2359304 | tf_op jit(solution)/shard_map/ppermute | solution.py:114
  43.7 26.7 %collective-permute-start.12 = (bf16[160,768]{0,1:T(8,128)(2,1)S(1)}, bf16[160,768]{0,1:T(8,128)(2,1)S(1)}, u32[]{:S(2)}, u32[]{:S(2)}) collective-permute-start(bf16[160,768]{0,1:T(8,128)(2,1)S(1)} %slice.86), channel_id=1, source_target_pairs={{4,6},{2,0},{5,7},{3,1},{12,14},{10,8},{13,15},{11,9},{20,22},{18,... | collective-permute-start | bytes 737288 | tf_op jit(solution)/shard_map/ppermute | solution.py:103
  45.4 33.5 %collective-permute-start.13 = (bf16[176,768]{0,1:T(8,128)(2,1)S(1)}, bf16[176,768]{0,1:T(8,128)(2,1)S(1)}, u32[]{:S(2)}, u32[]{:S(2)}) collective-permute-start(bf16[176,768]{0,1:T(8,128)(2,1)S(1)} %get-tuple-element.16), channel_id=1, source_target_pairs={{4,6},{2,0},{5,7},{3,1},{12,14},{10,8},{13,15},{11,9},{20,22},{18,... | collective-permute-start | bytes 811016 | tf_op jit(solution)/shard_map/ppermute | solution.py:103
  53.8 30.4 %collective-permute-start.14 = (bf16[176,768]{0,1:T(8,128)(2,1)S(1)}, bf16[176,768]{0,1:T(8,128)(2,1)S(1)}, u32[]{:S(2)}, u32[]{:S(2)}) collective-permute-start(bf16[176,768]{0,1:T(8,128)(2,1)S(1)} %get-tuple-element.15), channel_id=1, source_target_pairs={{4,6},{2,0},{5,7},{3,1},{12,14},{10,8},{13,15},{11,9},{20,22},{18,... | collective-permute-start | bytes 811016 | tf_op jit(solution)/shard_map/ppermute | solution.py:103
  55.5 6.6 %collective-permute-start.10 = (bf16[512,768]{0,1:T(8,128)(2,1)S(1)}, bf16[512,768]{0,1:T(8,128)(2,1)S(1)}, u32[]{:S(2)}, u32[]{:S(2)}) collective-permute-start(bf16[512,768]{0,1:T(8,128)(2,1)S(1)} %collective-permute-done.8), channel_id=1, source_target_pairs={{0,1},{1,0},{2,3},{3,2},{4,5},{5,4},{6,7},{7,6},{8,9},{9,8},{10,11... | collective-permute-start | bytes 2359304 | tf_op jit(solution)/shard_map/ppermute | solution.py:114
  56.1 6.2 %collective-permute-start.11 = (bf16[512,768]{0,1:T(8,128)(2,1)S(1)}, bf16[512,768]{0,1:T(8,128)(2,1)S(1)}, u32[]{:S(2)}, u32[]{:S(2)}) collective-permute-start(bf16[512,768]{0,1:T(8,128)(2,1)S(1)} %collective-permute-done.9), channel_id=1, source_target_pairs={{0,1},{1,0},{2,3},{3,2},{4,5},{5,4},{6,7},{7,6},{8,9},{9,8},{10,11... | collective-permute-start | bytes 2359304 | tf_op jit(solution)/shard_map/ppermute | solution.py:115
  84.2 5.0 %collective-permute-start.17 = (bf16[176,768]{0,1:T(8,128)(2,1)S(1)}, bf16[176,768]{0,1:T(8,128)(2,1)S(1)}, u32[]{:S(2)}, u32[]{:S(2)}) collective-permute-start(bf16[176,768]{0,1:T(8,128)(2,1)S(1)} %collective-permute-done.14), channel_id=1, source_target_pairs={{0,1},{1,0},{2,3},{3,2},{4,5},{5,4},{6,7},{7,6},{8,9},{9,8},{10,11... | collective-permute-start | bytes 811016 | tf_op jit(solution)/shard_map/ppermute | solution.py:108
  84.4 4.6 %collective-permute-start.16 = (bf16[176,768]{0,1:T(8,128)(2,1)S(1)}, bf16[176,768]{0,1:T(8,128)(2,1)S(1)}, u32[]{:S(2)}, u32[]{:S(2)}) collective-permute-start(bf16[176,768]{0,1:T(8,128)(2,1)S(1)} %collective-permute-done.13), channel_id=1, source_target_pairs={{0,1},{1,0},{2,3},{3,2},{4,5},{5,4},{6,7},{7,6},{8,9},{9,8},{10,11... | collective-permute-start | bytes 811016 | tf_op jit(solution)/shard_map/ppermute | solution.py:108
  85.0 3.0 %collective-permute-start.15 = (bf16[160,768]{0,1:T(8,128)(2,1)S(1)}, bf16[160,768]{0,1:T(8,128)(2,1)S(1)}, u32[]{:S(2)}, u32[]{:S(2)}) collective-permute-start(bf16[160,768]{0,1:T(8,128)(2,1)S(1)} %collective-permute-done.12), channel_id=1, source_target_pairs={{0,1},{1,0},{2,3},{3,2},{4,5},{5,4},{6,7},{7,6},{8,9},{9,8},{10,11... | collective-permute-start | bytes 737288 | tf_op jit(solution)/shard_map/ppermute | solution.py:108

commit v22 on v18

--- a/solution.py
+++ b/solution.py
@@ -90,8 +90,6 @@
     swapped = lax.ppermute(mine, "core", swap)
     acc = add_pair(acc, swapped, times_listed(chip, other_core))
     for step in range(1, chips):
-        if step + 1 == chips:
-            acc, received = lax.optimization_barrier((acc, received))
         by_exchange, by_across = received
         if step + 2 < chips or (step + 2 == chips and chips < 4):
             received = (lax.ppermute(by_across, "chip", exchange), lax.ppermute(by_exchange, "chip", across))

time: 82 us -> 90.9 us (1.11)
  waiting for transfers between devices: 27.7 us -> 46.8 us
  starting transfers between devices: 29 us -> 18.2 us
    ppermute x1, waiting for transfers between devices: 1.01 us -> 13.6 us  [per_device(): lax.ppermute(mine, 'chip', exchange)]
    ppermute x1, starting transfers between devices: 14.6 us -> 6.42 us  [per_device(): lax.ppermute(by_across, 'chip', exchange)]
    ppermute x1, waiting for transfers between devices: 7.26 us -> 13.2 us  [per_device(): lax.ppermute(by_across, 'chip', exchange)]
    ppermute x1, starting transfers between devices: 4.41 us -> 1.64 us  [per_device(): lax.ppermute(mine, 'chip', exchange)]
    ppermute x1, waiting for transfers between devices: 5.33 us -> 6.73 us  [per_device(): lax.ppermute(by_across[half:], 'chip', ends)]
    ppermute x1, waiting for transfers between devices: 5.89 us -> 4.96 us  [per_device(): lax.ppermute(by_across[:half], 'chip', ends)]
    reduce_sum x13 -> x14, other arithmetic: 2.6 us -> 2.7 us  [normalize(): jnp.sum(values * values, axis=-1, keepdims=True) + EPS]
  transfers between devices with their start and end apart: 16 -> 16, of which waited for: 6 -> 7; matrix products, arithmetic and copies ran while one was open for 24% -> 17% of each run, Pallas kernels for 0% -> 0%
where the time goes in v22:
time: 90.9 us; the launch traced here: 90.7 us
  waiting for transfers between devices  46.8 us (51%)
  matrix products  19.4 us (21%)
  starting transfers between devices  18.2 us (20%)
  other arithmetic  4.4 us (5%)
  local copies, waits for them, and re-layouts  1.03 us (1%)
    ppermute x1, waiting for transfers between devices, per_device(): lax.ppermute(mine, 'chip', exchange)  13.6 us
    ppermute x1, waiting for transfers between devices, per_device(): lax.ppermute(by_across, 'chip', exchange)  13.2 us
    dot_general x13, matrix products, pair_terms(): jnp.dot(weights.astype(jnp.bfloat16), got, preferred_element_type=jnp.flo...  9.46 us
    dot_general x14, matrix products, weigh(): scores = jnp.dot(unit_a, unit_b.T, preferred_element_type=jnp.float32)  9.33 us
    ppermute x3, waiting for transfers between devices, per_device(): lax.ppermute(outgoing, 'bucket', [(i, i ^ m) for i in range(buckets)])  8.15 us
    ppermute x1, waiting for transfers between devices, per_device(): lax.ppermute(by_across[half:], 'chip', ends)  6.73 us
    ppermute x1, starting transfers between devices, per_device(): lax.ppermute(by_across, 'chip', exchange)  6.42 us
    ppermute x1, waiting for transfers between devices, per_device(): lax.ppermute(by_across[:half], 'chip', ends)  4.96 us
  transfers between devices with their start and end apart: 16, of which 7 were waited for; matrix products, arithmetic and copies ran while one was open for 17% of the time, Pallas kernels for 0%

profile of v22, /device:TPU:0, one launch (start us, length us, event | category | flops | bytes accessed | tf_op | source)
XLA Modules:
  0.0 90.7 jit_solution(2612633066270222018)
XLA Ops:
  0.0 1.5 %fusion.21 = bf16[4,128,768]{2,1,0:T(8,128)(2,1)S(1)} fusion(bf16[1,1,4,128,768]{4,3,2,1,0:T(8,128)(2,1)} %param.2, s32[4]{0:T(128)} %bitcast.70, pred[768]{0:T(1024)(128)(4,1)S(1)} %iota_compare_fusion.2), kind=kLoop, calls=%fused_computation.43 | loop fusion | flops 1179648 | bytes 1573648 | tf_op jit(solution)/shard_map/jit(_where)/select_n | solution.py:40
  1.6 3.0 %collective-permute-start = (bf16[128,768]{1,0:T(8,128)(2,1)S(1)}, bf16[128,768]{1,0:T(8,128)(2,1)S(1)}, u32[]{:S(2)}, u32[]{:S(2)}) collective-permute-start(bf16[128,768]{1,0:T(8,128)(2,1)S(1)} %get-tuple-element.9), channel_id=1, source_target_pairs={{0,8},{8,0},{16,24},{24,16},{1,9},{9,1},{17,25},{25,17},{2,10},{10... | collective-permute-start | bytes 589832 | tf_op jit(solution)/shard_map/ppermute | solution.py:44
  4.6 1.5 %collective-permute-start.1 = (bf16[128,768]{1,0:T(8,128)(2,1)S(1)}, bf16[128,768]{1,0:T(8,128)(2,1)S(1)}, u32[]{:S(2)}, u32[]{:S(2)}) collective-permute-start(bf16[128,768]{1,0:T(8,128)(2,1)S(1)} %get-tuple-element.8), channel_id=1, source_target_pairs={{0,16},{8,24},{16,0},{24,8},{1,17},{9,25},{17,1},{25,9},{2,18},{10... | collective-permute-start | bytes 589832 | tf_op jit(solution)/shard_map/ppermute | solution.py:44
  6.9 3.5 %collective-permute-done = bf16[128,768]{1,0:T(8,128)(2,1)S(1)} collective-permute-done((bf16[128,768]{1,0:T(8,128)(2,1)S(1)}, bf16[128,768]{1,0:T(8,128)(2,1)S(1)}, u32[]{:S(2)}, u32[]{:S(2)}) %collective-permute-start) | collective-permute-done | bytes 196640 | tf_op jit(solution)/shard_map/ppermute | solution.py:44
  10.5 4.7 %collective-permute-done.1 = bf16[128,768]{1,0:T(8,128)(2,1)S(1)} collective-permute-done((bf16[128,768]{1,0:T(8,128)(2,1)S(1)}, bf16[128,768]{1,0:T(8,128)(2,1)S(1)}, u32[]{:S(2)}, u32[]{:S(2)}) %collective-permute-start.1) | collective-permute-done | bytes 196640 | tf_op jit(solution)/shard_map/ppermute | solution.py:44
  15.7 1.6 %collective-permute-start.4 = (bf16[512,768]{0,1:T(8,128)(2,1)S(1)}, bf16[512,768]{0,1:T(8,128)(2,1)S(1)}, u32[]{:S(2)}, u32[]{:S(2)}) collective-permute-start(bf16[512,768]{0,1:T(8,128)(2,1)S(1)} %constant_dynamic-update-slice_fusion), channel_id=1, source_target_pairs={{0,2},{2,0},{4,6},{6,4},{1,3},{3,1},{5,7},{7,5},{8,10},{10,8},{12,... | collective-permute-start | bytes 2359304 | tf_op jit(solution)/shard_map/ppermute | solution.py:89
  17.6 0.7 collective-permute-start.5
  18.4 0.8 multiply_reduce_fusion.9
  19.2 0.6 fusion.95
  20.1 13.6 %collective-permute-done.4 = bf16[512,768]{0,1:T(8,128)(2,1)S(1)} collective-permute-done((bf16[512,768]{0,1:T(8,128)(2,1)S(1)}, bf16[512,768]{0,1:T(8,128)(2,1)S(1)}, u32[]{:S(2)}, u32[]{:S(2)}) %collective-permute-start.4) | collective-permute-done | bytes 786464 | tf_op jit(solution)/shard_map/ppermute | solution.py:89
  33.7 0.7 collective-permute-start.9
  34.4 0.2 fusion.4
  34.7 0.2 fusion.6
  35.0 0.5 collective-permute-start.7
  35.5 6.4 %collective-permute-start.8 = (bf16[512,768]{0,1:T(8,128)(2,1)S(1)}, bf16[512,768]{0,1:T(8,128)(2,1)S(1)}, u32[]{:S(2)}, u32[]{:S(2)}) collective-permute-start(bf16[512,768]{0,1:T(8,128)(2,1)S(1)} %collective-permute-done.5), channel_id=1, source_target_pairs={{0,2},{2,0},{4,6},{6,4},{1,3},{3,1},{5,7},{7,5},{8,10},{10,8},{12,... | collective-permute-start | bytes 2359304 | tf_op jit(solution)/shard_map/ppermute | solution.py:95
  41.9 0.7 multiply_reduce_fusion.8
  42.6 0.6 fusion.93
  43.2 0.7 multiply_reduce_fusion.7
  44.0 0.6 fusion.91
  44.6 0.7 multiply_reduce_fusion.6
  45.4 0.6 fusion.89
  46.4 13.2 %collective-permute-done.8 = bf16[512,768]{0,1:T(8,128)(2,1)S(1)} collective-permute-done((bf16[512,768]{0,1:T(8,128)(2,1)S(1)}, bf16[512,768]{0,1:T(8,128)(2,1)S(1)}, u32[]{:S(2)}, u32[]{:S(2)}) %collective-permute-start.8) | collective-permute-done | bytes 786464 | tf_op jit(solution)/shard_map/ppermute | solution.py:95
  60.2 1.3 %collective-permute-start.12 = (bf16[256,768]{0,1:T(8,128)(2,1)S(1)}, bf16[256,768]{0,1:T(8,128)(2,1)S(1)}, u32[]{:S(2)}, u32[]{:S(2)}) collective-permute-start(bf16[256,768]{0,1:T(8,128)(2,1)S(1)} %get-tuple-element.5), channel_id=1, source_target_pairs={{4,6},{2,0},{5,7},{3,1},{12,14},{10,8},{13,15},{11,9},{20,22},{18,... | collective-permute-start | bytes 1179656 | tf_op jit(solution)/shard_map/ppermute | solution.py:100
  61.5 1.5 %collective-permute-start.14 = (bf16[256,768]{0,1:T(8,128)(2,1)S(1)}, bf16[256,768]{0,1:T(8,128)(2,1)S(1)}, u32[]{:S(2)}, u32[]{:S(2)}) collective-permute-start(bf16[256,768]{0,1:T(8,128)(2,1)S(1)} %get-tuple-element.6), channel_id=1, source_target_pairs={{4,6},{2,0},{5,7},{3,1},{12,14},{10,8},{13,15},{11,9},{20,22},{18,... | collective-permute-start | bytes 1179656 | tf_op jit(solution)/shard_map/ppermute | solution.py:101
  63.1 0.5 collective-permute-start.10
  63.7 0.7 multiply_reduce_fusion.5
  64.4 0.6 fusion.87
  65.0 0.7 multiply_reduce_fusion.4
  65.8 0.6 fusion.85
  66.4 0.7 multiply_reduce_fusion.3
  67.1 0.6 fusion.83
  67.7 0.7 multiply_reduce_fusion.2
  68.5 0.6 fusion.81
  69.1 5.0 %collective-permute-done.12 = bf16[256,768]{0,1:T(8,128)(2,1)S(1)} collective-permute-done((bf16[256,768]{0,1:T(8,128)(2,1)S(1)}, bf16[256,768]{0,1:T(8,128)(2,1)S(1)}, u32[]{:S(2)}, u32[]{:S(2)}) %collective-permute-start.12) | collective-permute-done | bytes 393248 | tf_op jit(solution)/shard_map/ppermute | solution.py:100
  74.3 6.7 %collective-permute-done.14 = bf16[256,768]{0,1:T(8,128)(2,1)S(1)} collective-permute-done((bf16[256,768]{0,1:T(8,128)(2,1)S(1)}, bf16[256,768]{0,1:T(8,128)(2,1)S(1)}, u32[]{:S(2)}, u32[]{:S(2)}) %collective-permute-start.14) | collective-permute-done | bytes 393248 | tf_op jit(solution)/shard_map/ppermute | solution.py:101
  81.3 0.5 multiply_reduce_fusion.13
  81.7 0.4 fusion.111
  82.2 0.5 multiply_reduce_fusion.11
  82.7 0.4 fusion.107
  83.5 0.2 fusion.16
  83.9 0.7 multiply_reduce_fusion
  84.6 0.7 multiply_reduce_fusion.1
  85.4 0.5 multiply_reduce_fusion.12
  85.9 0.5 multiply_reduce_fusion.10
  86.4 0.6 fusion.79
  87.0 0.4 fusion.109
  87.4 0.4 fusion.105
  87.8 2.8 %fusion.43 = bf16[1,1,512,768]{3,2,1,0:T(8,128)(2,1)} fusion(f32[512,768]{1,0:T(8,128)S(1)} %fusion.105, f32[512,768]{1,0:T(8,128)S(1)} %fusion.107, f32[512,768]{1,0:T(8,128)S(1)} %fusion.109, f32[512,768]{1,0:T(8,128)S(1)} %fusion.111, bf16[512,768]{0,1:T(8,128)(2,1)S(1)} %collective-permute-done.11, f32[512,768]{1,0:T(8,128)S(1)} %fusion.79, ...), kind=kOutput, calls=%fused_computation.75 | convolution fusion | flops 414056448 | bytes 22548524 | tf_op jit(solution)/shard_map/dot_general | solution.py:76
  (68 shorter events, 3.8 us)
Async XLA Ops:
  1.6 8.8 %collective-permute-start = (bf16[128,768]{1,0:T(8,128)(2,1)S(1)}, bf16[128,768]{1,0:T(8,128)(2,1)S(1)}, u32[]{:S(2)}, u32[]{:S(2)}) collective-permute-start(bf16[128,768]{1,0:T(8,128)(2,1)S(1)} %get-tuple-element.9), channel_id=1, source_target_pairs={{0,8},{8,0},{16,24},{24,16},{1,9},{9,1},{17,25},{25,17},{2,10},{10... | collective-permute-start | bytes 589832 | tf_op jit(solution)/shard_map/ppermute | solution.py:44
  4.6 10.6 %collective-permute-start.1 = (bf16[128,768]{1,0:T(8,128)(2,1)S(1)}, bf16[128,768]{1,0:T(8,128)(2,1)S(1)}, u32[]{:S(2)}, u32[]{:S(2)}) collective-permute-start(bf16[128,768]{1,0:T(8,128)(2,1)S(1)} %get-tuple-element.8), channel_id=1, source_target_pairs={{0,16},{8,24},{16,0},{24,8},{1,17},{9,25},{17,1},{25,9},{2,18},{10... | collective-permute-start | bytes 589832 | tf_op jit(solution)/shard_map/ppermute | solution.py:44
  6.1 9.3 %collective-permute-start.2 = (bf16[128,768]{1,0:T(8,128)(2,1)S(1)}, bf16[128,768]{1,0:T(8,128)(2,1)S(1)}, u32[]{:S(2)}, u32[]{:S(2)}) collective-permute-start(bf16[128,768]{1,0:T(8,128)(2,1)S(1)} %get-tuple-element.7), channel_id=1, source_target_pairs={{0,24},{8,16},{16,8},{24,0},{1,25},{9,17},{17,9},{25,1},{2,26},{10... | collective-permute-start | bytes 589832 | tf_op jit(solution)/shard_map/ppermute | solution.py:44
  15.7 18.0 %collective-permute-start.4 = (bf16[512,768]{0,1:T(8,128)(2,1)S(1)}, bf16[512,768]{0,1:T(8,128)(2,1)S(1)}, u32[]{:S(2)}, u32[]{:S(2)}) collective-permute-start(bf16[512,768]{0,1:T(8,128)(2,1)S(1)} %constant_dynamic-update-slice_fusion), channel_id=1, source_target_pairs={{0,2},{2,0},{4,6},{6,4},{1,3},{3,1},{5,7},{7,5},{8,10},{10,8},{12,... | collective-permute-start | bytes 2359304 | tf_op jit(solution)/shard_map/ppermute | solution.py:89
  17.6 2.3 %collective-permute-start.3 = (bf16[512,768]{0,1:T(8,128)(2,1)S(1)}, bf16[512,768]{0,1:T(8,128)(2,1)S(1)}, u32[]{:S(2)}, u32[]{:S(2)}) collective-permute-start(bf16[512,768]{0,1:T(8,128)(2,1)S(1)} %constant_dynamic-update-slice_fusion), channel_id=1, source_target_pairs={{0,1},{1,0},{2,3},{3,2},{4,5},{5,4},{6,7},{7,6},{8,9},{9,8},{10,11... | collective-permute-start | bytes 2359304 | tf_op jit(solution)/shard_map/ppermute | solution.py:90
  17.6 17.0 %collective-permute-start.5 = (bf16[512,768]{0,1:T(8,128)(2,1)S(1)}, bf16[512,768]{0,1:T(8,128)(2,1)S(1)}, u32[]{:S(2)}, u32[]{:S(2)}) collective-permute-start(bf16[512,768]{0,1:T(8,128)(2,1)S(1)} %constant_dynamic-update-slice_fusion), channel_id=1, source_target_pairs={{2,4},{4,2},{3,5},{5,3},{10,12},{12,10},{11,13},{13,11},{18,20},{2... | collective-permute-start | bytes 2359304 | tf_op jit(solution)/shard_map/ppermute | solution.py:89
  33.7 26.2 %collective-permute-start.9 = (bf16[512,768]{0,1:T(8,128)(2,1)S(1)}, bf16[512,768]{0,1:T(8,128)(2,1)S(1)}, u32[]{:S(2)}, u32[]{:S(2)}) collective-permute-start(bf16[512,768]{0,1:T(8,128)(2,1)S(1)} %collective-permute-done.4), channel_id=1, source_target_pairs={{2,4},{4,2},{3,5},{5,3},{10,12},{12,10},{11,13},{13,11},{18,20},{2... | collective-permute-start | bytes 2359304 | tf_op jit(solution)/shard_map/ppermute | solution.py:95
  34.9 11.1 %collective-permute-start.6 = (bf16[512,768]{0,1:T(8,128)(2,1)S(1)}, bf16[512,768]{0,1:T(8,128)(2,1)S(1)}, u32[]{:S(2)}, u32[]{:S(2)}) collective-permute-start(bf16[512,768]{0,1:T(8,128)(2,1)S(1)} %collective-permute-done.4), channel_id=1, source_target_pairs={{0,1},{1,0},{2,3},{3,2},{4,5},{5,4},{6,7},{7,6},{8,9},{9,8},{10,11... | collective-permute-start | bytes 2359304 | tf_op jit(solution)/shard_map/ppermute | solution.py:112
  35.0 11.2 %collective-permute-start.7 = (bf16[512,768]{0,1:T(8,128)(2,1)S(1)}, bf16[512,768]{0,1:T(8,128)(2,1)S(1)}, u32[]{:S(2)}, u32[]{:S(2)}) collective-permute-start(bf16[512,768]{0,1:T(8,128)(2,1)S(1)} %collective-permute-done.5), channel_id=1, source_target_pairs={{0,1},{1,0},{2,3},{3,2},{4,5},{5,4},{6,7},{7,6},{8,9},{9,8},{10,11... | collective-permute-start | bytes 2359304 | tf_op jit(solution)/shard_map/ppermute | solution.py:113
  35.5 24.2 %collective-permute-start.8 = (bf16[512,768]{0,1:T(8,128)(2,1)S(1)}, bf16[512,768]{0,1:T(8,128)(2,1)S(1)}, u32[]{:S(2)}, u32[]{:S(2)}) collective-permute-start(bf16[512,768]{0,1:T(8,128)(2,1)S(1)} %collective-permute-done.5), channel_id=1, source_target_pairs={{0,2},{2,0},{4,6},{6,4},{1,3},{3,1},{5,7},{7,5},{8,10},{10,8},{12,... | collective-permute-start | bytes 2359304 | tf_op jit(solution)/shard_map/ppermute | solution.py:95
  60.2 13.9 %collective-permute-start.12 = (bf16[256,768]{0,1:T(8,128)(2,1)S(1)}, bf16[256,768]{0,1:T(8,128)(2,1)S(1)}, u32[]{:S(2)}, u32[]{:S(2)}) collective-permute-start(bf16[256,768]{0,1:T(8,128)(2,1)S(1)} %get-tuple-element.5), channel_id=1, source_target_pairs={{4,6},{2,0},{5,7},{3,1},{12,14},{10,8},{13,15},{11,9},{20,22},{18,... | collective-permute-start | bytes 1179656 | tf_op jit(solution)/shard_map/ppermute | solution.py:100
  61.5 19.5 %collective-permute-start.14 = (bf16[256,768]{0,1:T(8,128)(2,1)S(1)}, bf16[256,768]{0,1:T(8,128)(2,1)S(1)}, u32[]{:S(2)}, u32[]{:S(2)}) collective-permute-start(bf16[256,768]{0,1:T(8,128)(2,1)S(1)} %get-tuple-element.6), channel_id=1, source_target_pairs={{4,6},{2,0},{5,7},{3,1},{12,14},{10,8},{13,15},{11,9},{20,22},{18,... | collective-permute-start | bytes 1179656 | tf_op jit(solution)/shard_map/ppermute | solution.py:101
  63.0 20.3 %collective-permute-start.11 = (bf16[512,768]{0,1:T(8,128)(2,1)S(1)}, bf16[512,768]{0,1:T(8,128)(2,1)S(1)}, u32[]{:S(2)}, u32[]{:S(2)}) collective-permute-start(bf16[512,768]{0,1:T(8,128)(2,1)S(1)} %collective-permute-done.9), channel_id=1, source_target_pairs={{0,1},{1,0},{2,3},{3,2},{4,5},{5,4},{6,7},{7,6},{8,9},{9,8},{10,11... | collective-permute-start | bytes 2359304 | tf_op jit(solution)/shard_map/ppermute | solution.py:113
  63.1 20.4 %collective-permute-start.10 = (bf16[512,768]{0,1:T(8,128)(2,1)S(1)}, bf16[512,768]{0,1:T(8,128)(2,1)S(1)}, u32[]{:S(2)}, u32[]{:S(2)}) collective-permute-start(bf16[512,768]{0,1:T(8,128)(2,1)S(1)} %collective-permute-done.8), channel_id=1, source_target_pairs={{0,1},{1,0},{2,3},{3,2},{4,5},{5,4},{6,7},{7,6},{8,9},{9,8},{10,11... | collective-permute-start | bytes 2359304 | tf_op jit(solution)/shard_map/ppermute | solution.py:112
  74.2 8.9 %collective-permute-start.13 = (bf16[256,768]{0,1:T(8,128)(2,1)S(1)}, bf16[256,768]{0,1:T(8,128)(2,1)S(1)}, u32[]{:S(2)}, u32[]{:S(2)}) collective-permute-start(bf16[256,768]{0,1:T(8,128)(2,1)S(1)} %collective-permute-done.12), channel_id=1, source_target_pairs={{0,1},{1,0},{2,3},{3,2},{4,5},{5,4},{6,7},{7,6},{8,9},{9,8},{10,11... | collective-permute-start | bytes 1179656 | tf_op jit(solution)/shard_map/ppermute | solution.py:106
  81.2 2.5 %collective-permute-start.15 = (bf16[256,768]{0,1:T(8,128)(2,1)S(1)}, bf16[256,768]{0,1:T(8,128)(2,1)S(1)}, u32[]{:S(2)}, u32[]{:S(2)}) collective-permute-start(bf16[256,768]{0,1:T(8,128)(2,1)S(1)} %collective-permute-done.14), channel_id=1, source_target_pairs={{0,1},{1,0},{2,3},{3,2},{4,5},{5,4},{6,7},{7,6},{8,9},{9,8},{10,11... | collective-permute-start | bytes 1179656 | tf_op jit(solution)/shard_map/ppermute | solution.py:106

commit v23 on v21

--- a/solution.py
+++ b/solution.py
@@ -10,7 +10,6 @@
 TEMP = 12.0
 DEAD = 1000.0
 CORES = 2
-LAST_PARTS = 3
 
 
 def normalize(block):
@@ -98,9 +97,9 @@
             received = (lax.ppermute(by_across, "chip", exchange), lax.ppermute(by_exchange, "chip", across))
         elif step + 2 == chips:
             ends = [(chips - 2, chips - 1), (1, 0)]
-            bounds = [(rows * i // LAST_PARTS) // 16 * 16 for i in range(LAST_PARTS)] + [rows]
+            bounds = [0, rows - rows // 4, rows]
             received = tuple(
-                lax.ppermute(by_across[bounds[i] : bounds[i + 1]], "chip", ends) for i in range(LAST_PARTS)
+                lax.ppermute(by_across[bounds[i] : bounds[i + 1]], "chip", ends) for i in range(len(bounds) - 1)
             )
         if step + 1 == chips and chips >= 4:
             far_chip = jnp.where(chip == 0, chips - 1, jnp.where(chip == chips - 1, 0, -1))

time: 92.7 us -> 80.4 us (0.87)
  starting transfers between devices: 30.4 us -> 16.6 us
  waiting for transfers between devices: 34.4 us -> 37.8 us
  matrix products: 20.9 us -> 19.4 us
    ppermute x1, waiting for transfers between devices: 1.01 us -> 14.3 us  [per_device(): lax.ppermute(mine, 'chip', exchange)]
    ppermute x1, starting transfers between devices: 14.6 us -> 1.8 us  [per_device(): lax.ppermute(by_across, 'chip', exchange)]
    ppermute x3 -> x2, waiting for transfers between devices: 18.3 us -> 8.38 us  [per_device(): lax.ppermute(by_across[bounds[i]:bounds[i + 1]], 'chip', ends)]
    ppermute x3 -> x2, starting transfers between devices: 4.05 us -> 2.76 us  [per_device(): lax.ppermute(by_across[bounds[i]:bounds[i + 1]], 'chip', ends)]
    dot_general x15 -> x13, matrix products: 10.3 us -> 9.41 us  [pair_terms(): jnp.dot(weights.astype(jnp.bfloat16), got, preferred_element_type=jnp.flo...]
    dot_general x16 -> x14, matrix products: 9.92 us -> 9.34 us  [weigh(): scores = jnp.dot(unit_a, unit_b.T, preferred_element_type=jnp.float32)]
    reduce_sum x15 -> x14, other arithmetic: 2.9 us -> 2.73 us  [normalize(): jnp.sum(values * values, axis=-1, keepdims=True) + EPS]
  transfers between devices with their start and end apart: 18 -> 16, of which waited for: 7 -> 5; matrix products, arithmetic and copies ran while one was open for 23% -> 25% of each run, Pallas kernels for 0% -> 0%
where the time goes in v23:
time: 80.4 us; the launch traced here: 80.2 us
  waiting for transfers between devices  37.8 us (47%)
  matrix products  19.4 us (24%)
  starting transfers between devices  16.6 us (21%)
  other arithmetic  4.46 us (6%)
  local copies, waits for them, and re-layouts  1.06 us (1%)
  between operations  0.84 us (1%)
    ppermute x1, waiting for transfers between devices, per_device(): lax.ppermute(mine, 'chip', exchange)  14.3 us
    dot_general x13, matrix products, pair_terms(): jnp.dot(weights.astype(jnp.bfloat16), got, preferred_element_type=jnp.flo...  9.41 us
    dot_general x14, matrix products, weigh(): scores = jnp.dot(unit_a, unit_b.T, preferred_element_type=jnp.float32)  9.34 us
    ppermute x2, waiting for transfers between devices, per_device(): lax.ppermute(by_across[bounds[i]:bounds[i + 1]], 'chip', ends)  8.38 us
    ppermute x3, waiting for transfers between devices, per_device(): lax.ppermute(outgoing, 'bucket', [(i, i ^ m) for i in range(buckets)])  8.15 us
    ppermute x1, waiting for transfers between devices, per_device(): lax.ppermute(by_across, 'chip', exchange)  7.03 us
    ppermute x3, starting transfers between devices, per_device(): lax.ppermute(outgoing, 'bucket', [(i, i ^ m) for i in range(buckets)])  4.57 us
    ppermute x1, starting transfers between devices, per_device(): lax.ppermute(mine, 'chip', exchange)  4.41 us
  transfers between devices with their start and end apart: 16, of which 5 were waited for; matrix products, arithmetic and copies ran while one was open for 25% of the time, Pallas kernels for 0%

profile of v23, /device:TPU:0, one launch (start us, length us, event | category | flops | bytes accessed | tf_op | source)
XLA Modules:
  0.0 80.2 jit_solution(7228515794729706503)
XLA Ops:
  0.0 1.5 %fusion.21 = bf16[4,128,768]{2,1,0:T(8,128)(2,1)S(1)} fusion(bf16[1,1,4,128,768]{4,3,2,1,0:T(8,128)(2,1)} %param.2, s32[4]{0:T(128)} %bitcast.66, pred[768]{0:T(1024)(128)(4,1)S(1)} %iota_compare_fusion.2), kind=kLoop, calls=%fused_computation.44 | loop fusion | flops 1179648 | bytes 1573648 | tf_op jit(solution)/shard_map/jit(_where)/select_n | solution.py:40
  1.6 3.0 %collective-permute-start = (bf16[128,768]{1,0:T(8,128)(2,1)S(1)}, bf16[128,768]{1,0:T(8,128)(2,1)S(1)}, u32[]{:S(2)}, u32[]{:S(2)}) collective-permute-start(bf16[128,768]{1,0:T(8,128)(2,1)S(1)} %get-tuple-element.15), channel_id=1, source_target_pairs={{0,8},{8,0},{16,24},{24,16},{1,9},{9,1},{17,25},{25,17},{2,10},{10... | collective-permute-start | bytes 589832 | tf_op jit(solution)/shard_map/ppermute | solution.py:44
  4.6 1.5 %collective-permute-start.1 = (bf16[128,768]{1,0:T(8,128)(2,1)S(1)}, bf16[128,768]{1,0:T(8,128)(2,1)S(1)}, u32[]{:S(2)}, u32[]{:S(2)}) collective-permute-start(bf16[128,768]{1,0:T(8,128)(2,1)S(1)} %get-tuple-element.14), channel_id=1, source_target_pairs={{0,16},{8,24},{16,0},{24,8},{1,17},{9,25},{17,1},{25,9},{2,18},{10... | collective-permute-start | bytes 589832 | tf_op jit(solution)/shard_map/ppermute | solution.py:44
  6.9 3.5 %collective-permute-done = bf16[128,768]{1,0:T(8,128)(2,1)S(1)} collective-permute-done((bf16[128,768]{1,0:T(8,128)(2,1)S(1)}, bf16[128,768]{1,0:T(8,128)(2,1)S(1)}, u32[]{:S(2)}, u32[]{:S(2)}) %collective-permute-start) | collective-permute-done | bytes 196640 | tf_op jit(solution)/shard_map/ppermute | solution.py:44
  10.5 4.7 %collective-permute-done.1 = bf16[128,768]{1,0:T(8,128)(2,1)S(1)} collective-permute-done((bf16[128,768]{1,0:T(8,128)(2,1)S(1)}, bf16[128,768]{1,0:T(8,128)(2,1)S(1)}, u32[]{:S(2)}, u32[]{:S(2)}) %collective-permute-start.1) | collective-permute-done | bytes 196640 | tf_op jit(solution)/shard_map/ppermute | solution.py:44
  15.7 0.7 collective-permute-start.5
  16.4 0.2 fusion
  16.6 4.4 %collective-permute-start.4 = (bf16[512,768]{0,1:T(8,128)(2,1)S(1)}, bf16[512,768]{0,1:T(8,128)(2,1)S(1)}, u32[]{:S(2)}, u32[]{:S(2)}) collective-permute-start(bf16[512,768]{0,1:T(8,128)(2,1)S(1)} %constant_dynamic-update-slice_fusion), channel_id=1, source_target_pairs={{0,2},{2,0},{4,6},{6,4},{1,3},{3,1},{5,7},{7,5},{8,10},{10,8},{12,... | collective-permute-start | bytes 2359304 | tf_op jit(solution)/shard_map/ppermute | solution.py:89
  21.1 0.8 multiply_reduce_fusion.9
  21.9 0.6 fusion.95
  22.5 0.2 fusion.6
  22.7 14.3 %collective-permute-done.4 = bf16[512,768]{0,1:T(8,128)(2,1)S(1)} collective-permute-done((bf16[512,768]{0,1:T(8,128)(2,1)S(1)}, bf16[512,768]{0,1:T(8,128)(2,1)S(1)}, u32[]{:S(2)}, u32[]{:S(2)}) %collective-permute-start.4) | collective-permute-done | bytes 786464 | tf_op jit(solution)/shard_map/ppermute | solution.py:89
  37.2 0.2 fusion.2
  37.4 1.8 %collective-permute-start.8 = (bf16[512,768]{0,1:T(8,128)(2,1)S(1)}, bf16[512,768]{0,1:T(8,128)(2,1)S(1)}, u32[]{:S(2)}, u32[]{:S(2)}) collective-permute-start(bf16[512,768]{0,1:T(8,128)(2,1)S(1)} %collective-permute-done.5), channel_id=1, source_target_pairs={{0,2},{2,0},{4,6},{6,4},{1,3},{3,1},{5,7},{7,5},{8,10},{10,8},{12,... | collective-permute-start | bytes 2359304 | tf_op jit(solution)/shard_map/ppermute | solution.py:97
  39.2 0.7 collective-permute-start.9
  40.0 0.5 collective-permute-start.6
  40.5 0.7 multiply_reduce_fusion.6
  41.3 0.6 fusion.89
  41.9 0.7 multiply_reduce_fusion.7
  42.6 0.7 multiply_reduce_fusion.8
  43.4 0.6 fusion.91
  44.0 0.6 fusion.93
  44.7 1.3 %collective-permute-start.12 = (bf16[384,768]{0,1:T(8,128)(2,1)S(1)}, bf16[384,768]{0,1:T(8,128)(2,1)S(1)}, u32[]{:S(2)}, u32[]{:S(2)}) collective-permute-start(bf16[384,768]{0,1:T(8,128)(2,1)S(1)} %slice.74), channel_id=1, source_target_pairs={{4,6},{2,0},{5,7},{3,1},{12,14},{10,8},{13,15},{11,9},{20,22},{18,... | collective-permute-start | bytes 1769480 | tf_op jit(solution)/shard_map/ppermute | solution.py:102
  46.0 1.5 %collective-permute-start.13 = (bf16[128,768]{0,1:T(8,128)(2,1)S(1)}, bf16[128,768]{0,1:T(8,128)(2,1)S(1)}, u32[]{:S(2)}, u32[]{:S(2)}) collective-permute-start(bf16[128,768]{0,1:T(8,128)(2,1)S(1)} %slice.75), channel_id=1, source_target_pairs={{4,6},{2,0},{5,7},{3,1},{12,14},{10,8},{13,15},{11,9},{20,22},{18,... | collective-permute-start | bytes 589832 | tf_op jit(solution)/shard_map/ppermute | solution.py:102
  47.5 7.0 %collective-permute-done.8 = bf16[512,768]{0,1:T(8,128)(2,1)S(1)} collective-permute-done((bf16[512,768]{0,1:T(8,128)(2,1)S(1)}, bf16[512,768]{0,1:T(8,128)(2,1)S(1)}, u32[]{:S(2)}, u32[]{:S(2)}) %collective-permute-start.8) | collective-permute-done | bytes 786464 | tf_op jit(solution)/shard_map/ppermute | solution.py:97
  55.5 0.6 collective-permute-start.11
  56.1 0.7 multiply_reduce_fusion.2
  56.8 0.6 fusion.81
  57.4 0.7 multiply_reduce_fusion.3
  58.2 0.6 fusion.83
  58.8 0.7 multiply_reduce_fusion.4
  59.5 0.6 fusion.85
  60.1 0.7 multiply_reduce_fusion.5
  60.9 0.6 fusion.87
  62.0 0.7 multiply_reduce_fusion.1
  62.7 0.6 fusion.79
  63.4 0.7 multiply_reduce_fusion
  64.1 1.2 %multiply_add_fusion = f32[512,768]{1,0:T(8,128)S(1)} fusion(f32[512,768]{1,0:T(8,128)S(1)} %fusion.79, f32[512,768]{1,0:T(8,128)S(1)} %fusion.81, f32[512,768]{1,0:T(8,128)S(1)} %fusion.83, f32[512,768]{1,0:T(8,128)S(1)} %fusion.85, f32[512,768]{1,0:T(8,128)S(1)} %fusion.87, f32[512,768]{1,0:T(8,128)S(1)} %fusion.89, f32[512,768]{1,0:T(8,128)S(1)} %fusion.91, ...), kind=kOutput, calls=%fused_computation.41 | convolution fusion | flops 409731072 | bytes 17039396 | tf_op jit(solution)/shard_map/dot_general | solution.py:76
  65.3 8.4 %collective-permute-done.13 = bf16[128,768]{0,1:T(8,128)(2,1)S(1)} collective-permute-done((bf16[128,768]{0,1:T(8,128)(2,1)S(1)}, bf16[128,768]{0,1:T(8,128)(2,1)S(1)}, u32[]{:S(2)}, u32[]{:S(2)}) %collective-permute-start.13) | collective-permute-done | bytes 196640 | tf_op jit(solution)/shard_map/ppermute | solution.py:102
  73.8 0.6 collective-permute-start.14
  74.6 0.6 multiply_reduce_fusion.11
  75.2 0.6 fusion.103
  75.8 0.4 multiply_reduce_fusion.13
  76.2 0.4 fusion.110
  76.7 0.4 multiply_reduce_fusion.12
  77.3 0.6 multiply_reduce_fusion.10
  77.9 0.6 fusion.101
  78.6 1.7 %fusion.43 = bf16[1,1,512,768]{3,2,1,0:T(8,128)(2,1)} fusion(bf16[128,768]{0,1:T(8,128)(2,1)S(1)} %collective-permute-done.15, f32[512,768]{1,0:T(8,128)S(1)} %fusion.110, f32[512,768]{1,0:T(8,128)S(1)} %fusion.101, f32[512,768]{1,0:T(8,128)S(1)} %multiply_add_fusion, f32[512,768]{1,0:T(8,128)S(1)} %fusion.103, f32[512]{0:T(512)S(1)} %bitcast.56, ...), kind=kOutput, calls=%fused_computation.80 | convolution fusion | flops 104988672 | bytes 7409672 | tf_op jit(solution)/shard_map/dot_general | solution.py:76
  (70 shorter events, 3.5 us)
Async XLA Ops:
  1.6 8.8 %collective-permute-start = (bf16[128,768]{1,0:T(8,128)(2,1)S(1)}, bf16[128,768]{1,0:T(8,128)(2,1)S(1)}, u32[]{:S(2)}, u32[]{:S(2)}) collective-permute-start(bf16[128,768]{1,0:T(8,128)(2,1)S(1)} %get-tuple-element.15), channel_id=1, source_target_pairs={{0,8},{8,0},{16,24},{24,16},{1,9},{9,1},{17,25},{25,17},{2,10},{10... | collective-permute-start | bytes 589832 | tf_op jit(solution)/shard_map/ppermute | solution.py:44
  4.6 10.6 %collective-permute-start.1 = (bf16[128,768]{1,0:T(8,128)(2,1)S(1)}, bf16[128,768]{1,0:T(8,128)(2,1)S(1)}, u32[]{:S(2)}, u32[]{:S(2)}) collective-permute-start(bf16[128,768]{1,0:T(8,128)(2,1)S(1)} %get-tuple-element.14), channel_id=1, source_target_pairs={{0,16},{8,24},{16,0},{24,8},{1,17},{9,25},{17,1},{25,9},{2,18},{10... | collective-permute-start | bytes 589832 | tf_op jit(solution)/shard_map/ppermute | solution.py:44
  6.1 9.3 %collective-permute-start.2 = (bf16[128,768]{1,0:T(8,128)(2,1)S(1)}, bf16[128,768]{1,0:T(8,128)(2,1)S(1)}, u32[]{:S(2)}, u32[]{:S(2)}) collective-permute-start(bf16[128,768]{1,0:T(8,128)(2,1)S(1)} %get-tuple-element.13), channel_id=1, source_target_pairs={{0,24},{8,16},{16,8},{24,0},{1,25},{9,17},{17,9},{25,1},{2,26},{10... | collective-permute-start | bytes 589832 | tf_op jit(solution)/shard_map/ppermute | solution.py:44
  15.7 6.8 %collective-permute-start.5 = (bf16[512,768]{0,1:T(8,128)(2,1)S(1)}, bf16[512,768]{0,1:T(8,128)(2,1)S(1)}, u32[]{:S(2)}, u32[]{:S(2)}) collective-permute-start(bf16[512,768]{0,1:T(8,128)(2,1)S(1)} %constant_dynamic-update-slice_fusion), channel_id=1, source_target_pairs={{2,4},{4,2},{3,5},{5,3},{10,12},{12,10},{11,13},{13,11},{18,20},{2... | collective-permute-start | bytes 2359304 | tf_op jit(solution)/shard_map/ppermute | solution.py:89
  16.6 20.3 %collective-permute-start.4 = (bf16[512,768]{0,1:T(8,128)(2,1)S(1)}, bf16[512,768]{0,1:T(8,128)(2,1)S(1)}, u32[]{:S(2)}, u32[]{:S(2)}) collective-permute-start(bf16[512,768]{0,1:T(8,128)(2,1)S(1)} %constant_dynamic-update-slice_fusion), channel_id=1, source_target_pairs={{0,2},{2,0},{4,6},{6,4},{1,3},{3,1},{5,7},{7,5},{8,10},{10,8},{12,... | collective-permute-start | bytes 2359304 | tf_op jit(solution)/shard_map/ppermute | solution.py:89
  21.1 16.1 %collective-permute-start.3 = (bf16[512,768]{0,1:T(8,128)(2,1)S(1)}, bf16[512,768]{0,1:T(8,128)(2,1)S(1)}, u32[]{:S(2)}, u32[]{:S(2)}) collective-permute-start(bf16[512,768]{0,1:T(8,128)(2,1)S(1)} %constant_dynamic-update-slice_fusion), channel_id=1, source_target_pairs={{0,1},{1,0},{2,3},{3,2},{4,5},{5,4},{6,7},{7,6},{8,9},{9,8},{10,11... | collective-permute-start | bytes 2359304 | tf_op jit(solution)/shard_map/ppermute | solution.py:90
  37.4 17.1 %collective-permute-start.8 = (bf16[512,768]{0,1:T(8,128)(2,1)S(1)}, bf16[512,768]{0,1:T(8,128)(2,1)S(1)}, u32[]{:S(2)}, u32[]{:S(2)}) collective-permute-start(bf16[512,768]{0,1:T(8,128)(2,1)S(1)} %collective-permute-done.5), channel_id=1, source_target_pairs={{0,2},{2,0},{4,6},{6,4},{1,3},{3,1},{5,7},{7,5},{8,10},{10,8},{12,... | collective-permute-start | bytes 2359304 | tf_op jit(solution)/shard_map/ppermute | solution.py:97
  39.2 5.4 %collective-permute-start.9 = (bf16[512,768]{0,1:T(8,128)(2,1)S(1)}, bf16[512,768]{0,1:T(8,128)(2,1)S(1)}, u32[]{:S(2)}, u32[]{:S(2)}) collective-permute-start(bf16[512,768]{0,1:T(8,128)(2,1)S(1)} %collective-permute-done.4), channel_id=1, source_target_pairs={{2,4},{4,2},{3,5},{5,3},{10,12},{12,10},{11,13},{13,11},{18,20},{2... | collective-permute-start | bytes 2359304 | tf_op jit(solution)/shard_map/ppermute | solution.py:97
  39.9 15.1 %collective-permute-start.7 = (bf16[512,768]{0,1:T(8,128)(2,1)S(1)}, bf16[512,768]{0,1:T(8,128)(2,1)S(1)}, u32[]{:S(2)}, u32[]{:S(2)}) collective-permute-start(bf16[512,768]{0,1:T(8,128)(2,1)S(1)} %collective-permute-done.5), channel_id=1, source_target_pairs={{0,1},{1,0},{2,3},{3,2},{4,5},{5,4},{6,7},{7,6},{8,9},{9,8},{10,11... | collective-permute-start | bytes 2359304 | tf_op jit(solution)/shard_map/ppermute | solution.py:114
  40.0 15.3 %collective-permute-start.6 = (bf16[512,768]{0,1:T(8,128)(2,1)S(1)}, bf16[512,768]{0,1:T(8,128)(2,1)S(1)}, u32[]{:S(2)}, u32[]{:S(2)}) collective-permute-start(bf16[512,768]{0,1:T(8,128)(2,1)S(1)} %collective-permute-done.4), channel_id=1, source_target_pairs={{0,1},{1,0},{2,3},{3,2},{4,5},{5,4},{6,7},{7,6},{8,9},{9,8},{10,11... | collective-permute-start | bytes 2359304 | tf_op jit(solution)/shard_map/ppermute | solution.py:113
  44.7 29.0 %collective-permute-start.12 = (bf16[384,768]{0,1:T(8,128)(2,1)S(1)}, bf16[384,768]{0,1:T(8,128)(2,1)S(1)}, u32[]{:S(2)}, u32[]{:S(2)}) collective-permute-start(bf16[384,768]{0,1:T(8,128)(2,1)S(1)} %slice.74), channel_id=1, source_target_pairs={{4,6},{2,0},{5,7},{3,1},{12,14},{10,8},{13,15},{11,9},{20,22},{18,... | collective-permute-start | bytes 1769480 | tf_op jit(solution)/shard_map/ppermute | solution.py:102
  46.0 27.7 %collective-permute-start.13 = (bf16[128,768]{0,1:T(8,128)(2,1)S(1)}, bf16[128,768]{0,1:T(8,128)(2,1)S(1)}, u32[]{:S(2)}, u32[]{:S(2)}) collective-permute-start(bf16[128,768]{0,1:T(8,128)(2,1)S(1)} %slice.75), channel_id=1, source_target_pairs={{4,6},{2,0},{5,7},{3,1},{12,14},{10,8},{13,15},{11,9},{20,22},{18,... | collective-permute-start | bytes 589832 | tf_op jit(solution)/shard_map/ppermute | solution.py:102
  54.5 7.0 %collective-permute-start.10 = (bf16[512,768]{0,1:T(8,128)(2,1)S(1)}, bf16[512,768]{0,1:T(8,128)(2,1)S(1)}, u32[]{:S(2)}, u32[]{:S(2)}) collective-permute-start(bf16[512,768]{0,1:T(8,128)(2,1)S(1)} %collective-permute-done.8), channel_id=1, source_target_pairs={{0,1},{1,0},{2,3},{3,2},{4,5},{5,4},{6,7},{7,6},{8,9},{9,8},{10,11... | collective-permute-start | bytes 2359304 | tf_op jit(solution)/shard_map/ppermute | solution.py:113
  55.5 6.3 %collective-permute-start.11 = (bf16[512,768]{0,1:T(8,128)(2,1)S(1)}, bf16[512,768]{0,1:T(8,128)(2,1)S(1)}, u32[]{:S(2)}, u32[]{:S(2)}) collective-permute-start(bf16[512,768]{0,1:T(8,128)(2,1)S(1)} %collective-permute-done.9), channel_id=1, source_target_pairs={{0,1},{1,0},{2,3},{3,2},{4,5},{5,4},{6,7},{7,6},{8,9},{9,8},{10,11... | collective-permute-start | bytes 2359304 | tf_op jit(solution)/shard_map/ppermute | solution.py:114
  73.7 2.9 %collective-permute-start.15 = (bf16[128,768]{0,1:T(8,128)(2,1)S(1)}, bf16[128,768]{0,1:T(8,128)(2,1)S(1)}, u32[]{:S(2)}, u32[]{:S(2)}) collective-permute-start(bf16[128,768]{0,1:T(8,128)(2,1)S(1)} %collective-permute-done.13), channel_id=1, source_target_pairs={{0,1},{1,0},{2,3},{3,2},{4,5},{5,4},{6,7},{7,6},{8,9},{9,8},{10,11... | collective-permute-start | bytes 589832 | tf_op jit(solution)/shard_map/ppermute | solution.py:107
  73.8 3.3 %collective-permute-start.14 = (bf16[384,768]{0,1:T(8,128)(2,1)S(1)}, bf16[384,768]{0,1:T(8,128)(2,1)S(1)}, u32[]{:S(2)}, u32[]{:S(2)}) collective-permute-start(bf16[384,768]{0,1:T(8,128)(2,1)S(1)} %collective-permute-done.12), channel_id=1, source_target_pairs={{0,1},{1,0},{2,3},{3,2},{4,5},{5,4},{6,7},{7,6},{8,9},{9,8},{10,11... | collective-permute-start | bytes 1769480 | tf_op jit(solution)/shard_map/ppermute | solution.py:107

commit v24 on v23

--- a/solution.py
+++ b/solution.py
@@ -97,7 +97,7 @@
             received = (lax.ppermute(by_across, "chip", exchange), lax.ppermute(by_exchange, "chip", across))
         elif step + 2 == chips:
             ends = [(chips - 2, chips - 1), (1, 0)]
-            bounds = [0, rows - rows // 4, rows]
+            bounds = [0, rows - rows // 8, rows]
             received = tuple(
                 lax.ppermute(by_across[bounds[i] : bounds[i + 1]], "chip", ends) for i in range(len(bounds) - 1)
             )

time: 80.4 us -> 81.7 us (1.016)
  other arithmetic: 4.46 us -> 6.22 us
  local copies, waits for them, and re-layouts: 1.06 us -> 0.24 us
    convert_element_type x14, other arithmetic: 0.11 us -> 1.65 us  [live_of(): return (block[:, 0] < DEAD / 2).astype(jnp.float32)]
    dot_general x14, matrix products: 9.34 us -> 10.4 us  [weigh(): scores = jnp.dot(unit_a, unit_b.T, preferred_element_type=jnp.float32)]
    ppermute x2, waiting for transfers between devices: 8.38 us -> 7.56 us  [per_device(): lax.ppermute(by_across[bounds[i]:bounds[i + 1]], 'chip', ends)]
  transfers between devices with their start and end apart: 16 -> 16, of which waited for: 5 -> 5; matrix products, arithmetic and copies ran while one was open for 25% -> 26% of each run, Pallas kernels for 0% -> 0%
where the time goes in v24:
time: 81.7 us; the launch traced here: 81.5 us
  waiting for transfers between devices  37.7 us (46%)
  matrix products  20.2 us (25%)
  starting transfers between devices  16.7 us (20%)
  other arithmetic  6.22 us (8%)
    ppermute x1, waiting for transfers between devices, per_device(): lax.ppermute(mine, 'chip', exchange)  14.3 us
    dot_general x14, matrix products, weigh(): scores = jnp.dot(unit_a, unit_b.T, preferred_element_type=jnp.float32)  10.4 us
    dot_general x13, matrix products, pair_terms(): jnp.dot(weights.astype(jnp.bfloat16), got, preferred_element_type=jnp.flo...  9.22 us
    ppermute x3, waiting for transfers between devices, per_device(): lax.ppermute(outgoing, 'bucket', [(i, i ^ m) for i in range(buckets)])  8.93 us
    ppermute x2, waiting for transfers between devices, per_device(): lax.ppermute(by_across[bounds[i]:bounds[i + 1]], 'chip', ends)  7.56 us
    ppermute x1, waiting for transfers between devices, per_device(): lax.ppermute(by_across, 'chip', exchange)  6.86 us
    ppermute x3, starting transfers between devices, per_device(): lax.ppermute(outgoing, 'bucket', [(i, i ^ m) for i in range(buckets)])  4.57 us
    ppermute x1, starting transfers between devices, per_device(): lax.ppermute(mine, 'chip', exchange)  4.41 us
  transfers between devices with their start and end apart: 16, of which 5 were waited for; matrix products, arithmetic and copies ran while one was open for 26% of the time, Pallas kernels for 0%

profile of v24, /device:TPU:0, one launch (start us, length us, event | category | flops | bytes accessed | tf_op | source)
XLA Modules:
  0.0 81.5 jit_solution(10271532750966211414)
XLA Ops:
  0.0 1.5 %fusion.21 = bf16[4,128,768]{2,1,0:T(8,128)(2,1)S(1)} fusion(bf16[1,1,4,128,768]{4,3,2,1,0:T(8,128)(2,1)} %param.2, s32[4]{0:T(128)} %bitcast.41, pred[768]{0:T(1024)(128)(4,1)S(1)} %iota_compare_fusion.2), kind=kLoop, calls=%fused_computation.48 | loop fusion | flops 1179648 | bytes 1573648 | tf_op jit(solution)/shard_map/jit(_where)/select_n | solution.py:40
  1.6 3.0 %collective-permute-start = (bf16[128,768]{1,0:T(8,128)(2,1)S(1)}, bf16[128,768]{1,0:T(8,128)(2,1)S(1)}, u32[]{:S(2)}, u32[]{:S(2)}) collective-permute-start(bf16[128,768]{1,0:T(8,128)(2,1)S(1)} %get-tuple-element.15), channel_id=1, source_target_pairs={{0,8},{8,0},{16,24},{24,16},{1,9},{9,1},{17,25},{25,17},{2,10},{10... | collective-permute-start | bytes 589832 | tf_op jit(solution)/shard_map/ppermute | solution.py:44
  4.6 1.5 %collective-permute-start.1 = (bf16[128,768]{1,0:T(8,128)(2,1)S(1)}, bf16[128,768]{1,0:T(8,128)(2,1)S(1)}, u32[]{:S(2)}, u32[]{:S(2)}) collective-permute-start(bf16[128,768]{1,0:T(8,128)(2,1)S(1)} %get-tuple-element.14), channel_id=1, source_target_pairs={{0,16},{8,24},{16,0},{24,8},{1,17},{9,25},{17,1},{25,9},{2,18},{10... | collective-permute-start | bytes 589832 | tf_op jit(solution)/shard_map/ppermute | solution.py:44
  6.2 4.1 %collective-permute-done = bf16[128,768]{1,0:T(8,128)(2,1)S(1)} collective-permute-done((bf16[128,768]{1,0:T(8,128)(2,1)S(1)}, bf16[128,768]{1,0:T(8,128)(2,1)S(1)}, u32[]{:S(2)}, u32[]{:S(2)}) %collective-permute-start) | collective-permute-done | bytes 196640 | tf_op jit(solution)/shard_map/ppermute | solution.py:44
  10.4 4.8 %collective-permute-done.1 = bf16[128,768]{1,0:T(8,128)(2,1)S(1)} collective-permute-done((bf16[128,768]{1,0:T(8,128)(2,1)S(1)}, bf16[128,768]{1,0:T(8,128)(2,1)S(1)}, u32[]{:S(2)}, u32[]{:S(2)}) %collective-permute-start.1) | collective-permute-done | bytes 196640 | tf_op jit(solution)/shard_map/ppermute | solution.py:44
  15.2 0.7 collective-permute-start.5
  16.0 0.2 fusion
  16.2 4.4 %collective-permute-start.4 = (bf16[512,768]{1,0:T(8,128)(2,1)S(1)}, bf16[512,768]{1,0:T(8,128)(2,1)S(1)}, u32[]{:S(2)}, u32[]{:S(2)}) collective-permute-start(bf16[512,768]{1,0:T(8,128)(2,1)S(1)} %constant_dynamic-update-slice_fusion), channel_id=1, source_target_pairs={{0,2},{2,0},{4,6},{6,4},{1,3},{3,1},{5,7},{7,5},{8,10},{10,8},{12,... | collective-permute-start | bytes 2359304 | tf_op jit(solution)/shard_map/ppermute | solution.py:89
  20.7 0.8 %multiply_reduce_fusion.9 = (f32[512]{0:T(512)S(1)}, bf16[512,512]{0,1:T(8,128)(2,1)S(1)}) fusion(f32[512]{0:T(512)S(1)} %convert_reduce_fusion.9, bf16[512,768]{1,0:T(8,128)(2,1)S(1)} %constant_dynamic-update-slice_fusion, f32[512]{0:T(512)S(1)} %add_rsqrt_fusion.12), kind=kOutput, calls=%fused_computation.106 | convolution fusion | flops 406191616 | bytes 1316864 | tf_op jit(solution)/shard_map/dot_general | solution.py:23
  21.6 0.6 fusion.95
  22.2 0.2 fusion.6
  22.4 14.3 %collective-permute-done.4 = bf16[512,768]{1,0:T(8,128)(2,1)S(1)} collective-permute-done((bf16[512,768]{1,0:T(8,128)(2,1)S(1)}, bf16[512,768]{1,0:T(8,128)(2,1)S(1)}, u32[]{:S(2)}, u32[]{:S(2)}) %collective-permute-start.4) | collective-permute-done | bytes 786464 | tf_op jit(solution)/shard_map/ppermute | solution.py:89
  37.3 1.8 %collective-permute-start.8 = (bf16[512,768]{1,0:T(8,128)(2,1)S(1)}, bf16[512,768]{1,0:T(8,128)(2,1)S(1)}, u32[]{:S(2)}, u32[]{:S(2)}) collective-permute-start(bf16[512,768]{1,0:T(8,128)(2,1)S(1)} %collective-permute-done.5), channel_id=1, source_target_pairs={{0,2},{2,0},{4,6},{6,4},{1,3},{3,1},{5,7},{7,5},{8,10},{10,8},{12,... | collective-permute-start | bytes 2359304 | tf_op jit(solution)/shard_map/ppermute | solution.py:97
  39.1 0.7 collective-permute-start.9
  39.9 0.5 collective-permute-start.6
  40.7 0.8 multiply_reduce_fusion.6
  41.5 0.6 fusion.89
  42.1 0.8 multiply_reduce_fusion.7
  42.9 0.8 multiply_reduce_fusion.8
  43.7 0.6 fusion.91
  44.3 0.6 fusion.93
  45.0 1.3 %collective-permute-start.12 = (bf16[448,768]{1,0:T(8,128)(2,1)S(1)}, bf16[448,768]{1,0:T(8,128)(2,1)S(1)}, u32[]{:S(2)}, u32[]{:S(2)}) collective-permute-start(bf16[448,768]{1,0:T(8,128)(2,1)S(1)} %slice.74), channel_id=1, source_target_pairs={{4,6},{2,0},{5,7},{3,1},{12,14},{10,8},{13,15},{11,9},{20,22},{18,... | collective-permute-start | bytes 2064392 | tf_op jit(solution)/shard_map/ppermute | solution.py:102
  46.3 1.5 %collective-permute-start.13 = (bf16[64,768]{1,0:T(8,128)(2,1)S(1)}, bf16[64,768]{1,0:T(8,128)(2,1)S(1)}, u32[]{:S(2)}, u32[]{:S(2)}) collective-permute-start(bf16[64,768]{1,0:T(8,128)(2,1)S(1)} %slice.75), channel_id=1, source_target_pairs={{4,6},{2,0},{5,7},{3,1},{12,14},{10,8},{13,15},{11,9},{20,22},{18,... | collective-permute-start | bytes 294920 | tf_op jit(solution)/shard_map/ppermute | solution.py:102
  47.8 6.9 %collective-permute-done.8 = bf16[512,768]{1,0:T(8,128)(2,1)S(1)} collective-permute-done((bf16[512,768]{1,0:T(8,128)(2,1)S(1)}, bf16[512,768]{1,0:T(8,128)(2,1)S(1)}, u32[]{:S(2)}, u32[]{:S(2)}) %collective-permute-start.8) | collective-permute-done | bytes 786464 | tf_op jit(solution)/shard_map/ppermute | solution.py:97
  54.9 0.2 fusion.14
  56.1 0.6 collective-permute-start.11
  56.7 0.8 multiply_reduce_fusion.2
  57.5 0.6 fusion.81
  58.1 0.8 multiply_reduce_fusion.3
  58.9 0.6 fusion.83
  59.5 0.8 multiply_reduce_fusion.4
  60.3 0.6 fusion.85
  60.9 0.8 multiply_reduce_fusion.5
  61.7 0.6 fusion.87
  63.0 0.8 multiply_reduce_fusion.1
  63.8 0.6 fusion.79
  64.4 0.8 multiply_reduce_fusion
  65.2 1.2 %multiply_add_fusion = f32[512,768]{1,0:T(8,128)S(1)} fusion(f32[512,768]{1,0:T(8,128)S(1)} %fusion.79, f32[512,768]{1,0:T(8,128)S(1)} %fusion.81, f32[512,768]{1,0:T(8,128)S(1)} %fusion.83, f32[512,768]{1,0:T(8,128)S(1)} %fusion.85, f32[512,768]{1,0:T(8,128)S(1)} %fusion.87, f32[512,768]{1,0:T(8,128)S(1)} %fusion.89, f32[512,768]{1,0:T(8,128)S(1)} %fusion.91, ...), kind=kOutput, calls=%fused_computation.45 | convolution fusion | flops 409731072 | bytes 17039396 | tf_op jit(solution)/shard_map/dot_general | solution.py:76
  66.5 7.6 %collective-permute-done.13 = bf16[64,768]{1,0:T(8,128)(2,1)S(1)} collective-permute-done((bf16[64,768]{1,0:T(8,128)(2,1)S(1)}, bf16[64,768]{1,0:T(8,128)(2,1)S(1)}, u32[]{:S(2)}, u32[]{:S(2)}) %collective-permute-start.13) | collective-permute-done | bytes 98336 | tf_op jit(solution)/shard_map/ppermute | solution.py:102
  74.3 0.6 collective-permute-start.14
  75.2 0.7 multiply_reduce_fusion.11
  75.9 0.6 fusion.99
  76.5 0.5 multiply_reduce_fusion.13
  77.0 0.4 fusion.110
  77.6 0.5 multiply_reduce_fusion.12
  78.5 0.7 multiply_reduce_fusion.10
  79.2 0.6 fusion.97
  79.8 1.6 %fusion.51 = bf16[1,1,512,768]{3,2,1,0:T(8,128)(2,1)} fusion(bf16[64,768]{1,0:T(8,128)(2,1)S(1)} %collective-permute-done.15, f32[512,768]{1,0:T(8,128)S(1)} %fusion.110, f32[512,768]{1,0:T(8,128)S(1)} %fusion.97, f32[512,768]{1,0:T(8,128)S(1)} %multiply_add_fusion, f32[512,768]{1,0:T(8,128)S(1)} %fusion.99, f32[512]{0:T(512)S(1)} %convert_reduce_fusion.9, ...), kind=kOutput, calls=%fused_computation.90 | convolution fusion | flops 54657024 | bytes 7245832 | tf_op jit(solution)/shard_map/dot_general | solution.py:76
  (66 shorter events, 4.4 us)
Async XLA Ops:
  1.6 8.8 %collective-permute-start = (bf16[128,768]{1,0:T(8,128)(2,1)S(1)}, bf16[128,768]{1,0:T(8,128)(2,1)S(1)}, u32[]{:S(2)}, u32[]{:S(2)}) collective-permute-start(bf16[128,768]{1,0:T(8,128)(2,1)S(1)} %get-tuple-element.15), channel_id=1, source_target_pairs={{0,8},{8,0},{16,24},{24,16},{1,9},{9,1},{17,25},{25,17},{2,10},{10... | collective-permute-start | bytes 589832 | tf_op jit(solution)/shard_map/ppermute | solution.py:44
  4.6 10.6 %collective-permute-start.1 = (bf16[128,768]{1,0:T(8,128)(2,1)S(1)}, bf16[128,768]{1,0:T(8,128)(2,1)S(1)}, u32[]{:S(2)}, u32[]{:S(2)}) collective-permute-start(bf16[128,768]{1,0:T(8,128)(2,1)S(1)} %get-tuple-element.14), channel_id=1, source_target_pairs={{0,16},{8,24},{16,0},{24,8},{1,17},{9,25},{17,1},{25,9},{2,18},{10... | collective-permute-start | bytes 589832 | tf_op jit(solution)/shard_map/ppermute | solution.py:44
  6.1 9.1 %collective-permute-start.2 = (bf16[128,768]{1,0:T(8,128)(2,1)S(1)}, bf16[128,768]{1,0:T(8,128)(2,1)S(1)}, u32[]{:S(2)}, u32[]{:S(2)}) collective-permute-start(bf16[128,768]{1,0:T(8,128)(2,1)S(1)} %get-tuple-element.13), channel_id=1, source_target_pairs={{0,24},{8,16},{16,8},{24,0},{1,25},{9,17},{17,9},{25,1},{2,26},{10... | collective-permute-start | bytes 589832 | tf_op jit(solution)/shard_map/ppermute | solution.py:44
  15.2 6.9 %collective-permute-start.5 = (bf16[512,768]{1,0:T(8,128)(2,1)S(1)}, bf16[512,768]{1,0:T(8,128)(2,1)S(1)}, u32[]{:S(2)}, u32[]{:S(2)}) collective-permute-start(bf16[512,768]{1,0:T(8,128)(2,1)S(1)} %constant_dynamic-update-slice_fusion), channel_id=1, source_target_pairs={{2,4},{4,2},{3,5},{5,3},{10,12},{12,10},{11,13},{13,11},{18,20},{2... | collective-permute-start | bytes 2359304 | tf_op jit(solution)/shard_map/ppermute | solution.py:89
  16.2 20.6 %collective-permute-start.4 = (bf16[512,768]{1,0:T(8,128)(2,1)S(1)}, bf16[512,768]{1,0:T(8,128)(2,1)S(1)}, u32[]{:S(2)}, u32[]{:S(2)}) collective-permute-start(bf16[512,768]{1,0:T(8,128)(2,1)S(1)} %constant_dynamic-update-slice_fusion), channel_id=1, source_target_pairs={{0,2},{2,0},{4,6},{6,4},{1,3},{3,1},{5,7},{7,5},{8,10},{10,8},{12,... | collective-permute-start | bytes 2359304 | tf_op jit(solution)/shard_map/ppermute | solution.py:89
  20.6 16.4 %collective-permute-start.3 = (bf16[512,768]{1,0:T(8,128)(2,1)S(1)}, bf16[512,768]{1,0:T(8,128)(2,1)S(1)}, u32[]{:S(2)}, u32[]{:S(2)}) collective-permute-start(bf16[512,768]{1,0:T(8,128)(2,1)S(1)} %constant_dynamic-update-slice_fusion), channel_id=1, source_target_pairs={{0,1},{1,0},{2,3},{3,2},{4,5},{5,4},{6,7},{7,6},{8,9},{9,8},{10,11... | collective-permute-start | bytes 2359304 | tf_op jit(solution)/shard_map/ppermute | solution.py:90
  37.3 17.4 %collective-permute-start.8 = (bf16[512,768]{1,0:T(8,128)(2,1)S(1)}, bf16[512,768]{1,0:T(8,128)(2,1)S(1)}, u32[]{:S(2)}, u32[]{:S(2)}) collective-permute-start(bf16[512,768]{1,0:T(8,128)(2,1)S(1)} %collective-permute-done.5), channel_id=1, source_target_pairs={{0,2},{2,0},{4,6},{6,4},{1,3},{3,1},{5,7},{7,5},{8,10},{10,8},{12,... | collective-permute-start | bytes 2359304 | tf_op jit(solution)/shard_map/ppermute | solution.py:97
  39.1 5.9 %collective-permute-start.9 = (bf16[512,768]{1,0:T(8,128)(2,1)S(1)}, bf16[512,768]{1,0:T(8,128)(2,1)S(1)}, u32[]{:S(2)}, u32[]{:S(2)}) collective-permute-start(bf16[512,768]{1,0:T(8,128)(2,1)S(1)} %collective-permute-done.4), channel_id=1, source_target_pairs={{2,4},{4,2},{3,5},{5,3},{10,12},{12,10},{11,13},{13,11},{18,20},{2... | collective-permute-start | bytes 2359304 | tf_op jit(solution)/shard_map/ppermute | solution.py:97
  39.8 15.6 %collective-permute-start.7 = (bf16[512,768]{1,0:T(8,128)(2,1)S(1)}, bf16[512,768]{1,0:T(8,128)(2,1)S(1)}, u32[]{:S(2)}, u32[]{:S(2)}) collective-permute-start(bf16[512,768]{1,0:T(8,128)(2,1)S(1)} %collective-permute-done.5), channel_id=1, source_target_pairs={{0,1},{1,0},{2,3},{3,2},{4,5},{5,4},{6,7},{7,6},{8,9},{9,8},{10,11... | collective-permute-start | bytes 2359304 | tf_op jit(solution)/shard_map/ppermute | solution.py:114
  39.9 15.9 %collective-permute-start.6 = (bf16[512,768]{1,0:T(8,128)(2,1)S(1)}, bf16[512,768]{1,0:T(8,128)(2,1)S(1)}, u32[]{:S(2)}, u32[]{:S(2)}) collective-permute-start(bf16[512,768]{1,0:T(8,128)(2,1)S(1)} %collective-permute-done.4), channel_id=1, source_target_pairs={{0,1},{1,0},{2,3},{3,2},{4,5},{5,4},{6,7},{7,6},{8,9},{9,8},{10,11... | collective-permute-start | bytes 2359304 | tf_op jit(solution)/shard_map/ppermute | solution.py:113
  45.0 29.1 %collective-permute-start.12 = (bf16[448,768]{1,0:T(8,128)(2,1)S(1)}, bf16[448,768]{1,0:T(8,128)(2,1)S(1)}, u32[]{:S(2)}, u32[]{:S(2)}) collective-permute-start(bf16[448,768]{1,0:T(8,128)(2,1)S(1)} %slice.74), channel_id=1, source_target_pairs={{4,6},{2,0},{5,7},{3,1},{12,14},{10,8},{13,15},{11,9},{20,22},{18,... | collective-permute-start | bytes 2064392 | tf_op jit(solution)/shard_map/ppermute | solution.py:102
  46.3 27.7 %collective-permute-start.13 = (bf16[64,768]{1,0:T(8,128)(2,1)S(1)}, bf16[64,768]{1,0:T(8,128)(2,1)S(1)}, u32[]{:S(2)}, u32[]{:S(2)}) collective-permute-start(bf16[64,768]{1,0:T(8,128)(2,1)S(1)} %slice.75), channel_id=1, source_target_pairs={{4,6},{2,0},{5,7},{3,1},{12,14},{10,8},{13,15},{11,9},{20,22},{18,... | collective-permute-start | bytes 294920 | tf_op jit(solution)/shard_map/ppermute | solution.py:102
  54.6 7.6 %collective-permute-start.10 = (bf16[512,768]{1,0:T(8,128)(2,1)S(1)}, bf16[512,768]{1,0:T(8,128)(2,1)S(1)}, u32[]{:S(2)}, u32[]{:S(2)}) collective-permute-start(bf16[512,768]{1,0:T(8,128)(2,1)S(1)} %collective-permute-done.8), channel_id=1, source_target_pairs={{0,1},{1,0},{2,3},{3,2},{4,5},{5,4},{6,7},{7,6},{8,9},{9,8},{10,11... | collective-permute-start | bytes 2359304 | tf_op jit(solution)/shard_map/ppermute | solution.py:113
  56.1 6.4 %collective-permute-start.11 = (bf16[512,768]{1,0:T(8,128)(2,1)S(1)}, bf16[512,768]{1,0:T(8,128)(2,1)S(1)}, u32[]{:S(2)}, u32[]{:S(2)}) collective-permute-start(bf16[512,768]{1,0:T(8,128)(2,1)S(1)} %collective-permute-done.9), channel_id=1, source_target_pairs={{0,1},{1,0},{2,3},{3,2},{4,5},{5,4},{6,7},{7,6},{8,9},{9,8},{10,11... | collective-permute-start | bytes 2359304 | tf_op jit(solution)/shard_map/ppermute | solution.py:114
  74.0 3.4 %collective-permute-start.15 = (bf16[64,768]{1,0:T(8,128)(2,1)S(1)}, bf16[64,768]{1,0:T(8,128)(2,1)S(1)}, u32[]{:S(2)}, u32[]{:S(2)}) collective-permute-start(bf16[64,768]{1,0:T(8,128)(2,1)S(1)} %collective-permute-done.13), channel_id=1, source_target_pairs={{0,1},{1,0},{2,3},{3,2},{4,5},{5,4},{6,7},{7,6},{8,9},{9,8},{10,11... | collective-permute-start | bytes 294920 | tf_op jit(solution)/shard_map/ppermute | solution.py:107
  74.3 3.9 %collective-permute-start.14 = (bf16[448,768]{1,0:T(8,128)(2,1)S(1)}, bf16[448,768]{1,0:T(8,128)(2,1)S(1)}, u32[]{:S(2)}, u32[]{:S(2)}) collective-permute-start(bf16[448,768]{1,0:T(8,128)(2,1)S(1)} %collective-permute-done.12), channel_id=1, source_target_pairs={{0,1},{1,0},{2,3},{3,2},{4,5},{5,4},{6,7},{7,6},{8,9},{9,8},{10,11... | collective-permute-start | bytes 2064392 | tf_op jit(solution)/shard_map/ppermute | solution.py:107

commit v25 on v24

--- a/solution.py
+++ b/solution.py
@@ -97,7 +97,7 @@
             received = (lax.ppermute(by_across, "chip", exchange), lax.ppermute(by_exchange, "chip", across))
         elif step + 2 == chips:
             ends = [(chips - 2, chips - 1), (1, 0)]
-            bounds = [0, rows - rows // 8, rows]
+            bounds = [0, rows - 3 * rows // 16, rows]
             received = tuple(
                 lax.ppermute(by_across[bounds[i] : bounds[i + 1]], "chip", ends) for i in range(len(bounds) - 1)
             )

time: 81.7 us -> 81.6 us (level)
  no operation moved by 1% of the time
where the time goes in v25:
time: 81.6 us; the launch traced here: 81.4 us
  waiting for transfers between devices  37.7 us (46%)
  matrix products  20.2 us (25%)
  starting transfers between devices  16.7 us (20%)
  other arithmetic  6.2 us (8%)
    ppermute x1, waiting for transfers between devices, per_device(): lax.ppermute(mine, 'chip', exchange)  14.3 us
    dot_general x14, matrix products, weigh(): scores = jnp.dot(unit_a, unit_b.T, preferred_element_type=jnp.float32)  10.4 us
    dot_general x13, matrix products, pair_terms(): jnp.dot(weights.astype(jnp.bfloat16), got, preferred_element_type=jnp.flo...  9.22 us
    ppermute x3, waiting for transfers between devices, per_device(): lax.ppermute(outgoing, 'bucket', [(i, i ^ m) for i in range(buckets)])  8.93 us
    ppermute x2, waiting for transfers between devices, per_device(): lax.ppermute(by_across[bounds[i]:bounds[i + 1]], 'chip', ends)  7.56 us
    ppermute x1, waiting for transfers between devices, per_device(): lax.ppermute(by_across, 'chip', exchange)  6.86 us
    ppermute x3, starting transfers between devices, per_device(): lax.ppermute(outgoing, 'bucket', [(i, i ^ m) for i in range(buckets)])  4.57 us
    ppermute x1, starting transfers between devices, per_device(): lax.ppermute(mine, 'chip', exchange)  4.41 us
  transfers between devices with their start and end apart: 16, of which 5 were waited for; matrix products, arithmetic and copies ran while one was open for 26% of the time, Pallas kernels for 0%

profile of v25, /device:TPU:0, one launch (start us, length us, event | category | flops | bytes accessed | tf_op | source)
XLA Modules:
  0.0 81.4 jit_solution(16055046252359233878)
XLA Ops:
  0.0 1.5 %fusion.21 = bf16[4,128,768]{2,1,0:T(8,128)(2,1)S(1)} fusion(bf16[1,1,4,128,768]{4,3,2,1,0:T(8,128)(2,1)} %param.2, s32[4]{0:T(128)} %bitcast.41, pred[768]{0:T(1024)(128)(4,1)S(1)} %iota_compare_fusion.2), kind=kLoop, calls=%fused_computation.48 | loop fusion | flops 1179648 | bytes 1573648 | tf_op jit(solution)/shard_map/jit(_where)/select_n | solution.py:40
  1.6 3.0 %collective-permute-start = (bf16[128,768]{1,0:T(8,128)(2,1)S(1)}, bf16[128,768]{1,0:T(8,128)(2,1)S(1)}, u32[]{:S(2)}, u32[]{:S(2)}) collective-permute-start(bf16[128,768]{1,0:T(8,128)(2,1)S(1)} %get-tuple-element.15), channel_id=1, source_target_pairs={{0,8},{8,0},{16,24},{24,16},{1,9},{9,1},{17,25},{25,17},{2,10},{10... | collective-permute-start | bytes 589832 | tf_op jit(solution)/shard_map/ppermute | solution.py:44
  4.6 1.5 %collective-permute-start.1 = (bf16[128,768]{1,0:T(8,128)(2,1)S(1)}, bf16[128,768]{1,0:T(8,128)(2,1)S(1)}, u32[]{:S(2)}, u32[]{:S(2)}) collective-permute-start(bf16[128,768]{1,0:T(8,128)(2,1)S(1)} %get-tuple-element.14), channel_id=1, source_target_pairs={{0,16},{8,24},{16,0},{24,8},{1,17},{9,25},{17,1},{25,9},{2,18},{10... | collective-permute-start | bytes 589832 | tf_op jit(solution)/shard_map/ppermute | solution.py:44
  6.2 4.1 %collective-permute-done = bf16[128,768]{1,0:T(8,128)(2,1)S(1)} collective-permute-done((bf16[128,768]{1,0:T(8,128)(2,1)S(1)}, bf16[128,768]{1,0:T(8,128)(2,1)S(1)}, u32[]{:S(2)}, u32[]{:S(2)}) %collective-permute-start) | collective-permute-done | bytes 196640 | tf_op jit(solution)/shard_map/ppermute | solution.py:44
  10.4 4.8 %collective-permute-done.1 = bf16[128,768]{1,0:T(8,128)(2,1)S(1)} collective-permute-done((bf16[128,768]{1,0:T(8,128)(2,1)S(1)}, bf16[128,768]{1,0:T(8,128)(2,1)S(1)}, u32[]{:S(2)}, u32[]{:S(2)}) %collective-permute-start.1) | collective-permute-done | bytes 196640 | tf_op jit(solution)/shard_map/ppermute | solution.py:44
  15.2 0.7 collective-permute-start.5
  16.0 0.2 fusion
  16.2 4.4 %collective-permute-start.4 = (bf16[512,768]{1,0:T(8,128)(2,1)S(1)}, bf16[512,768]{1,0:T(8,128)(2,1)S(1)}, u32[]{:S(2)}, u32[]{:S(2)}) collective-permute-start(bf16[512,768]{1,0:T(8,128)(2,1)S(1)} %constant_dynamic-update-slice_fusion), channel_id=1, source_target_pairs={{0,2},{2,0},{4,6},{6,4},{1,3},{3,1},{5,7},{7,5},{8,10},{10,8},{12,... | collective-permute-start | bytes 2359304 | tf_op jit(solution)/shard_map/ppermute | solution.py:89
  20.7 0.8 %multiply_reduce_fusion.9 = (f32[512]{0:T(512)S(1)}, bf16[512,512]{0,1:T(8,128)(2,1)S(1)}) fusion(f32[512]{0:T(512)S(1)} %convert_reduce_fusion.9, bf16[512,768]{1,0:T(8,128)(2,1)S(1)} %constant_dynamic-update-slice_fusion, f32[512]{0:T(512)S(1)} %add_rsqrt_fusion.12), kind=kOutput, calls=%fused_computation.106 | convolution fusion | flops 406191616 | bytes 1316864 | tf_op jit(solution)/shard_map/dot_general | solution.py:23
  21.6 0.6 fusion.95
  22.2 0.2 fusion.6
  22.4 14.3 %collective-permute-done.4 = bf16[512,768]{1,0:T(8,128)(2,1)S(1)} collective-permute-done((bf16[512,768]{1,0:T(8,128)(2,1)S(1)}, bf16[512,768]{1,0:T(8,128)(2,1)S(1)}, u32[]{:S(2)}, u32[]{:S(2)}) %collective-permute-start.4) | collective-permute-done | bytes 786464 | tf_op jit(solution)/shard_map/ppermute | solution.py:89
  37.0 0.2 fusion.2
  37.3 1.8 %collective-permute-start.8 = (bf16[512,768]{1,0:T(8,128)(2,1)S(1)}, bf16[512,768]{1,0:T(8,128)(2,1)S(1)}, u32[]{:S(2)}, u32[]{:S(2)}) collective-permute-start(bf16[512,768]{1,0:T(8,128)(2,1)S(1)} %collective-permute-done.5), channel_id=1, source_target_pairs={{0,2},{2,0},{4,6},{6,4},{1,3},{3,1},{5,7},{7,5},{8,10},{10,8},{12,... | collective-permute-start | bytes 2359304 | tf_op jit(solution)/shard_map/ppermute | solution.py:97
  39.1 0.7 collective-permute-start.9
  39.9 0.5 collective-permute-start.6
  40.7 0.8 multiply_reduce_fusion.6
  41.5 0.6 fusion.89
  42.1 0.8 multiply_reduce_fusion.7
  42.9 0.8 multiply_reduce_fusion.8
  43.7 0.6 fusion.91
  44.3 0.6 fusion.93
  45.0 1.3 %collective-permute-start.12 = (bf16[416,768]{1,0:T(8,128)(2,1)S(1)}, bf16[416,768]{1,0:T(8,128)(2,1)S(1)}, u32[]{:S(2)}, u32[]{:S(2)}) collective-permute-start(bf16[416,768]{1,0:T(8,128)(2,1)S(1)} %slice.74), channel_id=1, source_target_pairs={{4,6},{2,0},{5,7},{3,1},{12,14},{10,8},{13,15},{11,9},{20,22},{18,... | collective-permute-start | bytes 1916936 | tf_op jit(solution)/shard_map/ppermute | solution.py:102
  46.3 1.5 %collective-permute-start.13 = (bf16[96,768]{1,0:T(8,128)(2,1)S(1)}, bf16[96,768]{1,0:T(8,128)(2,1)S(1)}, u32[]{:S(2)}, u32[]{:S(2)}) collective-permute-start(bf16[96,768]{1,0:T(8,128)(2,1)S(1)} %slice.75), channel_id=1, source_target_pairs={{4,6},{2,0},{5,7},{3,1},{12,14},{10,8},{13,15},{11,9},{20,22},{18,... | collective-permute-start | bytes 442376 | tf_op jit(solution)/shard_map/ppermute | solution.py:102
  47.8 6.9 %collective-permute-done.8 = bf16[512,768]{1,0:T(8,128)(2,1)S(1)} collective-permute-done((bf16[512,768]{1,0:T(8,128)(2,1)S(1)}, bf16[512,768]{1,0:T(8,128)(2,1)S(1)}, u32[]{:S(2)}, u32[]{:S(2)}) %collective-permute-start.8) | collective-permute-done | bytes 786464 | tf_op jit(solution)/shard_map/ppermute | solution.py:97
  56.1 0.6 collective-permute-start.11
  56.7 0.8 multiply_reduce_fusion.2
  57.5 0.6 fusion.81
  58.1 0.8 multiply_reduce_fusion.3
  58.9 0.6 fusion.83
  59.5 0.8 multiply_reduce_fusion.4
  60.3 0.6 fusion.85
  60.9 0.8 multiply_reduce_fusion.5
  61.7 0.6 fusion.87
  63.0 0.8 multiply_reduce_fusion.1
  63.8 0.6 fusion.79
  64.4 0.8 multiply_reduce_fusion
  65.2 1.2 %multiply_add_fusion = f32[512,768]{1,0:T(8,128)S(1)} fusion(f32[512,768]{1,0:T(8,128)S(1)} %fusion.79, f32[512,768]{1,0:T(8,128)S(1)} %fusion.81, f32[512,768]{1,0:T(8,128)S(1)} %fusion.83, f32[512,768]{1,0:T(8,128)S(1)} %fusion.85, f32[512,768]{1,0:T(8,128)S(1)} %fusion.87, f32[512,768]{1,0:T(8,128)S(1)} %fusion.89, f32[512,768]{1,0:T(8,128)S(1)} %fusion.91, ...), kind=kOutput, calls=%fused_computation.45 | convolution fusion | flops 409731072 | bytes 17039396 | tf_op jit(solution)/shard_map/dot_general | solution.py:76
  66.5 7.6 %collective-permute-done.13 = bf16[96,768]{1,0:T(8,128)(2,1)S(1)} collective-permute-done((bf16[96,768]{1,0:T(8,128)(2,1)S(1)}, bf16[96,768]{1,0:T(8,128)(2,1)S(1)}, u32[]{:S(2)}, u32[]{:S(2)}) %collective-permute-start.13) | collective-permute-done | bytes 147488 | tf_op jit(solution)/shard_map/ppermute | solution.py:102
  74.3 0.6 collective-permute-start.14
  75.2 0.7 multiply_reduce_fusion.11
  75.9 0.6 fusion.99
  76.5 0.5 multiply_reduce_fusion.13
  77.0 0.4 fusion.110
  77.6 0.5 multiply_reduce_fusion.12
  78.5 0.7 multiply_reduce_fusion.10
  79.2 0.6 fusion.97
  79.8 1.7 %fusion.47 = bf16[1,1,512,768]{3,2,1,0:T(8,128)(2,1)} fusion(bf16[96,768]{1,0:T(8,128)(2,1)S(1)} %collective-permute-done.15, f32[512,768]{1,0:T(8,128)S(1)} %fusion.110, f32[512,768]{1,0:T(8,128)S(1)} %fusion.97, f32[512,768]{1,0:T(8,128)S(1)} %multiply_add_fusion, f32[512,768]{1,0:T(8,128)S(1)} %fusion.99, f32[512]{0:T(512)S(1)} %convert_reduce_fusion.9, ...), kind=kOutput, calls=%fused_computation.86 | convolution fusion | flops 79822848 | bytes 7327752 | tf_op jit(solution)/shard_map/dot_general | solution.py:76
  (66 shorter events, 4.4 us)
Async XLA Ops:
  1.6 8.8 %collective-permute-start = (bf16[128,768]{1,0:T(8,128)(2,1)S(1)}, bf16[128,768]{1,0:T(8,128)(2,1)S(1)}, u32[]{:S(2)}, u32[]{:S(2)}) collective-permute-start(bf16[128,768]{1,0:T(8,128)(2,1)S(1)} %get-tuple-element.15), channel_id=1, source_target_pairs={{0,8},{8,0},{16,24},{24,16},{1,9},{9,1},{17,25},{25,17},{2,10},{10... | collective-permute-start | bytes 589832 | tf_op jit(solution)/shard_map/ppermute | solution.py:44
  4.6 10.6 %collective-permute-start.1 = (bf16[128,768]{1,0:T(8,128)(2,1)S(1)}, bf16[128,768]{1,0:T(8,128)(2,1)S(1)}, u32[]{:S(2)}, u32[]{:S(2)}) collective-permute-start(bf16[128,768]{1,0:T(8,128)(2,1)S(1)} %get-tuple-element.14), channel_id=1, source_target_pairs={{0,16},{8,24},{16,0},{24,8},{1,17},{9,25},{17,1},{25,9},{2,18},{10... | collective-permute-start | bytes 589832 | tf_op jit(solution)/shard_map/ppermute | solution.py:44
  6.1 9.1 %collective-permute-start.2 = (bf16[128,768]{1,0:T(8,128)(2,1)S(1)}, bf16[128,768]{1,0:T(8,128)(2,1)S(1)}, u32[]{:S(2)}, u32[]{:S(2)}) collective-permute-start(bf16[128,768]{1,0:T(8,128)(2,1)S(1)} %get-tuple-element.13), channel_id=1, source_target_pairs={{0,24},{8,16},{16,8},{24,0},{1,25},{9,17},{17,9},{25,1},{2,26},{10... | collective-permute-start | bytes 589832 | tf_op jit(solution)/shard_map/ppermute | solution.py:44
  15.2 6.9 %collective-permute-start.5 = (bf16[512,768]{1,0:T(8,128)(2,1)S(1)}, bf16[512,768]{1,0:T(8,128)(2,1)S(1)}, u32[]{:S(2)}, u32[]{:S(2)}) collective-permute-start(bf16[512,768]{1,0:T(8,128)(2,1)S(1)} %constant_dynamic-update-slice_fusion), channel_id=1, source_target_pairs={{2,4},{4,2},{3,5},{5,3},{10,12},{12,10},{11,13},{13,11},{18,20},{2... | collective-permute-start | bytes 2359304 | tf_op jit(solution)/shard_map/ppermute | solution.py:89
  16.2 20.6 %collective-permute-start.4 = (bf16[512,768]{1,0:T(8,128)(2,1)S(1)}, bf16[512,768]{1,0:T(8,128)(2,1)S(1)}, u32[]{:S(2)}, u32[]{:S(2)}) collective-permute-start(bf16[512,768]{1,0:T(8,128)(2,1)S(1)} %constant_dynamic-update-slice_fusion), channel_id=1, source_target_pairs={{0,2},{2,0},{4,6},{6,4},{1,3},{3,1},{5,7},{7,5},{8,10},{10,8},{12,... | collective-permute-start | bytes 2359304 | tf_op jit(solution)/shard_map/ppermute | solution.py:89
  20.6 16.4 %collective-permute-start.3 = (bf16[512,768]{1,0:T(8,128)(2,1)S(1)}, bf16[512,768]{1,0:T(8,128)(2,1)S(1)}, u32[]{:S(2)}, u32[]{:S(2)}) collective-permute-start(bf16[512,768]{1,0:T(8,128)(2,1)S(1)} %constant_dynamic-update-slice_fusion), channel_id=1, source_target_pairs={{0,1},{1,0},{2,3},{3,2},{4,5},{5,4},{6,7},{7,6},{8,9},{9,8},{10,11... | collective-permute-start | bytes 2359304 | tf_op jit(solution)/shard_map/ppermute | solution.py:90
  37.3 17.4 %collective-permute-start.8 = (bf16[512,768]{1,0:T(8,128)(2,1)S(1)}, bf16[512,768]{1,0:T(8,128)(2,1)S(1)}, u32[]{:S(2)}, u32[]{:S(2)}) collective-permute-start(bf16[512,768]{1,0:T(8,128)(2,1)S(1)} %collective-permute-done.5), channel_id=1, source_target_pairs={{0,2},{2,0},{4,6},{6,4},{1,3},{3,1},{5,7},{7,5},{8,10},{10,8},{12,... | collective-permute-start | bytes 2359304 | tf_op jit(solution)/shard_map/ppermute | solution.py:97
  39.1 5.9 %collective-permute-start.9 = (bf16[512,768]{1,0:T(8,128)(2,1)S(1)}, bf16[512,768]{1,0:T(8,128)(2,1)S(1)}, u32[]{:S(2)}, u32[]{:S(2)}) collective-permute-start(bf16[512,768]{1,0:T(8,128)(2,1)S(1)} %collective-permute-done.4), channel_id=1, source_target_pairs={{2,4},{4,2},{3,5},{5,3},{10,12},{12,10},{11,13},{13,11},{18,20},{2... | collective-permute-start | bytes 2359304 | tf_op jit(solution)/shard_map/ppermute | solution.py:97
  39.8 15.6 %collective-permute-start.7 = (bf16[512,768]{1,0:T(8,128)(2,1)S(1)}, bf16[512,768]{1,0:T(8,128)(2,1)S(1)}, u32[]{:S(2)}, u32[]{:S(2)}) collective-permute-start(bf16[512,768]{1,0:T(8,128)(2,1)S(1)} %collective-permute-done.5), channel_id=1, source_target_pairs={{0,1},{1,0},{2,3},{3,2},{4,5},{5,4},{6,7},{7,6},{8,9},{9,8},{10,11... | collective-permute-start | bytes 2359304 | tf_op jit(solution)/shard_map/ppermute | solution.py:114
  39.9 15.9 %collective-permute-start.6 = (bf16[512,768]{1,0:T(8,128)(2,1)S(1)}, bf16[512,768]{1,0:T(8,128)(2,1)S(1)}, u32[]{:S(2)}, u32[]{:S(2)}) collective-permute-start(bf16[512,768]{1,0:T(8,128)(2,1)S(1)} %collective-permute-done.4), channel_id=1, source_target_pairs={{0,1},{1,0},{2,3},{3,2},{4,5},{5,4},{6,7},{7,6},{8,9},{9,8},{10,11... | collective-permute-start | bytes 2359304 | tf_op jit(solution)/shard_map/ppermute | solution.py:113
  45.0 29.1 %collective-permute-start.12 = (bf16[416,768]{1,0:T(8,128)(2,1)S(1)}, bf16[416,768]{1,0:T(8,128)(2,1)S(1)}, u32[]{:S(2)}, u32[]{:S(2)}) collective-permute-start(bf16[416,768]{1,0:T(8,128)(2,1)S(1)} %slice.74), channel_id=1, source_target_pairs={{4,6},{2,0},{5,7},{3,1},{12,14},{10,8},{13,15},{11,9},{20,22},{18,... | collective-permute-start | bytes 1916936 | tf_op jit(solution)/shard_map/ppermute | solution.py:102
  46.3 27.7 %collective-permute-start.13 = (bf16[96,768]{1,0:T(8,128)(2,1)S(1)}, bf16[96,768]{1,0:T(8,128)(2,1)S(1)}, u32[]{:S(2)}, u32[]{:S(2)}) collective-permute-start(bf16[96,768]{1,0:T(8,128)(2,1)S(1)} %slice.75), channel_id=1, source_target_pairs={{4,6},{2,0},{5,7},{3,1},{12,14},{10,8},{13,15},{11,9},{20,22},{18,... | collective-permute-start | bytes 442376 | tf_op jit(solution)/shard_map/ppermute | solution.py:102
  54.6 7.6 %collective-permute-start.10 = (bf16[512,768]{1,0:T(8,128)(2,1)S(1)}, bf16[512,768]{1,0:T(8,128)(2,1)S(1)}, u32[]{:S(2)}, u32[]{:S(2)}) collective-permute-start(bf16[512,768]{1,0:T(8,128)(2,1)S(1)} %collective-permute-done.8), channel_id=1, source_target_pairs={{0,1},{1,0},{2,3},{3,2},{4,5},{5,4},{6,7},{7,6},{8,9},{9,8},{10,11... | collective-permute-start | bytes 2359304 | tf_op jit(solution)/shard_map/ppermute | solution.py:113
  56.1 6.4 %collective-permute-start.11 = (bf16[512,768]{1,0:T(8,128)(2,1)S(1)}, bf16[512,768]{1,0:T(8,128)(2,1)S(1)}, u32[]{:S(2)}, u32[]{:S(2)}) collective-permute-start(bf16[512,768]{1,0:T(8,128)(2,1)S(1)} %collective-permute-done.9), channel_id=1, source_target_pairs={{0,1},{1,0},{2,3},{3,2},{4,5},{5,4},{6,7},{7,6},{8,9},{9,8},{10,11... | collective-permute-start | bytes 2359304 | tf_op jit(solution)/shard_map/ppermute | solution.py:114
  74.0 3.3 %collective-permute-start.15 = (bf16[96,768]{1,0:T(8,128)(2,1)S(1)}, bf16[96,768]{1,0:T(8,128)(2,1)S(1)}, u32[]{:S(2)}, u32[]{:S(2)}) collective-permute-start(bf16[96,768]{1,0:T(8,128)(2,1)S(1)} %collective-permute-done.13), channel_id=1, source_target_pairs={{0,1},{1,0},{2,3},{3,2},{4,5},{5,4},{6,7},{7,6},{8,9},{9,8},{10,11... | collective-permute-start | bytes 442376 | tf_op jit(solution)/shard_map/ppermute | solution.py:107
  74.3 3.8 %collective-permute-start.14 = (bf16[416,768]{1,0:T(8,128)(2,1)S(1)}, bf16[416,768]{1,0:T(8,128)(2,1)S(1)}, u32[]{:S(2)}, u32[]{:S(2)}) collective-permute-start(bf16[416,768]{1,0:T(8,128)(2,1)S(1)} %collective-permute-done.12), channel_id=1, source_target_pairs={{0,1},{1,0},{2,3},{3,2},{4,5},{5,4},{6,7},{7,6},{8,9},{9,8},{10,11... | collective-permute-start | bytes 1916936 | tf_op jit(solution)/shard_map/ppermute | solution.py:107
